TPU v7x, 256 devices: a whole 4x4x8 slice. The times are simulated.
256 devices in a mesh: ctx: 32 (over x, z), tp: 8 (over y, core).
Axes of the slice: x: 4, y: 4, z: 8, core: 2. Of those that a mesh axis runs over, the one named last changes fastest.
Arguments:
- query_in: bfloat16 [16384, 4096], P('ctx', 'tp'), may hold values from -6 to 6
- key_in: bfloat16 [16384, 4096], P('ctx', 'tp'), may hold values from -6 to 6
- value_in: bfloat16 [16384, 4096], P('ctx', 'tp'), may hold values from -6 to 6
- out_grad: bfloat16 [16384, 4096], P('ctx', 'tp'), may hold values from -6 to 6
- doc_ids: int32 [16384], replicated, may hold values from 0 to 15, never falling along the last dimension, each value on 1 to 2048 neighbouring positions
- skip_gain: float32 [4096], P('tp'), may hold values from -4 to 4
- filter_taps: bfloat16 [2048, 8], P(('ctx', 'tp')), may hold values from -0.125 to 0.125
Outputs:
- mixed_out: bfloat16 [16384, 4096], P('ctx', 'tp')
- query_grad: bfloat16 [16384, 4096], P('ctx', 'tp')
- key_grad: bfloat16 [16384, 4096], P('ctx', 'tp')
- value_grad: bfloat16 [16384, 4096], P('ctx', 'tp')
- filter_grad: float32 [2048, 8], P(('ctx', 'tp'))
Inputs may be any that keep to these rules, and one draw needn't show every extreme that they name: `doc_ids`: ids never fall along the tokens; each document is 1 to 2048 tokens long and one is exactly 2048 long.
All inputs are finite; a program needn't handle non-finite values.
Results may differ from a plain program's by a relative error of at most 0.0049.
Values may be sent and summed in bfloat16 or wider, within the bound.
No kernel may reach another device: no remote copies, remote signals or barrier semaphores. Data moves between devices by JAX's collectives and lax.ppermute only.
A program may use at most 128 MiB of HBM per device.

v0:
```python
from functools import partial
import math

import jax
import jax.numpy as jnp
from jax import lax
from jax.sharding import PartitionSpec as P

MAXCH = 8
FGROUP = 512
FLEN = 2048


def passed_along(value, axis, steps):
    count = lax.axis_size(axis)
    leading, last = (max(0, -steps), min(count, count - steps))
    return lax.ppermute(value, axis, [(source, source + steps) for source in range(leading, last)])


def shear_toeplitz(window, stretch):
    groups_n = window.shape[0]
    reverse = window[:, ::-1]
    repeated = jnp.tile(reverse, (1, stretch))
    repeated = repeated[:, : stretch * (2 * stretch - 1)].reshape(
        groups_n, stretch, 2 * stretch - 1
    )
    return repeated[:, :, stretch - 1 :]


def diagonal_sums(matrix, stretch):
    groups_n = matrix.shape[0]
    flipped = matrix[:, :, ::-1]
    padded = jnp.concatenate([flipped, jnp.zeros_like(flipped)], axis=2)
    flat = padded.reshape(groups_n, 2 * stretch * stretch)[:, : stretch * (2 * stretch - 1)]
    return jnp.sum(flat.reshape(groups_n, stretch, 2 * stretch - 1), axis=1)


def pair_mask(ids_reader, ids_source, base):
    stretch = ids_reader.shape[0]
    offset = (
        base
        + lax.broadcasted_iota(jnp.int32, (stretch, stretch), 0)
        - lax.broadcasted_iota(jnp.int32, (stretch, stretch), 1)
    )
    same = ids_reader[:, None] == ids_source[None, :]
    return same & (offset >= 0)


def reader_terms(tile, mask, source, grad, with_back):
    stretch = tile.shape[1]
    masked = tile * mask.astype(tile.dtype)[None]
    ahead = jnp.einsum("gab,bgc->agc", masked, source, preferred_element_type=jnp.float32)
    product = jnp.einsum("agc,bgc->gab", grad, source, preferred_element_type=jnp.float32)
    diags = diagonal_sums(product * mask.astype(jnp.float32)[None], stretch)
    back_term = jnp.einsum("gab,agc->bgc", masked, grad, preferred_element_type=jnp.float32)
    return (ahead, diags, back_term)


def shards(query_in, key_in, value_in, out_grad, doc_ids, skip_gain, filter_taps):
    rows_here, width = query_in.shape
    stretch = rows_here // 2
    groups_here = width // FGROUP
    count = lax.axis_size("ctx")
    here = lax.axis_index("ctx")
    span = MAXCH // 2
    pieces = lax.all_to_all(filter_taps, "tp", split_axis=1, concat_axis=0, tiled=True)
    taps = lax.all_gather(pieces.T, "ctx", axis=1, tiled=True)
    blank = jnp.zeros((groups_here, stretch), taps.dtype)
    padded = jnp.concatenate([blank, taps, blank], axis=1)
    tiles = [
        shear_toeplitz(
            lax.slice_in_dim(padded, lag * stretch, lag * stretch + 2 * stretch, axis=1), stretch
        )
        for lag in range(MAXCH + 1)
    ]
    mixed_in = (key_in.astype(jnp.float32) * value_in.astype(jnp.float32)).astype(jnp.bfloat16)
    conv_grad = (out_grad.astype(jnp.float32) * query_in.astype(jnp.float32)).astype(jnp.bfloat16)
    received = [mixed_in] + [passed_along(mixed_in, "ctx", step) for step in range(1, span + 1)]
    sources = [panel.reshape(2, stretch, groups_here, FGROUP) for panel in received]
    grads = conv_grad.reshape(2, stretch, groups_here, FGROUP)
    skip_four = skip_gain.reshape(groups_here, FGROUP)

    def doc_rows(offset):
        device = here - offset
        valid = (device >= 0) & (device < count)
        start = jnp.clip(device, 0, count - 1) * rows_here
        ids = lax.dynamic_slice_in_dim(doc_ids, start, rows_here).reshape(2, stretch)
        return (ids, valid)

    own_ids = doc_rows(0)[0]
    pairs = [
        (step, reader, source, 2 * step + reader - source)
        for step in range(span + 1)
        for reader in range(2)
        for source in range(2)
        if 0 <= 2 * step + reader - source <= MAXCH
    ]
    zero_rows = jnp.zeros((stretch, groups_here, FGROUP), jnp.float32)
    state = [skip_four * sources[0][part].astype(jnp.float32) for part in range(2)]
    behind = {(step, part): zero_rows for step in range(span + 1) for part in range(2)}
    filter_ext = jnp.zeros((groups_here, (MAXCH + 2) * stretch), jnp.float32)
    for step, reader, source, lag in pairs:
        src_ids, valid = doc_rows(step)
        mask = pair_mask(own_ids[reader], src_ids[source], lag * stretch)
        work = partial(reader_terms, tiles[lag], mask, sources[step][source], grads[reader], True)
        ahead, diags, back_term = work()
        behind[step, source] = behind[step, source] + back_term
        state[reader] = state[reader] + ahead
        filter_ext = filter_ext.at[:, lag * stretch : lag * stretch + 2 * stretch - 1].add(diags)
    back_rows = [skip_four * grads[part].astype(jnp.float32) for part in range(2)]
    for part in range(2):
        back_rows[part] = back_rows[part] + behind[0, part]
    for step in range(1, span + 1):
        outgoing = jnp.stack([behind[step, 0], behind[step, 1]]).reshape(rows_here, width)
        arrived = passed_along(outgoing, "ctx", -step).reshape(2, stretch, groups_here, FGROUP)
        for part in range(2):
            back_rows[part] = back_rows[part] + arrived[part]
    conv = jnp.stack(state).reshape(rows_here, width)
    mixed_out = (query_in.astype(jnp.float32) * conv).astype(jnp.bfloat16)
    query_grad = (out_grad.astype(jnp.float32) * conv).astype(jnp.bfloat16)
    mixed_grad = jnp.stack(back_rows).reshape(rows_here, width)
    key_grad = (mixed_grad * value_in.astype(jnp.float32)).astype(jnp.bfloat16)
    value_grad = (mixed_grad * key_in.astype(jnp.float32)).astype(jnp.bfloat16)
    filter_part = filter_ext[:, stretch - 1 : stretch - 1 + FLEN]
    summed = lax.psum_scatter(filter_part, "ctx", scatter_dimension=1, tiled=True)
    scale = 1.0 / math.sqrt(FGROUP * count * rows_here)
    scaled = (summed * scale).T
    filter_grad = lax.all_to_all(scaled, "tp", split_axis=0, concat_axis=1, tiled=True)
    return (mixed_out, query_grad, key_grad, value_grad, filter_grad)


def solution(mesh):
    in_specs = (
        P("ctx", "tp"),
        P("ctx", "tp"),
        P("ctx", "tp"),
        P("ctx", "tp"),
        P(),
        P("tp"),
        P(("ctx", "tp"), None),
    )
    out_specs = (
        P("ctx", "tp"),
        P("ctx", "tp"),
        P("ctx", "tp"),
        P("ctx", "tp"),
        P(("ctx", "tp"), None),
    )
    return jax.shard_map(shards, mesh=mesh, in_specs=in_specs, out_specs=out_specs, check_vma=False)
```

profile of v0, /device:TPU:1, one launch (start us, length us, event | category | flops | bytes accessed | tf_op | source)
XLA Modules:
  0.0 676.4 jit_solution(2386910963862172028)
XLA Ops:
  7.2 1.4 copy.17
  8.5 6.4 all-to-all-start
  17.3 1.3 fusion.35
  19.8 63.1 %all-reduce.21 = bf16[2048]{0:T(1024)(128)(2,1)S(1)} all-reduce(bf16[2048]{0:T(1024)(128)(2,1)S(1)} %dynamic-update-slice.54), channel_id=1, replica_groups=mesh['ctx'=32,'tp'=8] {'ctx'}, use_global_device_ids=true, to_apply=%add.21 | all-reduce | flops 2048 | bytes 8192
  83.8 1.5 slice_reduce_fusion.18
  86.6 1.5 slice_reduce_fusion.19
  90.9 1.5 collective-permute-start.7
  93.2 1.5 slice_reduce_fusion.20
  96.0 1.5 slice_reduce_fusion.21
  100.6 1.5 collective-permute-start.6
  103.0 1.5 slice_reduce_fusion.22
  105.8 1.5 slice_reduce_fusion.23
  110.4 1.7 collective-permute-start.5
  112.9 1.5 slice_reduce_fusion.24
  115.7 1.5 slice_reduce_fusion.25
  128.3 1.5 slice_reduce_fusion.26
  130.7 76.6 %collective-permute-done.5 = f32[512,512]{1,0:T(8,128)} collective-permute-done((f32[512,512]{1,0:T(8,128)}, f32[512,512]{1,0:T(8,128)}, u32[]{:S(2)}, u32[]{:S(2)}) %collective-permute-start.5) | collective-permute-done | bytes 1048608 | tf_op jit(solution)/shard_map/ppermute | solution.py:17
  207.3 1.8 fusion.37
  209.0 1.8 fusion.42
  213.4 67.7 %collective-permute-start.3 = (bf16[512,512]{1,0:T(8,128)(2,1)S(1)}, bf16[512,512]{1,0:T(8,128)(2,1)}, u32[]{:S(2)}, u32[]{:S(2)}) collective-permute-start(bf16[512,512]{1,0:T(8,128)(2,1)S(1)} %get-tuple-element.223), channel_id=1, source_target_pairs={{0,32},{8,40},{16,48},{24,56},{32,64},{40,72},{48,80},{56,88},{64,... | collective-permute-start | bytes 1572872 | tf_op jit(solution)/shard_map/ppermute | solution.py:17
  281.1 2.2 collective-permute-start.2
  283.3 2.1 collective-permute-start.1
  285.4 2.8 collective-permute-start
  290.9 1.4 slice_reduce_fusion.17
  294.6 1.4 slice_reduce_fusion.16
  297.4 1.4 slice_reduce_fusion.15
  302.6 61.8 %collective-permute-done = bf16[512,512]{1,0:T(8,128)(2,1)} collective-permute-done((bf16[512,512]{1,0:T(8,128)(2,1)S(1)}, bf16[512,512]{1,0:T(8,128)(2,1)}, u32[]{:S(2)}, u32[]{:S(2)}) %collective-permute-start) | collective-permute-done | bytes 524320 | tf_op jit(solution)/shard_map/ppermute | solution.py:17
  366.5 1.4 slice_reduce_fusion.14
  371.6 1.4 slice_reduce_fusion.13
  375.7 1.4 slice_reduce_fusion.12
  379.9 1.4 slice_reduce_fusion.11
  386.2 1.4 slice_reduce_fusion.10
  390.6 1.4 slice_reduce_fusion.9
  394.6 1.4 slice_reduce_fusion.8
  399.6 1.4 slice_reduce_fusion.7
  406.0 1.4 slice_reduce_fusion.6
  410.2 1.4 slice_reduce_fusion.5
  414.2 1.4 slice_reduce_fusion.4
  419.2 1.4 slice_reduce_fusion.3
  425.6 1.4 slice_reduce_fusion.2
  429.6 1.4 slice_reduce_fusion.1
  435.2 1.4 slice_reduce_fusion
  438.2 1.4 copy.20
  457.3 1.4 fusion.28
  458.6 1.3 fusion.18
  460.1 192.2 %reduce-scatter.4.cloned.1.call-done = f32[64,1]{1,0:T(8,128)} async-done(((f32[2048,1]{1,0:T(8,128)}), f32[64,1]{1,0:T(8,128)}) %reduce-scatter.4.cloned.1.call-update) | async-done | bytes 272
  653.8 10.3 %all-to-all-start.1 = ((f32[8,8,1]{1,2,0:T(1,128)}), f32[8,8,1]{1,2,0:T(1,128)S(1)}, u32[]{:S(2)}, u32[]{:S(2)}) async-start(f32[8,8,1]{1,2,0:T(1,128)} %bitcast.143), calls=%async_computation.1 | async-start | bytes 8192 | tf_op jit(solution)/shard_map/all_to_all | solution.py:128
  665.3 3.3 all-to-all-done.1
  (315 shorter events, 118.3 us)
Async XLA Ops:
  8.5 11.0 %all-to-all-start = ((bf16[8,8,1]{0,2,1:T(2,128)(2,1)}), bf16[8,8,1]{0,2,1:T(2,128)(2,1)S(1)}, u32[]{:S(2)}, u32[]{:S(2)}) async-start(bf16[8,8,1]{0,2,1:T(2,128)(2,1)} %copy.17), calls=%async_computation | async-start | bytes 8192 | tf_op jit(solution)/shard_map/all_to_all | solution.py:66
  14.9 637.3 %reduce-scatter.4.cloned.1.call-start = ((), (), s32[]{:S(2)}) async-start(), calls=%async_computation.3 | async-start | bytes 1081344
  16.0 0.7 copy-start.21
  85.8 13.4 %copy-start.6 = (bf16[1,256,511]{2,1,0:T(8,128)(2,1)}, bf16[1,256,511]{2,1,0:T(8,128)(2,1)S(1)}, u32[]{:S(2)}) copy-start(bf16[1,256,511]{2,1,0:T(8,128)(2,1)S(1)} %reshape.2291) | copy-start | bytes 784900
  88.6 0.8 copy-start.8
  90.9 39.8 %collective-permute-start.7 = (f32[512,512]{1,0:T(8,128)}, f32[512,512]{1,0:T(8,128)S(1)}, u32[]{:S(2)}, u32[]{:S(2)}) collective-permute-start(f32[512,512]{1,0:T(8,128)} %bitcast.95), channel_id=1, source_target_pairs={{32,0},{40,8},{48,16},{56,24},{64,32},{72,40},{80,48},{88,56},{96,... | collective-permute-start | bytes 3145736 | tf_op jit(solution)/shard_map/ppermute | solution.py:17
  95.1 13.8 %copy-start.10 = (bf16[1,256,511]{2,1,0:T(8,128)(2,1)}, bf16[1,256,511]{2,1,0:T(8,128)(2,1)S(1)}, u32[]{:S(2)}) copy-start(bf16[1,256,511]{2,1,0:T(8,128)(2,1)S(1)} %reshape.2287) | copy-start | bytes 784900
  97.9 0.8 copy-start.12
  100.6 30.1 %collective-permute-start.6 = (f32[512,512]{1,0:T(8,128)}, f32[512,512]{1,0:T(8,128)}, u32[]{:S(2)}, u32[]{:S(2)}) collective-permute-start(f32[512,512]{1,0:T(8,128)} %bitcast.87), channel_id=1, source_target_pairs={{24,0},{32,8},{40,16},{48,24},{56,32},{64,40},{72,48},{80,56},{88,... | collective-permute-start | bytes 3145736 | tf_op jit(solution)/shard_map/ppermute | solution.py:17
  107.7 0.8 copy-start.14
  110.4 96.9 %collective-permute-start.5 = (f32[512,512]{1,0:T(8,128)}, f32[512,512]{1,0:T(8,128)}, u32[]{:S(2)}, u32[]{:S(2)}) collective-permute-start(f32[512,512]{1,0:T(8,128)} %bitcast.79), channel_id=1, source_target_pairs={{16,0},{24,8},{32,16},{40,24},{48,32},{56,40},{64,48},{72,56},{80,... | collective-permute-start | bytes 3145736 | tf_op jit(solution)/shard_map/ppermute | solution.py:17
  114.9 187.4 %copy-start.2 = (bf16[1,256,511]{2,1,0:T(8,128)(2,1)}, bf16[1,256,511]{2,1,0:T(8,128)(2,1)S(1)}, u32[]{:S(2)}) copy-start(bf16[1,256,511]{2,1,0:T(8,128)(2,1)S(1)} %reshape.2279) | copy-start | bytes 784900
  117.7 0.8 copy-start.4
  120.4 86.9 %collective-permute-start.4 = (f32[512,512]{1,0:T(8,128)}, f32[512,512]{1,0:T(8,128)}, u32[]{:S(2)}, u32[]{:S(2)}) collective-permute-start(f32[512,512]{1,0:T(8,128)} %bitcast.71), channel_id=1, source_target_pairs={{8,0},{16,8},{24,16},{32,24},{40,32},{48,40},{56,48},{64,56},{72,6... | collective-permute-start | bytes 3145736 | tf_op jit(solution)/shard_map/ppermute | solution.py:17
  130.3 77.0 %copy-start.20 = (f32[512]{0:T(512)S(1)}, f32[512]{0:T(512)}, u32[]{:S(2)}) copy-start(f32[512]{0:T(512)} %param.48) | copy-start | bytes 6148
  210.8 1.0 copy-start.16
  210.9 1.2 copy-start.17
  213.4 209.8 %collective-permute-start.3 = (bf16[512,512]{1,0:T(8,128)(2,1)S(1)}, bf16[512,512]{1,0:T(8,128)(2,1)}, u32[]{:S(2)}, u32[]{:S(2)}) collective-permute-start(bf16[512,512]{1,0:T(8,128)(2,1)S(1)} %get-tuple-element.223), channel_id=1, source_target_pairs={{0,32},{8,40},{16,48},{24,56},{32,64},{40,72},{48,80},{56,88},{64,... | collective-permute-start | bytes 1572872 | tf_op jit(solution)/shard_map/ppermute | solution.py:17
  281.1 122.7 %collective-permute-start.2 = (bf16[512,512]{1,0:T(8,128)(2,1)S(1)}, bf16[512,512]{1,0:T(8,128)(2,1)}, u32[]{:S(2)}, u32[]{:S(2)}) collective-permute-start(bf16[512,512]{1,0:T(8,128)(2,1)S(1)} %get-tuple-element.223), channel_id=1, source_target_pairs={{0,24},{8,32},{16,40},{24,48},{32,56},{40,64},{48,72},{56,80},{64,... | collective-permute-start | bytes 1572872 | tf_op jit(solution)/shard_map/ppermute | solution.py:17
  283.3 100.7 %collective-permute-start.1 = (bf16[512,512]{1,0:T(8,128)(2,1)S(1)}, bf16[512,512]{1,0:T(8,128)(2,1)}, u32[]{:S(2)}, u32[]{:S(2)}) collective-permute-start(bf16[512,512]{1,0:T(8,128)(2,1)S(1)} %get-tuple-element.223), channel_id=1, source_target_pairs={{0,16},{8,24},{16,32},{24,40},{32,48},{40,56},{48,64},{56,72},{64,... | collective-permute-start | bytes 1572872 | tf_op jit(solution)/shard_map/ppermute | solution.py:17
  285.4 78.9 %collective-permute-start = (bf16[512,512]{1,0:T(8,128)(2,1)S(1)}, bf16[512,512]{1,0:T(8,128)(2,1)}, u32[]{:S(2)}, u32[]{:S(2)}) collective-permute-start(bf16[512,512]{1,0:T(8,128)(2,1)S(1)} %get-tuple-element.223), channel_id=1, source_target_pairs={{0,8},{8,16},{16,24},{24,32},{32,40},{40,48},{48,56},{56,64},{64,7... | collective-permute-start | bytes 1572872 | tf_op jit(solution)/shard_map/ppermute | solution.py:17
  292.7 1.0 copy-start.19
  439.5 0.9 copy-start.9
  440.5 1.3 copy-start.13
  441.8 1.3 copy-start.7
  443.1 1.3 copy-start.15
  444.4 1.3 copy-start.11
  445.8 1.3 copy-start.5
  454.7 1.3 copy-start.3
  457.3 1.4 copy-start.18
  460.0 204.1 %copy-start = (bf16[512,512]{1,0:T(8,128)(2,1)S(1)}, bf16[512,512]{1,0:T(8,128)(2,1)}, u32[]{:S(2)}) copy-start(bf16[512,512]{1,0:T(8,128)(2,1)} %param.46) | copy-start | bytes 1572868
  460.0 204.1 %copy-start.1 = (bf16[512,512]{1,0:T(8,128)(2,1)S(1)}, bf16[512,512]{1,0:T(8,128)(2,1)}, u32[]{:S(2)}) copy-start(bf16[512,512]{1,0:T(8,128)(2,1)} %param.43) | copy-start | bytes 1572868
  653.8 14.8 %all-to-all-start.1 = ((f32[8,8,1]{1,2,0:T(1,128)}), f32[8,8,1]{1,2,0:T(1,128)S(1)}, u32[]{:S(2)}, u32[]{:S(2)}) async-start(f32[8,8,1]{1,2,0:T(1,128)} %bitcast.143), calls=%async_computation.1 | async-start | bytes 8192 | tf_op jit(solution)/shard_map/all_to_all | solution.py:128
Sparse Core Ops, SparseCore 0:
  439.7 212.5 reduce-scatter.3
where the time goes:
time: 684 us; the launch traced here: 676 us
  waiting for transfers between devices  334 us (49%)
  starting transfers between devices  97.5 us (14%)
  local copies, waits for them, and re-layouts  87.9 us (13%)
  blocking collectives  63.1 us (9%)
  matrix products  50.7 us (7%)
  other arithmetic  26.5 us (4%)
  between operations  16.6 us (2%)
    unnamed x2, waiting for transfers between devices  192 us
    ppermute x8, waiting for transfers between devices, passed_along(): lax.ppermute(value, axis, [(source, source + steps) for source in range(l...  138 us
    ppermute x8, starting transfers between devices, passed_along(): lax.ppermute(value, axis, [(source, source + steps) for source in range(l...  80.8 us
    unnamed x1, blocking collectives  63.1 us
    slice x18, local copies, waits for them, and re-layouts, diagonal_sums(): padded.reshape(groups_n, 2 * stretch * stretch)  24.5 us
    dot_general x18, matrix products, reader_terms(): jnp.einsum('gab,bgc->agc', masked, source, preferred_element_type=jnp.flo...  21.1 us
    unnamed x105, local copies, waits for them, and re-layouts  20.9 us
    dot_general x18, matrix products, reader_terms(): jnp.einsum('agc,bgc->gab', grad, source, preferred_element_type=jnp.float32)  19.8 us
  transfers between devices with their start and end apart: 11, of which 5 were waited for; matrix products, arithmetic and copies ran while one was open for 19% of the time, Pallas kernels for 0%

commit v1 on v0

v1 whole, which is shorter than its diff:
```python
import math

import jax
import jax.numpy as jnp
from jax import lax
from jax.sharding import PartitionSpec as P

MAXCH = 8
FGROUP = 512
FLEN = 2048


def shifted(value, axis, steps):
    count = lax.axis_size(axis)
    leading, last = (max(0, -steps), min(count, count - steps))
    return lax.ppermute(value, axis, [(source, source + steps) for source in range(leading, last)])


def band(window, rows, cols):
    groups_n = window.shape[0]
    flat = jnp.tile(window, (1, rows))[:, : rows * cols]
    return flat.reshape(groups_n, rows, cols)


def shards(query_in, key_in, value_in, out_grad, doc_ids, skip_gain, filter_taps):
    rows, width = query_in.shape
    groups_here = width // FGROUP
    here = lax.axis_index("ctx")
    span = -(-FLEN // rows)
    hist = span * rows
    wide = hist + rows
    assert hist == FLEN

    full_taps = lax.all_gather(filter_taps, ("ctx", "tp"), axis=0, tiled=True)
    first_group = lax.axis_index("tp") * groups_here
    taps = lax.dynamic_slice_in_dim(full_taps, first_group, groups_here, axis=1).T

    mixed_in = (key_in.astype(jnp.float32) * value_in.astype(jnp.float32)).astype(jnp.bfloat16)
    conv_grad = (out_grad.astype(jnp.float32) * query_in.astype(jnp.float32)).astype(jnp.bfloat16)

    ahead = [mixed_in]
    behind = [conv_grad]
    for _ in range(span):
        ahead.append(shifted(ahead[-1], "ctx", 1))
        behind.append(shifted(behind[-1], "ctx", -1))
    sources = jnp.concatenate(ahead[::-1], axis=0).reshape(wide, groups_here, FGROUP)
    readers = jnp.concatenate(behind, axis=0).reshape(wide, groups_here, FGROUP)

    ids_pad = jnp.concatenate(
        [jnp.full((hist,), -1, jnp.int32), doc_ids, jnp.full((hist,), -2, jnp.int32)]
    )
    ids_own = lax.dynamic_slice_in_dim(doc_ids, here * rows, rows)
    ids_src = lax.dynamic_slice_in_dim(ids_pad, here * rows, wide)
    ids_rdr = lax.dynamic_slice_in_dim(ids_pad, here * rows + hist, wide)
    same_src = ids_own[:, None] == ids_src[None, :]
    same_rdr = ids_own[:, None] == ids_rdr[None, :]

    zero_taps = jnp.zeros((groups_here, wide + 1 - FLEN), taps.dtype)
    fwd_window = jnp.concatenate([zero_taps[:, :1], taps[:, ::-1], zero_taps[:, 1:]], axis=1)
    bwd_window = jnp.concatenate([taps, zero_taps], axis=1)
    fwd_tile = jnp.where(same_src[None], band(fwd_window, rows, wide), 0)
    bwd_tile = jnp.where(same_rdr[None], band(bwd_window, rows, wide), 0)

    skip = skip_gain.reshape(groups_here, FGROUP)
    own_src = mixed_in.reshape(rows, groups_here, FGROUP)
    own_grad = conv_grad.reshape(rows, groups_here, FGROUP)
    conv = skip * own_src.astype(jnp.float32) + jnp.einsum(
        "gab,bgc->agc", fwd_tile, sources, preferred_element_type=jnp.float32
    )
    mixed_grad = skip * own_grad.astype(jnp.float32) + jnp.einsum(
        "gab,bgc->agc", bwd_tile, readers, preferred_element_type=jnp.float32
    )
    product = jnp.einsum("agc,bgc->gab", own_grad, sources, preferred_element_type=jnp.float32)
    product = jnp.where(same_src[None], product, 0.0)
    skewed = jnp.pad(product.reshape(groups_here, rows * wide), ((0, 0), (0, rows)))
    diag = jnp.sum(skewed.reshape(groups_here, rows, wide + 1), axis=1)
    filter_part = diag[:, 1 : hist + 1][:, ::-1]

    conv = conv.reshape(rows, width)
    mixed_grad = mixed_grad.reshape(rows, width)
    mixed_out = (query_in.astype(jnp.float32) * conv).astype(jnp.bfloat16)
    query_grad = (out_grad.astype(jnp.float32) * conv).astype(jnp.bfloat16)
    key_grad = (mixed_grad * value_in.astype(jnp.float32)).astype(jnp.bfloat16)
    value_grad = (mixed_grad * key_in.astype(jnp.float32)).astype(jnp.bfloat16)

    placed = jnp.zeros((FLEN, full_taps.shape[1]), jnp.float32)
    placed = lax.dynamic_update_slice_in_dim(placed, filter_part.T, first_group, axis=1)
    summed = lax.psum_scatter(placed, ("ctx", "tp"), scatter_dimension=0, tiled=True)
    tokens = lax.axis_size("ctx") * rows
    filter_grad = summed * (1.0 / math.sqrt(FGROUP * tokens))
    return (mixed_out, query_grad, key_grad, value_grad, filter_grad)


def solution(mesh):
    in_specs = (
        P("ctx", "tp"),
        P("ctx", "tp"),
        P("ctx", "tp"),
        P("ctx", "tp"),
        P(),
        P("tp"),
        P(("ctx", "tp"), None),
    )
    out_specs = (
        P("ctx", "tp"),
        P("ctx", "tp"),
        P("ctx", "tp"),
        P("ctx", "tp"),
        P(("ctx", "tp"), None),
    )
    return jax.shard_map(shards, mesh=mesh, in_specs=in_specs, out_specs=out_specs, check_vma=False)
```

time: 684 us -> 734 us (1.073)
  local copies, waits for them, and re-layouts: 87.9 us -> 228 us
  starting transfers between devices: 97.5 us -> 23.2 us
  matrix products: 50.7 us -> 12.6 us
  other arithmetic: 26.5 us -> 63.3 us
  waiting for transfers between devices: 334 us -> 300 us
  blocking collectives: 63.1 us -> 80.3 us
    ppermute x8, waiting for transfers between devices: 138 us -> 41.8 us  [shifted(): lax.ppermute(value, axis, [(source, source + steps) for source in range(l...]
    all_gather x0 -> x1, blocking collectives: none -> 80.3 us  [shards(): full_taps = lax.all_gather(filter_taps, ('ctx', 'tp'), axis=0, tiled=True)]
    unnamed x2, waiting for transfers between devices: 192 us -> 259 us
    unnamed x105 -> x61, local copies, waits for them, and re-layouts: 20.9 us -> 86.8 us
    unnamed x1 -> x0, blocking collectives: 63.1 us -> none
    select_n x0 -> x1, other arithmetic: none -> 58.1 us  [shards(): bwd_tile = jnp.where(same_rdr[None], band(bwd_window, rows, wide), 0)]
    pad x0 -> x1, local copies, waits for them, and re-layouts: none -> 57.9 us  [shards(): jnp.pad(product.reshape(groups_here, rows * wide), ((0, 0), (0, rows)))]
    ppermute x8, starting transfers between devices: 80.8 us -> 23.2 us  [shifted(): lax.ppermute(value, axis, [(source, source + steps) for source in range(l...]
  transfers between devices with their start and end apart: 11 -> 9, of which waited for: 5 -> 5; matrix products, arithmetic and copies ran while one was open for 19% -> 27% of each run, Pallas kernels for 0% -> 0%
where the time goes in v1:
time: 734 us; the launch traced here: 723 us
  waiting for transfers between devices  300 us (41%)
  local copies, waits for them, and re-layouts  228 us (31%)
  blocking collectives  80.3 us (11%)
  other arithmetic  63.3 us (9%)
  starting transfers between devices  23.2 us (3%)
  between operations  14.8 us (2%)
  matrix products  12.6 us (2%)
    unnamed x2, waiting for transfers between devices  259 us
    unnamed x61, local copies, waits for them, and re-layouts  86.8 us
    all_gather x1, blocking collectives, shards(): full_taps = lax.all_gather(filter_taps, ('ctx', 'tp'), axis=0, tiled=True)  80.3 us
    select_n x1, other arithmetic, shards(): bwd_tile = jnp.where(same_rdr[None], band(bwd_window, rows, wide), 0)  58.1 us
    pad x1, local copies, waits for them, and re-layouts, shards(): jnp.pad(product.reshape(groups_here, rows * wide), ((0, 0), (0, rows)))  57.9 us
    another operation x4, local copies, waits for them, and re-layouts, band(): flat = jnp.tile(window, (1, rows))[:, :rows * cols]  53.5 us
    ppermute x8, waiting for transfers between devices, shifted(): lax.ppermute(value, axis, [(source, source + steps) for source in range(l...  41.8 us
    ppermute x8, starting transfers between devices, shifted(): lax.ppermute(value, axis, [(source, source + steps) for source in range(l...  23.2 us
  transfers between devices with their start and end apart: 9, of which 5 were waited for; matrix products, arithmetic and copies ran while one was open for 27% of the time, Pallas kernels for 0%

profile of v1, /device:TPU:1, one launch (start us, length us, event | category | flops | bytes accessed | tf_op | source)
XLA Modules:
  0.0 722.8 jit_solution(13073037169013701247)
XLA Ops:
  7.2 1.3 copy.29
  8.5 1.4 copy.32
  10.9 1.3 collective-permute-start.4
  12.4 12.7 %collective-permute-done.4 = bf16[512,512]{0,1:T(8,128)(2,1)S(1)} collective-permute-done((bf16[512,512]{0,1:T(8,128)(2,1)S(1)}, bf16[512,512]{0,1:T(8,128)(2,1)S(1)}, u32[]{:S(2)}, u32[]{:S(2)}) %collective-permute-start.4) | collective-permute-done | bytes 524320 | tf_op jit(solution)/shard_map/ppermute | solution.py:16
  25.1 1.3 collective-permute-start.5
  26.4 5.3 broadcast_bitcast_fusion
  31.7 10.2 %copy.39 = s32[1,1,512,2560]{3,1,2,0:T(1,128)} copy(s32[1,1,512,2560]{3,2,1,0:T(8,128)} %get-tuple-element.32) | data formatting | bytes 10485760
  41.8 10.5 %copy.40 = s32[1,1,512,2560]{3,1,2,0:T(1,128)} copy(s32[1,1,512,2560]{3,2,1,0:T(8,128)} %get-tuple-element.31) | data formatting | bytes 10485760
  52.4 1.3 collective-permute-start.6
  53.7 2.7 broadcast_bitcast_fusion.2
  56.4 10.2 %copy.38 = s32[1,1,512,2560]{3,1,2,0:T(1,128)} copy(s32[1,1,512,2560]{3,2,1,0:T(8,128)} %broadcast_bitcast_fusion.2) | data formatting | bytes 10485760
  66.6 80.3 %all_gather.3 = bf16[2048,8]{1,0:T(8,128)(2,1)S(1)} all-gather(bf16[8,8]{1,0:T(8,128)(2,1)S(1)} %copy-done.17), channel_id=1, replica_groups=mesh['ctx'=32,'tp'=8] {'ctx','tp'}, dimensions={0}, use_global_device_ids=true | all-gather | bytes 32896 | tf_op jit(solution)/shard_map/all_gather | solution.py:34
  147.3 1.9 rev.6
  149.5 5.8 reshape.151
  155.3 26.5 %tile.24 = bf16[1,1311232]{1,0:T(2,128)(2,1)} reshape(bf16[1311232]{0:T(1024)(128)(2,1)} %reshape.151) | data formatting | bytes 5244928 | tf_op jit(solution)/shard_map/tile | solution.py:21
  182.0 5.8 reshape.153
  187.8 26.6 %tile.27 = bf16[1,1311232]{1,0:T(2,128)(2,1)} reshape(bf16[1311232]{0:T(1024)(128)(2,1)} %reshape.153) | data formatting | bytes 5244928 | tf_op jit(solution)/shard_map/tile | solution.py:21
  214.5 1.3 collective-permute-start.7
  215.8 58.1 %fusion.1 = (bf16[1310720]{0:T(1024)(128)(2,1)}, bf16[1310720]{0:T(1024)(128)(2,1)S(1)}) fusion(bf16[1,1311232]{1,0:T(2,128)(2,1)} %tile.27, s32[1,1310720]{1,0:T(1,128)} %bitcast.50, s32[1,1310720]{1,0:T(1,128)} %bitcast.49, bf16[1,1311232]{1,0:T(2,128)(2,1)} %tile.24, s32[1,1310720]{1,0:T(1,128)} %bitcast.48), kind=kLoop, calls=%fused_computation.5 | loop fusion | flops 5242880 | bytes 26214400 | tf_op jit(solution)/shard_map/jit(_where)/select_n | solution.py:62
  273.9 6.1 select_n.44
  280.0 2.0 copy.30
  282.0 2.1 copy.31
  284.1 2.0 constant_dynamic-update-slice_fusion.8
  286.2 2.0 constant_dynamic-update-slice_fusion.7
  288.1 1.9 constant_dynamic-update-slice_fusion.6
  290.1 1.9 constant_dynamic-update-slice_fusion.5
  292.0 4.4 fusion.7
  297.2 4.0 collective-permute-start
  301.2 10.8 %collective-permute-done = bf16[512,512]{0,1:T(8,128)(2,1)S(1)} collective-permute-done((bf16[512,512]{0,1:T(8,128)(2,1)S(1)}, bf16[512,512]{0,1:T(8,128)(2,1)S(1)}, u32[]{:S(2)}, u32[]{:S(2)}) %collective-permute-start) | collective-permute-done | bytes 524320 | tf_op jit(solution)/shard_map/ppermute | solution.py:16
  312.8 4.1 collective-permute-start.1
  317.0 9.9 %collective-permute-done.1 = bf16[512,512]{0,1:T(8,128)(2,1)S(1)} collective-permute-done((bf16[512,512]{0,1:T(8,128)(2,1)S(1)}, bf16[512,512]{0,1:T(8,128)(2,1)S(1)}, u32[]{:S(2)}, u32[]{:S(2)}) %collective-permute-start.1) | collective-permute-done | bytes 524320 | tf_op jit(solution)/shard_map/ppermute | solution.py:16
  327.7 4.9 collective-permute-start.2
  332.6 8.3 %collective-permute-done.2 = bf16[512,512]{0,1:T(8,128)(2,1)} collective-permute-done((bf16[512,512]{0,1:T(8,128)(2,1)S(1)}, bf16[512,512]{0,1:T(8,128)(2,1)}, u32[]{:S(2)}, u32[]{:S(2)}) %collective-permute-start.2) | collective-permute-done | bytes 524320 | tf_op jit(solution)/shard_map/ppermute | solution.py:16
  340.9 5.1 collective-permute-start.3
  346.0 4.1 select_n.41
  350.1 2.1 copy.36
  352.2 2.1 copy.37
  356.7 1.5 copy-done.1
  358.2 3.9 select_bitcast_fusion
  362.1 10.1 %copy.41 = f32[1,1,512,2560]{3,1,2,0:T(1,128)} copy(f32[1,1,512,2560]{3,2,1,0:T(8,128)} %select_bitcast_fusion) | data formatting | bytes 10485760
  372.3 57.9 %pad_reduce_fusion = f32[1311232]{0:T(1024)} fusion(f32[1,1310720]{1,0:T(1,128)} %bitcast.47), kind=kLoop, calls=%fused_computation.2 | loop fusion | bytes 10487808 | tf_op jit(solution)/shard_map/jit(_pad)/pad | solution.py:75
  430.1 8.6 %reshape.144 = f32[512,2561]{1,0:T(8,128)} reshape(f32[1311232]{0:T(1024)} %pad_reduce_fusion) | data formatting | bytes 10489856 | tf_op jit(solution)/shard_map/reshape | solution.py:76
  438.8 2.8 reduce_sum.11
  441.7 1.4 rev.7
  443.6 4.7 dynamic_update_slice.3
  449.3 4.3 fusion.10
  455.6 258.6 %all-reduce.5.cloned.1.call-done = f32[2048,8]{1,0:T(8,128)} async-done(((f32[2048,8]{1,0:T(8,128)}), f32[2048,8]{1,0:T(8,128)}) %all-reduce.5.cloned.1.call-update) | async-done | bytes 65552
  714.2 1.3 dynamic-slice_multiply_fusion
  (68 shorter events, 10.5 us)
Async XLA Ops:
  7.2 5.1 copy-start.16
  7.2 707.1 %all-reduce.5.cloned.1.call-start = ((), (), s32[]{:S(2)}) async-start(), calls=%async_computation | async-start | bytes 2097152
  8.5 23.2 %copy-start.3 = (bf16[512,512]{0,1:T(8,128)(2,1)}, bf16[512,512]{0,1:T(8,128)(2,1)S(1)}, u32[]{:S(2)}) copy-start(bf16[512,512]{0,1:T(8,128)(2,1)S(1)} %copy.29) | copy-start | bytes 1572868
  9.9 21.7 %copy-start.5 = (bf16[512,512]{0,1:T(8,128)(2,1)}, bf16[512,512]{0,1:T(8,128)(2,1)S(1)}, u32[]{:S(2)}) copy-start(bf16[512,512]{0,1:T(8,128)(2,1)S(1)} %copy.32) | copy-start | bytes 1572868
  10.9 14.2 %collective-permute-start.4 = (bf16[512,512]{0,1:T(8,128)(2,1)S(1)}, bf16[512,512]{0,1:T(8,128)(2,1)S(1)}, u32[]{:S(2)}, u32[]{:S(2)}) collective-permute-start(bf16[512,512]{0,1:T(8,128)(2,1)S(1)} %get-tuple-element.23), channel_id=1, source_target_pairs={{8,0},{16,8},{24,16},{32,24},{40,32},{48,40},{56,48},{64,56},{72,6... | collective-permute-start | bytes 1572872 | tf_op jit(solution)/shard_map/ppermute | solution.py:16
  25.1 6.5 copy-start.7
  25.1 27.3 %collective-permute-start.5 = (bf16[512,512]{0,1:T(8,128)(2,1)S(1)}, bf16[512,512]{0,1:T(8,128)(2,1)}, u32[]{:S(2)}, u32[]{:S(2)}) collective-permute-start(bf16[512,512]{0,1:T(8,128)(2,1)S(1)} %collective-permute-done.4), channel_id=1, source_target_pairs={{8,0},{16,8},{24,16},{32,24},{40,32},{48,40},{56,48},{64,56},{72,6... | collective-permute-start | bytes 1572872 | tf_op jit(solution)/shard_map/ppermute | solution.py:16
  52.4 162.1 %collective-permute-start.6 = (bf16[512,512]{0,1:T(8,128)(2,1)}, bf16[512,512]{0,1:T(8,128)(2,1)}, u32[]{:S(2)}, u32[]{:S(2)}) collective-permute-start(bf16[512,512]{0,1:T(8,128)(2,1)} %collective-permute-done.5), channel_id=1, source_target_pairs={{8,0},{16,8},{24,16},{32,24},{40,32},{48,40},{56,48},{64,56},{72,6... | collective-permute-start | bytes 1572872 | tf_op jit(solution)/shard_map/ppermute | solution.py:16
  56.4 10.2 %copy-start.17 = (bf16[8,8]{1,0:T(8,128)(2,1)S(1)}, bf16[8,8]{1,0:T(8,128)(2,1)}, u32[]{:S(2)}) copy-start(bf16[8,8]{1,0:T(8,128)(2,1)} %param.13) | copy-start | bytes 388
  214.5 75.6 %collective-permute-start.7 = (bf16[512,512]{0,1:T(8,128)(2,1)}, bf16[512,512]{0,1:T(8,128)(2,1)}, u32[]{:S(2)}, u32[]{:S(2)}) collective-permute-start(bf16[512,512]{0,1:T(8,128)(2,1)} %collective-permute-done.6), channel_id=1, source_target_pairs={{8,0},{16,8},{24,16},{32,24},{40,32},{48,40},{56,48},{64,56},{72,6... | collective-permute-start | bytes 1572872 | tf_op jit(solution)/shard_map/ppermute | solution.py:16
  282.0 9.9 %copy-start.18 = (f32[512]{0:T(512)S(1)}, f32[512]{0:T(512)}, u32[]{:S(2)}) copy-start(f32[512]{0:T(512)} %param.12) | copy-start | bytes 6148
  284.1 7.9 %copy-start.2 = (bf16[512,2560]{1,0:T(8,128)(2,1)S(1)}, bf16[512,2560]{1,0:T(8,128)(2,1)}, u32[]{:S(2)}) copy-start(bf16[512,2560]{1,0:T(8,128)(2,1)} %select_n.44) | copy-start | bytes 7864324
  284.1 7.9 %copy-start.14 = (bf16[512,512]{0,1:T(8,128)(2,1)S(1)}, bf16[512,512]{0,1:T(8,128)(2,1)}, u32[]{:S(2)}) copy-start(bf16[512,512]{0,1:T(8,128)(2,1)} %copy.30) | copy-start | bytes 1572868
  284.1 7.9 %copy-start.15 = (bf16[512,512]{0,1:T(8,128)(2,1)S(1)}, bf16[512,512]{0,1:T(8,128)(2,1)}, u32[]{:S(2)}) copy-start(bf16[512,512]{0,1:T(8,128)(2,1)} %copy.31) | copy-start | bytes 1572868
  296.4 0.8 copy-start.8
  297.2 14.8 %collective-permute-start = (bf16[512,512]{0,1:T(8,128)(2,1)S(1)}, bf16[512,512]{0,1:T(8,128)(2,1)S(1)}, u32[]{:S(2)}, u32[]{:S(2)}) collective-permute-start(bf16[512,512]{0,1:T(8,128)(2,1)S(1)} %get-tuple-element.26), channel_id=1, source_target_pairs={{0,8},{8,16},{16,24},{24,32},{32,40},{40,48},{48,56},{56,64},{64,7... | collective-permute-start | bytes 1572872 | tf_op jit(solution)/shard_map/ppermute | solution.py:16
  312.0 0.8 copy-start.10
  312.8 14.1 %collective-permute-start.1 = (bf16[512,512]{0,1:T(8,128)(2,1)S(1)}, bf16[512,512]{0,1:T(8,128)(2,1)S(1)}, u32[]{:S(2)}, u32[]{:S(2)}) collective-permute-start(bf16[512,512]{0,1:T(8,128)(2,1)S(1)} %collective-permute-done), channel_id=1, source_target_pairs={{0,8},{8,16},{16,24},{24,32},{32,40},{40,48},{48,56},{56,64},{64,7... | collective-permute-start | bytes 1572872 | tf_op jit(solution)/shard_map/ppermute | solution.py:16
  326.9 0.8 copy-start.12
  327.7 13.2 %collective-permute-start.2 = (bf16[512,512]{0,1:T(8,128)(2,1)S(1)}, bf16[512,512]{0,1:T(8,128)(2,1)}, u32[]{:S(2)}, u32[]{:S(2)}) collective-permute-start(bf16[512,512]{0,1:T(8,128)(2,1)S(1)} %collective-permute-done.1), channel_id=1, source_target_pairs={{0,8},{8,16},{16,24},{24,32},{32,40},{40,48},{48,56},{56,64},{64,7... | collective-permute-start | bytes 1572872 | tf_op jit(solution)/shard_map/ppermute | solution.py:16
  340.9 13.4 %collective-permute-start.3 = (bf16[512,512]{0,1:T(8,128)(2,1)}, bf16[512,512]{0,1:T(8,128)(2,1)}, u32[]{:S(2)}, u32[]{:S(2)}) collective-permute-start(bf16[512,512]{0,1:T(8,128)(2,1)} %collective-permute-done.2), channel_id=1, source_target_pairs={{0,8},{8,16},{16,24},{24,32},{32,40},{40,48},{48,56},{56,64},{64,7... | collective-permute-start | bytes 1572872 | tf_op jit(solution)/shard_map/ppermute | solution.py:16
  350.1 6.4 copy-start.13
  350.1 6.5 copy-start.11
  352.2 4.4 copy-start.9
  356.7 1.5 copy-start.1
  443.1 6.2 copy-start.4
  443.1 6.2 copy-start.6
  448.3 1.0 copy-start
Sparse Core Ops, SparseCore 0:
  449.4 264.7 all-reduce.4

commit v2 on v1

v2 whole, which is shorter than its diff:
```python
import math

import jax
import jax.numpy as jnp
from jax import lax
from jax.experimental import pallas as pl
from jax.experimental.pallas import tpu as pltpu
from jax.sharding import PartitionSpec as P

MAXCH = 8
FGROUP = 512
FLEN = 2048
C = 256
INTERPRET = False


def shifted(value, axis, steps):
    count = lax.axis_size(axis)
    leading, last = (max(0, -steps), min(count, count - steps))
    return lax.ppermute(value, axis, [(source, source + steps) for source in range(leading, last)])


def swapped(value, axis, bit):
    count = lax.axis_size(axis)
    return lax.ppermute(value, axis, [(source, source ^ bit) for source in range(count)])


def gather_chunks(chunk, axis):
    here = lax.axis_index(axis)
    count = lax.axis_size(axis)
    held = chunk
    bit = 1
    while bit < count:
        other = swapped(held, axis, bit)
        upper = (here & bit) != 0
        held = jnp.concatenate([jnp.where(upper, other, held), jnp.where(upper, held, other)])
        bit *= 2
    return held


def scatter_sums(vector, axis):
    here = lax.axis_index(axis)
    count = lax.axis_size(axis)
    held = vector
    bit = count // 2
    while bit >= 1:
        half = held.shape[0] // 2
        low, high = held[:half], held[half:]
        upper = (here & bit) != 0
        other = swapped(jnp.where(upper, low, high), axis, bit)
        held = jnp.where(upper, high, low) + other
        bit //= 2
    return held


def conv_kernel(fwd_rows, bwd_rows, ids_own, ids_rev, ids_src, ids_rdr, skip, src, grads, grads_rev,
                conv_out, mgrad_out, filt_out, fwd_tiles, bwd_tiles):
    lags = MAXCH + 1
    own = src.shape[0] - MAXCH * C
    parts = own // C
    for lag in range(lags):
        wide = jnp.broadcast_to(fwd_rows[lag : lag + 1, :], (C, 2 * C))
        fwd_tiles[lag] = pltpu.roll(wide, 0, 1, stride=1, stride_axis=0)[:, C:].astype(jnp.bfloat16)
        wide = jnp.broadcast_to(bwd_rows[lag : lag + 1, :], (C, 2 * C))
        bwd_tiles[lag] = pltpu.roll(wide, 0, 1, stride=1, stride_axis=0)[:, C:].astype(jnp.bfloat16)
    skip_row = skip[...]
    sums = [jnp.zeros((1, 2 * C), jnp.float32) for _ in range(lags)]
    for r in range(parts):
        rows = slice(r * C, (r + 1) * C)
        reader_ids = ids_own[rows, :]
        reader_rev = ids_rev[rows, :]
        own_rows = slice(MAXCH * C + r * C, MAXCH * C + (r + 1) * C)
        acc = skip_row * src[own_rows, :].astype(jnp.float32)
        grad_rev = grads_rev[rows, :]
        for j in range(MAXCH + parts):
            lag = MAXCH + r - j
            if not 0 <= lag <= MAXCH:
                continue
            cols = slice(j * C, (j + 1) * C)
            block = src[cols, :]
            same = reader_ids == ids_src[:, cols]
            tile = jnp.where(same, fwd_tiles[lag], jnp.zeros((), jnp.bfloat16))
            acc = acc + jnp.dot(tile, block, preferred_element_type=jnp.float32)
            prod = lax.dot_general(grad_rev, block, (((1,), (1,)), ((), ())),
                                   preferred_element_type=jnp.float32)
            prod = jnp.where(reader_rev == ids_src[:, cols], prod, 0.0)
            wide = jnp.concatenate([prod, jnp.zeros((C, C), jnp.float32)], axis=1)
            wide = pltpu.roll(wide, 0, 1, stride=1, stride_axis=0)
            sums[lag] = sums[lag] + jnp.sum(wide, axis=0, keepdims=True)
        conv_out[rows, :] = acc
    for s in range(parts):
        rows = slice(s * C, (s + 1) * C)
        source_ids = ids_own[rows, :]
        acc = skip_row * grads[rows, :].astype(jnp.float32)
        for lag in range(lags):
            j = s + lag
            cols = slice(j * C, (j + 1) * C)
            same = source_ids == ids_rdr[:, cols]
            tile = jnp.where(same, bwd_tiles[lag], jnp.zeros((), jnp.bfloat16))
            acc = acc + jnp.dot(tile, grads[cols, :], preferred_element_type=jnp.float32)
        mgrad_out[rows, :] = acc
    for lag in range(lags):
        filt_out[lag : lag + 1, :] = sums[lag]


def local_conv(taps, ids_own, ids_src, ids_rdr, skip, src, grads):
    own, width = grads.shape[0] - MAXCH * C, grads.shape[1]
    lags = MAXCH + 1
    big = jnp.concatenate([jnp.zeros((2 * C,), jnp.float32), taps.astype(jnp.float32),
                           jnp.zeros((2 * C,), jnp.float32)])
    fwd_rows = jnp.stack([big[C * lag + C + 1 : C * lag + 3 * C + 1][::-1] for lag in range(lags)])
    bwd_rows = jnp.stack([big[C * lag + C : C * lag + 3 * C] for lag in range(lags)])
    parts = own // C
    ids_rev = ids_own.reshape(parts, C)[:, ::-1].reshape(own, 1)
    grads_rev = grads[:own].reshape(parts, C, width)[:, ::-1].reshape(own, width)
    conv, mgrad, sums = pl.pallas_call(
        conv_kernel,
        out_shape=(
            jax.ShapeDtypeStruct((own, width), jnp.float32),
            jax.ShapeDtypeStruct((own, width), jnp.float32),
            jax.ShapeDtypeStruct((lags, 2 * C), jnp.float32),
        ),
        scratch_shapes=[pltpu.VMEM((lags, C, C), jnp.bfloat16), pltpu.VMEM((lags, C, C), jnp.bfloat16)],
        compiler_params=pltpu.CompilerParams(vmem_limit_bytes=60 * 1024 * 1024),
        interpret=INTERPRET,
    )(fwd_rows, bwd_rows, ids_own.reshape(own, 1), ids_rev, ids_src.reshape(1, -1),
      ids_rdr.reshape(1, -1), skip.reshape(1, width), src, grads, grads_rev)
    ext = sum(
        jnp.pad(sums[lag, : 2 * C - 1][::-1], (C * lag + 1, (lags + 1) * C - C * lag - 2 * C))
        for lag in range(lags)
    )
    return conv, mgrad, ext[C : C + FLEN]


def shards(query_in, key_in, value_in, out_grad, doc_ids, skip_gain, filter_taps):
    rows, width = query_in.shape
    assert width == FGROUP and rows % C == 0
    here = lax.axis_index("ctx")
    span = -(-FLEN // rows)
    hist = span * rows
    assert hist == MAXCH * C

    pieces = lax.all_to_all(filter_taps, "tp", split_axis=1, concat_axis=0, tiled=True)
    taps = gather_chunks(pieces[:, 0], "ctx")

    mixed_in = (key_in.astype(jnp.float32) * value_in.astype(jnp.float32)).astype(jnp.bfloat16)
    conv_grad = (out_grad.astype(jnp.float32) * query_in.astype(jnp.float32)).astype(jnp.bfloat16)

    ahead = [mixed_in]
    behind = [conv_grad]
    for _ in range(span):
        ahead.append(shifted(ahead[-1], "ctx", 1))
        behind.append(shifted(behind[-1], "ctx", -1))
    sources = jnp.concatenate(ahead[::-1], axis=0)
    readers = jnp.concatenate(behind, axis=0)

    ids_pad = jnp.concatenate(
        [jnp.full((hist,), -1, jnp.int32), doc_ids, jnp.full((hist,), -2, jnp.int32)]
    )
    ids_own = lax.dynamic_slice_in_dim(doc_ids, here * rows, rows)
    ids_src = lax.dynamic_slice_in_dim(ids_pad, here * rows, hist + rows)
    ids_rdr = lax.dynamic_slice_in_dim(ids_pad, here * rows + hist, hist + rows)

    conv, mixed_grad, filter_part = local_conv(taps, ids_own, ids_src, ids_rdr, skip_gain, sources, readers)

    mixed_out = (query_in.astype(jnp.float32) * conv).astype(jnp.bfloat16)
    query_grad = (out_grad.astype(jnp.float32) * conv).astype(jnp.bfloat16)
    key_grad = (mixed_grad * value_in.astype(jnp.float32)).astype(jnp.bfloat16)
    value_grad = (mixed_grad * key_in.astype(jnp.float32)).astype(jnp.bfloat16)

    summed = scatter_sums(filter_part, "ctx")
    tokens = lax.axis_size("ctx") * rows
    scaled = (summed * (1.0 / math.sqrt(FGROUP * tokens)))[:, None]
    filter_grad = lax.all_to_all(scaled, "tp", split_axis=0, concat_axis=1, tiled=True)
    return (mixed_out, query_grad, key_grad, value_grad, filter_grad)


def solution(mesh):
    in_specs = (
        P("ctx", "tp"),
        P("ctx", "tp"),
        P("ctx", "tp"),
        P("ctx", "tp"),
        P(),
        P("tp"),
        P(("ctx", "tp"), None),
    )
    out_specs = (
        P("ctx", "tp"),
        P("ctx", "tp"),
        P("ctx", "tp"),
        P("ctx", "tp"),
        P(("ctx", "tp"), None),
    )
    return jax.shard_map(shards, mesh=mesh, in_specs=in_specs, out_specs=out_specs, check_vma=False)
```

time: 734 us -> 142 us (0.19); the launches traced: 723 us -> 141 us
  waiting for transfers between devices: 300 us -> 37 us
  local copies, waits for them, and re-layouts: 228 us -> 26 us
  blocking collectives: 80.3 us -> 0 us
  other arithmetic: 63.3 us -> 7.53 us
  starting transfers between devices: 23.2 us -> 61.7 us
  between operations: 14.8 us -> 0.92 us
  matrix products: 12.6 us -> 0 us
  Pallas kernels: 0 us -> 8 us
    unnamed x2 -> x0, waiting for transfers between devices: 259 us -> none
    all_gather x1 -> x0, blocking collectives: 80.3 us -> none  [shards(): full_taps = lax.all_gather(filter_taps, ('ctx', 'tp'), axis=0, tiled=True)]
    unnamed x61 -> x37, local copies, waits for them, and re-layouts: 86.8 us -> 10.3 us
    select_n x1 -> x10, other arithmetic: 58.1 us -> 0.21 us  [the longest x5 0.11 us: gather_chunks(): jnp.where(upper, other, held)]
    pad x1 -> x0, local copies, waits for them, and re-layouts: 57.9 us -> none  [shards(): jnp.pad(product.reshape(groups_here, rows * wide), ((0, 0), (0, rows)))]
    another operation x4 -> x2, local copies, waits for them, and re-layouts: 53.5 us -> 2.48 us  [the longest x1 1.24 us: local_conv(): jnp.stack([big[C * lag + C + 1:C * lag + 3 * C + 1][::-1] for lag in rang...]
    ppermute x8, waiting for transfers between devices: 41.8 us -> 10.2 us  [shifted(): lax.ppermute(value, axis, [(source, source + steps) for source in range(l...]
    all_to_all x0 -> x2, starting transfers between devices: none -> 21.5 us  [the longest x1 15.1 us: shards(): lax.all_to_all(scaled, 'tp', split_axis=0, concat_axis=1, tiled=True)]
  transfers between devices with their start and end apart: 9 -> 20, of which waited for: 5 -> 12; matrix products, arithmetic and copies ran while one was open for 27% -> 19% of each run, Pallas kernels for 0% -> 0%
where the time goes in v2:
time: 142 us; the launch traced here: 141 us
  starting transfers between devices  61.7 us (43%)
  waiting for transfers between devices  37 us (26%)
  local copies, waits for them, and re-layouts  26 us (18%)
  Pallas kernels  8 us (6%)
  other arithmetic  7.53 us (5%)
    ppermute x10, waiting for transfers between devices, swapped(): lax.ppermute(value, axis, [(source, source ^ bit) for source in range(cou...  21.3 us
    ppermute x10, starting transfers between devices, swapped(): lax.ppermute(value, axis, [(source, source ^ bit) for source in range(cou...  20.7 us
    ppermute x8, starting transfers between devices, shifted(): lax.ppermute(value, axis, [(source, source + steps) for source in range(l...  19.5 us
    all_to_all x1, starting transfers between devices, shards(): lax.all_to_all(scaled, 'tp', split_axis=0, concat_axis=1, tiled=True)  15.1 us
    unnamed x37, local copies, waits for them, and re-layouts  10.3 us
    ppermute x8, waiting for transfers between devices, shifted(): lax.ppermute(value, axis, [(source, source + steps) for source in range(l...  10.2 us
    pallas_call x1, Pallas kernels, local_conv(): pl.pallas_call(conv_kernel, out_shape=(jax.ShapeDtypeStruct((own, width),...  8 us
    all_to_all x1, starting transfers between devices, shards(): lax.all_to_all(filter_taps, 'tp', split_axis=1, concat_axis=0, tiled=True)  6.41 us
  transfers between devices with their start and end apart: 20, of which 12 were waited for; matrix products, arithmetic and copies ran while one was open for 19% of the time, Pallas kernels for 0%

profile of v2, /device:TPU:1, one launch (start us, length us, event | category | flops | bytes accessed | tf_op | source)
XLA Modules:
  0.0 141.1 jit_solution(7106968493968099203)
XLA Ops:
  0.6 1.4 copy.23
  2.0 6.4 %all-to-all-start = ((bf16[8,8,1]{0,2,1:T(2,128)(2,1)}), bf16[8,8,1]{0,2,1:T(2,128)(2,1)S(1)}, u32[]{:S(2)}, u32[]{:S(2)}) async-start(bf16[8,8,1]{0,2,1:T(2,128)(2,1)} %copy.23), calls=%async_computation | async-start | bytes 8192 | tf_op jit(solution)/shard_map/all_to_all | solution.py:143
  8.4 4.5 %all-to-all-done = bf16[8,8,1]{0,2,1:T(2,128)(2,1)S(1)} async-done(((bf16[8,8,1]{0,2,1:T(2,128)(2,1)}), bf16[8,8,1]{0,2,1:T(2,128)(2,1)S(1)}, u32[]{:S(2)}, u32[]{:S(2)}) %all-to-all-start) | async-done | bytes 160 | tf_op jit(solution)/shard_map/all_to_all | solution.py:143
  13.1 1.2 collective-permute-start
  14.3 1.3 collective-permute-done
  15.6 2.7 %collective-permute-start.1 = (bf16[128]{0:T(256)(128)(2,1)S(1)}, bf16[128]{0:T(256)(128)(2,1)S(1)}, u32[]{:S(2)}, u32[]{:S(2)}) collective-permute-start(bf16[128]{0:T(256)(128)(2,1)S(1)} %pad_maximum_fusion.2), channel_id=1, source_target_pairs={{0,16},{8,24},{16,0},{24,8},{32,48},{40,56},{48,32},{56,40},{64,80... | collective-permute-start | bytes 776 | tf_op jit(solution)/shard_map/ppermute | solution.py:25
  18.3 1.3 fusion.2
  19.7 3.4 %collective-permute-start.5 = (bf16[512,512]{1,0:T(8,128)(2,1)S(1)}, bf16[512,512]{1,0:T(8,128)(2,1)S(1)}, u32[]{:S(2)}, u32[]{:S(2)}) collective-permute-start(bf16[512,512]{1,0:T(8,128)(2,1)S(1)} %fusion.2), channel_id=1, source_target_pairs={{0,8},{8,16},{16,24},{24,32},{32,40},{40,48},{48,56},{56,64},{64,7... | collective-permute-start | bytes 1572872 | tf_op jit(solution)/shard_map/ppermute | solution.py:20
  23.2 4.3 %collective-permute-start.2 = (bf16[256]{0:T(256)(128)(2,1)S(1)}, bf16[256]{0:T(256)(128)(2,1)S(1)}, u32[]{:S(2)}, u32[]{:S(2)}) collective-permute-start(bf16[256]{0:T(256)(128)(2,1)S(1)} %pad_maximum_fusion.3), channel_id=1, source_target_pairs={{0,32},{8,40},{16,48},{24,56},{32,0},{40,8},{48,16},{56,24},{64,96... | collective-permute-start | bytes 1544 | tf_op jit(solution)/shard_map/ppermute | solution.py:25
  27.4 2.1 %constant_dynamic-update-slice_fusion.9 = (bf16[2560,512]{1,0:T(8,128)(2,1)}, bf16[512,512]{1,0:T(8,128)(2,1)S(1)}) fusion(bf16[512,512]{1,0:T(8,128)(2,1)} %param.7, bf16[512,512]{1,0:T(8,128)(2,1)} %param.10), kind=kLoop, calls=%fused_computation.22 | loop fusion | flops 1048575 | bytes 2097152
  29.6 1.3 collective-permute-start.9
  30.9 6.0 %collective-permute-done.2 = bf16[256]{0:T(256)(128)(2,1)S(1)} collective-permute-done((bf16[256]{0:T(256)(128)(2,1)S(1)}, bf16[256]{0:T(256)(128)(2,1)S(1)}, u32[]{:S(2)}, u32[]{:S(2)}) %collective-permute-start.2) | collective-permute-done | bytes 544 | tf_op jit(solution)/shard_map/ppermute | solution.py:25
  36.9 1.3 collective-permute-start.3
  38.2 1.3 collective-permute-start.6
  39.6 2.7 %collective-permute-done.9 = bf16[512,512]{1,0:T(8,128)(2,1)S(1)} collective-permute-done((bf16[512,512]{1,0:T(8,128)(2,1)S(1)}, bf16[512,512]{1,0:T(8,128)(2,1)S(1)}, u32[]{:S(2)}, u32[]{:S(2)}) %collective-permute-start.9) | collective-permute-done | bytes 524320 | tf_op jit(solution)/shard_map/ppermute | solution.py:20
  42.3 1.3 collective-permute-start.10
  43.6 3.9 %collective-permute-done.6 = bf16[512,512]{1,0:T(8,128)(2,1)S(1)} collective-permute-done((bf16[512,512]{1,0:T(8,128)(2,1)S(1)}, bf16[512,512]{1,0:T(8,128)(2,1)S(1)}, u32[]{:S(2)}, u32[]{:S(2)}) %collective-permute-start.6) | collective-permute-done | bytes 524320 | tf_op jit(solution)/shard_map/ppermute | solution.py:20
  47.5 4.9 %collective-permute-start.7 = (bf16[512,512]{1,0:T(8,128)(2,1)S(1)}, bf16[512,512]{1,0:T(8,128)(2,1)}, u32[]{:S(2)}, u32[]{:S(2)}) collective-permute-start(bf16[512,512]{1,0:T(8,128)(2,1)S(1)} %collective-permute-done.6), channel_id=1, source_target_pairs={{0,8},{8,16},{16,24},{24,32},{32,40},{40,48},{48,56},{56,64},{64,7... | collective-permute-start | bytes 1572872 | tf_op jit(solution)/shard_map/ppermute | solution.py:20
  52.4 4.2 %collective-permute-start.4 = (bf16[1024]{0:T(1024)(128)(2,1)S(1)}, bf16[1024]{0:T(1024)(128)(2,1)S(1)}, u32[]{:S(2)}, u32[]{:S(2)}) collective-permute-start(bf16[1024]{0:T(1024)(128)(2,1)S(1)} %pad_maximum_fusion), channel_id=1, source_target_pairs={{0,128},{8,136},{16,144},{24,152},{32,160},{40,168},{48,176},{56,1... | collective-permute-start | bytes 6152 | tf_op jit(solution)/shard_map/ppermute | solution.py:25
  58.1 0.9 copy.29
  59.0 0.9 copy.24.ids_own
  59.9 5.1 %rev.70 = bf16[2,256,512]{2,1,0:T(8,128)(2,1)} reverse(bf16[2,256,512]{2,1,0:T(8,128)(2,1)S(1)} %bitcast.52), dimensions={1} | reverse | bytes 1048576 | tf_op jit(solution)/shard_map/rev | solution.py:115
  65.0 1.3 collective-permute-start.11
  66.3 4.8 %collective-permute-start.8 = (bf16[512,512]{1,0:T(8,128)(2,1)}, bf16[512,512]{1,0:T(8,128)(2,1)}, u32[]{:S(2)}, u32[]{:S(2)}) collective-permute-start(bf16[512,512]{1,0:T(8,128)(2,1)} %collective-permute-done.7), channel_id=1, source_target_pairs={{0,8},{8,16},{16,24},{24,32},{32,40},{40,48},{48,56},{56,64},{64,7... | collective-permute-start | bytes 1572872 | tf_op jit(solution)/shard_map/ppermute | solution.py:20
  72.0 1.2 stack.69.fwd_rows
  73.3 1.2 stack.79.bwd_rows
  74.5 0.8 constant_dynamic-update-slice_fusion.8
  75.3 1.9 %constant_dynamic-update-slice_fusion.7 = bf16[2560,512]{1,0:T(8,128)(2,1)} fusion(bf16[2560,512]{1,0:T(8,128)(2,1)} %constant_dynamic-update-slice_fusion.8, bf16[512,512]{1,0:T(8,128)(2,1)} %collective-permute-done.10), kind=kLoop, calls=%fused_computation.20 | loop fusion | bytes 1048576
  77.2 1.3 collective-permute-start.12
  78.5 1.9 %constant_dynamic-update-slice_fusion.6 = bf16[2560,512]{1,0:T(8,128)(2,1)} fusion(bf16[2560,512]{1,0:T(8,128)(2,1)} %constant_dynamic-update-slice_fusion.7, bf16[512,512]{1,0:T(8,128)(2,1)} %collective-permute-done.11), kind=kLoop, calls=%fused_computation.19 | loop fusion | bytes 1048576
  80.4 1.1 constant_dynamic-update-slice_fusion.4
  81.5 1.1 constant_dynamic-update-slice_fusion.3
  82.6 1.1 constant_dynamic-update-slice_fusion.2
  83.8 3.6 %collective-permute-done.12 = bf16[512,512]{1,0:T(8,128)(2,1)S(1)} collective-permute-done((bf16[512,512]{1,0:T(8,128)(2,1)}, bf16[512,512]{1,0:T(8,128)(2,1)S(1)}, u32[]{:S(2)}, u32[]{:S(2)}) %collective-permute-start.12) | collective-permute-done | bytes 524320 | tf_op jit(solution)/shard_map/ppermute | solution.py:20
  87.3 0.9 constant_dynamic-update-slice_fusion.5.grads
  88.2 8.0 %shard_map.110 = (f32[512,512]{1,0:T(8,128)}, f32[512,512]{1,0:T(8,128)}, f32[9,512]{1,0:T(8,128)}) custom-call(f32[9,512]{1,0:T(8,128)} %stack.69.fwd_rows, f32[9,512]{1,0:T(8,128)} %stack.79.bwd_rows, s32[512,1]{1,0:T(8,128)} %copy.24.ids_own, s32[512,1]{1,0:T(8,128)} %bitcast.53, s32[1,2560]{1,0:T(1,128)} %reshape.45.ids_src, s32[1,2560]{1,0:T(1,128)} %reshape.46.ids_rdr, ...), custom_call_target="tpu_custom_call" | custom-call | tf_op jit(solution)/shard_map/pallas_call | solution.py:116
  96.2 1.0 fusion.11
  98.9 3.2 %collective-permute-start.13 = (f32[1024]{0:T(1024)S(1)}, f32[1024]{0:T(1024)S(1)}, u32[]{:S(2)}, u32[]{:S(2)}) collective-permute-start(f32[1024]{0:T(1024)S(1)} %slice_select_fusion), channel_id=1, source_target_pairs={{0,128},{8,136},{16,144},{24,152},{32,160},{40,168},{48,176},{56,1... | collective-permute-start | bytes 12296 | tf_op jit(solution)/shard_map/ppermute | solution.py:25
  102.1 1.0 collective-permute-done.13
  103.1 3.6 %collective-permute-start.14 = (f32[512]{0:T(512)S(1)}, f32[512]{0:T(512)S(1)}, u32[]{:S(2)}, u32[]{:S(2)}) collective-permute-start(f32[512]{0:T(512)S(1)} %slice_select_fusion.1), channel_id=1, source_target_pairs={{0,64},{8,72},{16,80},{24,88},{32,96},{40,104},{48,112},{56,120},{... | collective-permute-start | bytes 6152 | tf_op jit(solution)/shard_map/ppermute | solution.py:25
  106.7 1.0 collective-permute-done.14
  107.8 6.3 %collective-permute-done.15 = f32[256]{0:T(256)S(1)} collective-permute-done((f32[256]{0:T(256)S(1)}, f32[256]{0:T(256)S(1)}, u32[]{:S(2)}, u32[]{:S(2)}) %collective-permute-start.15) | collective-permute-done | bytes 1056 | tf_op jit(solution)/shard_map/ppermute | solution.py:25
  114.2 3.3 %collective-permute-done.16 = f32[128]{0:T(128)S(1)} collective-permute-done((f32[128]{0:T(128)S(1)}, f32[128]{0:T(128)S(1)}, u32[]{:S(2)}, u32[]{:S(2)}) %collective-permute-start.16) | collective-permute-done | bytes 544 | tf_op jit(solution)/shard_map/ppermute | solution.py:25
  117.6 2.4 %collective-permute-done.17 = f32[64]{0:T(128)S(1)} collective-permute-done((f32[64]{0:T(128)S(1)}, f32[64]{0:T(128)S(1)}, u32[]{:S(2)}, u32[]{:S(2)}) %collective-permute-start.17) | collective-permute-done | bytes 288 | tf_op jit(solution)/shard_map/ppermute | solution.py:25
  120.1 0.7 all_to_all.29
  120.8 15.1 %all-to-all-start.1 = ((f32[8,8,1]{1,2,0:T(1,128)}), f32[8,8,1]{1,2,0:T(1,128)S(1)}, u32[]{:S(2)}, u32[]{:S(2)}) async-start(f32[8,8,1]{1,2,0:T(1,128)} %bitcast.33), calls=%async_computation.1 | async-start | bytes 8192 | tf_op jit(solution)/shard_map/all_to_all | solution.py:174
  135.9 3.5 %fusion.1 = (bf16[512,512]{1,0:T(8,128)(2,1)}, bf16[512,512]{1,0:T(8,128)(2,1)}, bf16[512,512]{1,0:T(8,128)(2,1)}, bf16[512,512]{1,0:T(8,128)(2,1)}) fusion(f32[512,512]{1,0:T(8,128)} %get-tuple-element.9, bf16[512,512]{1,0:T(8,128)(2,1)S(1)} %copy-done.2, bf16[512,512]{1,0:T(8,128)(2,1)S(1)} %copy-done.1, f32[512,512]{1,0:T(8,128)} %get-tuple-element.8, ...), kind=kLoop, calls=%fused_computation.7 | loop fusion | flops 3145728 | bytes 6291456 | tf_op jit(solution)/shard_map/convert_element_type | solution.py:169
  139.4 1.0 all-to-all-done.1
  (85 shorter events, 5.7 us)
Async XLA Ops:
  0.6 38.9 %copy-start.4 = (s32[16384]{0:T(1024)S(1)}, s32[16384]{0:T(1024)}, u32[]{:S(2)}) copy-start(s32[16384]{0:T(1024)} %param.11) | copy-start | bytes 196612
  2.0 11.0 %all-to-all-start = ((bf16[8,8,1]{0,2,1:T(2,128)(2,1)}), bf16[8,8,1]{0,2,1:T(2,128)(2,1)S(1)}, u32[]{:S(2)}, u32[]{:S(2)}) async-start(bf16[8,8,1]{0,2,1:T(2,128)(2,1)} %copy.23), calls=%async_computation | async-start | bytes 8192 | tf_op jit(solution)/shard_map/all_to_all | solution.py:143
  13.1 2.4 %collective-permute-start = (bf16[64]{0:T(256)(128)(2,1)S(1)}, bf16[64]{0:T(256)(128)(2,1)S(1)}, u32[]{:S(2)}, u32[]{:S(2)}) collective-permute-start(bf16[64]{0:T(256)(128)(2,1)S(1)} %squeeze.30), channel_id=1, source_target_pairs={{0,8},{8,0},{16,24},{24,16},{32,40},{40,32},{48,56},{56,48},{64,72... | collective-permute-start | bytes 392 | tf_op jit(solution)/shard_map/ppermute | solution.py:25
  15.6 7.5 %collective-permute-start.1 = (bf16[128]{0:T(256)(128)(2,1)S(1)}, bf16[128]{0:T(256)(128)(2,1)S(1)}, u32[]{:S(2)}, u32[]{:S(2)}) collective-permute-start(bf16[128]{0:T(256)(128)(2,1)S(1)} %pad_maximum_fusion.2), channel_id=1, source_target_pairs={{0,16},{8,24},{16,0},{24,8},{32,48},{40,56},{48,32},{56,40},{64,80... | collective-permute-start | bytes 776 | tf_op jit(solution)/shard_map/ppermute | solution.py:25
  19.7 18.5 %collective-permute-start.5 = (bf16[512,512]{1,0:T(8,128)(2,1)S(1)}, bf16[512,512]{1,0:T(8,128)(2,1)S(1)}, u32[]{:S(2)}, u32[]{:S(2)}) collective-permute-start(bf16[512,512]{1,0:T(8,128)(2,1)S(1)} %fusion.2), channel_id=1, source_target_pairs={{0,8},{8,16},{16,24},{24,32},{32,40},{40,48},{48,56},{56,64},{64,7... | collective-permute-start | bytes 1572872 | tf_op jit(solution)/shard_map/ppermute | solution.py:20
  23.2 13.7 %collective-permute-start.2 = (bf16[256]{0:T(256)(128)(2,1)S(1)}, bf16[256]{0:T(256)(128)(2,1)S(1)}, u32[]{:S(2)}, u32[]{:S(2)}) collective-permute-start(bf16[256]{0:T(256)(128)(2,1)S(1)} %pad_maximum_fusion.3), channel_id=1, source_target_pairs={{0,32},{8,40},{16,48},{24,56},{32,0},{40,8},{48,16},{56,24},{64,96... | collective-permute-start | bytes 1544 | tf_op jit(solution)/shard_map/ppermute | solution.py:25
  29.6 12.7 %collective-permute-start.9 = (bf16[512,512]{1,0:T(8,128)(2,1)S(1)}, bf16[512,512]{1,0:T(8,128)(2,1)S(1)}, u32[]{:S(2)}, u32[]{:S(2)}) collective-permute-start(bf16[512,512]{1,0:T(8,128)(2,1)S(1)} %get-tuple-element.12), channel_id=1, source_target_pairs={{8,0},{16,8},{24,16},{32,24},{40,32},{48,40},{56,48},{64,56},{72,6... | collective-permute-start | bytes 1572872 | tf_op jit(solution)/shard_map/ppermute | solution.py:20
  36.9 6.7 %collective-permute-start.3 = (bf16[512]{0:T(512)(128)(2,1)S(1)}, bf16[512]{0:T(512)(128)(2,1)S(1)}, u32[]{:S(2)}, u32[]{:S(2)}) collective-permute-start(bf16[512]{0:T(512)(128)(2,1)S(1)} %pad_maximum_fusion.1), channel_id=1, source_target_pairs={{0,64},{8,72},{16,80},{24,88},{32,96},{40,104},{48,112},{56,120},{... | collective-permute-start | bytes 3080 | tf_op jit(solution)/shard_map/ppermute | solution.py:25
  38.2 9.3 %collective-permute-start.6 = (bf16[512,512]{1,0:T(8,128)(2,1)S(1)}, bf16[512,512]{1,0:T(8,128)(2,1)S(1)}, u32[]{:S(2)}, u32[]{:S(2)}) collective-permute-start(bf16[512,512]{1,0:T(8,128)(2,1)S(1)} %collective-permute-done.5), channel_id=1, source_target_pairs={{0,8},{8,16},{16,24},{24,32},{32,40},{40,48},{48,56},{56,64},{64,7... | collective-permute-start | bytes 1572872 | tf_op jit(solution)/shard_map/ppermute | solution.py:20
  42.3 22.7 %collective-permute-start.10 = (bf16[512,512]{1,0:T(8,128)(2,1)S(1)}, bf16[512,512]{1,0:T(8,128)(2,1)}, u32[]{:S(2)}, u32[]{:S(2)}) collective-permute-start(bf16[512,512]{1,0:T(8,128)(2,1)S(1)} %collective-permute-done.9), channel_id=1, source_target_pairs={{8,0},{16,8},{24,16},{32,24},{40,32},{48,40},{56,48},{64,56},{72,6... | collective-permute-start | bytes 1572872 | tf_op jit(solution)/shard_map/ppermute | solution.py:20
  47.5 32.9 %copy-start.3 = (bf16[512,512]{1,0:T(8,128)(2,1)}, bf16[512,512]{1,0:T(8,128)(2,1)S(1)}, u32[]{:S(2)}) copy-start(bf16[512,512]{1,0:T(8,128)(2,1)S(1)} %collective-permute-done.6) | copy-start | bytes 1572868
  47.5 18.8 %collective-permute-start.7 = (bf16[512,512]{1,0:T(8,128)(2,1)S(1)}, bf16[512,512]{1,0:T(8,128)(2,1)}, u32[]{:S(2)}, u32[]{:S(2)}) collective-permute-start(bf16[512,512]{1,0:T(8,128)(2,1)S(1)} %collective-permute-done.6), channel_id=1, source_target_pairs={{0,8},{8,16},{16,24},{24,32},{32,40},{40,48},{48,56},{56,64},{64,7... | collective-permute-start | bytes 1572872 | tf_op jit(solution)/shard_map/ppermute | solution.py:20
  52.4 12.6 %collective-permute-start.4 = (bf16[1024]{0:T(1024)(128)(2,1)S(1)}, bf16[1024]{0:T(1024)(128)(2,1)S(1)}, u32[]{:S(2)}, u32[]{:S(2)}) collective-permute-start(bf16[1024]{0:T(1024)(128)(2,1)S(1)} %pad_maximum_fusion), channel_id=1, source_target_pairs={{0,128},{8,136},{16,144},{24,152},{32,160},{40,168},{48,176},{56,1... | collective-permute-start | bytes 6152 | tf_op jit(solution)/shard_map/ppermute | solution.py:25
  65.0 12.2 %collective-permute-start.11 = (bf16[512,512]{1,0:T(8,128)(2,1)}, bf16[512,512]{1,0:T(8,128)(2,1)}, u32[]{:S(2)}, u32[]{:S(2)}) collective-permute-start(bf16[512,512]{1,0:T(8,128)(2,1)} %collective-permute-done.10), channel_id=1, source_target_pairs={{8,0},{16,8},{24,16},{32,24},{40,32},{48,40},{56,48},{64,56},{72,6... | collective-permute-start | bytes 1572872 | tf_op jit(solution)/shard_map/ppermute | solution.py:20
  66.3 14.1 %collective-permute-start.8 = (bf16[512,512]{1,0:T(8,128)(2,1)}, bf16[512,512]{1,0:T(8,128)(2,1)}, u32[]{:S(2)}, u32[]{:S(2)}) collective-permute-start(bf16[512,512]{1,0:T(8,128)(2,1)} %collective-permute-done.7), channel_id=1, source_target_pairs={{0,8},{8,16},{16,24},{24,32},{32,40},{40,48},{48,56},{56,64},{64,7... | collective-permute-start | bytes 1572872 | tf_op jit(solution)/shard_map/ppermute | solution.py:20
  77.2 10.1 %collective-permute-start.12 = (bf16[512,512]{1,0:T(8,128)(2,1)}, bf16[512,512]{1,0:T(8,128)(2,1)S(1)}, u32[]{:S(2)}, u32[]{:S(2)}) collective-permute-start(bf16[512,512]{1,0:T(8,128)(2,1)} %collective-permute-done.11), channel_id=1, source_target_pairs={{8,0},{16,8},{24,16},{32,24},{40,32},{48,40},{56,48},{64,56},{72,6... | collective-permute-start | bytes 1572872 | tf_op jit(solution)/shard_map/ppermute | solution.py:20
  83.7 4.5 %copy-start = (bf16[2560,512]{1,0:T(8,128)(2,1)}, bf16[2560,512]{1,0:T(8,128)(2,1)S(1)}, u32[]{:S(2)}) copy-start(bf16[2560,512]{1,0:T(8,128)(2,1)S(1)} %constant_dynamic-update-slice_fusion.src) | copy-start | bytes 7864324
  88.2 47.7 %copy-start.1 = (bf16[512,512]{1,0:T(8,128)(2,1)S(1)}, bf16[512,512]{1,0:T(8,128)(2,1)}, u32[]{:S(2)}) copy-start(bf16[512,512]{1,0:T(8,128)(2,1)} %param.9) | copy-start | bytes 1572868
  88.2 47.7 %copy-start.2 = (bf16[512,512]{1,0:T(8,128)(2,1)S(1)}, bf16[512,512]{1,0:T(8,128)(2,1)}, u32[]{:S(2)}) copy-start(bf16[512,512]{1,0:T(8,128)(2,1)} %param.8) | copy-start | bytes 1572868
  98.9 4.2 %collective-permute-start.13 = (f32[1024]{0:T(1024)S(1)}, f32[1024]{0:T(1024)S(1)}, u32[]{:S(2)}, u32[]{:S(2)}) collective-permute-start(f32[1024]{0:T(1024)S(1)} %slice_select_fusion), channel_id=1, source_target_pairs={{0,128},{8,136},{16,144},{24,152},{32,160},{40,168},{48,176},{56,1... | collective-permute-start | bytes 12296 | tf_op jit(solution)/shard_map/ppermute | solution.py:25
  103.1 4.6 %collective-permute-start.14 = (f32[512]{0:T(512)S(1)}, f32[512]{0:T(512)S(1)}, u32[]{:S(2)}, u32[]{:S(2)}) collective-permute-start(f32[512]{0:T(512)S(1)} %slice_select_fusion.1), channel_id=1, source_target_pairs={{0,64},{8,72},{16,80},{24,88},{32,96},{40,104},{48,112},{56,120},{... | collective-permute-start | bytes 6152 | tf_op jit(solution)/shard_map/ppermute | solution.py:25
  107.7 6.4 %collective-permute-start.15 = (f32[256]{0:T(256)S(1)}, f32[256]{0:T(256)S(1)}, u32[]{:S(2)}, u32[]{:S(2)}) collective-permute-start(f32[256]{0:T(256)S(1)} %broadcast_select_fusion.10), channel_id=1, source_target_pairs={{0,32},{8,40},{16,48},{24,56},{32,0},{40,8},{48,16},{56,24},{64,96... | collective-permute-start | bytes 3080 | tf_op jit(solution)/shard_map/ppermute | solution.py:25
  114.1 3.4 %collective-permute-start.16 = (f32[128]{0:T(128)S(1)}, f32[128]{0:T(128)S(1)}, u32[]{:S(2)}, u32[]{:S(2)}) collective-permute-start(f32[128]{0:T(128)S(1)} %broadcast_select_fusion.6), channel_id=1, source_target_pairs={{0,16},{8,24},{16,0},{24,8},{32,48},{40,56},{48,32},{56,40},{64,80... | collective-permute-start | bytes 1544 | tf_op jit(solution)/shard_map/ppermute | solution.py:25
  117.6 2.4 %collective-permute-start.17 = (f32[64]{0:T(128)S(1)}, f32[64]{0:T(128)S(1)}, u32[]{:S(2)}, u32[]{:S(2)}) collective-permute-start(f32[64]{0:T(128)S(1)} %broadcast_select_fusion.2), channel_id=1, source_target_pairs={{0,8},{8,0},{16,24},{24,16},{32,40},{40,32},{48,56},{56,48},{64,72... | collective-permute-start | bytes 776 | tf_op jit(solution)/shard_map/ppermute | solution.py:25
  120.8 19.6 %all-to-all-start.1 = ((f32[8,8,1]{1,2,0:T(1,128)}), f32[8,8,1]{1,2,0:T(1,128)S(1)}, u32[]{:S(2)}, u32[]{:S(2)}) async-start(f32[8,8,1]{1,2,0:T(1,128)} %bitcast.33), calls=%async_computation.1 | async-start | bytes 8192 | tf_op jit(solution)/shard_map/all_to_all | solution.py:174

commit v3 on v2

--- a/solution.py
+++ b/solution.py
@@ -38,26 +38,22 @@
     return held
 
 
-def scatter_sums(vector, axis):
-    here = lax.axis_index(axis)
-    count = lax.axis_size(axis)
-    held = vector
-    bit = count // 2
-    while bit >= 1:
-        half = held.shape[0] // 2
-        low, high = held[:half], held[half:]
-        upper = (here & bit) != 0
-        other = swapped(jnp.where(upper, low, high), axis, bit)
-        held = jnp.where(upper, high, low) + other
-        bit //= 2
-    return held
+def conv_kernel(fwd_rows, bwd_rows, ids_own, ids_rev, ids_src, ids_rdr, skip, *refs):
+    lags = MAXCH + 1
+    count = (len(refs) - 5) // 2
+    src_refs, grad_refs = refs[:count], refs[count : 2 * count]
+    conv_out, mgrad_out, filt_out, fwd_tiles, bwd_tiles = refs[2 * count :]
+    own = src_refs[0].shape[0]
+    parts = own // C
 
+    def src(j):
+        return src_refs[j // parts][(j % parts) * C : (j % parts + 1) * C, :]
 
-def conv_kernel(fwd_rows, bwd_rows, ids_own, ids_rev, ids_src, ids_rdr, skip, src, grads, grads_rev,
-                conv_out, mgrad_out, filt_out, fwd_tiles, bwd_tiles):
-    lags = MAXCH + 1
-    own = src.shape[0] - MAXCH * C
-    parts = own // C
+    def grads(j):
+        return grad_refs[j // parts][(j % parts) * C : (j % parts + 1) * C, :]
+
+    exchange = (lax.broadcasted_iota(jnp.int32, (C, C), 0) + lax.broadcasted_iota(jnp.int32, (C, C), 1)
+                == C - 1).astype(jnp.bfloat16)
     for lag in range(lags):
         wide = jnp.broadcast_to(fwd_rows[lag : lag + 1, :], (C, 2 * C))
         fwd_tiles[lag] = pltpu.roll(wide, 0, 1, stride=1, stride_axis=0)[:, C:].astype(jnp.bfloat16)
@@ -69,15 +65,14 @@
         rows = slice(r * C, (r + 1) * C)
         reader_ids = ids_own[rows, :]
         reader_rev = ids_rev[rows, :]
-        own_rows = slice(MAXCH * C + r * C, MAXCH * C + (r + 1) * C)
-        acc = skip_row * src[own_rows, :].astype(jnp.float32)
-        grad_rev = grads_rev[rows, :]
+        acc = skip_row * src(MAXCH + r).astype(jnp.float32)
+        grad_rev = jnp.dot(exchange, grads(r), preferred_element_type=jnp.float32).astype(jnp.bfloat16)
         for j in range(MAXCH + parts):
             lag = MAXCH + r - j
             if not 0 <= lag <= MAXCH:
                 continue
             cols = slice(j * C, (j + 1) * C)
-            block = src[cols, :]
+            block = src(j)
             same = reader_ids == ids_src[:, cols]
             tile = jnp.where(same, fwd_tiles[lag], jnp.zeros((), jnp.bfloat16))
             acc = acc + jnp.dot(tile, block, preferred_element_type=jnp.float32)
@@ -91,20 +86,20 @@
     for s in range(parts):
         rows = slice(s * C, (s + 1) * C)
         source_ids = ids_own[rows, :]
-        acc = skip_row * grads[rows, :].astype(jnp.float32)
+        acc = skip_row * grads(s).astype(jnp.float32)
         for lag in range(lags):
             j = s + lag
             cols = slice(j * C, (j + 1) * C)
             same = source_ids == ids_rdr[:, cols]
             tile = jnp.where(same, bwd_tiles[lag], jnp.zeros((), jnp.bfloat16))
-            acc = acc + jnp.dot(tile, grads[cols, :], preferred_element_type=jnp.float32)
+            acc = acc + jnp.dot(tile, grads(j), preferred_element_type=jnp.float32)
         mgrad_out[rows, :] = acc
     for lag in range(lags):
         filt_out[lag : lag + 1, :] = sums[lag]
 
 
 def local_conv(taps, ids_own, ids_src, ids_rdr, skip, src, grads):
-    own, width = grads.shape[0] - MAXCH * C, grads.shape[1]
+    own, width = grads[0].shape
     lags = MAXCH + 1
     big = jnp.concatenate([jnp.zeros((2 * C,), jnp.float32), taps.astype(jnp.float32),
                            jnp.zeros((2 * C,), jnp.float32)])
@@ -112,7 +107,6 @@
     bwd_rows = jnp.stack([big[C * lag + C : C * lag + 3 * C] for lag in range(lags)])
     parts = own // C
     ids_rev = ids_own.reshape(parts, C)[:, ::-1].reshape(own, 1)
-    grads_rev = grads[:own].reshape(parts, C, width)[:, ::-1].reshape(own, width)
     conv, mgrad, sums = pl.pallas_call(
         conv_kernel,
         out_shape=(
@@ -124,7 +118,7 @@
         compiler_params=pltpu.CompilerParams(vmem_limit_bytes=60 * 1024 * 1024),
         interpret=INTERPRET,
     )(fwd_rows, bwd_rows, ids_own.reshape(own, 1), ids_rev, ids_src.reshape(1, -1),
-      ids_rdr.reshape(1, -1), skip.reshape(1, width), src, grads, grads_rev)
+      ids_rdr.reshape(1, -1), skip.reshape(1, width), *src, *grads)
     ext = sum(
         jnp.pad(sums[lag, : 2 * C - 1][::-1], (C * lag + 1, (lags + 1) * C - C * lag - 2 * C))
         for lag in range(lags)
@@ -151,8 +145,6 @@
     for _ in range(span):
         ahead.append(shifted(ahead[-1], "ctx", 1))
         behind.append(shifted(behind[-1], "ctx", -1))
-    sources = jnp.concatenate(ahead[::-1], axis=0)
-    readers = jnp.concatenate(behind, axis=0)
 
     ids_pad = jnp.concatenate(
         [jnp.full((hist,), -1, jnp.int32), doc_ids, jnp.full((hist,), -2, jnp.int32)]
@@ -161,17 +153,20 @@
     ids_src = lax.dynamic_slice_in_dim(ids_pad, here * rows, hist + rows)
     ids_rdr = lax.dynamic_slice_in_dim(ids_pad, here * rows + hist, hist + rows)
 
-    conv, mixed_grad, filter_part = local_conv(taps, ids_own, ids_src, ids_rdr, skip_gain, sources, readers)
+    conv, mixed_grad, filter_part = local_conv(taps, ids_own, ids_src, ids_rdr, skip_gain, ahead[::-1], behind)
 
     mixed_out = (query_in.astype(jnp.float32) * conv).astype(jnp.bfloat16)
     query_grad = (out_grad.astype(jnp.float32) * conv).astype(jnp.bfloat16)
     key_grad = (mixed_grad * value_in.astype(jnp.float32)).astype(jnp.bfloat16)
     value_grad = (mixed_grad * key_in.astype(jnp.float32)).astype(jnp.bfloat16)
 
-    summed = scatter_sums(filter_part, "ctx")
+    every = ("ctx", "tp")
+    devices = lax.axis_size(every)
+    groups = lax.axis_size("tp")
+    spread = lax.all_to_all(filter_part.reshape(devices, FLEN // devices), every, 0, 0, tiled=True)
+    summed = jnp.sum(spread.reshape(devices // groups, groups, FLEN // devices), axis=0).T
     tokens = lax.axis_size("ctx") * rows
-    scaled = (summed * (1.0 / math.sqrt(FGROUP * tokens)))[:, None]
-    filter_grad = lax.all_to_all(scaled, "tp", split_axis=0, concat_axis=1, tiled=True)
+    filter_grad = summed * (1.0 / math.sqrt(FGROUP * tokens))
     return (mixed_out, query_grad, key_grad, value_grad, filter_grad)
 
 

time: 142 us -> 114 us (0.80)
  local copies, waits for them, and re-layouts: 26 us -> 11.6 us
  waiting for transfers between devices: 37 us -> 28.5 us
  starting transfers between devices: 61.7 us -> 59.3 us
  other arithmetic: 7.53 us -> 5.26 us
    ppermute x10 -> x5, waiting for transfers between devices: 21.3 us -> 7.92 us  [swapped(): lax.ppermute(value, axis, [(source, source ^ bit) for source in range(cou...]
    all_to_all x1, waiting for transfers between devices: 0.99 us -> 9.58 us  [shards(): lax.all_to_all(filter_part.reshape(devices, FLEN // devices), every, 0, 0...]
    unnamed x37 -> x43, local copies, waits for them, and re-layouts: 10.3 us -> 3.14 us
    ppermute x10 -> x5, starting transfers between devices: 20.7 us -> 15.4 us  [swapped(): lax.ppermute(value, axis, [(source, source ^ bit) for source in range(cou...]
    rev x1 -> x0, local copies, waits for them, and re-layouts: 5.1 us -> none  [local_conv(): grads[:own].reshape(parts, C, width)[:, ::-1].reshape(own, width)]
    ppermute x8, starting transfers between devices: 19.5 us -> 23.7 us  [shifted(): lax.ppermute(value, axis, [(source, source + steps) for source in range(l...]
    ppermute x8, waiting for transfers between devices: 10.2 us -> 6.47 us  [shifted(): lax.ppermute(value, axis, [(source, source + steps) for source in range(l...]
    unnamed x1 -> x0, other arithmetic: 2.13 us -> none
  transfers between devices with their start and end apart: 20 -> 15, of which waited for: 12 -> 7; matrix products, arithmetic and copies ran while one was open for 19% -> 10% of each run, Pallas kernels for 0% -> 0%
where the time goes in v3:
time: 114 us
  starting transfers between devices  59.3 us (52%)
  waiting for transfers between devices  28.5 us (25%)
  local copies, waits for them, and re-layouts  11.6 us (10%)
  Pallas kernels  7.98 us (7%)
  other arithmetic  5.26 us (5%)
    ppermute x8, starting transfers between devices, shifted(): lax.ppermute(value, axis, [(source, source + steps) for source in range(l...  23.7 us
    ppermute x5, starting transfers between devices, swapped(): lax.ppermute(value, axis, [(source, source ^ bit) for source in range(cou...  15.4 us
    all_to_all x1, starting transfers between devices, shards(): lax.all_to_all(filter_part.reshape(devices, FLEN // devices), every, 0, 0...  14.8 us
    all_to_all x1, waiting for transfers between devices, shards(): lax.all_to_all(filter_part.reshape(devices, FLEN // devices), every, 0, 0...  9.58 us
    pallas_call x1, Pallas kernels, local_conv(): pl.pallas_call(conv_kernel, out_shape=(jax.ShapeDtypeStruct((own, width),...  7.98 us
    ppermute x5, waiting for transfers between devices, swapped(): lax.ppermute(value, axis, [(source, source ^ bit) for source in range(cou...  7.92 us
    ppermute x8, waiting for transfers between devices, shifted(): lax.ppermute(value, axis, [(source, source + steps) for source in range(l...  6.47 us
    all_to_all x1, starting transfers between devices, shards(): lax.all_to_all(filter_taps, 'tp', split_axis=1, concat_axis=0, tiled=True)  5.42 us
  transfers between devices with their start and end apart: 15, of which 7 were waited for; matrix products, arithmetic and copies ran while one was open for 10% of the time, Pallas kernels for 0%

profile of v3, /device:TPU:1, one launch (start us, length us, event | category | flops | bytes accessed | tf_op | source)
XLA Modules:
  0.0 113.6 jit_solution(3230503173025349631)
XLA Ops:
  0.7 1.4 %fusion.2.refs_4_ = bf16[512,512]{1,0:T(8,128)(2,1)S(1)} fusion(bf16[512,512]{1,0:T(8,128)(2,1)} %param.9, bf16[512,512]{1,0:T(8,128)(2,1)} %param.8), kind=kLoop, calls=%fused_computation.8 | loop fusion | flops 1048576 | bytes 1572864 | tf_op jit(solution)/shard_map/convert_element_type | solution.py:140
  2.1 4.4 %collective-permute-start.5 = (bf16[512,512]{1,0:T(8,128)(2,1)S(1)}, bf16[512,512]{1,0:T(8,128)(2,1)S(1)}, u32[]{:S(2)}, u32[]{:S(2)}) collective-permute-start(bf16[512,512]{1,0:T(8,128)(2,1)S(1)} %fusion.2.refs_4_), channel_id=1, source_target_pairs={{0,8},{8,16},{16,24},{24,32},{32,40},{40,48},{48,56},{56,64},{64,7... | collective-permute-start | bytes 1572872 | tf_op jit(solution)/shard_map/ppermute | solution.py:20
  6.5 0.1 fusion.4.refs_5_
  6.7 1.4 %collective-permute-start.9 = (bf16[512,512]{1,0:T(8,128)(2,1)S(1)}, bf16[512,512]{1,0:T(8,128)(2,1)S(1)}, u32[]{:S(2)}, u32[]{:S(2)}) collective-permute-start(bf16[512,512]{1,0:T(8,128)(2,1)S(1)} %fusion.4.refs_5_), channel_id=1, source_target_pairs={{8,0},{16,8},{24,16},{32,24},{40,32},{48,40},{56,48},{64,56},{72,6... | collective-permute-start | bytes 1572872 | tf_op jit(solution)/shard_map/ppermute | solution.py:20
  8.1 0.7 copy.21
  8.8 5.4 %all-to-all-start = ((bf16[8,8,1]{0,2,1:T(2,128)(2,1)}), bf16[8,8,1]{0,2,1:T(2,128)(2,1)S(1)}, u32[]{:S(2)}, u32[]{:S(2)}) async-start(bf16[8,8,1]{0,2,1:T(2,128)(2,1)} %copy.21), calls=%async_computation | async-start | bytes 8192 | tf_op jit(solution)/shard_map/all_to_all | solution.py:137
  14.2 4.5 %all-to-all-done = bf16[8,8,1]{0,2,1:T(2,128)(2,1)S(1)} async-done(((bf16[8,8,1]{0,2,1:T(2,128)(2,1)}), bf16[8,8,1]{0,2,1:T(2,128)(2,1)S(1)}, u32[]{:S(2)}, u32[]{:S(2)}) %all-to-all-start) | async-done | bytes 160 | tf_op jit(solution)/shard_map/all_to_all | solution.py:137
  18.9 2.4 %collective-permute-start = (bf16[64]{0:T(256)(128)(2,1)S(1)}, bf16[64]{0:T(256)(128)(2,1)S(1)}, u32[]{:S(2)}, u32[]{:S(2)}) collective-permute-start(bf16[64]{0:T(256)(128)(2,1)S(1)} %squeeze.30), channel_id=1, source_target_pairs={{0,8},{8,0},{16,24},{24,16},{32,40},{40,32},{48,56},{56,48},{64,72... | collective-permute-start | bytes 392 | tf_op jit(solution)/shard_map/ppermute | solution.py:25
  21.3 1.3 %collective-permute-done = bf16[64]{0:T(256)(128)(2,1)S(1)} collective-permute-done((bf16[64]{0:T(256)(128)(2,1)S(1)}, bf16[64]{0:T(256)(128)(2,1)S(1)}, u32[]{:S(2)}, u32[]{:S(2)}) %collective-permute-start) | collective-permute-done | bytes 160 | tf_op jit(solution)/shard_map/ppermute | solution.py:25
  22.6 4.1 %collective-permute-start.1 = (bf16[128]{0:T(256)(128)(2,1)S(1)}, bf16[128]{0:T(256)(128)(2,1)S(1)}, u32[]{:S(2)}, u32[]{:S(2)}) collective-permute-start(bf16[128]{0:T(256)(128)(2,1)S(1)} %pad_maximum_fusion.2), channel_id=1, source_target_pairs={{0,16},{8,24},{16,0},{24,8},{32,48},{40,56},{48,32},{56,40},{64,80... | collective-permute-start | bytes 776 | tf_op jit(solution)/shard_map/ppermute | solution.py:25
  26.7 3.4 %collective-permute-start.6 = (bf16[512,512]{1,0:T(8,128)(2,1)S(1)}, bf16[512,512]{1,0:T(8,128)(2,1)S(1)}, u32[]{:S(2)}, u32[]{:S(2)}) collective-permute-start(bf16[512,512]{1,0:T(8,128)(2,1)S(1)} %collective-permute-done.5.refs_3_), channel_id=1, source_target_pairs={{0,8},{8,16},{16,24},{24,32},{32,40},{40,48},{48,56},{56,64},{64,7... | collective-permute-start | bytes 1572872 | tf_op jit(solution)/shard_map/ppermute | solution.py:20
  30.1 1.3 %collective-permute-start.10 = (bf16[512,512]{1,0:T(8,128)(2,1)S(1)}, bf16[512,512]{1,0:T(8,128)(2,1)}, u32[]{:S(2)}, u32[]{:S(2)}) collective-permute-start(bf16[512,512]{1,0:T(8,128)(2,1)S(1)} %collective-permute-done.9.refs_6_), channel_id=1, source_target_pairs={{8,0},{16,8},{24,16},{32,24},{40,32},{48,40},{56,48},{64,56},{72,6... | collective-permute-start | bytes 1572872 | tf_op jit(solution)/shard_map/ppermute | solution.py:20
  31.5 5.5 %collective-permute-start.2 = (bf16[256]{0:T(256)(128)(2,1)S(1)}, bf16[256]{0:T(256)(128)(2,1)S(1)}, u32[]{:S(2)}, u32[]{:S(2)}) collective-permute-start(bf16[256]{0:T(256)(128)(2,1)S(1)} %pad_maximum_fusion.3), channel_id=1, source_target_pairs={{0,32},{8,40},{16,48},{24,56},{32,0},{40,8},{48,16},{56,24},{64,96... | collective-permute-start | bytes 1544 | tf_op jit(solution)/shard_map/ppermute | solution.py:25
  37.0 6.7 %collective-permute-done.2 = bf16[256]{0:T(256)(128)(2,1)S(1)} collective-permute-done((bf16[256]{0:T(256)(128)(2,1)S(1)}, bf16[256]{0:T(256)(128)(2,1)S(1)}, u32[]{:S(2)}, u32[]{:S(2)}) %collective-permute-start.2) | collective-permute-done | bytes 544 | tf_op jit(solution)/shard_map/ppermute | solution.py:25
  43.7 1.3 %collective-permute-start.3 = (bf16[512]{0:T(512)(128)(2,1)S(1)}, bf16[512]{0:T(512)(128)(2,1)S(1)}, u32[]{:S(2)}, u32[]{:S(2)}) collective-permute-start(bf16[512]{0:T(512)(128)(2,1)S(1)} %pad_maximum_fusion.1), channel_id=1, source_target_pairs={{0,64},{8,72},{16,80},{24,88},{32,96},{40,104},{48,112},{56,120},{... | collective-permute-start | bytes 3080 | tf_op jit(solution)/shard_map/ppermute | solution.py:25
  45.0 5.6 %collective-permute-start.7 = (bf16[512,512]{1,0:T(8,128)(2,1)S(1)}, bf16[512,512]{1,0:T(8,128)(2,1)}, u32[]{:S(2)}, u32[]{:S(2)}) collective-permute-start(bf16[512,512]{1,0:T(8,128)(2,1)S(1)} %collective-permute-done.6.refs_2_), channel_id=1, source_target_pairs={{0,8},{8,16},{16,24},{24,32},{32,40},{40,48},{48,56},{56,64},{64,7... | collective-permute-start | bytes 1572872 | tf_op jit(solution)/shard_map/ppermute | solution.py:20
  50.6 1.3 %collective-permute-start.11 = (bf16[512,512]{1,0:T(8,128)(2,1)}, bf16[512,512]{1,0:T(8,128)(2,1)}, u32[]{:S(2)}, u32[]{:S(2)}) collective-permute-start(bf16[512,512]{1,0:T(8,128)(2,1)} %collective-permute-done.10.refs_7_), channel_id=1, source_target_pairs={{8,0},{16,8},{24,16},{32,24},{40,32},{48,40},{56,48},{64,56},{72,6... | collective-permute-start | bytes 1572872 | tf_op jit(solution)/shard_map/ppermute | solution.py:20
  52.0 2.2 %collective-permute-start.4 = (bf16[1024]{0:T(1024)(128)(2,1)S(1)}, bf16[1024]{0:T(1024)(128)(2,1)S(1)}, u32[]{:S(2)}, u32[]{:S(2)}) collective-permute-start(bf16[1024]{0:T(1024)(128)(2,1)S(1)} %pad_maximum_fusion), channel_id=1, source_target_pairs={{0,128},{8,136},{16,144},{24,152},{32,160},{40,168},{48,176},{56,1... | collective-permute-start | bytes 6152 | tf_op jit(solution)/shard_map/ppermute | solution.py:25
  54.3 0.2 rev.66
  54.5 0.6 reshape.52.ids_rdr
  55.1 0.6 reshape.51.ids_src
  55.7 0.9 copy.27
  56.6 0.9 copy.22.ids_own
  57.5 0.1 collective-permute-done.7.refs_1_
  57.6 5.0 %collective-permute-start.8 = (bf16[512,512]{1,0:T(8,128)(2,1)}, bf16[512,512]{1,0:T(8,128)(2,1)}, u32[]{:S(2)}, u32[]{:S(2)}) collective-permute-start(bf16[512,512]{1,0:T(8,128)(2,1)} %collective-permute-done.7.refs_1_), channel_id=1, source_target_pairs={{0,8},{8,16},{16,24},{24,32},{32,40},{40,48},{48,56},{56,64},{64,7... | collective-permute-start | bytes 1572872 | tf_op jit(solution)/shard_map/ppermute | solution.py:20
  62.6 1.3 %collective-permute-start.12 = (bf16[512,512]{1,0:T(8,128)(2,1)}, bf16[512,512]{1,0:T(8,128)(2,1)}, u32[]{:S(2)}, u32[]{:S(2)}) collective-permute-start(bf16[512,512]{1,0:T(8,128)(2,1)} %collective-permute-done.11.refs_8_), channel_id=1, source_target_pairs={{8,0},{16,8},{24,16},{32,24},{40,32},{48,40},{56,48},{64,56},{72,6... | collective-permute-start | bytes 1572872 | tf_op jit(solution)/shard_map/ppermute | solution.py:20
  64.0 0.1 rev.65
  64.1 0.1 rev.64
  64.2 0.1 rev.63
  64.3 0.1 rev.62
  64.4 0.1 rev.61
  64.5 0.1 rev.60
  64.6 0.1 rev.59
  64.7 0.1 rev.58
  64.9 1.2 %stack.69.fwd_rows = f32[9,512]{1,0:T(8,128)} concatenate(f32[1,512]{1,0:T(1,128)S(1)} %bitcast.81, f32[1,512]{1,0:T(1,128)S(1)} %bitcast.79, f32[1,512]{1,0:T(1,128)S(1)} %bitcast.78, f32[1,512]{1,0:T(1,128)S(1)} %bitcast.77, f32[1,512]{1,0:T(1,128)S(1)} %bitcast.75, f32[1,512]{1,0:T(1,128)S(1)} %bitcast.74, f32[1,512]{1,0:T(1,128)S(1)} %bitcast.73, f32[1,512]{1,0:T(1,128)S(1)} %bitcast.71, ...), dimensions={0} | concatenate | bytes 36864 | tf_op jit(solution)/shard_map/stack | solution.py:106
  66.1 1.2 %stack.79.bwd_rows = f32[9,512]{1,0:T(8,128)} concatenate(f32[1,512]{1,0:T(1,128)S(1)} %bitcast.56, f32[1,512]{1,0:T(1,128)S(1)} %bitcast.63, f32[1,512]{1,0:T(1,128)S(1)} %bitcast.62, f32[1,512]{1,0:T(1,128)S(1)} %bitcast.61, f32[1,512]{1,0:T(1,128)S(1)} %bitcast.60, f32[1,512]{1,0:T(1,128)S(1)} %bitcast.59, f32[1,512]{1,0:T(1,128)S(1)} %bitcast.58, f32[1,512]{1,0:T(1,128)S(1)} %bitcast.57, ...), dimensions={0} | concatenate | bytes 36864 | tf_op jit(solution)/shard_map/stack | solution.py:107
  67.4 1.7 %collective-permute-done.8.refs_0_ = bf16[512,512]{1,0:T(8,128)(2,1)} collective-permute-done((bf16[512,512]{1,0:T(8,128)(2,1)}, bf16[512,512]{1,0:T(8,128)(2,1)}, u32[]{:S(2)}, u32[]{:S(2)}) %collective-permute-start.8) | collective-permute-done | bytes 524320 | tf_op jit(solution)/shard_map/ppermute | solution.py:20
  69.1 4.6 %collective-permute-done.12.refs_9_ = bf16[512,512]{1,0:T(8,128)(2,1)} collective-permute-done((bf16[512,512]{1,0:T(8,128)(2,1)}, bf16[512,512]{1,0:T(8,128)(2,1)}, u32[]{:S(2)}, u32[]{:S(2)}) %collective-permute-start.12) | collective-permute-done | bytes 524320 | tf_op jit(solution)/shard_map/ppermute | solution.py:20
  73.7 8.0 %shard_map.110 = (f32[512,512]{1,0:T(8,128)}, f32[512,512]{1,0:T(8,128)}, f32[9,512]{1,0:T(8,128)}) custom-call(f32[9,512]{1,0:T(8,128)} %stack.69.fwd_rows, f32[9,512]{1,0:T(8,128)} %stack.79.bwd_rows, s32[512,1]{1,0:T(8,128)} %copy.22.ids_own, s32[512,1]{1,0:T(8,128)} %bitcast.51, s32[1,2560]{1,0:T(1,128)} %reshape.51.ids_src, s32[1,2560]{1,0:T(1,128)} %reshape.52.ids_rdr, ...), custom_call_target="tpu_custom_call" | custom-call | tf_op jit(solution)/shard_map/pallas_call | solution.py:110
  81.7 1.0 fusion.7
  82.7 0.1 reverse.8
  82.9 0.1 reverse
  83.6 0.1 reverse.4
  84.4 0.8 slice.127
  85.2 14.8 %all-to-all-start.1 = ((f32[256,1,8]{2,1,0:T(1,128)}), f32[256,1,8]{2,1,0:T(1,128)S(1)}, u32[]{:S(2)}, u32[]{:S(2)}) async-start(f32[256,1,8]{2,1,0:T(1,128)} %bitcast.31), calls=%async_computation.1 | async-start | bytes 262144 | tf_op jit(solution)/shard_map/all_to_all | solution.py:166
  100.0 3.3 %fusion.1 = (bf16[512,512]{1,0:T(8,128)(2,1)}, bf16[512,512]{1,0:T(8,128)(2,1)}, bf16[512,512]{1,0:T(8,128)(2,1)}, bf16[512,512]{1,0:T(8,128)(2,1)}) fusion(f32[512,512]{1,0:T(8,128)} %get-tuple-element.9, bf16[512,512]{1,0:T(8,128)(2,1)S(1)} %copy-done.1, bf16[512,512]{1,0:T(8,128)(2,1)S(1)} %copy-done, f32[512,512]{1,0:T(8,128)} %get-tuple-element.8, ...), kind=kLoop, calls=%fused_computation.7 | loop fusion | flops 3145728 | bytes 6291456 | tf_op jit(solution)/shard_map/convert_element_type | solution.py:161
  103.3 9.6 %all-to-all-done.1 = f32[256,1,8]{2,1,0:T(1,128)S(1)} async-done(((f32[256,1,8]{2,1,0:T(1,128)}), f32[256,1,8]{2,1,0:T(1,128)S(1)}, u32[]{:S(2)}, u32[]{:S(2)}) %all-to-all-start.1) | async-done | bytes 8224 | tf_op jit(solution)/shard_map/all_to_all | solution.py:166
  112.9 0.7 copy.25
  (70 shorter events, 2.2 us)
Async XLA Ops:
  0.6 5.9 %copy-start.3 = (bf16[512,512]{1,0:T(8,128)(2,1)S(1)}, bf16[512,512]{1,0:T(8,128)(2,1)}, u32[]{:S(2)}) copy-start(bf16[512,512]{1,0:T(8,128)(2,1)} %param.10) | copy-start | bytes 1572868
  0.6 5.9 %copy-start.2 = (bf16[512,512]{1,0:T(8,128)(2,1)S(1)}, bf16[512,512]{1,0:T(8,128)(2,1)}, u32[]{:S(2)}) copy-start(bf16[512,512]{1,0:T(8,128)(2,1)} %param.7) | copy-start | bytes 1572868
  2.1 4.6 %copy-start.4 = (bf16[512,512]{1,0:T(8,128)(2,1)}, bf16[512,512]{1,0:T(8,128)(2,1)S(1)}, u32[]{:S(2)}) copy-start(bf16[512,512]{1,0:T(8,128)(2,1)S(1)} %fusion.2.refs_4_) | copy-start | bytes 1572868
  2.1 24.6 %collective-permute-start.5 = (bf16[512,512]{1,0:T(8,128)(2,1)S(1)}, bf16[512,512]{1,0:T(8,128)(2,1)S(1)}, u32[]{:S(2)}, u32[]{:S(2)}) collective-permute-start(bf16[512,512]{1,0:T(8,128)(2,1)S(1)} %fusion.2.refs_4_), channel_id=1, source_target_pairs={{0,8},{8,16},{16,24},{24,32},{32,40},{40,48},{48,56},{56,64},{64,7... | collective-permute-start | bytes 1572872 | tf_op jit(solution)/shard_map/ppermute | solution.py:20
  6.5 1.6 %copy-start.10 = (bf16[8,8]{1,0:T(8,128)(2,1)S(1)}, bf16[8,8]{1,0:T(8,128)(2,1)}, u32[]{:S(2)}) copy-start(bf16[8,8]{1,0:T(8,128)(2,1)} %param.13) | copy-start | bytes 388
  6.7 57.5 %copy-start.5 = (bf16[512,512]{1,0:T(8,128)(2,1)}, bf16[512,512]{1,0:T(8,128)(2,1)S(1)}, u32[]{:S(2)}) copy-start(bf16[512,512]{1,0:T(8,128)(2,1)S(1)} %fusion.4.refs_5_) | copy-start | bytes 1572868
  6.7 45.2 %copy-start.9 = (s32[16384]{0:T(1024)S(1)}, s32[16384]{0:T(1024)}, u32[]{:S(2)}) copy-start(s32[16384]{0:T(1024)} %param.11) | copy-start | bytes 196612
  6.7 23.4 %collective-permute-start.9 = (bf16[512,512]{1,0:T(8,128)(2,1)S(1)}, bf16[512,512]{1,0:T(8,128)(2,1)S(1)}, u32[]{:S(2)}, u32[]{:S(2)}) collective-permute-start(bf16[512,512]{1,0:T(8,128)(2,1)S(1)} %fusion.4.refs_5_), channel_id=1, source_target_pairs={{8,0},{16,8},{24,16},{32,24},{40,32},{48,40},{56,48},{64,56},{72,6... | collective-permute-start | bytes 1572872 | tf_op jit(solution)/shard_map/ppermute | solution.py:20
  8.8 9.9 %all-to-all-start = ((bf16[8,8,1]{0,2,1:T(2,128)(2,1)}), bf16[8,8,1]{0,2,1:T(2,128)(2,1)S(1)}, u32[]{:S(2)}, u32[]{:S(2)}) async-start(bf16[8,8,1]{0,2,1:T(2,128)(2,1)} %copy.21), calls=%async_computation | async-start | bytes 8192 | tf_op jit(solution)/shard_map/all_to_all | solution.py:137
  18.9 3.6 %collective-permute-start = (bf16[64]{0:T(256)(128)(2,1)S(1)}, bf16[64]{0:T(256)(128)(2,1)S(1)}, u32[]{:S(2)}, u32[]{:S(2)}) collective-permute-start(bf16[64]{0:T(256)(128)(2,1)S(1)} %squeeze.30), channel_id=1, source_target_pairs={{0,8},{8,0},{16,24},{24,16},{32,40},{40,32},{48,56},{56,48},{64,72... | collective-permute-start | bytes 392 | tf_op jit(solution)/shard_map/ppermute | solution.py:25
  22.6 8.8 %collective-permute-start.1 = (bf16[128]{0:T(256)(128)(2,1)S(1)}, bf16[128]{0:T(256)(128)(2,1)S(1)}, u32[]{:S(2)}, u32[]{:S(2)}) collective-permute-start(bf16[128]{0:T(256)(128)(2,1)S(1)} %pad_maximum_fusion.2), channel_id=1, source_target_pairs={{0,16},{8,24},{16,0},{24,8},{32,48},{40,56},{48,32},{56,40},{64,80... | collective-permute-start | bytes 776 | tf_op jit(solution)/shard_map/ppermute | solution.py:25
  26.7 38.2 %copy-start.6 = (bf16[512,512]{1,0:T(8,128)(2,1)}, bf16[512,512]{1,0:T(8,128)(2,1)S(1)}, u32[]{:S(2)}) copy-start(bf16[512,512]{1,0:T(8,128)(2,1)S(1)} %collective-permute-done.5.refs_3_) | copy-start | bytes 1572868
  26.7 18.3 %collective-permute-start.6 = (bf16[512,512]{1,0:T(8,128)(2,1)S(1)}, bf16[512,512]{1,0:T(8,128)(2,1)S(1)}, u32[]{:S(2)}, u32[]{:S(2)}) collective-permute-start(bf16[512,512]{1,0:T(8,128)(2,1)S(1)} %collective-permute-done.5.refs_3_), channel_id=1, source_target_pairs={{0,8},{8,16},{16,24},{24,32},{32,40},{40,48},{48,56},{56,64},{64,7... | collective-permute-start | bytes 1572872 | tf_op jit(solution)/shard_map/ppermute | solution.py:20
  30.1 43.6 %copy-start.7 = (bf16[512,512]{1,0:T(8,128)(2,1)}, bf16[512,512]{1,0:T(8,128)(2,1)S(1)}, u32[]{:S(2)}) copy-start(bf16[512,512]{1,0:T(8,128)(2,1)S(1)} %collective-permute-done.9.refs_6_) | copy-start | bytes 1572868
  30.1 20.5 %collective-permute-start.10 = (bf16[512,512]{1,0:T(8,128)(2,1)S(1)}, bf16[512,512]{1,0:T(8,128)(2,1)}, u32[]{:S(2)}, u32[]{:S(2)}) collective-permute-start(bf16[512,512]{1,0:T(8,128)(2,1)S(1)} %collective-permute-done.9.refs_6_), channel_id=1, source_target_pairs={{8,0},{16,8},{24,16},{32,24},{40,32},{48,40},{56,48},{64,56},{72,6... | collective-permute-start | bytes 1572872 | tf_op jit(solution)/shard_map/ppermute | solution.py:20
  31.5 12.1 %collective-permute-start.2 = (bf16[256]{0:T(256)(128)(2,1)S(1)}, bf16[256]{0:T(256)(128)(2,1)S(1)}, u32[]{:S(2)}, u32[]{:S(2)}) collective-permute-start(bf16[256]{0:T(256)(128)(2,1)S(1)} %pad_maximum_fusion.3), channel_id=1, source_target_pairs={{0,32},{8,40},{16,48},{24,56},{32,0},{40,8},{48,16},{56,24},{64,96... | collective-permute-start | bytes 1544 | tf_op jit(solution)/shard_map/ppermute | solution.py:25
  43.7 8.3 %collective-permute-start.3 = (bf16[512]{0:T(512)(128)(2,1)S(1)}, bf16[512]{0:T(512)(128)(2,1)S(1)}, u32[]{:S(2)}, u32[]{:S(2)}) collective-permute-start(bf16[512]{0:T(512)(128)(2,1)S(1)} %pad_maximum_fusion.1), channel_id=1, source_target_pairs={{0,64},{8,72},{16,80},{24,88},{32,96},{40,104},{48,112},{56,120},{... | collective-permute-start | bytes 3080 | tf_op jit(solution)/shard_map/ppermute | solution.py:25
  45.0 28.7 %copy-start.8 = (bf16[512,512]{1,0:T(8,128)(2,1)}, bf16[512,512]{1,0:T(8,128)(2,1)S(1)}, u32[]{:S(2)}) copy-start(bf16[512,512]{1,0:T(8,128)(2,1)S(1)} %collective-permute-done.6.refs_2_) | copy-start | bytes 1572868
  45.0 12.6 %collective-permute-start.7 = (bf16[512,512]{1,0:T(8,128)(2,1)S(1)}, bf16[512,512]{1,0:T(8,128)(2,1)}, u32[]{:S(2)}, u32[]{:S(2)}) collective-permute-start(bf16[512,512]{1,0:T(8,128)(2,1)S(1)} %collective-permute-done.6.refs_2_), channel_id=1, source_target_pairs={{0,8},{8,16},{16,24},{24,32},{32,40},{40,48},{48,56},{56,64},{64,7... | collective-permute-start | bytes 1572872 | tf_op jit(solution)/shard_map/ppermute | solution.py:20
  50.6 12.0 %collective-permute-start.11 = (bf16[512,512]{1,0:T(8,128)(2,1)}, bf16[512,512]{1,0:T(8,128)(2,1)}, u32[]{:S(2)}, u32[]{:S(2)}) collective-permute-start(bf16[512,512]{1,0:T(8,128)(2,1)} %collective-permute-done.10.refs_7_), channel_id=1, source_target_pairs={{8,0},{16,8},{24,16},{32,24},{40,32},{48,40},{56,48},{64,56},{72,6... | collective-permute-start | bytes 1572872 | tf_op jit(solution)/shard_map/ppermute | solution.py:20
  52.0 11.9 %collective-permute-start.4 = (bf16[1024]{0:T(1024)(128)(2,1)S(1)}, bf16[1024]{0:T(1024)(128)(2,1)S(1)}, u32[]{:S(2)}, u32[]{:S(2)}) collective-permute-start(bf16[1024]{0:T(1024)(128)(2,1)S(1)} %pad_maximum_fusion), channel_id=1, source_target_pairs={{0,128},{8,136},{16,144},{24,152},{32,160},{40,168},{48,176},{56,1... | collective-permute-start | bytes 6152 | tf_op jit(solution)/shard_map/ppermute | solution.py:25
  57.6 11.5 %collective-permute-start.8 = (bf16[512,512]{1,0:T(8,128)(2,1)}, bf16[512,512]{1,0:T(8,128)(2,1)}, u32[]{:S(2)}, u32[]{:S(2)}) collective-permute-start(bf16[512,512]{1,0:T(8,128)(2,1)} %collective-permute-done.7.refs_1_), channel_id=1, source_target_pairs={{0,8},{8,16},{16,24},{24,32},{32,40},{40,48},{48,56},{56,64},{64,7... | collective-permute-start | bytes 1572872 | tf_op jit(solution)/shard_map/ppermute | solution.py:20
  62.6 11.1 %collective-permute-start.12 = (bf16[512,512]{1,0:T(8,128)(2,1)}, bf16[512,512]{1,0:T(8,128)(2,1)}, u32[]{:S(2)}, u32[]{:S(2)}) collective-permute-start(bf16[512,512]{1,0:T(8,128)(2,1)} %collective-permute-done.11.refs_8_), channel_id=1, source_target_pairs={{8,0},{16,8},{24,16},{32,24},{40,32},{48,40},{56,48},{64,56},{72,6... | collective-permute-start | bytes 1572872 | tf_op jit(solution)/shard_map/ppermute | solution.py:20
  73.7 26.3 %copy-start.1 = (bf16[512,512]{1,0:T(8,128)(2,1)S(1)}, bf16[512,512]{1,0:T(8,128)(2,1)}, u32[]{:S(2)}) copy-start(bf16[512,512]{1,0:T(8,128)(2,1)} %param.8) | copy-start | bytes 1572868
  81.7 18.3 %copy-start = (bf16[512,512]{1,0:T(8,128)(2,1)S(1)}, bf16[512,512]{1,0:T(8,128)(2,1)}, u32[]{:S(2)}) copy-start(bf16[512,512]{1,0:T(8,128)(2,1)} %param.9) | copy-start | bytes 1572868
  85.2 27.7 %all-to-all-start.1 = ((f32[256,1,8]{2,1,0:T(1,128)}), f32[256,1,8]{2,1,0:T(1,128)S(1)}, u32[]{:S(2)}, u32[]{:S(2)}) async-start(f32[256,1,8]{2,1,0:T(1,128)} %bitcast.31), calls=%async_computation.1 | async-start | bytes 262144 | tf_op jit(solution)/shard_map/all_to_all | solution.py:166

commit v4 on v3

v4 whole, which is shorter than its diff:
```python
import math

import jax
import jax.numpy as jnp
from jax import lax
from jax.experimental import pallas as pl
from jax.experimental.pallas import tpu as pltpu
from jax.sharding import PartitionSpec as P

MAXCH = 8
FGROUP = 512
FLEN = 2048
C = 256
INTERPRET = False


def shifted(value, axis, steps):
    count = lax.axis_size(axis)
    leading, last = (max(0, -steps), min(count, count - steps))
    return lax.ppermute(value, axis, [(source, source + steps) for source in range(leading, last)])


def band_tiles(rows_ref, tiles):
    for lag in range(MAXCH + 1):
        wide = jnp.broadcast_to(rows_ref[lag : lag + 1, :], (C, 2 * C))
        tiles[lag] = pltpu.roll(wide, 0, 1, stride=1, stride_axis=0)[:, C:].astype(jnp.bfloat16)


def filter_kernel(ids_rev, ids_src, *refs):
    lags = MAXCH + 1
    count = len(refs) - 2
    src_refs, grad_ref, filt_out = refs[:count], refs[count], refs[count + 1]
    own = grad_ref.shape[0]
    parts = own // C

    def src(j):
        return src_refs[j // parts][(j % parts) * C : (j % parts + 1) * C, :]

    exchange = (lax.broadcasted_iota(jnp.int32, (C, C), 0) + lax.broadcasted_iota(jnp.int32, (C, C), 1)
                == C - 1).astype(jnp.bfloat16)
    sums = [jnp.zeros((1, 2 * C), jnp.float32) for _ in range(lags)]
    for r in range(parts):
        reader_rev = ids_rev[r * C : (r + 1) * C, :]
        grad_rev = jnp.dot(exchange, grad_ref[r * C : (r + 1) * C, :],
                           preferred_element_type=jnp.float32).astype(jnp.bfloat16)
        for j in range(MAXCH + parts):
            lag = MAXCH + r - j
            if not 0 <= lag <= MAXCH:
                continue
            cols = slice(j * C, (j + 1) * C)
            prod = lax.dot_general(grad_rev, src(j), (((1,), (1,)), ((), ())),
                                   preferred_element_type=jnp.float32)
            prod = jnp.where(reader_rev == ids_src[:, cols], prod, 0.0)
            wide = jnp.concatenate([prod, jnp.zeros((C, C), jnp.float32)], axis=1)
            wide = pltpu.roll(wide, 0, 1, stride=1, stride_axis=0)
            sums[lag] = sums[lag] + jnp.sum(wide, axis=0, keepdims=True)
    for lag in range(lags):
        filt_out[lag : lag + 1, :] = sums[lag]


def conv_kernel(fwd_rows, bwd_rows, ids_own, ids_src, ids_rdr, skip, *refs):
    lags = MAXCH + 1
    count = (len(refs) - 4) // 2
    src_refs, grad_refs = refs[:count], refs[count : 2 * count]
    conv_out, mgrad_out, fwd_tiles, bwd_tiles = refs[2 * count :]
    own = src_refs[0].shape[0]
    parts = own // C

    def src(j):
        return src_refs[j // parts][(j % parts) * C : (j % parts + 1) * C, :]

    def grads(j):
        return grad_refs[j // parts][(j % parts) * C : (j % parts + 1) * C, :]

    band_tiles(fwd_rows, fwd_tiles)
    band_tiles(bwd_rows, bwd_tiles)
    skip_row = skip[...]
    for r in range(parts):
        reader_ids = ids_own[r * C : (r + 1) * C, :]
        acc = skip_row * src(MAXCH + r).astype(jnp.float32)
        for j in range(MAXCH + parts):
            lag = MAXCH + r - j
            if not 0 <= lag <= MAXCH:
                continue
            same = reader_ids == ids_src[:, j * C : (j + 1) * C]
            tile = jnp.where(same, fwd_tiles[lag], jnp.zeros((), jnp.bfloat16))
            acc = acc + jnp.dot(tile, src(j), preferred_element_type=jnp.float32)
        conv_out[r * C : (r + 1) * C, :] = acc
    for s in range(parts):
        source_ids = ids_own[s * C : (s + 1) * C, :]
        acc = skip_row * grads(s).astype(jnp.float32)
        for lag in range(lags):
            j = s + lag
            same = source_ids == ids_rdr[:, j * C : (j + 1) * C]
            tile = jnp.where(same, bwd_tiles[lag], jnp.zeros((), jnp.bfloat16))
            acc = acc + jnp.dot(tile, grads(j), preferred_element_type=jnp.float32)
        mgrad_out[s * C : (s + 1) * C, :] = acc


def filter_sums(ids_own, ids_src, src, grad):
    own = grad.shape[0]
    lags = MAXCH + 1
    parts = own // C
    ids_rev = ids_own.reshape(parts, C)[:, ::-1].reshape(own, 1)
    sums = pl.pallas_call(
        filter_kernel,
        out_shape=jax.ShapeDtypeStruct((lags, 2 * C), jnp.float32),
        compiler_params=pltpu.CompilerParams(vmem_limit_bytes=40 * 1024 * 1024),
        interpret=INTERPRET,
    )(ids_rev, ids_src.reshape(1, -1), *src, grad)
    ext = sum(
        jnp.pad(sums[lag, : 2 * C - 1][::-1], (C * lag + 1, (lags + 1) * C - C * lag - 2 * C))
        for lag in range(lags)
    )
    return ext[C : C + FLEN]


def local_conv(taps, ids_own, ids_src, ids_rdr, skip, src, grads):
    own, width = grads[0].shape
    lags = MAXCH + 1
    big = jnp.concatenate([jnp.zeros((2 * C,), jnp.float32), taps.astype(jnp.float32),
                           jnp.zeros((2 * C,), jnp.float32)])
    fwd_rows = jnp.stack([big[C * lag + C + 1 : C * lag + 3 * C + 1][::-1] for lag in range(lags)])
    bwd_rows = jnp.stack([big[C * lag + C : C * lag + 3 * C] for lag in range(lags)])
    return pl.pallas_call(
        conv_kernel,
        out_shape=(
            jax.ShapeDtypeStruct((own, width), jnp.float32),
            jax.ShapeDtypeStruct((own, width), jnp.float32),
        ),
        scratch_shapes=[pltpu.VMEM((lags, C, C), jnp.bfloat16), pltpu.VMEM((lags, C, C), jnp.bfloat16)],
        compiler_params=pltpu.CompilerParams(vmem_limit_bytes=60 * 1024 * 1024),
        interpret=INTERPRET,
    )(fwd_rows, bwd_rows, ids_own.reshape(own, 1), ids_src.reshape(1, -1),
      ids_rdr.reshape(1, -1), skip.reshape(1, width), *src, *grads)


def shards(query_in, key_in, value_in, out_grad, doc_ids, skip_gain, filter_taps):
    rows, width = query_in.shape
    assert width == FGROUP and rows % C == 0
    here = lax.axis_index("ctx")
    span = -(-FLEN // rows)
    hist = span * rows
    assert hist == MAXCH * C

    every = ("ctx", "tp")
    devices = lax.axis_size(every)
    groups = lax.axis_size("tp")
    offered = jnp.tile(filter_taps.T, (devices // groups, 1))
    taps = lax.all_to_all(offered, every, 0, 0, tiled=True).reshape(FLEN)

    mixed_in = (key_in.astype(jnp.float32) * value_in.astype(jnp.float32)).astype(jnp.bfloat16)
    conv_grad = (out_grad.astype(jnp.float32) * query_in.astype(jnp.float32)).astype(jnp.bfloat16)

    ahead = [mixed_in]
    behind = [conv_grad]
    for _ in range(span):
        ahead.append(shifted(ahead[-1], "ctx", 1))
        behind.append(shifted(behind[-1], "ctx", -1))

    ids_pad = jnp.concatenate(
        [jnp.full((hist,), -1, jnp.int32), doc_ids, jnp.full((hist,), -2, jnp.int32)]
    )
    ids_own = lax.dynamic_slice_in_dim(doc_ids, here * rows, rows)
    ids_src = lax.dynamic_slice_in_dim(ids_pad, here * rows, hist + rows)
    ids_rdr = lax.dynamic_slice_in_dim(ids_pad, here * rows + hist, hist + rows)

    filter_part = filter_sums(ids_own, ids_src, ahead[::-1], conv_grad)
    spread = lax.all_to_all(filter_part.reshape(devices, FLEN // devices), every, 0, 0, tiled=True)
    conv, mixed_grad = local_conv(taps, ids_own, ids_src, ids_rdr, skip_gain, ahead[::-1], behind)

    mixed_out = (query_in.astype(jnp.float32) * conv).astype(jnp.bfloat16)
    query_grad = (out_grad.astype(jnp.float32) * conv).astype(jnp.bfloat16)
    key_grad = (mixed_grad * value_in.astype(jnp.float32)).astype(jnp.bfloat16)
    value_grad = (mixed_grad * key_in.astype(jnp.float32)).astype(jnp.bfloat16)

    summed = jnp.sum(spread.reshape(devices // groups, groups, FLEN // devices), axis=0).T
    tokens = lax.axis_size("ctx") * rows
    filter_grad = summed * (1.0 / math.sqrt(FGROUP * tokens))
    return (mixed_out, query_grad, key_grad, value_grad, filter_grad)


def solution(mesh):
    in_specs = (
        P("ctx", "tp"),
        P("ctx", "tp"),
        P("ctx", "tp"),
        P("ctx", "tp"),
        P(),
        P("tp"),
        P(("ctx", "tp"), None),
    )
    out_specs = (
        P("ctx", "tp"),
        P("ctx", "tp"),
        P("ctx", "tp"),
        P("ctx", "tp"),
        P(("ctx", "tp"), None),
    )
    return jax.shard_map(shards, mesh=mesh, in_specs=in_specs, out_specs=out_specs, check_vma=False)
```

time: 114 us -> 124 us (1.088)
  local copies, waits for them, and re-layouts: 11.6 us -> 30.3 us
  starting transfers between devices: 59.3 us -> 51.2 us
  waiting for transfers between devices: 28.5 us -> 25.9 us
    ppermute x5 -> x0, starting transfers between devices: 15.4 us -> none  [swapped(): lax.ppermute(value, axis, [(source, source ^ bit) for source in range(cou...]
    all_to_all x1, starting transfers between devices: 5.42 us -> 18.2 us  [shards(): taps = lax.all_to_all(offered, every, 0, 0, tiled=True).reshape(FLEN)]
    ppermute x8, waiting for transfers between devices: 6.47 us -> 17.5 us  [shifted(): lax.ppermute(value, axis, [(source, source + steps) for source in range(l...]
    rev x9, local copies, waits for them, and re-layouts: 0.86 us -> 11.3 us  [local_conv(): big[C * lag + C + 1:C * lag + 3 * C + 1][::-1]]
    ppermute x5 -> x0, waiting for transfers between devices: 7.92 us -> none  [swapped(): lax.ppermute(value, axis, [(source, source ^ bit) for source in range(cou...]
    all_to_all x1, waiting for transfers between devices: 9.58 us -> 3.09 us  [shards(): lax.all_to_all(filter_part.reshape(devices, FLEN // devices), every, 0, 0...]
    another operation x1 -> x8, local copies, waits for them, and re-layouts: 1.23 us -> 5.86 us  [local_conv(): jnp.stack([big[C * lag + C:C * lag + 3 * C] for lag in range(lags)])]
    all_to_all x1, starting transfers between devices: 14.8 us -> 11 us  [shards(): lax.all_to_all(filter_part.reshape(devices, FLEN // devices), every, 0, 0...]
  transfers between devices with their start and end apart: 15 -> 10, of which waited for: 7 -> 5; matrix products, arithmetic and copies ran while one was open for 10% -> 27% of each run, Pallas kernels for 0% -> 7%
where the time goes in v4:
time: 124 us; the launch traced here: 123 us
  starting transfers between devices  51.2 us (41%)
  local copies, waits for them, and re-layouts  30.3 us (24%)
  waiting for transfers between devices  25.9 us (21%)
  Pallas kernels  8.35 us (7%)
  other arithmetic  6.19 us (5%)
    ppermute x8, starting transfers between devices, shifted(): lax.ppermute(value, axis, [(source, source + steps) for source in range(l...  21.9 us
    all_to_all x1, starting transfers between devices, shards(): taps = lax.all_to_all(offered, every, 0, 0, tiled=True).reshape(FLEN)  18.2 us
    ppermute x8, waiting for transfers between devices, shifted(): lax.ppermute(value, axis, [(source, source + steps) for source in range(l...  17.5 us
    rev x9, local copies, waits for them, and re-layouts, local_conv(): big[C * lag + C + 1:C * lag + 3 * C + 1][::-1]  11.3 us
    all_to_all x1, starting transfers between devices, shards(): lax.all_to_all(filter_part.reshape(devices, FLEN // devices), every, 0, 0...  11 us
    pallas_call x1, Pallas kernels, local_conv(): pl.pallas_call(conv_kernel, out_shape=(jax.ShapeDtypeStruct((own, width),...  6.43 us
    another operation x8, local copies, waits for them, and re-layouts, local_conv(): jnp.stack([big[C * lag + C:C * lag + 3 * C] for lag in range(lags)])  5.86 us
    all_to_all x1, waiting for transfers between devices, shards(): taps = lax.all_to_all(offered, every, 0, 0, tiled=True).reshape(FLEN)  5.32 us
  transfers between devices with their start and end apart: 10, of which 5 were waited for; matrix products, arithmetic and copies ran while one was open for 27% of the time, Pallas kernels for 7%

profile of v4, /device:TPU:1, one launch (start us, length us, event | category | flops | bytes accessed | tf_op | source)
XLA Modules:
  0.0 123.1 jit_solution(367878853927474657)
XLA Ops:
  0.7 1.4 %fusion.2.refs_4_ = bf16[512,512]{1,0:T(8,128)(2,1)S(1)} fusion(bf16[512,512]{1,0:T(8,128)(2,1)} %param.9, bf16[512,512]{1,0:T(8,128)(2,1)} %param.8), kind=kLoop, calls=%fused_computation.8 | loop fusion | flops 1048576 | bytes 1572864 | tf_op jit(solution)/shard_map/convert_element_type | solution.py:152
  2.1 4.4 %collective-permute-start = (bf16[512,512]{1,0:T(8,128)(2,1)S(1)}, bf16[512,512]{1,0:T(8,128)(2,1)S(1)}, u32[]{:S(2)}, u32[]{:S(2)}) collective-permute-start(bf16[512,512]{1,0:T(8,128)(2,1)S(1)} %fusion.2.refs_4_), channel_id=1, source_target_pairs={{0,8},{8,16},{16,24},{24,32},{32,40},{40,48},{48,56},{56,64},{64,7... | collective-permute-start | bytes 1572872 | tf_op jit(solution)/shard_map/ppermute | solution.py:20
  6.7 1.3 %collective-permute-start.4 = (bf16[512,512]{1,0:T(8,128)(2,1)S(1)}, bf16[512,512]{1,0:T(8,128)(2,1)S(1)}, u32[]{:S(2)}, u32[]{:S(2)}) collective-permute-start(bf16[512,512]{1,0:T(8,128)(2,1)S(1)} %fusion.4.refs_5_), channel_id=1, source_target_pairs={{8,0},{16,8},{24,16},{32,24},{40,32},{48,40},{56,48},{64,56},{72,6... | collective-permute-start | bytes 1572872 | tf_op jit(solution)/shard_map/ppermute | solution.py:20
  8.0 9.1 %collective-permute-done.refs_3_ = bf16[512,512]{1,0:T(8,128)(2,1)S(1)} collective-permute-done((bf16[512,512]{1,0:T(8,128)(2,1)S(1)}, bf16[512,512]{1,0:T(8,128)(2,1)S(1)}, u32[]{:S(2)}, u32[]{:S(2)}) %collective-permute-start) | collective-permute-done | bytes 524320 | tf_op jit(solution)/shard_map/ppermute | solution.py:20
  17.0 4.1 %collective-permute-start.1 = (bf16[512,512]{1,0:T(8,128)(2,1)S(1)}, bf16[512,512]{1,0:T(8,128)(2,1)S(1)}, u32[]{:S(2)}, u32[]{:S(2)}) collective-permute-start(bf16[512,512]{1,0:T(8,128)(2,1)S(1)} %collective-permute-done.refs_3_), channel_id=1, source_target_pairs={{0,8},{8,16},{16,24},{24,32},{32,40},{40,48},{48,56},{56,64},{64,7... | collective-permute-start | bytes 1572872 | tf_op jit(solution)/shard_map/ppermute | solution.py:20
  21.2 0.2 collective-permute-done.4.refs_6_
  21.4 1.3 %collective-permute-start.5 = (bf16[512,512]{1,0:T(8,128)(2,1)S(1)}, bf16[512,512]{1,0:T(8,128)(2,1)}, u32[]{:S(2)}, u32[]{:S(2)}) collective-permute-start(bf16[512,512]{1,0:T(8,128)(2,1)S(1)} %collective-permute-done.4.refs_6_), channel_id=1, source_target_pairs={{8,0},{16,8},{24,16},{32,24},{40,32},{48,40},{56,48},{64,56},{72,6... | collective-permute-start | bytes 1572872 | tf_op jit(solution)/shard_map/ppermute | solution.py:20
  22.7 8.2 %collective-permute-done.1.refs_2_ = bf16[512,512]{1,0:T(8,128)(2,1)S(1)} collective-permute-done((bf16[512,512]{1,0:T(8,128)(2,1)S(1)}, bf16[512,512]{1,0:T(8,128)(2,1)S(1)}, u32[]{:S(2)}, u32[]{:S(2)}) %collective-permute-start.1) | collective-permute-done | bytes 524320 | tf_op jit(solution)/shard_map/ppermute | solution.py:20
  30.9 4.2 %collective-permute-start.2 = (bf16[512,512]{1,0:T(8,128)(2,1)S(1)}, bf16[512,512]{1,0:T(8,128)(2,1)S(1)}, u32[]{:S(2)}, u32[]{:S(2)}) collective-permute-start(bf16[512,512]{1,0:T(8,128)(2,1)S(1)} %collective-permute-done.1.refs_2_), channel_id=1, source_target_pairs={{0,8},{8,16},{16,24},{24,32},{32,40},{40,48},{48,56},{56,64},{64,7... | collective-permute-start | bytes 1572872 | tf_op jit(solution)/shard_map/ppermute | solution.py:20
  35.3 0.8 copy.21
  36.1 18.2 %all-to-all-start = ((bf16[256,1,8]{2,1,0:T(2,128)(2,1)}), bf16[256,1,8]{2,1,0:T(2,128)(2,1)S(1)}, u32[]{:S(2)}, u32[]{:S(2)}) async-start(bf16[256,1,8]{2,1,0:T(2,128)(2,1)} %copy.21), calls=%async_computation | async-start | bytes 262144 | tf_op jit(solution)/shard_map/all_to_all | solution.py:150
  54.4 1.3 %collective-permute-start.6 = (bf16[512,512]{1,0:T(8,128)(2,1)}, bf16[512,512]{1,0:T(8,128)(2,1)}, u32[]{:S(2)}, u32[]{:S(2)}) collective-permute-start(bf16[512,512]{1,0:T(8,128)(2,1)} %collective-permute-done.5.refs_7_), channel_id=1, source_target_pairs={{8,0},{16,8},{24,16},{32,24},{40,32},{48,40},{56,48},{64,56},{72,6... | collective-permute-start | bytes 1572872 | tf_op jit(solution)/shard_map/ppermute | solution.py:20
  55.7 4.0 %collective-permute-start.3 = (bf16[512,512]{1,0:T(8,128)(2,1)S(1)}, bf16[512,512]{1,0:T(8,128)(2,1)S(1)}, u32[]{:S(2)}, u32[]{:S(2)}) collective-permute-start(bf16[512,512]{1,0:T(8,128)(2,1)S(1)} %collective-permute-done.2.refs_1_), channel_id=1, source_target_pairs={{0,8},{8,16},{16,24},{24,32},{32,40},{40,48},{48,56},{56,64},{64,7... | collective-permute-start | bytes 1572872 | tf_op jit(solution)/shard_map/ppermute | solution.py:20
  60.0 0.9 copy.22.ids_own
  60.9 0.6 reshape.71.ids_rdr
  61.5 0.2 rev.66
  61.6 0.1 copy.27
  61.8 5.3 %all-to-all-done = bf16[256,1,8]{2,1,0:T(2,128)(2,1)S(1)} async-done(((bf16[256,1,8]{2,1,0:T(2,128)(2,1)}), bf16[256,1,8]{2,1,0:T(2,128)(2,1)S(1)}, u32[]{:S(2)}, u32[]{:S(2)}) %all-to-all-start) | async-done | bytes 4128 | tf_op jit(solution)/shard_map/all_to_all | solution.py:150
  67.1 1.0 convert_reduce_fusion
  68.2 1.6 %convert_element_type.60 = f32[2048]{0:T(1024)} reshape(f32[256,8]{1,0:T(8,128)} %convert_reduce_fusion) | data formatting | bytes 16384 | tf_op jit(solution)/shard_map/convert_element_type | solution.py:121
  69.8 1.6 %pad_slice_fusion = (f32[512]{0:T(512)}, f32[512]{0:T(512)}, f32[512]{0:T(512)S(1)}, f32[512]{0:T(512)}, f32[512]{0:T(512)}, /*index=5*/f32[512]{0:T(512)}, f32[...) fusion(f32[2048]{0:T(1024)} %convert_element_type.60), kind=kLoop, calls=%fused_computation.21 | loop fusion | bytes 43008 | tf_op jit(solution)/shard_map/slice | solution.py:124
  71.4 1.3 %rev.57 = f32[512]{0:T(512)} reverse(f32[512]{0:T(512)} %get-tuple-element.51), dimensions={0} | reverse | bytes 4096 | tf_op jit(solution)/shard_map/rev | solution.py:123
  72.7 1.3 %rev.58 = f32[512]{0:T(512)} reverse(f32[512]{0:T(512)} %get-tuple-element.50), dimensions={0} | reverse | bytes 4096 | tf_op jit(solution)/shard_map/rev | solution.py:123
  74.1 1.3 %rev.59 = f32[512]{0:T(512)} reverse(f32[512]{0:T(512)} %get-tuple-element.49), dimensions={0} | reverse | bytes 4096 | tf_op jit(solution)/shard_map/rev | solution.py:123
  75.4 1.3 %rev.60 = f32[512]{0:T(512)} reverse(f32[512]{0:T(512)} %get-tuple-element.48), dimensions={0} | reverse | bytes 4096 | tf_op jit(solution)/shard_map/rev | solution.py:123
  76.8 1.3 %rev.61 = f32[512]{0:T(512)} reverse(f32[512]{0:T(512)} %get-tuple-element.47), dimensions={0} | reverse | bytes 4096 | tf_op jit(solution)/shard_map/rev | solution.py:123
  78.1 1.3 %rev.62 = f32[512]{0:T(512)} reverse(f32[512]{0:T(512)} %get-tuple-element.46), dimensions={0} | reverse | bytes 4096 | tf_op jit(solution)/shard_map/rev | solution.py:123
  79.4 1.3 %rev.63 = f32[512]{0:T(512)} reverse(f32[512]{0:T(512)} %get-tuple-element.45), dimensions={0} | reverse | bytes 4096 | tf_op jit(solution)/shard_map/rev | solution.py:123
  80.7 1.3 %rev.64 = f32[512]{0:T(512)} reverse(f32[512]{0:T(512)} %get-tuple-element.44), dimensions={0} | reverse | bytes 4096 | tf_op jit(solution)/shard_map/rev | solution.py:123
  82.1 0.7 rev.65
  82.7 0.1 convert_element_type.59
  82.9 1.2 slice_reduce_fusion
  84.1 0.8 stack.71
  84.9 1.4 %stack.72 = f32[1,512]{1,0:T(1,128)} reshape(f32[64,8]{1,0:T(8,128)} %get-tuple-element.24) | data formatting | bytes 4096 | tf_op jit(solution)/shard_map/stack | solution.py:124
  86.3 1.4 %stack.73 = f32[1,512]{1,0:T(1,128)} reshape(f32[64,8]{1,0:T(8,128)} %get-tuple-element.23) | data formatting | bytes 4096 | tf_op jit(solution)/shard_map/stack | solution.py:124
  87.8 0.7 stack.74
  88.8 0.5 copy-done.26
  89.5 1.2 %stack.69.fwd_rows = f32[9,512]{1,0:T(8,128)} concatenate(f32[1,512]{1,0:T(1,128)S(1)} %bitcast.48, f32[1,512]{1,0:T(1,128)S(1)} %bitcast.49, f32[1,512]{1,0:T(1,128)S(1)} %bitcast.50, f32[1,512]{1,0:T(1,128)S(1)} %bitcast.51, f32[1,512]{1,0:T(1,128)S(1)} %bitcast.52, f32[1,512]{1,0:T(1,128)S(1)} %bitcast.53, f32[1,512]{1,0:T(1,128)S(1)} %bitcast.54, f32[1,512]{1,0:T(1,128)S(1)} %bitcast.55, ...), dimensions={0} | concatenate | bytes 36864 | tf_op jit(solution)/shard_map/stack | solution.py:123
  90.7 0.7 copy-done.17
  91.4 1.2 %stack.79.bwd_rows = f32[9,512]{1,0:T(8,128)} concatenate(f32[1,512]{1,0:T(1,128)S(1)} %bitcast.68, f32[1,512]{1,0:T(1,128)S(1)} %stack.71, f32[1,512]{1,0:T(1,128)S(1)} %copy-done.15, f32[1,512]{1,0:T(1,128)S(1)} %copy-done.16, f32[1,512]{1,0:T(1,128)S(1)} %copy-done.17, f32[1,512]{1,0:T(1,128)S(1)} %stack.75, f32[1,512]{1,0:T(1,128)S(1)} %stack.76, f32[1,512]{1,0:T(1,128)S(1)} %stack.77, ...), dimensions={0} | concatenate | bytes 36864 | tf_op jit(solution)/shard_map/stack | solution.py:124
  92.7 1.3 %collective-permute-start.7 = (bf16[512,512]{1,0:T(8,128)(2,1)}, bf16[512,512]{1,0:T(8,128)(2,1)}, u32[]{:S(2)}, u32[]{:S(2)}) collective-permute-start(bf16[512,512]{1,0:T(8,128)(2,1)} %collective-permute-done.6.refs_8_), channel_id=1, source_target_pairs={{8,0},{16,8},{24,16},{32,24},{40,32},{48,40},{56,48},{64,56},{72,6... | collective-permute-start | bytes 1572872 | tf_op jit(solution)/shard_map/ppermute | solution.py:20
  94.0 1.9 %shard_map.111 = f32[9,512]{1,0:T(8,128)S(1)} custom-call(s32[512,1]{1,0:T(8,128)S(1)} %bitcast.44, s32[1,2560]{1,0:T(1,128)S(1)} %reshape.70.ids_src, bf16[512,512]{1,0:T(8,128)(2,1)S(1)} %collective-permute-done.3.refs_0_, bf16[512,512]{1,0:T(8,128)(2,1)S(1)} %collective-permute-done.2.refs_1_, bf16[512,512]{1,0:T(8,128)(2,1)S(1)} %collective-permute-done.1.refs_2_, ...), custom_call_target="tpu_custom_call" | custom-call | tf_op jit(solution)/shard_map/pallas_call | solution.py:105
  97.7 0.8 slice.134
  98.5 11.0 %all-to-all-start.1 = ((f32[256,1,8]{2,1,0:T(1,128)}), f32[256,1,8]{2,1,0:T(1,128)S(1)}, u32[]{:S(2)}, u32[]{:S(2)}) async-start(f32[256,1,8]{2,1,0:T(1,128)} %bitcast.23), calls=%async_computation.1 | async-start | bytes 262144 | tf_op jit(solution)/shard_map/all_to_all | solution.py:169
  109.6 6.4 %shard_map.110 = (f32[512,512]{1,0:T(8,128)}, f32[512,512]{1,0:T(8,128)}) custom-call(f32[9,512]{1,0:T(8,128)} %stack.69.fwd_rows, f32[9,512]{1,0:T(8,128)} %stack.79.bwd_rows, s32[512,1]{1,0:T(8,128)} %copy.22.ids_own, s32[1,2560]{1,0:T(1,128)} %copy-done.6, s32[1,2560]{1,0:T(1,128)} %reshape.71.ids_rdr, f32[1,512]{1,0:T(1,128)} %bitcast.69, ...), custom_call_target="tpu_custom_call" | custom-call | tf_op jit(solution)/shard_map/pallas_call | solution.py:125
  116.0 3.3 %fusion.1 = (bf16[512,512]{1,0:T(8,128)(2,1)}, bf16[512,512]{1,0:T(8,128)(2,1)}, bf16[512,512]{1,0:T(8,128)(2,1)}, bf16[512,512]{1,0:T(8,128)(2,1)}) fusion(f32[512,512]{1,0:T(8,128)} %get-tuple-element.8, bf16[512,512]{1,0:T(8,128)(2,1)S(1)} %copy-done.8, bf16[512,512]{1,0:T(8,128)(2,1)S(1)} %copy-done.7, f32[512,512]{1,0:T(8,128)} %get-tuple-element.7, ...), kind=kLoop, calls=%fused_computation.7 | loop fusion | flops 3145728 | bytes 6291456 | tf_op jit(solution)/shard_map/convert_element_type | solution.py:175
  119.3 3.1 %all-to-all-done.1 = f32[256,1,8]{2,1,0:T(1,128)S(1)} async-done(((f32[256,1,8]{2,1,0:T(1,128)}), f32[256,1,8]{2,1,0:T(1,128)S(1)}, u32[]{:S(2)}, u32[]{:S(2)}) %all-to-all-start.1) | async-done | bytes 8224 | tf_op jit(solution)/shard_map/all_to_all | solution.py:169
  122.4 0.7 copy.25
  (100 shorter events, 2.8 us)
Async XLA Ops:
  0.6 5.9 %copy-start.9 = (bf16[512,512]{1,0:T(8,128)(2,1)S(1)}, bf16[512,512]{1,0:T(8,128)(2,1)}, u32[]{:S(2)}) copy-start(bf16[512,512]{1,0:T(8,128)(2,1)} %param.7) | copy-start | bytes 1572868
  0.6 5.9 %copy-start.11 = (bf16[512,512]{1,0:T(8,128)(2,1)S(1)}, bf16[512,512]{1,0:T(8,128)(2,1)}, u32[]{:S(2)}) copy-start(bf16[512,512]{1,0:T(8,128)(2,1)} %param.10) | copy-start | bytes 1572868
  2.1 91.9 %copy-start = (bf16[512,512]{1,0:T(8,128)(2,1)}, bf16[512,512]{1,0:T(8,128)(2,1)S(1)}, u32[]{:S(2)}) copy-start(bf16[512,512]{1,0:T(8,128)(2,1)S(1)} %fusion.2.refs_4_) | copy-start | bytes 1572868
  2.1 15.0 %collective-permute-start = (bf16[512,512]{1,0:T(8,128)(2,1)S(1)}, bf16[512,512]{1,0:T(8,128)(2,1)S(1)}, u32[]{:S(2)}, u32[]{:S(2)}) collective-permute-start(bf16[512,512]{1,0:T(8,128)(2,1)S(1)} %fusion.2.refs_4_), channel_id=1, source_target_pairs={{0,8},{8,16},{16,24},{24,32},{32,40},{40,48},{48,56},{56,64},{64,7... | collective-permute-start | bytes 1572872 | tf_op jit(solution)/shard_map/ppermute | solution.py:20
  6.5 28.6 %copy-start.29 = (bf16[8,8]{1,0:T(8,128)(2,1)S(1)}, bf16[8,8]{1,0:T(8,128)(2,1)}, u32[]{:S(2)}) copy-start(bf16[8,8]{1,0:T(8,128)(2,1)} %param.13) | copy-start | bytes 388
  6.7 87.3 %copy-start.1 = (bf16[512,512]{1,0:T(8,128)(2,1)}, bf16[512,512]{1,0:T(8,128)(2,1)S(1)}, u32[]{:S(2)}) copy-start(bf16[512,512]{1,0:T(8,128)(2,1)S(1)} %fusion.4.refs_5_) | copy-start | bytes 1572868
  6.7 14.7 %collective-permute-start.4 = (bf16[512,512]{1,0:T(8,128)(2,1)S(1)}, bf16[512,512]{1,0:T(8,128)(2,1)S(1)}, u32[]{:S(2)}, u32[]{:S(2)}) collective-permute-start(bf16[512,512]{1,0:T(8,128)(2,1)S(1)} %fusion.4.refs_5_), channel_id=1, source_target_pairs={{8,0},{16,8},{24,16},{32,24},{40,32},{48,40},{56,48},{64,56},{72,6... | collective-permute-start | bytes 1572872 | tf_op jit(solution)/shard_map/ppermute | solution.py:20
  17.0 76.9 %copy-start.2 = (bf16[512,512]{1,0:T(8,128)(2,1)}, bf16[512,512]{1,0:T(8,128)(2,1)S(1)}, u32[]{:S(2)}) copy-start(bf16[512,512]{1,0:T(8,128)(2,1)S(1)} %collective-permute-done.refs_3_) | copy-start | bytes 1572868
  17.0 13.8 %collective-permute-start.1 = (bf16[512,512]{1,0:T(8,128)(2,1)S(1)}, bf16[512,512]{1,0:T(8,128)(2,1)S(1)}, u32[]{:S(2)}, u32[]{:S(2)}) collective-permute-start(bf16[512,512]{1,0:T(8,128)(2,1)S(1)} %collective-permute-done.refs_3_), channel_id=1, source_target_pairs={{0,8},{8,16},{16,24},{24,32},{32,40},{40,48},{48,56},{56,64},{64,7... | collective-permute-start | bytes 1572872 | tf_op jit(solution)/shard_map/ppermute | solution.py:20
  21.4 34.3 %copy-start.13 = (bf16[512,512]{1,0:T(8,128)(2,1)}, bf16[512,512]{1,0:T(8,128)(2,1)S(1)}, u32[]{:S(2)}) copy-start(bf16[512,512]{1,0:T(8,128)(2,1)S(1)} %collective-permute-done.4.refs_6_) | copy-start | bytes 1572868
  21.4 33.0 %collective-permute-start.5 = (bf16[512,512]{1,0:T(8,128)(2,1)S(1)}, bf16[512,512]{1,0:T(8,128)(2,1)}, u32[]{:S(2)}, u32[]{:S(2)}) collective-permute-start(bf16[512,512]{1,0:T(8,128)(2,1)S(1)} %collective-permute-done.4.refs_6_), channel_id=1, source_target_pairs={{8,0},{16,8},{24,16},{32,24},{40,32},{48,40},{56,48},{64,56},{72,6... | collective-permute-start | bytes 1572872 | tf_op jit(solution)/shard_map/ppermute | solution.py:20
  30.9 63.1 %copy-start.3 = (bf16[512,512]{1,0:T(8,128)(2,1)}, bf16[512,512]{1,0:T(8,128)(2,1)S(1)}, u32[]{:S(2)}) copy-start(bf16[512,512]{1,0:T(8,128)(2,1)S(1)} %collective-permute-done.1.refs_2_) | copy-start | bytes 1572868
  30.9 24.8 %collective-permute-start.2 = (bf16[512,512]{1,0:T(8,128)(2,1)S(1)}, bf16[512,512]{1,0:T(8,128)(2,1)S(1)}, u32[]{:S(2)}, u32[]{:S(2)}) collective-permute-start(bf16[512,512]{1,0:T(8,128)(2,1)S(1)} %collective-permute-done.1.refs_2_), channel_id=1, source_target_pairs={{0,8},{8,16},{16,24},{24,32},{32,40},{40,48},{48,56},{56,64},{64,7... | collective-permute-start | bytes 1572872 | tf_op jit(solution)/shard_map/ppermute | solution.py:20
  36.1 18.3 %copy-start.14 = (s32[16384]{0:T(1024)S(1)}, s32[16384]{0:T(1024)}, u32[]{:S(2)}) copy-start(s32[16384]{0:T(1024)} %param.11) | copy-start | bytes 196612
  36.1 31.0 %all-to-all-start = ((bf16[256,1,8]{2,1,0:T(2,128)(2,1)}), bf16[256,1,8]{2,1,0:T(2,128)(2,1)S(1)}, u32[]{:S(2)}, u32[]{:S(2)}) async-start(bf16[256,1,8]{2,1,0:T(2,128)(2,1)} %copy.21), calls=%async_computation | async-start | bytes 262144 | tf_op jit(solution)/shard_map/all_to_all | solution.py:150
  54.4 38.3 %collective-permute-start.6 = (bf16[512,512]{1,0:T(8,128)(2,1)}, bf16[512,512]{1,0:T(8,128)(2,1)}, u32[]{:S(2)}, u32[]{:S(2)}) collective-permute-start(bf16[512,512]{1,0:T(8,128)(2,1)} %collective-permute-done.5.refs_7_), channel_id=1, source_target_pairs={{8,0},{16,8},{24,16},{32,24},{40,32},{48,40},{56,48},{64,56},{72,6... | collective-permute-start | bytes 1572872 | tf_op jit(solution)/shard_map/ppermute | solution.py:20
  55.7 38.3 %copy-start.4 = (bf16[512,512]{1,0:T(8,128)(2,1)}, bf16[512,512]{1,0:T(8,128)(2,1)S(1)}, u32[]{:S(2)}) copy-start(bf16[512,512]{1,0:T(8,128)(2,1)S(1)} %collective-permute-done.2.refs_1_) | copy-start | bytes 1572868
  55.7 38.2 %collective-permute-start.3 = (bf16[512,512]{1,0:T(8,128)(2,1)S(1)}, bf16[512,512]{1,0:T(8,128)(2,1)S(1)}, u32[]{:S(2)}, u32[]{:S(2)}) collective-permute-start(bf16[512,512]{1,0:T(8,128)(2,1)S(1)} %collective-permute-done.2.refs_1_), channel_id=1, source_target_pairs={{0,8},{8,16},{16,24},{24,32},{32,40},{40,48},{48,56},{56,64},{64,7... | collective-permute-start | bytes 1572872 | tf_op jit(solution)/shard_map/ppermute | solution.py:20
  60.8 33.2 %copy-start.6 = (s32[1,2560]{1,0:T(1,128)}, s32[1,2560]{1,0:T(1,128)S(1)}, u32[]{:S(2)}) copy-start(s32[1,2560]{1,0:T(1,128)S(1)} %reshape.70.ids_src) | copy-start | bytes 30724
  88.6 0.7 copy-start.26
  88.7 0.7 copy-start.20
  88.7 0.7 copy-start.21
  88.7 0.7 copy-start.22
  88.7 0.7 copy-start.23
  88.8 0.7 copy-start.24
  88.8 0.7 copy-start.25
  88.8 0.7 copy-start.19
  88.8 0.7 copy-start.18
  89.5 1.3 %copy-start.27 = (f32[512]{0:T(512)S(1)}, f32[512]{0:T(512)}, u32[]{:S(2)}) copy-start(f32[512]{0:T(512)} %get-tuple-element.41) | copy-start | bytes 6148
  89.5 1.3 %copy-start.28 = (f32[512]{0:T(512)S(1)}, f32[512]{0:T(512)}, u32[]{:S(2)}) copy-start(f32[512]{0:T(512)} %get-tuple-element.42) | copy-start | bytes 6148
  90.7 0.7 copy-start.17
  90.7 0.7 copy-start.16
  90.7 0.7 copy-start.15
  92.7 16.8 %collective-permute-start.7 = (bf16[512,512]{1,0:T(8,128)(2,1)}, bf16[512,512]{1,0:T(8,128)(2,1)}, u32[]{:S(2)}, u32[]{:S(2)}) collective-permute-start(bf16[512,512]{1,0:T(8,128)(2,1)} %collective-permute-done.6.refs_8_), channel_id=1, source_target_pairs={{8,0},{16,8},{24,16},{32,24},{40,32},{48,40},{56,48},{64,56},{72,6... | collective-permute-start | bytes 1572872 | tf_op jit(solution)/shard_map/ppermute | solution.py:20
  94.0 2.0 %copy-start.5 = (bf16[512,512]{1,0:T(8,128)(2,1)}, bf16[512,512]{1,0:T(8,128)(2,1)S(1)}, u32[]{:S(2)}) copy-start(bf16[512,512]{1,0:T(8,128)(2,1)S(1)} %collective-permute-done.3.refs_0_) | copy-start | bytes 1572868
  98.5 23.9 %all-to-all-start.1 = ((f32[256,1,8]{2,1,0:T(1,128)}), f32[256,1,8]{2,1,0:T(1,128)S(1)}, u32[]{:S(2)}, u32[]{:S(2)}) async-start(f32[256,1,8]{2,1,0:T(1,128)} %bitcast.23), calls=%async_computation.1 | async-start | bytes 262144 | tf_op jit(solution)/shard_map/all_to_all | solution.py:169
  109.5 6.5 %copy-start.7 = (bf16[512,512]{1,0:T(8,128)(2,1)S(1)}, bf16[512,512]{1,0:T(8,128)(2,1)}, u32[]{:S(2)}) copy-start(bf16[512,512]{1,0:T(8,128)(2,1)} %param.9) | copy-start | bytes 1572868
  109.5 6.5 %copy-start.8 = (bf16[512,512]{1,0:T(8,128)(2,1)S(1)}, bf16[512,512]{1,0:T(8,128)(2,1)}, u32[]{:S(2)}) copy-start(bf16[512,512]{1,0:T(8,128)(2,1)} %param.8) | copy-start | bytes 1572868
  109.5 6.5 %copy-start.10 = (bf16[512,512]{1,0:T(8,128)(2,1)S(1)}, bf16[512,512]{1,0:T(8,128)(2,1)}, u32[]{:S(2)}) copy-start(bf16[512,512]{1,0:T(8,128)(2,1)} %param.7) | copy-start | bytes 1572868
  109.5 6.5 %copy-start.12 = (bf16[512,512]{1,0:T(8,128)(2,1)S(1)}, bf16[512,512]{1,0:T(8,128)(2,1)}, u32[]{:S(2)}) copy-start(bf16[512,512]{1,0:T(8,128)(2,1)} %param.10) | copy-start | bytes 1572868

commit v5 on v4

--- a/solution.py
+++ b/solution.py
@@ -20,45 +20,52 @@
     return lax.ppermute(value, axis, [(source, source + steps) for source in range(leading, last)])
 
 
-def band_tiles(rows_ref, tiles):
+def band_tiles(taps_row, fwd_tiles, bwd_tiles):
     for lag in range(MAXCH + 1):
-        wide = jnp.broadcast_to(rows_ref[lag : lag + 1, :], (C, 2 * C))
-        tiles[lag] = pltpu.roll(wide, 0, 1, stride=1, stride_axis=0)[:, C:].astype(jnp.bfloat16)
+        start = C * lag + C
+        wide = jnp.broadcast_to(taps_row[:, start : start + 2 * C], (C, 2 * C))
+        tile = pltpu.roll(wide, 0, 1, stride=1, stride_axis=0)[:, C:]
+        bwd_tiles[lag] = tile.astype(jnp.bfloat16)
+        fwd_tiles[lag] = tile.T.astype(jnp.bfloat16)
 
 
-def filter_kernel(ids_rev, ids_src, *refs):
+def filter_kernel(ids_own, ids_rev, *refs):
     lags = MAXCH + 1
     count = len(refs) - 2
     src_refs, grad_ref, filt_out = refs[:count], refs[count], refs[count + 1]
     own = grad_ref.shape[0]
     parts = own // C
 
-    def src(j):
-        return src_refs[j // parts][(j % parts) * C : (j % parts + 1) * C, :]
-
     exchange = (lax.broadcasted_iota(jnp.int32, (C, C), 0) + lax.broadcasted_iota(jnp.int32, (C, C), 1)
                 == C - 1).astype(jnp.bfloat16)
+    flipped = {}
+
+    def src_rev(j):
+        if j not in flipped:
+            block = src_refs[j // parts][(j % parts) * C : (j % parts + 1) * C, :]
+            flipped[j] = jnp.dot(exchange, block, preferred_element_type=jnp.float32).astype(jnp.bfloat16)
+        return flipped[j]
+
     sums = [jnp.zeros((1, 2 * C), jnp.float32) for _ in range(lags)]
     for r in range(parts):
-        reader_rev = ids_rev[r * C : (r + 1) * C, :]
-        grad_rev = jnp.dot(exchange, grad_ref[r * C : (r + 1) * C, :],
-                           preferred_element_type=jnp.float32).astype(jnp.bfloat16)
+        reader_ids = ids_own[r * C : (r + 1) * C, :]
+        grad = grad_ref[r * C : (r + 1) * C, :]
         for j in range(MAXCH + parts):
             lag = MAXCH + r - j
             if not 0 <= lag <= MAXCH:
                 continue
-            cols = slice(j * C, (j + 1) * C)
-            prod = lax.dot_general(grad_rev, src(j), (((1,), (1,)), ((), ())),
+            prod = lax.dot_general(grad, src_rev(j), (((1,), (1,)), ((), ())),
                                    preferred_element_type=jnp.float32)
-            prod = jnp.where(reader_rev == ids_src[:, cols], prod, 0.0)
+            prod = jnp.where(reader_ids == ids_rev[:, j * C : (j + 1) * C], prod, 0.0)
             wide = jnp.concatenate([prod, jnp.zeros((C, C), jnp.float32)], axis=1)
             wide = pltpu.roll(wide, 0, 1, stride=1, stride_axis=0)
             sums[lag] = sums[lag] + jnp.sum(wide, axis=0, keepdims=True)
+    filt_out[...] = jnp.zeros(filt_out.shape, jnp.float32)
     for lag in range(lags):
-        filt_out[lag : lag + 1, :] = sums[lag]
+        filt_out[:, C * lag : C * lag + 2 * C] += sums[lag]
 
 
-def conv_kernel(fwd_rows, bwd_rows, ids_own, ids_src, ids_rdr, skip, *refs):
+def conv_kernel(taps_row, ids_own, ids_src, ids_rdr, skip, *refs):
     lags = MAXCH + 1
     count = (len(refs) - 4) // 2
     src_refs, grad_refs = refs[:count], refs[count : 2 * count]
@@ -72,8 +79,7 @@
     def grads(j):
         return grad_refs[j // parts][(j % parts) * C : (j % parts + 1) * C, :]
 
-    band_tiles(fwd_rows, fwd_tiles)
-    band_tiles(bwd_rows, bwd_tiles)
+    band_tiles(taps_row, fwd_tiles, bwd_tiles)
     skip_row = skip[...]
     for r in range(parts):
         reader_ids = ids_own[r * C : (r + 1) * C, :]
@@ -99,29 +105,21 @@
 
 def filter_sums(ids_own, ids_src, src, grad):
     own = grad.shape[0]
-    lags = MAXCH + 1
-    parts = own // C
-    ids_rev = ids_own.reshape(parts, C)[:, ::-1].reshape(own, 1)
-    sums = pl.pallas_call(
+    blocks = ids_src.shape[0] // C
+    ids_rev = ids_src.reshape(blocks, C)[:, ::-1].reshape(1, blocks * C)
+    ext = pl.pallas_call(
         filter_kernel,
-        out_shape=jax.ShapeDtypeStruct((lags, 2 * C), jnp.float32),
+        out_shape=jax.ShapeDtypeStruct((1, (MAXCH + 2) * C), jnp.float32),
         compiler_params=pltpu.CompilerParams(vmem_limit_bytes=40 * 1024 * 1024),
         interpret=INTERPRET,
-    )(ids_rev, ids_src.reshape(1, -1), *src, grad)
-    ext = sum(
-        jnp.pad(sums[lag, : 2 * C - 1][::-1], (C * lag + 1, (lags + 1) * C - C * lag - 2 * C))
-        for lag in range(lags)
-    )
-    return ext[C : C + FLEN]
+    )(ids_own.reshape(own, 1), ids_rev, *src, grad)
+    return ext[0, C - 1 : C - 1 + FLEN]
 
 
 def local_conv(taps, ids_own, ids_src, ids_rdr, skip, src, grads):
     own, width = grads[0].shape
     lags = MAXCH + 1
-    big = jnp.concatenate([jnp.zeros((2 * C,), jnp.float32), taps.astype(jnp.float32),
-                           jnp.zeros((2 * C,), jnp.float32)])
-    fwd_rows = jnp.stack([big[C * lag + C + 1 : C * lag + 3 * C + 1][::-1] for lag in range(lags)])
-    bwd_rows = jnp.stack([big[C * lag + C : C * lag + 3 * C] for lag in range(lags)])
+    taps_row = jnp.pad(taps.astype(jnp.float32), (2 * C, 2 * C)).reshape(1, -1)
     return pl.pallas_call(
         conv_kernel,
         out_shape=(
@@ -131,7 +129,7 @@
         scratch_shapes=[pltpu.VMEM((lags, C, C), jnp.bfloat16), pltpu.VMEM((lags, C, C), jnp.bfloat16)],
         compiler_params=pltpu.CompilerParams(vmem_limit_bytes=60 * 1024 * 1024),
         interpret=INTERPRET,
-    )(fwd_rows, bwd_rows, ids_own.reshape(own, 1), ids_src.reshape(1, -1),
+    )(taps_row, ids_own.reshape(own, 1), ids_src.reshape(1, -1),
       ids_rdr.reshape(1, -1), skip.reshape(1, width), *src, *grads)
 
 

time: 124 us -> 108 us (0.87)
  local copies, waits for them, and re-layouts: 30.3 us -> 5.99 us
  starting transfers between devices: 51.2 us -> 56.9 us
  Pallas kernels: 8.35 us -> 9.6 us
    rev x10 -> x1, local copies, waits for them, and re-layouts: 11.5 us -> 0.15 us  [filter_sums(): ids_rev = ids_src.reshape(blocks, C)[:, ::-1].reshape(1, blocks * C)]
    another operation x9 -> x0, local copies, waits for them, and re-layouts: 7.09 us -> none  [the longest x8 5.86 us: local_conv(): jnp.stack([big[C * lag + C:C * lag + 3 * C] for lag in range(lags)])]
    all_to_all x1, starting transfers between devices: 11 us -> 15.1 us  [shards(): lax.all_to_all(filter_part.reshape(devices, FLEN // devices), every, 0, 0...]
    slice x4 -> x1, local copies, waits for them, and re-layouts: 3.65 us -> 0.09 us  [filter_sums(): return ext[0, C - 1:C - 1 + FLEN]]
    all_to_all x1, starting transfers between devices: 18.2 us -> 20.5 us  [shards(): taps = lax.all_to_all(offered, every, 0, 0, tiled=True).reshape(FLEN)]
    unnamed x81 -> x34, local copies, waits for them, and re-layouts: 3.8 us -> 1.54 us
  transfers between devices with their start and end apart: 10 -> 10, of which waited for: 5 -> 7; matrix products, arithmetic and copies ran while one was open for 27% -> 8% of each run, Pallas kernels for 7% -> 9%
where the time goes in v5:
time: 108 us; the launch traced here: 107 us
  starting transfers between devices  56.9 us (53%)
  waiting for transfers between devices  27.1 us (25%)
  Pallas kernels  9.6 us (9%)
  other arithmetic  6.48 us (6%)
  local copies, waits for them, and re-layouts  5.99 us (6%)
    ppermute x8, starting transfers between devices, shifted(): lax.ppermute(value, axis, [(source, source + steps) for source in range(l...  21.3 us
    all_to_all x1, starting transfers between devices, shards(): taps = lax.all_to_all(offered, every, 0, 0, tiled=True).reshape(FLEN)  20.5 us
    ppermute x8, waiting for transfers between devices, shifted(): lax.ppermute(value, axis, [(source, source + steps) for source in range(l...  18.4 us
    all_to_all x1, starting transfers between devices, shards(): lax.all_to_all(filter_part.reshape(devices, FLEN // devices), every, 0, 0...  15.1 us
    pallas_call x1, Pallas kernels, local_conv(): pl.pallas_call(conv_kernel, out_shape=(jax.ShapeDtypeStruct((own, width),...  7 us
    all_to_all x1, waiting for transfers between devices, shards(): taps = lax.all_to_all(offered, every, 0, 0, tiled=True).reshape(FLEN)  6.27 us
    convert_element_type x1, other arithmetic, shards(): value_grad = (mixed_grad * key_in.astype(jnp.float32)).astype(jnp.bfloat16)  3.26 us
    pallas_call x1, Pallas kernels, filter_sums(): pl.pallas_call(filter_kernel, out_shape=jax.ShapeDtypeStruct((1, (MAXCH +...  2.6 us
  transfers between devices with their start and end apart: 10, of which 7 were waited for; matrix products, arithmetic and copies ran while one was open for 8% of the time, Pallas kernels for 9%

profile of v5, /device:TPU:1, one launch (start us, length us, event | category | flops | bytes accessed | tf_op | source)
XLA Modules:
  0.0 107.1 jit_solution(14129617799070624096)
XLA Ops:
  0.6 0.0 copy-start.11
  0.6 0.0 copy-start.9
  0.7 1.4 %fusion.2.refs_4_ = bf16[512,512]{1,0:T(8,128)(2,1)S(1)} fusion(bf16[512,512]{1,0:T(8,128)(2,1)} %param.9, bf16[512,512]{1,0:T(8,128)(2,1)} %param.8), kind=kLoop, calls=%fused_computation.8 | loop fusion | flops 1048576 | bytes 1572864 | tf_op jit(solution)/shard_map/convert_element_type | solution.py:150
  2.1 4.4 %collective-permute-start = (bf16[512,512]{1,0:T(8,128)(2,1)S(1)}, bf16[512,512]{1,0:T(8,128)(2,1)S(1)}, u32[]{:S(2)}, u32[]{:S(2)}) collective-permute-start(bf16[512,512]{1,0:T(8,128)(2,1)S(1)} %fusion.2.refs_4_), channel_id=1, source_target_pairs={{0,8},{8,16},{16,24},{24,32},{32,40},{40,48},{48,56},{56,64},{64,7... | collective-permute-start | bytes 1572872 | tf_op jit(solution)/shard_map/ppermute | solution.py:20
  6.5 0.0 copy-start.15
  6.5 0.1 fusion.4.refs_5_
  6.7 1.3 %collective-permute-start.4 = (bf16[512,512]{1,0:T(8,128)(2,1)S(1)}, bf16[512,512]{1,0:T(8,128)(2,1)S(1)}, u32[]{:S(2)}, u32[]{:S(2)}) collective-permute-start(bf16[512,512]{1,0:T(8,128)(2,1)S(1)} %fusion.4.refs_5_), channel_id=1, source_target_pairs={{8,0},{16,8},{24,16},{32,24},{40,32},{48,40},{56,48},{64,56},{72,6... | collective-permute-start | bytes 1572872 | tf_op jit(solution)/shard_map/ppermute | solution.py:20
  8.0 9.1 %collective-permute-done.refs_3_ = bf16[512,512]{1,0:T(8,128)(2,1)S(1)} collective-permute-done((bf16[512,512]{1,0:T(8,128)(2,1)S(1)}, bf16[512,512]{1,0:T(8,128)(2,1)S(1)}, u32[]{:S(2)}, u32[]{:S(2)}) %collective-permute-start) | collective-permute-done | bytes 524320 | tf_op jit(solution)/shard_map/ppermute | solution.py:20
  17.0 4.1 %collective-permute-start.1 = (bf16[512,512]{1,0:T(8,128)(2,1)S(1)}, bf16[512,512]{1,0:T(8,128)(2,1)S(1)}, u32[]{:S(2)}, u32[]{:S(2)}) collective-permute-start(bf16[512,512]{1,0:T(8,128)(2,1)S(1)} %collective-permute-done.refs_3_), channel_id=1, source_target_pairs={{0,8},{8,16},{16,24},{24,32},{32,40},{40,48},{48,56},{56,64},{64,7... | collective-permute-start | bytes 1572872 | tf_op jit(solution)/shard_map/ppermute | solution.py:20
  21.2 0.2 collective-permute-done.4.refs_6_
  21.4 1.3 %collective-permute-start.5 = (bf16[512,512]{1,0:T(8,128)(2,1)S(1)}, bf16[512,512]{1,0:T(8,128)(2,1)}, u32[]{:S(2)}, u32[]{:S(2)}) collective-permute-start(bf16[512,512]{1,0:T(8,128)(2,1)S(1)} %collective-permute-done.4.refs_6_), channel_id=1, source_target_pairs={{8,0},{16,8},{24,16},{32,24},{40,32},{48,40},{56,48},{64,56},{72,6... | collective-permute-start | bytes 1572872 | tf_op jit(solution)/shard_map/ppermute | solution.py:20
  22.7 8.2 %collective-permute-done.1.refs_2_ = bf16[512,512]{1,0:T(8,128)(2,1)S(1)} collective-permute-done((bf16[512,512]{1,0:T(8,128)(2,1)S(1)}, bf16[512,512]{1,0:T(8,128)(2,1)S(1)}, u32[]{:S(2)}, u32[]{:S(2)}) %collective-permute-start.1) | collective-permute-done | bytes 524320 | tf_op jit(solution)/shard_map/ppermute | solution.py:20
  30.9 4.2 %collective-permute-start.2 = (bf16[512,512]{1,0:T(8,128)(2,1)S(1)}, bf16[512,512]{1,0:T(8,128)(2,1)S(1)}, u32[]{:S(2)}, u32[]{:S(2)}) collective-permute-start(bf16[512,512]{1,0:T(8,128)(2,1)S(1)} %collective-permute-done.1.refs_2_), channel_id=1, source_target_pairs={{0,8},{8,16},{16,24},{24,32},{32,40},{40,48},{48,56},{56,64},{64,7... | collective-permute-start | bytes 1572872 | tf_op jit(solution)/shard_map/ppermute | solution.py:20
  35.1 0.5 collective-permute-done.5.refs_7_
  35.6 1.3 %collective-permute-start.6 = (bf16[512,512]{1,0:T(8,128)(2,1)}, bf16[512,512]{1,0:T(8,128)(2,1)}, u32[]{:S(2)}, u32[]{:S(2)}) collective-permute-start(bf16[512,512]{1,0:T(8,128)(2,1)} %collective-permute-done.5.refs_7_), channel_id=1, source_target_pairs={{8,0},{16,8},{24,16},{32,24},{40,32},{48,40},{56,48},{64,56},{72,6... | collective-permute-start | bytes 1572872 | tf_op jit(solution)/shard_map/ppermute | solution.py:20
  37.0 0.1 all_to_all.12
  37.1 0.8 copy.21
  37.9 20.5 %all-to-all-start = ((bf16[256,1,8]{2,1,0:T(2,128)(2,1)}), bf16[256,1,8]{2,1,0:T(2,128)(2,1)S(1)}, u32[]{:S(2)}, u32[]{:S(2)}) async-start(bf16[256,1,8]{2,1,0:T(2,128)(2,1)} %copy.21), calls=%async_computation | async-start | bytes 262144 | tf_op jit(solution)/shard_map/all_to_all | solution.py:148
  58.5 0.0 collective-permute-done.2.refs_1_
  58.5 0.0 copy-start.5
  58.5 3.4 %collective-permute-start.3 = (bf16[512,512]{1,0:T(8,128)(2,1)S(1)}, bf16[512,512]{1,0:T(8,128)(2,1)S(1)}, u32[]{:S(2)}, u32[]{:S(2)}) collective-permute-start(bf16[512,512]{1,0:T(8,128)(2,1)S(1)} %collective-permute-done.2.refs_1_), channel_id=1, source_target_pairs={{0,8},{8,16},{16,24},{24,32},{32,40},{40,48},{48,56},{56,64},{64,7... | collective-permute-start | bytes 1572872 | tf_op jit(solution)/shard_map/ppermute | solution.py:20
  61.9 1.3 %collective-permute-start.7 = (bf16[512,512]{1,0:T(8,128)(2,1)}, bf16[512,512]{1,0:T(8,128)(2,1)}, u32[]{:S(2)}, u32[]{:S(2)}) collective-permute-start(bf16[512,512]{1,0:T(8,128)(2,1)} %collective-permute-done.6.refs_8_), channel_id=1, source_target_pairs={{8,0},{16,8},{24,16},{32,24},{40,32},{48,40},{56,48},{64,56},{72,6... | collective-permute-start | bytes 1572872 | tf_op jit(solution)/shard_map/ppermute | solution.py:20
  63.3 0.1 fusion.6
  63.4 0.6 reshape.55.ids_src
  64.0 0.1 dynamic_slice.9
  64.1 0.6 reshape.56.ids_rdr
  64.7 0.1 rev.3
  64.8 0.1 copy.22.ids_own
  65.0 6.3 %all-to-all-done = bf16[256,1,8]{2,1,0:T(2,128)(2,1)S(1)} async-done(((bf16[256,1,8]{2,1,0:T(2,128)(2,1)}), bf16[256,1,8]{2,1,0:T(2,128)(2,1)S(1)}, u32[]{:S(2)}, u32[]{:S(2)}) %all-to-all-start) | async-done | bytes 4128 | tf_op jit(solution)/shard_map/all_to_all | solution.py:148
  71.3 1.0 reduce
  72.3 1.0 convert_element_type.41
  73.2 0.6 pad_convert_fusion
  73.8 0.4 collective-permute-done.3.refs_0_
  74.2 2.6 %shard_map.111 = f32[1,2560]{1,0:T(1,128)S(1)} custom-call(s32[512,1]{1,0:T(8,128)S(1)} %copy.22.ids_own, s32[1,2560]{1,0:T(1,128)S(1)} %bitcast.15, bf16[512,512]{1,0:T(8,128)(2,1)S(1)} %collective-permute-done.3.refs_0_, bf16[512,512]{1,0:T(8,128)(2,1)S(1)} %collective-permute-done.2.refs_1_, bf16[512,512]{1,0:T(8,128)(2,1)S(1)} %collective-permute-done.1.refs_2_, ...), custom_call_target="tpu_custom_call" | custom-call | tf_op jit(solution)/shard_map/pallas_call | solution.py:110
  76.8 0.0 copy-start.4
  76.9 0.8 copy-done.4
  77.6 0.1 slice_reduce_fusion
  77.7 0.8 all_to_all.14
  78.5 15.1 %all-to-all-start.1 = ((f32[256,1,8]{2,1,0:T(1,128)}), f32[256,1,8]{2,1,0:T(1,128)S(1)}, u32[]{:S(2)}, u32[]{:S(2)}) async-start(f32[256,1,8]{2,1,0:T(1,128)} %bitcast.4), calls=%async_computation.1 | async-start | bytes 262144 | tf_op jit(solution)/shard_map/all_to_all | solution.py:167
  93.6 0.0 collective-permute-done.7.refs_9_
  93.6 0.0 copy-start.7
  93.6 0.0 copy-start.8
  93.6 0.0 copy-start.10
  93.6 0.0 copy-start.12
  93.6 7.0 %shard_map.110 = (f32[512,512]{1,0:T(8,128)}, f32[512,512]{1,0:T(8,128)}) custom-call(f32[1,3072]{1,0:T(1,128)} %bitcast.18, s32[512,1]{1,0:T(8,128)} %copy-done.2, s32[1,2560]{1,0:T(1,128)} %reshape.55.ids_src, s32[1,2560]{1,0:T(1,128)} %reshape.56.ids_rdr, f32[1,512]{1,0:T(1,128)} %bitcast.20, bf16[512,512]{1,0:T(8,128)(2,1)} %copy-done.6, ...), custom_call_target="tpu_custom_call" | custom-call | tf_op jit(solution)/shard_map/pallas_call | solution.py:123
  100.7 3.3 %fusion.1 = (bf16[512,512]{1,0:T(8,128)(2,1)}, bf16[512,512]{1,0:T(8,128)(2,1)}, bf16[512,512]{1,0:T(8,128)(2,1)}, bf16[512,512]{1,0:T(8,128)(2,1)}) fusion(f32[512,512]{1,0:T(8,128)} %get-tuple-element.8, bf16[512,512]{1,0:T(8,128)(2,1)S(1)} %copy-done.8, bf16[512,512]{1,0:T(8,128)(2,1)S(1)} %copy-done.7, f32[512,512]{1,0:T(8,128)} %get-tuple-element.7, ...), kind=kLoop, calls=%fused_computation.7 | loop fusion | flops 3145728 | bytes 6291456 | tf_op jit(solution)/shard_map/convert_element_type | solution.py:173
  103.9 2.5 %all-to-all-done.1 = f32[256,1,8]{2,1,0:T(1,128)S(1)} async-done(((f32[256,1,8]{2,1,0:T(1,128)}), f32[256,1,8]{2,1,0:T(1,128)S(1)}, u32[]{:S(2)}, u32[]{:S(2)}) %all-to-all-start.1) | async-done | bytes 8224 | tf_op jit(solution)/shard_map/all_to_all | solution.py:167
  106.5 0.7 copy.25
  (31 shorter events, 0.1 us)
Async XLA Ops:
  0.6 5.9 %copy-start.11 = (bf16[512,512]{1,0:T(8,128)(2,1)S(1)}, bf16[512,512]{1,0:T(8,128)(2,1)}, u32[]{:S(2)}) copy-start(bf16[512,512]{1,0:T(8,128)(2,1)} %param.10) | copy-start | bytes 1572868
  0.6 5.9 %copy-start.9 = (bf16[512,512]{1,0:T(8,128)(2,1)S(1)}, bf16[512,512]{1,0:T(8,128)(2,1)}, u32[]{:S(2)}) copy-start(bf16[512,512]{1,0:T(8,128)(2,1)} %param.7) | copy-start | bytes 1572868
  2.1 72.1 %copy-start = (bf16[512,512]{1,0:T(8,128)(2,1)}, bf16[512,512]{1,0:T(8,128)(2,1)S(1)}, u32[]{:S(2)}) copy-start(bf16[512,512]{1,0:T(8,128)(2,1)S(1)} %fusion.2.refs_4_) | copy-start | bytes 1572868
  2.1 15.0 %collective-permute-start = (bf16[512,512]{1,0:T(8,128)(2,1)S(1)}, bf16[512,512]{1,0:T(8,128)(2,1)S(1)}, u32[]{:S(2)}, u32[]{:S(2)}) collective-permute-start(bf16[512,512]{1,0:T(8,128)(2,1)S(1)} %fusion.2.refs_4_), channel_id=1, source_target_pairs={{0,8},{8,16},{16,24},{24,32},{32,40},{40,48},{48,56},{56,64},{64,7... | collective-permute-start | bytes 1572872 | tf_op jit(solution)/shard_map/ppermute | solution.py:20
  6.5 30.4 %copy-start.15 = (bf16[8,8]{1,0:T(8,128)(2,1)S(1)}, bf16[8,8]{1,0:T(8,128)(2,1)}, u32[]{:S(2)}) copy-start(bf16[8,8]{1,0:T(8,128)(2,1)} %param.13) | copy-start | bytes 388
  6.7 67.5 %copy-start.1 = (bf16[512,512]{1,0:T(8,128)(2,1)}, bf16[512,512]{1,0:T(8,128)(2,1)S(1)}, u32[]{:S(2)}) copy-start(bf16[512,512]{1,0:T(8,128)(2,1)S(1)} %fusion.4.refs_5_) | copy-start | bytes 1572868
  6.7 14.7 %collective-permute-start.4 = (bf16[512,512]{1,0:T(8,128)(2,1)S(1)}, bf16[512,512]{1,0:T(8,128)(2,1)S(1)}, u32[]{:S(2)}, u32[]{:S(2)}) collective-permute-start(bf16[512,512]{1,0:T(8,128)(2,1)S(1)} %fusion.4.refs_5_), channel_id=1, source_target_pairs={{8,0},{16,8},{24,16},{32,24},{40,32},{48,40},{56,48},{64,56},{72,6... | collective-permute-start | bytes 1572872 | tf_op jit(solution)/shard_map/ppermute | solution.py:20
  17.0 57.2 %copy-start.3 = (bf16[512,512]{1,0:T(8,128)(2,1)}, bf16[512,512]{1,0:T(8,128)(2,1)S(1)}, u32[]{:S(2)}) copy-start(bf16[512,512]{1,0:T(8,128)(2,1)S(1)} %collective-permute-done.refs_3_) | copy-start | bytes 1572868
  17.0 13.8 %collective-permute-start.1 = (bf16[512,512]{1,0:T(8,128)(2,1)S(1)}, bf16[512,512]{1,0:T(8,128)(2,1)S(1)}, u32[]{:S(2)}, u32[]{:S(2)}) collective-permute-start(bf16[512,512]{1,0:T(8,128)(2,1)S(1)} %collective-permute-done.refs_3_), channel_id=1, source_target_pairs={{0,8},{8,16},{16,24},{24,32},{32,40},{40,48},{48,56},{56,64},{64,7... | collective-permute-start | bytes 1572872 | tf_op jit(solution)/shard_map/ppermute | solution.py:20
  21.4 9.5 %copy-start.13 = (bf16[512,512]{1,0:T(8,128)(2,1)}, bf16[512,512]{1,0:T(8,128)(2,1)S(1)}, u32[]{:S(2)}) copy-start(bf16[512,512]{1,0:T(8,128)(2,1)S(1)} %collective-permute-done.4.refs_6_) | copy-start | bytes 1572868
  21.4 14.2 %collective-permute-start.5 = (bf16[512,512]{1,0:T(8,128)(2,1)S(1)}, bf16[512,512]{1,0:T(8,128)(2,1)}, u32[]{:S(2)}, u32[]{:S(2)}) collective-permute-start(bf16[512,512]{1,0:T(8,128)(2,1)S(1)} %collective-permute-done.4.refs_6_), channel_id=1, source_target_pairs={{8,0},{16,8},{24,16},{32,24},{40,32},{48,40},{56,48},{64,56},{72,6... | collective-permute-start | bytes 1572872 | tf_op jit(solution)/shard_map/ppermute | solution.py:20
  30.9 27.6 %collective-permute-start.2 = (bf16[512,512]{1,0:T(8,128)(2,1)S(1)}, bf16[512,512]{1,0:T(8,128)(2,1)S(1)}, u32[]{:S(2)}, u32[]{:S(2)}) collective-permute-start(bf16[512,512]{1,0:T(8,128)(2,1)S(1)} %collective-permute-done.1.refs_2_), channel_id=1, source_target_pairs={{0,8},{8,16},{16,24},{24,32},{32,40},{40,48},{48,56},{56,64},{64,7... | collective-permute-start | bytes 1572872 | tf_op jit(solution)/shard_map/ppermute | solution.py:20
  35.6 26.3 %collective-permute-start.6 = (bf16[512,512]{1,0:T(8,128)(2,1)}, bf16[512,512]{1,0:T(8,128)(2,1)}, u32[]{:S(2)}, u32[]{:S(2)}) collective-permute-start(bf16[512,512]{1,0:T(8,128)(2,1)} %collective-permute-done.5.refs_7_), channel_id=1, source_target_pairs={{8,0},{16,8},{24,16},{32,24},{40,32},{48,40},{56,48},{64,56},{72,6... | collective-permute-start | bytes 1572872 | tf_op jit(solution)/shard_map/ppermute | solution.py:20
  37.9 25.3 %copy-start.14 = (s32[16384]{0:T(1024)S(1)}, s32[16384]{0:T(1024)}, u32[]{:S(2)}) copy-start(s32[16384]{0:T(1024)} %param.11) | copy-start | bytes 196612
  37.9 33.3 %all-to-all-start = ((bf16[256,1,8]{2,1,0:T(2,128)(2,1)}), bf16[256,1,8]{2,1,0:T(2,128)(2,1)S(1)}, u32[]{:S(2)}, u32[]{:S(2)}) async-start(bf16[256,1,8]{2,1,0:T(2,128)(2,1)} %copy.21), calls=%async_computation | async-start | bytes 262144 | tf_op jit(solution)/shard_map/all_to_all | solution.py:148
  58.5 18.3 %copy-start.5 = (bf16[512,512]{1,0:T(8,128)(2,1)}, bf16[512,512]{1,0:T(8,128)(2,1)S(1)}, u32[]{:S(2)}) copy-start(bf16[512,512]{1,0:T(8,128)(2,1)S(1)} %collective-permute-done.2.refs_1_) | copy-start | bytes 1572868
  58.5 15.7 %collective-permute-start.3 = (bf16[512,512]{1,0:T(8,128)(2,1)S(1)}, bf16[512,512]{1,0:T(8,128)(2,1)S(1)}, u32[]{:S(2)}, u32[]{:S(2)}) collective-permute-start(bf16[512,512]{1,0:T(8,128)(2,1)S(1)} %collective-permute-done.2.refs_1_), channel_id=1, source_target_pairs={{0,8},{8,16},{16,24},{24,32},{32,40},{40,48},{48,56},{56,64},{64,7... | collective-permute-start | bytes 1572872 | tf_op jit(solution)/shard_map/ppermute | solution.py:20
  61.9 31.6 %collective-permute-start.7 = (bf16[512,512]{1,0:T(8,128)(2,1)}, bf16[512,512]{1,0:T(8,128)(2,1)}, u32[]{:S(2)}, u32[]{:S(2)}) collective-permute-start(bf16[512,512]{1,0:T(8,128)(2,1)} %collective-permute-done.6.refs_8_), channel_id=1, source_target_pairs={{8,0},{16,8},{24,16},{32,24},{40,32},{48,40},{56,48},{64,56},{72,6... | collective-permute-start | bytes 1572872 | tf_op jit(solution)/shard_map/ppermute | solution.py:20
  65.0 11.8 %copy-start.2 = (s32[512,1]{1,0:T(8,128)}, s32[512,1]{1,0:T(8,128)S(1)}, u32[]{:S(2)}) copy-start(s32[512,1]{1,0:T(8,128)S(1)} %copy.22.ids_own) | copy-start | bytes 6148
  74.2 2.6 %copy-start.6 = (bf16[512,512]{1,0:T(8,128)(2,1)}, bf16[512,512]{1,0:T(8,128)(2,1)S(1)}, u32[]{:S(2)}) copy-start(bf16[512,512]{1,0:T(8,128)(2,1)S(1)} %collective-permute-done.3.refs_0_) | copy-start | bytes 1572868
  76.8 0.8 copy-start.4
  78.5 27.9 %all-to-all-start.1 = ((f32[256,1,8]{2,1,0:T(1,128)}), f32[256,1,8]{2,1,0:T(1,128)S(1)}, u32[]{:S(2)}, u32[]{:S(2)}) async-start(f32[256,1,8]{2,1,0:T(1,128)} %bitcast.4), calls=%async_computation.1 | async-start | bytes 262144 | tf_op jit(solution)/shard_map/all_to_all | solution.py:167
  93.6 7.1 %copy-start.7 = (bf16[512,512]{1,0:T(8,128)(2,1)S(1)}, bf16[512,512]{1,0:T(8,128)(2,1)}, u32[]{:S(2)}) copy-start(bf16[512,512]{1,0:T(8,128)(2,1)} %param.9) | copy-start | bytes 1572868
  93.6 7.0 %copy-start.8 = (bf16[512,512]{1,0:T(8,128)(2,1)S(1)}, bf16[512,512]{1,0:T(8,128)(2,1)}, u32[]{:S(2)}) copy-start(bf16[512,512]{1,0:T(8,128)(2,1)} %param.8) | copy-start | bytes 1572868
  93.6 7.0 %copy-start.10 = (bf16[512,512]{1,0:T(8,128)(2,1)S(1)}, bf16[512,512]{1,0:T(8,128)(2,1)}, u32[]{:S(2)}) copy-start(bf16[512,512]{1,0:T(8,128)(2,1)} %param.7) | copy-start | bytes 1572868
  93.6 7.0 %copy-start.12 = (bf16[512,512]{1,0:T(8,128)(2,1)S(1)}, bf16[512,512]{1,0:T(8,128)(2,1)}, u32[]{:S(2)}) copy-start(bf16[512,512]{1,0:T(8,128)(2,1)} %param.10) | copy-start | bytes 1572868

commit v6 on v5

--- a/solution.py
+++ b/solution.py
@@ -152,9 +152,11 @@
 
     ahead = [mixed_in]
     behind = [conv_grad]
-    for _ in range(span):
+    for step in range(span):
         ahead.append(shifted(ahead[-1], "ctx", 1))
         behind.append(shifted(behind[-1], "ctx", -1))
+        if step == 0:
+            ahead[-1], behind[-1], taps = lax.optimization_barrier((ahead[-1], behind[-1], taps))
 
     ids_pad = jnp.concatenate(
         [jnp.full((hist,), -1, jnp.int32), doc_ids, jnp.full((hist,), -2, jnp.int32)]
@@ -164,13 +166,15 @@
     ids_rdr = lax.dynamic_slice_in_dim(ids_pad, here * rows + hist, hist + rows)
 
     filter_part = filter_sums(ids_own, ids_src, ahead[::-1], conv_grad)
-    spread = lax.all_to_all(filter_part.reshape(devices, FLEN // devices), every, 0, 0, tiled=True)
     conv, mixed_grad = local_conv(taps, ids_own, ids_src, ids_rdr, skip_gain, ahead[::-1], behind)
 
     mixed_out = (query_in.astype(jnp.float32) * conv).astype(jnp.bfloat16)
     query_grad = (out_grad.astype(jnp.float32) * conv).astype(jnp.bfloat16)
     key_grad = (mixed_grad * value_in.astype(jnp.float32)).astype(jnp.bfloat16)
     value_grad = (mixed_grad * key_in.astype(jnp.float32)).astype(jnp.bfloat16)
+    filter_part, mixed_out, query_grad, key_grad, value_grad = lax.optimization_barrier(
+        (filter_part, mixed_out, query_grad, key_grad, value_grad))
+    spread = lax.all_to_all(filter_part.reshape(devices, FLEN // devices), every, 0, 0, tiled=True)
 
     summed = jnp.sum(spread.reshape(devices // groups, groups, FLEN // devices), axis=0).T
     tokens = lax.axis_size("ctx") * rows

time: 108 us -> 123 us (1.14)
  blocking collectives: 0 us -> 56.2 us
  starting transfers between devices: 56.9 us -> 20.8 us
  local copies, waits for them, and re-layouts: 5.99 us -> 3.05 us
    all_to_all x0 -> x2, blocking collectives: none -> 56.2 us  [the longest x1 29.7 us: shards(): taps = lax.all_to_all(offered, every, 0, 0, tiled=True).reshape(FLEN)]
    all_to_all x2 -> x0, starting transfers between devices: 35.6 us -> none  [the longest x1 20.5 us: shards(): taps = lax.all_to_all(offered, every, 0, 0, tiled=True).reshape(FLEN)]
    all_to_all x2 -> x0, waiting for transfers between devices: 8.76 us -> none  [the longest x1 6.27 us: shards(): taps = lax.all_to_all(offered, every, 0, 0, tiled=True).reshape(FLEN)]
    ppermute x8, waiting for transfers between devices: 18.4 us -> 25.9 us  [shifted(): lax.ppermute(value, axis, [(source, source + steps) for source in range(l...]
  transfers between devices with their start and end apart: 10 -> 8, of which waited for: 7 -> 4; matrix products, arithmetic and copies ran while one was open for 8% -> 3% of each run, Pallas kernels for 9% -> 2%
where the time goes in v6:
time: 123 us; the launch traced here: 122 us
  blocking collectives  56.2 us (46%)
  waiting for transfers between devices  25.9 us (21%)
  starting transfers between devices  20.8 us (17%)
  Pallas kernels  9.61 us (8%)
  other arithmetic  5.85 us (5%)
  local copies, waits for them, and re-layouts  3.05 us (2%)
    all_to_all x1, blocking collectives, shards(): taps = lax.all_to_all(offered, every, 0, 0, tiled=True).reshape(FLEN)  29.7 us
    all_to_all x1, blocking collectives, shards(): lax.all_to_all(filter_part.reshape(devices, FLEN // devices), every, 0, 0...  26.5 us
    ppermute x8, waiting for transfers between devices, shifted(): lax.ppermute(value, axis, [(source, source + steps) for source in range(l...  25.9 us
    ppermute x8, starting transfers between devices, shifted(): lax.ppermute(value, axis, [(source, source + steps) for source in range(l...  20.8 us
    pallas_call x1, Pallas kernels, local_conv(): pl.pallas_call(conv_kernel, out_shape=(jax.ShapeDtypeStruct((own, width),...  7.02 us
    convert_element_type x1, other arithmetic, shards(): value_grad = (mixed_grad * key_in.astype(jnp.float32)).astype(jnp.bfloat16)  3.26 us
    pallas_call x1, Pallas kernels, filter_sums(): pl.pallas_call(filter_kernel, out_shape=jax.ShapeDtypeStruct((1, (MAXCH +...  2.59 us
  transfers between devices with their start and end apart: 8, of which 4 were waited for; matrix products, arithmetic and copies ran while one was open for 3% of the time, Pallas kernels for 2%

profile of v6, /device:TPU:1, one launch (start us, length us, event | category | flops | bytes accessed | tf_op | source)
XLA Modules:
  0.0 122.5 jit_solution(2076124883151767885)
XLA Ops:
  0.6 0.0 copy-start.9
  0.6 0.0 copy-start.11
  0.7 1.4 %fusion.1.refs_4_ = bf16[512,512]{1,0:T(8,128)(2,1)S(1)} fusion(bf16[512,512]{1,0:T(8,128)(2,1)} %param.9, bf16[512,512]{1,0:T(8,128)(2,1)} %param.8), kind=kLoop, calls=%fused_computation.7 | loop fusion | flops 1048576 | bytes 1572864 | tf_op jit(solution)/shard_map/convert_element_type | solution.py:150
  2.1 0.0 copy-start
  2.1 4.4 %collective-permute-start = (bf16[512,512]{1,0:T(8,128)(2,1)S(1)}, bf16[512,512]{1,0:T(8,128)(2,1)S(1)}, u32[]{:S(2)}, u32[]{:S(2)}) collective-permute-start(bf16[512,512]{1,0:T(8,128)(2,1)S(1)} %fusion.1.refs_4_), channel_id=1, source_target_pairs={{0,8},{8,16},{16,24},{24,32},{32,40},{40,48},{48,56},{56,64},{64,7... | collective-permute-start | bytes 1572872 | tf_op jit(solution)/shard_map/ppermute | solution.py:20
  6.5 0.0 copy-done.9
  6.5 0.0 copy-done.11
  6.5 0.0 copy-start.15
  6.5 0.1 fusion.4.refs_5_
  6.7 0.0 copy-start.1
  6.7 1.3 %collective-permute-start.1 = (bf16[512,512]{1,0:T(8,128)(2,1)S(1)}, bf16[512,512]{1,0:T(8,128)(2,1)S(1)}, u32[]{:S(2)}, u32[]{:S(2)}) collective-permute-start(bf16[512,512]{1,0:T(8,128)(2,1)S(1)} %fusion.4.refs_5_), channel_id=1, source_target_pairs={{8,0},{16,8},{24,16},{32,24},{40,32},{48,40},{56,48},{64,56},{72,6... | collective-permute-start | bytes 1572872 | tf_op jit(solution)/shard_map/ppermute | solution.py:20
  8.0 0.0 copy-done.15
  8.0 0.1 all_to_all.12
  8.1 0.2 copy.21
  8.3 29.7 %all_to_all.18 = bf16[256,1,8]{2,1,0:T(2,128)(2,1)S(1)} all-to-all(bf16[256,1,8]{2,1,0:T(2,128)(2,1)S(1)} %copy.21), channel_id=1, replica_groups=mesh['ctx'=32,'tp'=8] {'ctx','tp'}, dimensions={0} | all-to-all | bytes 8192 | tf_op jit(solution)/shard_map/all_to_all | solution.py:148
  38.0 0.4 reduce
  38.4 0.0 copy-start.14
  38.4 0.1 reshape.56
  38.5 0.0 collective-permute-done.refs_3_
  38.5 0.0 copy-start.3
  38.5 0.0 collective-permute-done.1.refs_6_
  38.5 2.8 %collective-permute-start.2 = (bf16[512,512]{1,0:T(8,128)(2,1)S(1)}, bf16[512,512]{1,0:T(8,128)(2,1)S(1)}, u32[]{:S(2)}, u32[]{:S(2)}) collective-permute-start(bf16[512,512]{1,0:T(8,128)(2,1)S(1)} %collective-permute-done.refs_3_), channel_id=1, source_target_pairs={{0,8},{8,16},{16,24},{24,32},{32,40},{40,48},{48,56},{56,64},{64,7... | collective-permute-start | bytes 1572872 | tf_op jit(solution)/shard_map/ppermute | solution.py:20
  41.3 1.3 %collective-permute-start.5 = (bf16[512,512]{1,0:T(8,128)(2,1)S(1)}, bf16[512,512]{1,0:T(8,128)(2,1)}, u32[]{:S(2)}, u32[]{:S(2)}) collective-permute-start(bf16[512,512]{1,0:T(8,128)(2,1)S(1)} %collective-permute-done.1.refs_6_), channel_id=1, source_target_pairs={{8,0},{16,8},{24,16},{32,24},{40,32},{48,40},{56,48},{64,56},{72,6... | collective-permute-start | bytes 1572872 | tf_op jit(solution)/shard_map/ppermute | solution.py:20
  42.6 9.7 %collective-permute-done.2.refs_2_ = bf16[512,512]{1,0:T(8,128)(2,1)S(1)} collective-permute-done((bf16[512,512]{1,0:T(8,128)(2,1)S(1)}, bf16[512,512]{1,0:T(8,128)(2,1)S(1)}, u32[]{:S(2)}, u32[]{:S(2)}) %collective-permute-start.2) | collective-permute-done | bytes 524320 | tf_op jit(solution)/shard_map/ppermute | solution.py:20
  52.4 4.2 %collective-permute-start.3 = (bf16[512,512]{1,0:T(8,128)(2,1)S(1)}, bf16[512,512]{1,0:T(8,128)(2,1)S(1)}, u32[]{:S(2)}, u32[]{:S(2)}) collective-permute-start(bf16[512,512]{1,0:T(8,128)(2,1)S(1)} %collective-permute-done.2.refs_2_), channel_id=1, source_target_pairs={{0,8},{8,16},{16,24},{24,32},{32,40},{40,48},{48,56},{56,64},{64,7... | collective-permute-start | bytes 1572872 | tf_op jit(solution)/shard_map/ppermute | solution.py:20
  56.6 0.0 collective-permute-done.5.refs_7_
  56.6 1.3 %collective-permute-start.6 = (bf16[512,512]{1,0:T(8,128)(2,1)}, bf16[512,512]{1,0:T(8,128)(2,1)}, u32[]{:S(2)}, u32[]{:S(2)}) collective-permute-start(bf16[512,512]{1,0:T(8,128)(2,1)} %collective-permute-done.5.refs_7_), channel_id=1, source_target_pairs={{8,0},{16,8},{24,16},{32,24},{40,32},{48,40},{56,48},{64,56},{72,6... | collective-permute-start | bytes 1572872 | tf_op jit(solution)/shard_map/ppermute | solution.py:20
  57.9 8.9 %collective-permute-done.3.refs_1_ = bf16[512,512]{1,0:T(8,128)(2,1)S(1)} collective-permute-done((bf16[512,512]{1,0:T(8,128)(2,1)S(1)}, bf16[512,512]{1,0:T(8,128)(2,1)S(1)}, u32[]{:S(2)}, u32[]{:S(2)}) %collective-permute-start.3) | collective-permute-done | bytes 524320 | tf_op jit(solution)/shard_map/ppermute | solution.py:20
  66.9 4.2 %collective-permute-start.4 = (bf16[512,512]{1,0:T(8,128)(2,1)S(1)}, bf16[512,512]{1,0:T(8,128)(2,1)S(1)}, u32[]{:S(2)}, u32[]{:S(2)}) collective-permute-start(bf16[512,512]{1,0:T(8,128)(2,1)S(1)} %collective-permute-done.3.refs_1_), channel_id=1, source_target_pairs={{0,8},{8,16},{16,24},{24,32},{32,40},{40,48},{48,56},{56,64},{64,7... | collective-permute-start | bytes 1572872 | tf_op jit(solution)/shard_map/ppermute | solution.py:20
  71.1 0.0 collective-permute-done.6.refs_8_
  71.1 1.3 %collective-permute-start.7 = (bf16[512,512]{1,0:T(8,128)(2,1)}, bf16[512,512]{1,0:T(8,128)(2,1)}, u32[]{:S(2)}, u32[]{:S(2)}) collective-permute-start(bf16[512,512]{1,0:T(8,128)(2,1)} %collective-permute-done.6.refs_8_), channel_id=1, source_target_pairs={{8,0},{16,8},{24,16},{32,24},{40,32},{48,40},{56,48},{64,56},{72,6... | collective-permute-start | bytes 1572872 | tf_op jit(solution)/shard_map/ppermute | solution.py:20
  72.5 0.1 fusion.6
  72.6 0.6 reshape.59.ids_src
  73.2 0.1 dynamic_slice.9
  73.3 0.1 copy.22.ids_own
  73.4 0.0 copy-start.2
  73.4 0.2 rev.3
  73.6 0.6 reshape.60.ids_rdr
  74.2 0.6 pad_convert_fusion
  74.8 5.8 %collective-permute-done.4.refs_0_ = bf16[512,512]{1,0:T(8,128)(2,1)S(1)} collective-permute-done((bf16[512,512]{1,0:T(8,128)(2,1)S(1)}, bf16[512,512]{1,0:T(8,128)(2,1)S(1)}, u32[]{:S(2)}, u32[]{:S(2)}) %collective-permute-start.4) | collective-permute-done | bytes 524320 | tf_op jit(solution)/shard_map/ppermute | solution.py:20
  80.7 2.6 %shard_map.110 = f32[1,2560]{1,0:T(1,128)S(1)} custom-call(s32[512,1]{1,0:T(8,128)S(1)} %copy.22.ids_own, s32[1,2560]{1,0:T(1,128)S(1)} %bitcast.16, bf16[512,512]{1,0:T(8,128)(2,1)S(1)} %collective-permute-done.4.refs_0_, bf16[512,512]{1,0:T(8,128)(2,1)S(1)} %collective-permute-done.3.refs_1_, bf16[512,512]{1,0:T(8,128)(2,1)S(1)} %collective-permute-done.2.refs_2_, ...), custom_call_target="tpu_custom_call" | custom-call | tf_op jit(solution)/shard_map/pallas_call | solution.py:110
  83.3 0.1 slice.4
  83.4 1.4 %collective-permute-done.7.refs_9_ = bf16[512,512]{1,0:T(8,128)(2,1)} collective-permute-done((bf16[512,512]{1,0:T(8,128)(2,1)}, bf16[512,512]{1,0:T(8,128)(2,1)}, u32[]{:S(2)}, u32[]{:S(2)}) %collective-permute-start.7) | collective-permute-done | bytes 524320 | tf_op jit(solution)/shard_map/ppermute | solution.py:20
  84.8 7.0 %shard_map.111 = (f32[512,512]{1,0:T(8,128)}, f32[512,512]{1,0:T(8,128)}) custom-call(f32[1,3072]{1,0:T(1,128)} %bitcast.20, s32[512,1]{1,0:T(8,128)} %copy-done.2, s32[1,2560]{1,0:T(1,128)} %reshape.59.ids_src, s32[1,2560]{1,0:T(1,128)} %reshape.60.ids_rdr, f32[1,512]{1,0:T(1,128)} %bitcast.23, bf16[512,512]{1,0:T(8,128)(2,1)} %copy-done.6, ...), custom_call_target="tpu_custom_call" | custom-call | tf_op jit(solution)/shard_map/pallas_call | solution.py:123
  91.9 3.3 %fusion = (bf16[512,512]{1,0:T(8,128)(2,1)}, bf16[512,512]{1,0:T(8,128)(2,1)}, bf16[512,512]{1,0:T(8,128)(2,1)}, bf16[512,512]{1,0:T(8,128)(2,1)}) fusion(f32[512,512]{1,0:T(8,128)} %get-tuple-element.19, bf16[512,512]{1,0:T(8,128)(2,1)S(1)} %copy-done.8, bf16[512,512]{1,0:T(8,128)(2,1)S(1)} %copy-done.7, f32[512,512]{1,0:T(8,128)} %get-tuple-element.18, ...), kind=kLoop, calls=%fused_computation.6 | loop fusion | flops 3145728 | bytes 6291456 | tf_op jit(solution)/shard_map/convert_element_type | solution.py:174
  95.1 0.1 all_to_all.14
  95.2 26.5 %all_to_all.19 = f32[256,1,8]{2,1,0:T(1,128)S(1)} all-to-all(f32[256,1,8]{2,1,0:T(1,128)S(1)} %bitcast.17), channel_id=1, replica_groups=mesh['ctx'=32,'tp'=8] {'ctx','tp'}, dimensions={0} | all-to-all | bytes 16384 | tf_op jit(solution)/shard_map/all_to_all | solution.py:177
  121.8 0.7 copy.25
  (29 shorter events, 0.1 us)
Async XLA Ops:
  0.6 5.9 %copy-start.9 = (bf16[512,512]{1,0:T(8,128)(2,1)S(1)}, bf16[512,512]{1,0:T(8,128)(2,1)}, u32[]{:S(2)}) copy-start(bf16[512,512]{1,0:T(8,128)(2,1)} %param.7) | copy-start | bytes 1572868
  0.6 5.9 %copy-start.11 = (bf16[512,512]{1,0:T(8,128)(2,1)S(1)}, bf16[512,512]{1,0:T(8,128)(2,1)}, u32[]{:S(2)}) copy-start(bf16[512,512]{1,0:T(8,128)(2,1)} %param.10) | copy-start | bytes 1572868
  2.1 78.6 %copy-start = (bf16[512,512]{1,0:T(8,128)(2,1)}, bf16[512,512]{1,0:T(8,128)(2,1)S(1)}, u32[]{:S(2)}) copy-start(bf16[512,512]{1,0:T(8,128)(2,1)S(1)} %fusion.1.refs_4_) | copy-start | bytes 1572868
  2.1 36.4 %collective-permute-start = (bf16[512,512]{1,0:T(8,128)(2,1)S(1)}, bf16[512,512]{1,0:T(8,128)(2,1)S(1)}, u32[]{:S(2)}, u32[]{:S(2)}) collective-permute-start(bf16[512,512]{1,0:T(8,128)(2,1)S(1)} %fusion.1.refs_4_), channel_id=1, source_target_pairs={{0,8},{8,16},{16,24},{24,32},{32,40},{40,48},{48,56},{56,64},{64,7... | collective-permute-start | bytes 1572872 | tf_op jit(solution)/shard_map/ppermute | solution.py:20
  6.5 1.5 %copy-start.15 = (bf16[8,8]{1,0:T(8,128)(2,1)S(1)}, bf16[8,8]{1,0:T(8,128)(2,1)}, u32[]{:S(2)}) copy-start(bf16[8,8]{1,0:T(8,128)(2,1)} %param.13) | copy-start | bytes 388
  6.7 74.0 %copy-start.1 = (bf16[512,512]{1,0:T(8,128)(2,1)}, bf16[512,512]{1,0:T(8,128)(2,1)S(1)}, u32[]{:S(2)}) copy-start(bf16[512,512]{1,0:T(8,128)(2,1)S(1)} %fusion.4.refs_5_) | copy-start | bytes 1572868
  6.7 31.9 %collective-permute-start.1 = (bf16[512,512]{1,0:T(8,128)(2,1)S(1)}, bf16[512,512]{1,0:T(8,128)(2,1)S(1)}, u32[]{:S(2)}, u32[]{:S(2)}) collective-permute-start(bf16[512,512]{1,0:T(8,128)(2,1)S(1)} %fusion.4.refs_5_), channel_id=1, source_target_pairs={{8,0},{16,8},{24,16},{32,24},{40,32},{48,40},{56,48},{64,56},{72,6... | collective-permute-start | bytes 1572872 | tf_op jit(solution)/shard_map/ppermute | solution.py:20
  38.4 34.1 %copy-start.14 = (s32[16384]{0:T(1024)S(1)}, s32[16384]{0:T(1024)}, u32[]{:S(2)}) copy-start(s32[16384]{0:T(1024)} %param.11) | copy-start | bytes 196612
  38.5 44.7 %copy-start.3 = (bf16[512,512]{1,0:T(8,128)(2,1)}, bf16[512,512]{1,0:T(8,128)(2,1)S(1)}, u32[]{:S(2)}) copy-start(bf16[512,512]{1,0:T(8,128)(2,1)S(1)} %collective-permute-done.refs_3_) | copy-start | bytes 1572868
  38.5 19.4 %copy-start.13 = (bf16[512,512]{1,0:T(8,128)(2,1)}, bf16[512,512]{1,0:T(8,128)(2,1)S(1)}, u32[]{:S(2)}) copy-start(bf16[512,512]{1,0:T(8,128)(2,1)S(1)} %collective-permute-done.1.refs_6_) | copy-start | bytes 1572868
  38.5 13.8 %collective-permute-start.2 = (bf16[512,512]{1,0:T(8,128)(2,1)S(1)}, bf16[512,512]{1,0:T(8,128)(2,1)S(1)}, u32[]{:S(2)}, u32[]{:S(2)}) collective-permute-start(bf16[512,512]{1,0:T(8,128)(2,1)S(1)} %collective-permute-done.refs_3_), channel_id=1, source_target_pairs={{0,8},{8,16},{16,24},{24,32},{32,40},{40,48},{48,56},{56,64},{64,7... | collective-permute-start | bytes 1572872 | tf_op jit(solution)/shard_map/ppermute | solution.py:20
  41.3 15.3 %collective-permute-start.5 = (bf16[512,512]{1,0:T(8,128)(2,1)S(1)}, bf16[512,512]{1,0:T(8,128)(2,1)}, u32[]{:S(2)}, u32[]{:S(2)}) collective-permute-start(bf16[512,512]{1,0:T(8,128)(2,1)S(1)} %collective-permute-done.1.refs_6_), channel_id=1, source_target_pairs={{8,0},{16,8},{24,16},{32,24},{40,32},{48,40},{56,48},{64,56},{72,6... | collective-permute-start | bytes 1572872 | tf_op jit(solution)/shard_map/ppermute | solution.py:20
  52.4 30.9 %copy-start.4 = (bf16[512,512]{1,0:T(8,128)(2,1)}, bf16[512,512]{1,0:T(8,128)(2,1)S(1)}, u32[]{:S(2)}) copy-start(bf16[512,512]{1,0:T(8,128)(2,1)S(1)} %collective-permute-done.2.refs_2_) | copy-start | bytes 1572868
  52.4 14.5 %collective-permute-start.3 = (bf16[512,512]{1,0:T(8,128)(2,1)S(1)}, bf16[512,512]{1,0:T(8,128)(2,1)S(1)}, u32[]{:S(2)}, u32[]{:S(2)}) collective-permute-start(bf16[512,512]{1,0:T(8,128)(2,1)S(1)} %collective-permute-done.2.refs_2_), channel_id=1, source_target_pairs={{0,8},{8,16},{16,24},{24,32},{32,40},{40,48},{48,56},{56,64},{64,7... | collective-permute-start | bytes 1572872 | tf_op jit(solution)/shard_map/ppermute | solution.py:20
  56.6 14.5 %collective-permute-start.6 = (bf16[512,512]{1,0:T(8,128)(2,1)}, bf16[512,512]{1,0:T(8,128)(2,1)}, u32[]{:S(2)}, u32[]{:S(2)}) collective-permute-start(bf16[512,512]{1,0:T(8,128)(2,1)} %collective-permute-done.5.refs_7_), channel_id=1, source_target_pairs={{8,0},{16,8},{24,16},{32,24},{40,32},{48,40},{56,48},{64,56},{72,6... | collective-permute-start | bytes 1572872 | tf_op jit(solution)/shard_map/ppermute | solution.py:20
  66.9 16.4 %copy-start.5 = (bf16[512,512]{1,0:T(8,128)(2,1)}, bf16[512,512]{1,0:T(8,128)(2,1)S(1)}, u32[]{:S(2)}) copy-start(bf16[512,512]{1,0:T(8,128)(2,1)S(1)} %collective-permute-done.3.refs_1_) | copy-start | bytes 1572868
  66.9 13.8 %collective-permute-start.4 = (bf16[512,512]{1,0:T(8,128)(2,1)S(1)}, bf16[512,512]{1,0:T(8,128)(2,1)S(1)}, u32[]{:S(2)}, u32[]{:S(2)}) collective-permute-start(bf16[512,512]{1,0:T(8,128)(2,1)S(1)} %collective-permute-done.3.refs_1_), channel_id=1, source_target_pairs={{0,8},{8,16},{16,24},{24,32},{32,40},{40,48},{48,56},{56,64},{64,7... | collective-permute-start | bytes 1572872 | tf_op jit(solution)/shard_map/ppermute | solution.py:20
  71.1 13.7 %collective-permute-start.7 = (bf16[512,512]{1,0:T(8,128)(2,1)}, bf16[512,512]{1,0:T(8,128)(2,1)}, u32[]{:S(2)}, u32[]{:S(2)}) collective-permute-start(bf16[512,512]{1,0:T(8,128)(2,1)} %collective-permute-done.6.refs_8_), channel_id=1, source_target_pairs={{8,0},{16,8},{24,16},{32,24},{40,32},{48,40},{56,48},{64,56},{72,6... | collective-permute-start | bytes 1572872 | tf_op jit(solution)/shard_map/ppermute | solution.py:20
  73.4 9.9 %copy-start.2 = (s32[512,1]{1,0:T(8,128)}, s32[512,1]{1,0:T(8,128)S(1)}, u32[]{:S(2)}) copy-start(s32[512,1]{1,0:T(8,128)S(1)} %copy.22.ids_own) | copy-start | bytes 6148
  80.6 2.6 %copy-start.6 = (bf16[512,512]{1,0:T(8,128)(2,1)}, bf16[512,512]{1,0:T(8,128)(2,1)S(1)}, u32[]{:S(2)}) copy-start(bf16[512,512]{1,0:T(8,128)(2,1)S(1)} %collective-permute-done.4.refs_0_) | copy-start | bytes 1572868
  84.8 7.0 %copy-start.7 = (bf16[512,512]{1,0:T(8,128)(2,1)S(1)}, bf16[512,512]{1,0:T(8,128)(2,1)}, u32[]{:S(2)}) copy-start(bf16[512,512]{1,0:T(8,128)(2,1)} %param.9) | copy-start | bytes 1572868
  84.8 7.0 %copy-start.8 = (bf16[512,512]{1,0:T(8,128)(2,1)S(1)}, bf16[512,512]{1,0:T(8,128)(2,1)}, u32[]{:S(2)}) copy-start(bf16[512,512]{1,0:T(8,128)(2,1)} %param.8) | copy-start | bytes 1572868
  84.8 7.0 %copy-start.10 = (bf16[512,512]{1,0:T(8,128)(2,1)S(1)}, bf16[512,512]{1,0:T(8,128)(2,1)}, u32[]{:S(2)}) copy-start(bf16[512,512]{1,0:T(8,128)(2,1)} %param.7) | copy-start | bytes 1572868
  84.8 7.0 %copy-start.12 = (bf16[512,512]{1,0:T(8,128)(2,1)S(1)}, bf16[512,512]{1,0:T(8,128)(2,1)}, u32[]{:S(2)}) copy-start(bf16[512,512]{1,0:T(8,128)(2,1)} %param.10) | copy-start | bytes 1572868

commit v7 on v5

--- a/solution.py
+++ b/solution.py
@@ -141,11 +141,10 @@
     hist = span * rows
     assert hist == MAXCH * C
 
-    every = ("ctx", "tp")
-    devices = lax.axis_size(every)
+    count = lax.axis_size("ctx")
     groups = lax.axis_size("tp")
-    offered = jnp.tile(filter_taps.T, (devices // groups, 1))
-    taps = lax.all_to_all(offered, every, 0, 0, tiled=True).reshape(FLEN)
+    pieces = lax.all_to_all(filter_taps, "tp", split_axis=1, concat_axis=0, tiled=True)
+    taps = lax.all_to_all(jnp.tile(pieces, (count, 1)), "ctx", 0, 0, tiled=True).reshape(FLEN)
 
     mixed_in = (key_in.astype(jnp.float32) * value_in.astype(jnp.float32)).astype(jnp.bfloat16)
     conv_grad = (out_grad.astype(jnp.float32) * query_in.astype(jnp.float32)).astype(jnp.bfloat16)
@@ -164,7 +163,8 @@
     ids_rdr = lax.dynamic_slice_in_dim(ids_pad, here * rows + hist, hist + rows)
 
     filter_part = filter_sums(ids_own, ids_src, ahead[::-1], conv_grad)
-    spread = lax.all_to_all(filter_part.reshape(devices, FLEN // devices), every, 0, 0, tiled=True)
+    spread = lax.all_to_all(filter_part.reshape(count, FLEN // count), "ctx", 0, 0, tiled=True)
+    block_sum = jnp.sum(spread, axis=0).reshape(groups, FLEN // (count * groups))
     conv, mixed_grad = local_conv(taps, ids_own, ids_src, ids_rdr, skip_gain, ahead[::-1], behind)
 
     mixed_out = (query_in.astype(jnp.float32) * conv).astype(jnp.bfloat16)
@@ -172,7 +172,7 @@
     key_grad = (mixed_grad * value_in.astype(jnp.float32)).astype(jnp.bfloat16)
     value_grad = (mixed_grad * key_in.astype(jnp.float32)).astype(jnp.bfloat16)
 
-    summed = jnp.sum(spread.reshape(devices // groups, groups, FLEN // devices), axis=0).T
+    summed = lax.all_to_all(block_sum, "tp", 0, 0, tiled=True).T
     tokens = lax.axis_size("ctx") * rows
     filter_grad = summed * (1.0 / math.sqrt(FGROUP * tokens))
     return (mixed_out, query_grad, key_grad, value_grad, filter_grad)

time: 108 us -> 109 us (level)
  waiting for transfers between devices: 27.1 us -> 28.4 us
  starting transfers between devices: 56.9 us -> 58.1 us
    ppermute x8, starting transfers between devices: 21.3 us -> 23.4 us  [shifted(): lax.ppermute(value, axis, [(source, source + steps) for source in range(l...]
    all_to_all x2 -> x4, starting transfers between devices: 35.6 us -> 34.7 us  [the longest x1 13.6 us: shards(): lax.all_to_all(jnp.tile(pieces, (count, 1)), 'ctx', 0, 0, tiled=True)]
    all_to_all x2 -> x4, waiting for transfers between devices: 8.76 us -> 9.14 us  [the longest x1 6.88 us: shards(): lax.all_to_all(jnp.tile(pieces, (count, 1)), 'ctx', 0, 0, tiled=True)]
  transfers between devices with their start and end apart: 10 -> 12, of which waited for: 7 -> 8; matrix products, arithmetic and copies ran while one was open for 8% -> 7% of each run, Pallas kernels for 9% -> 9%
where the time goes in v7:
time: 109 us; the launch traced here: 108 us
  starting transfers between devices  58.1 us (53%)
  waiting for transfers between devices  28.4 us (26%)
  Pallas kernels  9.6 us (9%)
  other arithmetic  5.53 us (5%)
  local copies, waits for them, and re-layouts  5.37 us (5%)
    ppermute x8, starting transfers between devices, shifted(): lax.ppermute(value, axis, [(source, source + steps) for source in range(l...  23.4 us
    ppermute x8, waiting for transfers between devices, shifted(): lax.ppermute(value, axis, [(source, source + steps) for source in range(l...  19.3 us
    all_to_all x1, starting transfers between devices, shards(): lax.all_to_all(jnp.tile(pieces, (count, 1)), 'ctx', 0, 0, tiled=True)  13.6 us
    all_to_all x1, starting transfers between devices, shards(): summed = lax.all_to_all(block_sum, 'tp', 0, 0, tiled=True).T  10.4 us
    pallas_call x1, Pallas kernels, local_conv(): pl.pallas_call(conv_kernel, out_shape=(jax.ShapeDtypeStruct((own, width),...  7.01 us
    all_to_all x1, waiting for transfers between devices, shards(): lax.all_to_all(jnp.tile(pieces, (count, 1)), 'ctx', 0, 0, tiled=True)  6.88 us
    all_to_all x1, starting transfers between devices, shards(): lax.all_to_all(filter_taps, 'tp', split_axis=1, concat_axis=0, tiled=True)  6.77 us
    all_to_all x1, starting transfers between devices, shards(): lax.all_to_all(filter_part.reshape(count, FLEN // count), 'ctx', 0, 0, ti...  3.89 us
  transfers between devices with their start and end apart: 12, of which 8 were waited for; matrix products, arithmetic and copies ran while one was open for 7% of the time, Pallas kernels for 9%

profile of v7, /device:TPU:1, one launch (start us, length us, event | category | flops | bytes accessed | tf_op | source)
XLA Modules:
  0.0 107.9 jit_solution(7948544496407289830)
XLA Ops:
  0.6 0.0 copy-start.11
  0.6 0.0 copy-start.9
  0.7 1.4 %fusion.2.refs_4_ = bf16[512,512]{1,0:T(8,128)(2,1)S(1)} fusion(bf16[512,512]{1,0:T(8,128)(2,1)} %param.9, bf16[512,512]{1,0:T(8,128)(2,1)} %param.8), kind=kLoop, calls=%fused_computation.8 | loop fusion | flops 1048576 | bytes 1572864 | tf_op jit(solution)/shard_map/convert_element_type | solution.py:149
  2.1 4.4 %collective-permute-start = (bf16[512,512]{1,0:T(8,128)(2,1)S(1)}, bf16[512,512]{1,0:T(8,128)(2,1)S(1)}, u32[]{:S(2)}, u32[]{:S(2)}) collective-permute-start(bf16[512,512]{1,0:T(8,128)(2,1)S(1)} %fusion.2.refs_4_), channel_id=1, source_target_pairs={{0,8},{8,16},{16,24},{24,32},{32,40},{40,48},{48,56},{56,64},{64,7... | collective-permute-start | bytes 1572872 | tf_op jit(solution)/shard_map/ppermute | solution.py:20
  6.5 0.0 copy-start.15
  6.5 0.0 copy-start.14
  6.5 0.1 fusion.4.refs_5_
  6.7 1.3 %collective-permute-start.4 = (bf16[512,512]{1,0:T(8,128)(2,1)S(1)}, bf16[512,512]{1,0:T(8,128)(2,1)S(1)}, u32[]{:S(2)}, u32[]{:S(2)}) collective-permute-start(bf16[512,512]{1,0:T(8,128)(2,1)S(1)} %fusion.4.refs_5_), channel_id=1, source_target_pairs={{8,0},{16,8},{24,16},{32,24},{40,32},{48,40},{56,48},{64,56},{72,6... | collective-permute-start | bytes 1572872 | tf_op jit(solution)/shard_map/ppermute | solution.py:20
  8.0 9.1 %collective-permute-done.refs_3_ = bf16[512,512]{1,0:T(8,128)(2,1)S(1)} collective-permute-done((bf16[512,512]{1,0:T(8,128)(2,1)S(1)}, bf16[512,512]{1,0:T(8,128)(2,1)S(1)}, u32[]{:S(2)}, u32[]{:S(2)}) %collective-permute-start) | collective-permute-done | bytes 524320 | tf_op jit(solution)/shard_map/ppermute | solution.py:20
  17.0 4.1 %collective-permute-start.1 = (bf16[512,512]{1,0:T(8,128)(2,1)S(1)}, bf16[512,512]{1,0:T(8,128)(2,1)S(1)}, u32[]{:S(2)}, u32[]{:S(2)}) collective-permute-start(bf16[512,512]{1,0:T(8,128)(2,1)S(1)} %collective-permute-done.refs_3_), channel_id=1, source_target_pairs={{0,8},{8,16},{16,24},{24,32},{32,40},{40,48},{48,56},{56,64},{64,7... | collective-permute-start | bytes 1572872 | tf_op jit(solution)/shard_map/ppermute | solution.py:20
  21.2 0.2 collective-permute-done.4.refs_6_
  21.4 1.3 %collective-permute-start.5 = (bf16[512,512]{1,0:T(8,128)(2,1)S(1)}, bf16[512,512]{1,0:T(8,128)(2,1)}, u32[]{:S(2)}, u32[]{:S(2)}) collective-permute-start(bf16[512,512]{1,0:T(8,128)(2,1)S(1)} %collective-permute-done.4.refs_6_), channel_id=1, source_target_pairs={{8,0},{16,8},{24,16},{32,24},{40,32},{48,40},{56,48},{64,56},{72,6... | collective-permute-start | bytes 1572872 | tf_op jit(solution)/shard_map/ppermute | solution.py:20
  22.7 8.2 %collective-permute-done.1.refs_2_ = bf16[512,512]{1,0:T(8,128)(2,1)S(1)} collective-permute-done((bf16[512,512]{1,0:T(8,128)(2,1)S(1)}, bf16[512,512]{1,0:T(8,128)(2,1)S(1)}, u32[]{:S(2)}, u32[]{:S(2)}) %collective-permute-start.1) | collective-permute-done | bytes 524320 | tf_op jit(solution)/shard_map/ppermute | solution.py:20
  30.9 4.2 %collective-permute-start.2 = (bf16[512,512]{1,0:T(8,128)(2,1)S(1)}, bf16[512,512]{1,0:T(8,128)(2,1)S(1)}, u32[]{:S(2)}, u32[]{:S(2)}) collective-permute-start(bf16[512,512]{1,0:T(8,128)(2,1)S(1)} %collective-permute-done.1.refs_2_), channel_id=1, source_target_pairs={{0,8},{8,16},{16,24},{24,32},{32,40},{40,48},{48,56},{56,64},{64,7... | collective-permute-start | bytes 1572872 | tf_op jit(solution)/shard_map/ppermute | solution.py:20
  35.1 0.5 collective-permute-done.5.refs_7_
  35.7 1.3 %collective-permute-start.6 = (bf16[512,512]{1,0:T(8,128)(2,1)}, bf16[512,512]{1,0:T(8,128)(2,1)}, u32[]{:S(2)}, u32[]{:S(2)}) collective-permute-start(bf16[512,512]{1,0:T(8,128)(2,1)} %collective-permute-done.5.refs_7_), channel_id=1, source_target_pairs={{8,0},{16,8},{24,16},{32,24},{40,32},{48,40},{56,48},{64,56},{72,6... | collective-permute-start | bytes 1572872 | tf_op jit(solution)/shard_map/ppermute | solution.py:20
  37.0 0.7 copy.25
  37.6 6.8 %all-to-all-start = ((bf16[8,8,1]{0,2,1:T(2,128)(2,1)}), bf16[8,8,1]{0,2,1:T(2,128)(2,1)S(1)}, u32[]{:S(2)}, u32[]{:S(2)}) async-start(bf16[8,8,1]{0,2,1:T(2,128)(2,1)} %copy.25), calls=%async_computation | async-start | bytes 8192 | tf_op jit(solution)/shard_map/all_to_all | solution.py:146
  44.4 0.0 collective-permute-done.2.refs_1_
  44.4 5.5 %collective-permute-start.3 = (bf16[512,512]{1,0:T(8,128)(2,1)S(1)}, bf16[512,512]{1,0:T(8,128)(2,1)S(1)}, u32[]{:S(2)}, u32[]{:S(2)}) collective-permute-start(bf16[512,512]{1,0:T(8,128)(2,1)S(1)} %collective-permute-done.2.refs_1_), channel_id=1, source_target_pairs={{0,8},{8,16},{16,24},{24,32},{32,40},{40,48},{48,56},{56,64},{64,7... | collective-permute-start | bytes 1572872 | tf_op jit(solution)/shard_map/ppermute | solution.py:20
  49.9 1.3 %collective-permute-done.6.refs_8_ = bf16[512,512]{1,0:T(8,128)(2,1)} collective-permute-done((bf16[512,512]{1,0:T(8,128)(2,1)}, bf16[512,512]{1,0:T(8,128)(2,1)}, u32[]{:S(2)}, u32[]{:S(2)}) %collective-permute-start.6) | collective-permute-done | bytes 524320 | tf_op jit(solution)/shard_map/ppermute | solution.py:20
  51.2 1.3 %collective-permute-start.7 = (bf16[512,512]{1,0:T(8,128)(2,1)}, bf16[512,512]{1,0:T(8,128)(2,1)}, u32[]{:S(2)}, u32[]{:S(2)}) collective-permute-start(bf16[512,512]{1,0:T(8,128)(2,1)} %collective-permute-done.6.refs_8_), channel_id=1, source_target_pairs={{8,0},{16,8},{24,16},{32,24},{40,32},{48,40},{56,48},{64,56},{72,6... | collective-permute-start | bytes 1572872 | tf_op jit(solution)/shard_map/ppermute | solution.py:20
  52.6 0.1 tile.4
  52.7 0.6 tile.10
  53.3 13.6 %all-to-all-start.1 = ((bf16[32,64,1]{1,2,0:T(2,128)(2,1)}), bf16[32,64,1]{1,2,0:T(2,128)(2,1)S(1)}, u32[]{:S(2)}, u32[]{:S(2)}) async-start(bf16[32,64,1]{1,2,0:T(2,128)(2,1)} %tile.10), calls=%async_computation.1 | async-start | bytes 32768 | tf_op jit(solution)/shard_map/all_to_all | solution.py:147
  66.9 0.1 fusion.6
  66.9 0.6 reshape.62.ids_src
  67.6 0.1 dynamic_slice.9
  67.6 0.6 reshape.63.ids_rdr
  68.2 0.1 rev.3
  68.4 0.1 copy.26.ids_own
  68.6 6.9 %all-to-all-done.1 = bf16[32,64,1]{1,2,0:T(2,128)(2,1)S(1)} async-done(((bf16[32,64,1]{1,2,0:T(2,128)(2,1)}), bf16[32,64,1]{1,2,0:T(2,128)(2,1)S(1)}, u32[]{:S(2)}, u32[]{:S(2)}) %all-to-all-start.1) | async-done | bytes 4128 | tf_op jit(solution)/shard_map/all_to_all | solution.py:147
  75.4 0.1 reduce.2
  75.5 0.1 convert_element_type.41
  75.6 2.6 %shard_map.111 = f32[1,2560]{1,0:T(1,128)S(1)} custom-call(s32[512,1]{1,0:T(8,128)S(1)} %copy.26.ids_own, s32[1,2560]{1,0:T(1,128)S(1)} %bitcast.16, bf16[512,512]{1,0:T(8,128)(2,1)S(1)} %collective-permute-done.3.refs_0_, bf16[512,512]{1,0:T(8,128)(2,1)S(1)} %collective-permute-done.2.refs_1_, bf16[512,512]{1,0:T(8,128)(2,1)S(1)} %collective-permute-done.1.refs_2_, ...), custom_call_target="tpu_custom_call" | custom-call | tf_op jit(solution)/shard_map/pallas_call | solution.py:110
  78.2 0.1 slice_reduce_fusion
  78.3 0.7 all_to_all.32
  79.0 3.9 %all-to-all-start.2 = ((f32[32,1,64]{2,1,0:T(1,128)}), f32[32,1,64]{2,1,0:T(1,128)S(1)}, u32[]{:S(2)}, u32[]{:S(2)}) async-start(f32[32,1,64]{2,1,0:T(1,128)} %bitcast.5), calls=%async_computation.2 | async-start | bytes 32768 | tf_op jit(solution)/shard_map/all_to_all | solution.py:166
  82.9 0.6 pad_convert_fusion
  83.5 0.0 copy-start.12
  83.5 7.0 %shard_map.110 = (f32[512,512]{1,0:T(8,128)}, f32[512,512]{1,0:T(8,128)}) custom-call(f32[1,3072]{1,0:T(1,128)} %bitcast.18, s32[512,1]{1,0:T(8,128)} %copy-done.2, s32[1,2560]{1,0:T(1,128)} %reshape.62.ids_src, s32[1,2560]{1,0:T(1,128)} %reshape.63.ids_rdr, f32[1,512]{1,0:T(1,128)} %bitcast.21, bf16[512,512]{1,0:T(8,128)(2,1)} %copy-done.6, ...), custom_call_target="tpu_custom_call" | custom-call | tf_op jit(solution)/shard_map/pallas_call | solution.py:123
  90.6 1.0 all-to-all-done.2
  91.6 0.1 reduce_sum.9
  91.6 0.7 all_to_all.34
  92.3 10.4 %all-to-all-start.3 = ((f32[8,1,8]{2,1,0:T(1,128)}), f32[8,1,8]{2,1,0:T(1,128)S(1)}, u32[]{:S(2)}, u32[]{:S(2)}) async-start(f32[8,1,8]{2,1,0:T(1,128)} %bitcast.6), calls=%async_computation.3 | async-start | bytes 8192 | tf_op jit(solution)/shard_map/all_to_all | solution.py:175
  102.8 3.3 %fusion.1 = (bf16[512,512]{1,0:T(8,128)(2,1)}, bf16[512,512]{1,0:T(8,128)(2,1)}, bf16[512,512]{1,0:T(8,128)(2,1)}, bf16[512,512]{1,0:T(8,128)(2,1)}) fusion(f32[512,512]{1,0:T(8,128)} %get-tuple-element.8, bf16[512,512]{1,0:T(8,128)(2,1)S(1)} %copy-done.8, bf16[512,512]{1,0:T(8,128)(2,1)S(1)} %copy-done.7, f32[512,512]{1,0:T(8,128)} %get-tuple-element.7, ...), kind=kLoop, calls=%fused_computation.7 | loop fusion | flops 3145728 | bytes 6291456 | tf_op jit(solution)/shard_map/convert_element_type | solution.py:173
  106.0 1.2 %all-to-all-done.3 = f32[8,1,8]{2,1,0:T(1,128)S(1)} async-done(((f32[8,1,8]{2,1,0:T(1,128)}), f32[8,1,8]{2,1,0:T(1,128)S(1)}, u32[]{:S(2)}, u32[]{:S(2)}) %all-to-all-start.3) | async-done | bytes 288 | tf_op jit(solution)/shard_map/all_to_all | solution.py:175
  107.3 0.7 copy.31
  (37 shorter events, 0.1 us)
Async XLA Ops:
  0.6 5.9 %copy-start.11 = (bf16[512,512]{1,0:T(8,128)(2,1)S(1)}, bf16[512,512]{1,0:T(8,128)(2,1)}, u32[]{:S(2)}) copy-start(bf16[512,512]{1,0:T(8,128)(2,1)} %param.10) | copy-start | bytes 1572868
  0.6 5.9 %copy-start.9 = (bf16[512,512]{1,0:T(8,128)(2,1)S(1)}, bf16[512,512]{1,0:T(8,128)(2,1)}, u32[]{:S(2)}) copy-start(bf16[512,512]{1,0:T(8,128)(2,1)} %param.7) | copy-start | bytes 1572868
  2.1 73.5 %copy-start = (bf16[512,512]{1,0:T(8,128)(2,1)}, bf16[512,512]{1,0:T(8,128)(2,1)S(1)}, u32[]{:S(2)}) copy-start(bf16[512,512]{1,0:T(8,128)(2,1)S(1)} %fusion.2.refs_4_) | copy-start | bytes 1572868
  2.1 15.0 %collective-permute-start = (bf16[512,512]{1,0:T(8,128)(2,1)S(1)}, bf16[512,512]{1,0:T(8,128)(2,1)S(1)}, u32[]{:S(2)}, u32[]{:S(2)}) collective-permute-start(bf16[512,512]{1,0:T(8,128)(2,1)S(1)} %fusion.2.refs_4_), channel_id=1, source_target_pairs={{0,8},{8,16},{16,24},{24,32},{32,40},{40,48},{48,56},{56,64},{64,7... | collective-permute-start | bytes 1572872 | tf_op jit(solution)/shard_map/ppermute | solution.py:20
  6.5 30.4 %copy-start.15 = (bf16[8,8]{1,0:T(8,128)(2,1)S(1)}, bf16[8,8]{1,0:T(8,128)(2,1)}, u32[]{:S(2)}) copy-start(bf16[8,8]{1,0:T(8,128)(2,1)} %param.13) | copy-start | bytes 388
  6.5 46.0 %copy-start.14 = (s32[16384]{0:T(1024)S(1)}, s32[16384]{0:T(1024)}, u32[]{:S(2)}) copy-start(s32[16384]{0:T(1024)} %param.11) | copy-start | bytes 196612
  6.7 71.5 %copy-start.1 = (bf16[512,512]{1,0:T(8,128)(2,1)}, bf16[512,512]{1,0:T(8,128)(2,1)S(1)}, u32[]{:S(2)}) copy-start(bf16[512,512]{1,0:T(8,128)(2,1)S(1)} %fusion.4.refs_5_) | copy-start | bytes 1572868
  6.7 14.7 %collective-permute-start.4 = (bf16[512,512]{1,0:T(8,128)(2,1)S(1)}, bf16[512,512]{1,0:T(8,128)(2,1)S(1)}, u32[]{:S(2)}, u32[]{:S(2)}) collective-permute-start(bf16[512,512]{1,0:T(8,128)(2,1)S(1)} %fusion.4.refs_5_), channel_id=1, source_target_pairs={{8,0},{16,8},{24,16},{32,24},{40,32},{48,40},{56,48},{64,56},{72,6... | collective-permute-start | bytes 1572872 | tf_op jit(solution)/shard_map/ppermute | solution.py:20
  17.0 61.1 %copy-start.3 = (bf16[512,512]{1,0:T(8,128)(2,1)}, bf16[512,512]{1,0:T(8,128)(2,1)S(1)}, u32[]{:S(2)}) copy-start(bf16[512,512]{1,0:T(8,128)(2,1)S(1)} %collective-permute-done.refs_3_) | copy-start | bytes 1572868
  17.0 13.8 %collective-permute-start.1 = (bf16[512,512]{1,0:T(8,128)(2,1)S(1)}, bf16[512,512]{1,0:T(8,128)(2,1)S(1)}, u32[]{:S(2)}, u32[]{:S(2)}) collective-permute-start(bf16[512,512]{1,0:T(8,128)(2,1)S(1)} %collective-permute-done.refs_3_), channel_id=1, source_target_pairs={{0,8},{8,16},{16,24},{24,32},{32,40},{40,48},{48,56},{56,64},{64,7... | collective-permute-start | bytes 1572872 | tf_op jit(solution)/shard_map/ppermute | solution.py:20
  21.4 9.5 %copy-start.13 = (bf16[512,512]{1,0:T(8,128)(2,1)}, bf16[512,512]{1,0:T(8,128)(2,1)S(1)}, u32[]{:S(2)}) copy-start(bf16[512,512]{1,0:T(8,128)(2,1)S(1)} %collective-permute-done.4.refs_6_) | copy-start | bytes 1572868
  21.4 14.2 %collective-permute-start.5 = (bf16[512,512]{1,0:T(8,128)(2,1)S(1)}, bf16[512,512]{1,0:T(8,128)(2,1)}, u32[]{:S(2)}, u32[]{:S(2)}) collective-permute-start(bf16[512,512]{1,0:T(8,128)(2,1)S(1)} %collective-permute-done.4.refs_6_), channel_id=1, source_target_pairs={{8,0},{16,8},{24,16},{32,24},{40,32},{48,40},{56,48},{64,56},{72,6... | collective-permute-start | bytes 1572872 | tf_op jit(solution)/shard_map/ppermute | solution.py:20
  30.9 47.3 %copy-start.4 = (bf16[512,512]{1,0:T(8,128)(2,1)}, bf16[512,512]{1,0:T(8,128)(2,1)S(1)}, u32[]{:S(2)}) copy-start(bf16[512,512]{1,0:T(8,128)(2,1)S(1)} %collective-permute-done.1.refs_2_) | copy-start | bytes 1572868
  30.9 13.5 %collective-permute-start.2 = (bf16[512,512]{1,0:T(8,128)(2,1)S(1)}, bf16[512,512]{1,0:T(8,128)(2,1)S(1)}, u32[]{:S(2)}, u32[]{:S(2)}) collective-permute-start(bf16[512,512]{1,0:T(8,128)(2,1)S(1)} %collective-permute-done.1.refs_2_), channel_id=1, source_target_pairs={{0,8},{8,16},{16,24},{24,32},{32,40},{40,48},{48,56},{56,64},{64,7... | collective-permute-start | bytes 1572872 | tf_op jit(solution)/shard_map/ppermute | solution.py:20
  35.7 15.5 %collective-permute-start.6 = (bf16[512,512]{1,0:T(8,128)(2,1)}, bf16[512,512]{1,0:T(8,128)(2,1)}, u32[]{:S(2)}, u32[]{:S(2)}) collective-permute-start(bf16[512,512]{1,0:T(8,128)(2,1)} %collective-permute-done.5.refs_7_), channel_id=1, source_target_pairs={{8,0},{16,8},{24,16},{32,24},{40,32},{48,40},{56,48},{64,56},{72,6... | collective-permute-start | bytes 1572872 | tf_op jit(solution)/shard_map/ppermute | solution.py:20
  37.6 14.9 %all-to-all-start = ((bf16[8,8,1]{0,2,1:T(2,128)(2,1)}), bf16[8,8,1]{0,2,1:T(2,128)(2,1)S(1)}, u32[]{:S(2)}, u32[]{:S(2)}) async-start(bf16[8,8,1]{0,2,1:T(2,128)(2,1)} %copy.25), calls=%async_computation | async-start | bytes 8192 | tf_op jit(solution)/shard_map/all_to_all | solution.py:146
  44.4 33.8 %copy-start.5 = (bf16[512,512]{1,0:T(8,128)(2,1)}, bf16[512,512]{1,0:T(8,128)(2,1)S(1)}, u32[]{:S(2)}) copy-start(bf16[512,512]{1,0:T(8,128)(2,1)S(1)} %collective-permute-done.2.refs_1_) | copy-start | bytes 1572868
  44.4 31.2 %collective-permute-start.3 = (bf16[512,512]{1,0:T(8,128)(2,1)S(1)}, bf16[512,512]{1,0:T(8,128)(2,1)S(1)}, u32[]{:S(2)}, u32[]{:S(2)}) collective-permute-start(bf16[512,512]{1,0:T(8,128)(2,1)S(1)} %collective-permute-done.2.refs_1_), channel_id=1, source_target_pairs={{0,8},{8,16},{16,24},{24,32},{32,40},{40,48},{48,56},{56,64},{64,7... | collective-permute-start | bytes 1572872 | tf_op jit(solution)/shard_map/ppermute | solution.py:20
  51.2 32.3 %collective-permute-start.7 = (bf16[512,512]{1,0:T(8,128)(2,1)}, bf16[512,512]{1,0:T(8,128)(2,1)}, u32[]{:S(2)}, u32[]{:S(2)}) collective-permute-start(bf16[512,512]{1,0:T(8,128)(2,1)} %collective-permute-done.6.refs_8_), channel_id=1, source_target_pairs={{8,0},{16,8},{24,16},{32,24},{40,32},{48,40},{56,48},{64,56},{72,6... | collective-permute-start | bytes 1572872 | tf_op jit(solution)/shard_map/ppermute | solution.py:20
  53.3 22.2 %all-to-all-start.1 = ((bf16[32,64,1]{1,2,0:T(2,128)(2,1)}), bf16[32,64,1]{1,2,0:T(2,128)(2,1)S(1)}, u32[]{:S(2)}, u32[]{:S(2)}) async-start(bf16[32,64,1]{1,2,0:T(2,128)(2,1)} %tile.10), calls=%async_computation.1 | async-start | bytes 32768 | tf_op jit(solution)/shard_map/all_to_all | solution.py:147
  68.6 9.7 %copy-start.2 = (s32[512,1]{1,0:T(8,128)}, s32[512,1]{1,0:T(8,128)S(1)}, u32[]{:S(2)}) copy-start(s32[512,1]{1,0:T(8,128)S(1)} %copy.26.ids_own) | copy-start | bytes 6148
  75.6 2.6 %copy-start.6 = (bf16[512,512]{1,0:T(8,128)(2,1)}, bf16[512,512]{1,0:T(8,128)(2,1)S(1)}, u32[]{:S(2)}) copy-start(bf16[512,512]{1,0:T(8,128)(2,1)S(1)} %collective-permute-done.3.refs_0_) | copy-start | bytes 1572868
  79.0 12.6 %all-to-all-start.2 = ((f32[32,1,64]{2,1,0:T(1,128)}), f32[32,1,64]{2,1,0:T(1,128)S(1)}, u32[]{:S(2)}, u32[]{:S(2)}) async-start(f32[32,1,64]{2,1,0:T(1,128)} %bitcast.5), calls=%async_computation.2 | async-start | bytes 32768 | tf_op jit(solution)/shard_map/all_to_all | solution.py:166
  83.5 19.2 %copy-start.7 = (bf16[512,512]{1,0:T(8,128)(2,1)S(1)}, bf16[512,512]{1,0:T(8,128)(2,1)}, u32[]{:S(2)}) copy-start(bf16[512,512]{1,0:T(8,128)(2,1)} %param.9) | copy-start | bytes 1572868
  83.5 19.2 %copy-start.8 = (bf16[512,512]{1,0:T(8,128)(2,1)S(1)}, bf16[512,512]{1,0:T(8,128)(2,1)}, u32[]{:S(2)}) copy-start(bf16[512,512]{1,0:T(8,128)(2,1)} %param.8) | copy-start | bytes 1572868
  83.5 19.2 %copy-start.10 = (bf16[512,512]{1,0:T(8,128)(2,1)S(1)}, bf16[512,512]{1,0:T(8,128)(2,1)}, u32[]{:S(2)}) copy-start(bf16[512,512]{1,0:T(8,128)(2,1)} %param.7) | copy-start | bytes 1572868
  83.5 19.2 %copy-start.12 = (bf16[512,512]{1,0:T(8,128)(2,1)S(1)}, bf16[512,512]{1,0:T(8,128)(2,1)}, u32[]{:S(2)}) copy-start(bf16[512,512]{1,0:T(8,128)(2,1)} %param.10) | copy-start | bytes 1572868
  92.3 15.0 %all-to-all-start.3 = ((f32[8,1,8]{2,1,0:T(1,128)}), f32[8,1,8]{2,1,0:T(1,128)S(1)}, u32[]{:S(2)}, u32[]{:S(2)}) async-start(f32[8,1,8]{2,1,0:T(1,128)} %bitcast.6), calls=%async_computation.3 | async-start | bytes 8192 | tf_op jit(solution)/shard_map/all_to_all | solution.py:175

commit v8 on v7

--- a/solution.py
+++ b/solution.py
@@ -144,7 +144,8 @@
     count = lax.axis_size("ctx")
     groups = lax.axis_size("tp")
     pieces = lax.all_to_all(filter_taps, "tp", split_axis=1, concat_axis=0, tiled=True)
-    taps = lax.all_to_all(jnp.tile(pieces, (count, 1)), "ctx", 0, 0, tiled=True).reshape(FLEN)
+    row = pieces.reshape(1, FLEN // count)
+    taps = lax.all_to_all(jnp.tile(row, (count, 1)), "ctx", 0, 0, tiled=True).reshape(FLEN)
 
     mixed_in = (key_in.astype(jnp.float32) * value_in.astype(jnp.float32)).astype(jnp.bfloat16)
     conv_grad = (out_grad.astype(jnp.float32) * query_in.astype(jnp.float32)).astype(jnp.bfloat16)

time: 109 us -> 109 us (level)
  no operation moved by 1% of the time
where the time goes in v8:
time: 109 us; the launch traced here: 108 us
  starting transfers between devices  58.1 us (53%)
  waiting for transfers between devices  28.4 us (26%)
  Pallas kernels  9.6 us (9%)
  other arithmetic  5.53 us (5%)
  local copies, waits for them, and re-layouts  5.37 us (5%)
    ppermute x8, starting transfers between devices, shifted(): lax.ppermute(value, axis, [(source, source + steps) for source in range(l...  23.4 us
    ppermute x8, waiting for transfers between devices, shifted(): lax.ppermute(value, axis, [(source, source + steps) for source in range(l...  19.3 us
    all_to_all x1, starting transfers between devices, shards(): lax.all_to_all(jnp.tile(row, (count, 1)), 'ctx', 0, 0, tiled=True)  13.6 us
    all_to_all x1, starting transfers between devices, shards(): summed = lax.all_to_all(block_sum, 'tp', 0, 0, tiled=True).T  10.4 us
    pallas_call x1, Pallas kernels, local_conv(): pl.pallas_call(conv_kernel, out_shape=(jax.ShapeDtypeStruct((own, width),...  7.01 us
    all_to_all x1, waiting for transfers between devices, shards(): lax.all_to_all(jnp.tile(row, (count, 1)), 'ctx', 0, 0, tiled=True)  6.88 us
    all_to_all x1, starting transfers between devices, shards(): lax.all_to_all(filter_taps, 'tp', split_axis=1, concat_axis=0, tiled=True)  6.77 us
    all_to_all x1, starting transfers between devices, shards(): lax.all_to_all(filter_part.reshape(count, FLEN // count), 'ctx', 0, 0, ti...  3.89 us
  transfers between devices with their start and end apart: 12, of which 8 were waited for; matrix products, arithmetic and copies ran while one was open for 7% of the time, Pallas kernels for 9%

profile of v8, /device:TPU:1, one launch (start us, length us, event | category | flops | bytes accessed | tf_op | source)
XLA Modules:
  0.0 107.9 jit_solution(7948544496407289830)
XLA Ops:
  0.6 0.0 copy-start.11
  0.6 0.0 copy-start.9
  0.7 1.4 %fusion.2.refs_4_ = bf16[512,512]{1,0:T(8,128)(2,1)S(1)} fusion(bf16[512,512]{1,0:T(8,128)(2,1)} %param.9, bf16[512,512]{1,0:T(8,128)(2,1)} %param.8), kind=kLoop, calls=%fused_computation.8 | loop fusion | flops 1048576 | bytes 1572864 | tf_op jit(solution)/shard_map/convert_element_type | solution.py:150
  2.1 4.4 %collective-permute-start = (bf16[512,512]{1,0:T(8,128)(2,1)S(1)}, bf16[512,512]{1,0:T(8,128)(2,1)S(1)}, u32[]{:S(2)}, u32[]{:S(2)}) collective-permute-start(bf16[512,512]{1,0:T(8,128)(2,1)S(1)} %fusion.2.refs_4_), channel_id=1, source_target_pairs={{0,8},{8,16},{16,24},{24,32},{32,40},{40,48},{48,56},{56,64},{64,7... | collective-permute-start | bytes 1572872 | tf_op jit(solution)/shard_map/ppermute | solution.py:20
  6.5 0.0 copy-start.15
  6.5 0.0 copy-start.14
  6.5 0.1 fusion.4.refs_5_
  6.7 1.3 %collective-permute-start.4 = (bf16[512,512]{1,0:T(8,128)(2,1)S(1)}, bf16[512,512]{1,0:T(8,128)(2,1)S(1)}, u32[]{:S(2)}, u32[]{:S(2)}) collective-permute-start(bf16[512,512]{1,0:T(8,128)(2,1)S(1)} %fusion.4.refs_5_), channel_id=1, source_target_pairs={{8,0},{16,8},{24,16},{32,24},{40,32},{48,40},{56,48},{64,56},{72,6... | collective-permute-start | bytes 1572872 | tf_op jit(solution)/shard_map/ppermute | solution.py:20
  8.0 9.1 %collective-permute-done.refs_3_ = bf16[512,512]{1,0:T(8,128)(2,1)S(1)} collective-permute-done((bf16[512,512]{1,0:T(8,128)(2,1)S(1)}, bf16[512,512]{1,0:T(8,128)(2,1)S(1)}, u32[]{:S(2)}, u32[]{:S(2)}) %collective-permute-start) | collective-permute-done | bytes 524320 | tf_op jit(solution)/shard_map/ppermute | solution.py:20
  17.0 4.1 %collective-permute-start.1 = (bf16[512,512]{1,0:T(8,128)(2,1)S(1)}, bf16[512,512]{1,0:T(8,128)(2,1)S(1)}, u32[]{:S(2)}, u32[]{:S(2)}) collective-permute-start(bf16[512,512]{1,0:T(8,128)(2,1)S(1)} %collective-permute-done.refs_3_), channel_id=1, source_target_pairs={{0,8},{8,16},{16,24},{24,32},{32,40},{40,48},{48,56},{56,64},{64,7... | collective-permute-start | bytes 1572872 | tf_op jit(solution)/shard_map/ppermute | solution.py:20
  21.2 0.2 collective-permute-done.4.refs_6_
  21.4 1.3 %collective-permute-start.5 = (bf16[512,512]{1,0:T(8,128)(2,1)S(1)}, bf16[512,512]{1,0:T(8,128)(2,1)}, u32[]{:S(2)}, u32[]{:S(2)}) collective-permute-start(bf16[512,512]{1,0:T(8,128)(2,1)S(1)} %collective-permute-done.4.refs_6_), channel_id=1, source_target_pairs={{8,0},{16,8},{24,16},{32,24},{40,32},{48,40},{56,48},{64,56},{72,6... | collective-permute-start | bytes 1572872 | tf_op jit(solution)/shard_map/ppermute | solution.py:20
  22.7 8.2 %collective-permute-done.1.refs_2_ = bf16[512,512]{1,0:T(8,128)(2,1)S(1)} collective-permute-done((bf16[512,512]{1,0:T(8,128)(2,1)S(1)}, bf16[512,512]{1,0:T(8,128)(2,1)S(1)}, u32[]{:S(2)}, u32[]{:S(2)}) %collective-permute-start.1) | collective-permute-done | bytes 524320 | tf_op jit(solution)/shard_map/ppermute | solution.py:20
  30.9 4.2 %collective-permute-start.2 = (bf16[512,512]{1,0:T(8,128)(2,1)S(1)}, bf16[512,512]{1,0:T(8,128)(2,1)S(1)}, u32[]{:S(2)}, u32[]{:S(2)}) collective-permute-start(bf16[512,512]{1,0:T(8,128)(2,1)S(1)} %collective-permute-done.1.refs_2_), channel_id=1, source_target_pairs={{0,8},{8,16},{16,24},{24,32},{32,40},{40,48},{48,56},{56,64},{64,7... | collective-permute-start | bytes 1572872 | tf_op jit(solution)/shard_map/ppermute | solution.py:20
  35.1 0.5 collective-permute-done.5.refs_7_
  35.7 1.3 %collective-permute-start.6 = (bf16[512,512]{1,0:T(8,128)(2,1)}, bf16[512,512]{1,0:T(8,128)(2,1)}, u32[]{:S(2)}, u32[]{:S(2)}) collective-permute-start(bf16[512,512]{1,0:T(8,128)(2,1)} %collective-permute-done.5.refs_7_), channel_id=1, source_target_pairs={{8,0},{16,8},{24,16},{32,24},{40,32},{48,40},{56,48},{64,56},{72,6... | collective-permute-start | bytes 1572872 | tf_op jit(solution)/shard_map/ppermute | solution.py:20
  37.0 0.7 copy.25
  37.6 6.8 %all-to-all-start = ((bf16[8,8,1]{0,2,1:T(2,128)(2,1)}), bf16[8,8,1]{0,2,1:T(2,128)(2,1)S(1)}, u32[]{:S(2)}, u32[]{:S(2)}) async-start(bf16[8,8,1]{0,2,1:T(2,128)(2,1)} %copy.25), calls=%async_computation | async-start | bytes 8192 | tf_op jit(solution)/shard_map/all_to_all | solution.py:146
  44.4 0.0 collective-permute-done.2.refs_1_
  44.4 5.5 %collective-permute-start.3 = (bf16[512,512]{1,0:T(8,128)(2,1)S(1)}, bf16[512,512]{1,0:T(8,128)(2,1)S(1)}, u32[]{:S(2)}, u32[]{:S(2)}) collective-permute-start(bf16[512,512]{1,0:T(8,128)(2,1)S(1)} %collective-permute-done.2.refs_1_), channel_id=1, source_target_pairs={{0,8},{8,16},{16,24},{24,32},{32,40},{40,48},{48,56},{56,64},{64,7... | collective-permute-start | bytes 1572872 | tf_op jit(solution)/shard_map/ppermute | solution.py:20
  49.9 1.3 %collective-permute-done.6.refs_8_ = bf16[512,512]{1,0:T(8,128)(2,1)} collective-permute-done((bf16[512,512]{1,0:T(8,128)(2,1)}, bf16[512,512]{1,0:T(8,128)(2,1)}, u32[]{:S(2)}, u32[]{:S(2)}) %collective-permute-start.6) | collective-permute-done | bytes 524320 | tf_op jit(solution)/shard_map/ppermute | solution.py:20
  51.2 1.3 %collective-permute-start.7 = (bf16[512,512]{1,0:T(8,128)(2,1)}, bf16[512,512]{1,0:T(8,128)(2,1)}, u32[]{:S(2)}, u32[]{:S(2)}) collective-permute-start(bf16[512,512]{1,0:T(8,128)(2,1)} %collective-permute-done.6.refs_8_), channel_id=1, source_target_pairs={{8,0},{16,8},{24,16},{32,24},{40,32},{48,40},{56,48},{64,56},{72,6... | collective-permute-start | bytes 1572872 | tf_op jit(solution)/shard_map/ppermute | solution.py:20
  52.6 0.1 tile.8
  52.7 0.6 tile.9
  53.3 13.6 %all-to-all-start.1 = ((bf16[32,1,64]{2,1,0:T(2,128)(2,1)}), bf16[32,1,64]{2,1,0:T(2,128)(2,1)S(1)}, u32[]{:S(2)}, u32[]{:S(2)}) async-start(bf16[32,1,64]{2,1,0:T(2,128)(2,1)} %tile.9), calls=%async_computation.1 | async-start | bytes 32768 | tf_op jit(solution)/shard_map/all_to_all | solution.py:148
  66.9 0.1 fusion.6
  66.9 0.6 reshape.64.ids_src
  67.6 0.1 dynamic_slice.9
  67.6 0.6 reshape.65.ids_rdr
  68.2 0.1 rev.3
  68.4 0.1 copy.26.ids_own
  68.6 6.9 %all-to-all-done.1 = bf16[32,1,64]{2,1,0:T(2,128)(2,1)S(1)} async-done(((bf16[32,1,64]{2,1,0:T(2,128)(2,1)}), bf16[32,1,64]{2,1,0:T(2,128)(2,1)S(1)}, u32[]{:S(2)}, u32[]{:S(2)}) %all-to-all-start.1) | async-done | bytes 4128 | tf_op jit(solution)/shard_map/all_to_all | solution.py:148
  75.4 0.1 reduce.2
  75.5 0.1 convert_element_type.41
  75.6 2.6 %shard_map.111 = f32[1,2560]{1,0:T(1,128)S(1)} custom-call(s32[512,1]{1,0:T(8,128)S(1)} %copy.26.ids_own, s32[1,2560]{1,0:T(1,128)S(1)} %bitcast.16, bf16[512,512]{1,0:T(8,128)(2,1)S(1)} %collective-permute-done.3.refs_0_, bf16[512,512]{1,0:T(8,128)(2,1)S(1)} %collective-permute-done.2.refs_1_, bf16[512,512]{1,0:T(8,128)(2,1)S(1)} %collective-permute-done.1.refs_2_, ...), custom_call_target="tpu_custom_call" | custom-call | tf_op jit(solution)/shard_map/pallas_call | solution.py:110
  78.2 0.1 slice_reduce_fusion
  78.3 0.7 all_to_all.32
  79.0 3.9 %all-to-all-start.2 = ((f32[32,1,64]{2,1,0:T(1,128)}), f32[32,1,64]{2,1,0:T(1,128)S(1)}, u32[]{:S(2)}, u32[]{:S(2)}) async-start(f32[32,1,64]{2,1,0:T(1,128)} %bitcast.5), calls=%async_computation.2 | async-start | bytes 32768 | tf_op jit(solution)/shard_map/all_to_all | solution.py:167
  82.9 0.6 pad_convert_fusion
  83.5 0.0 copy-start.12
  83.5 7.0 %shard_map.110 = (f32[512,512]{1,0:T(8,128)}, f32[512,512]{1,0:T(8,128)}) custom-call(f32[1,3072]{1,0:T(1,128)} %bitcast.18, s32[512,1]{1,0:T(8,128)} %copy-done.2, s32[1,2560]{1,0:T(1,128)} %reshape.64.ids_src, s32[1,2560]{1,0:T(1,128)} %reshape.65.ids_rdr, f32[1,512]{1,0:T(1,128)} %bitcast.21, bf16[512,512]{1,0:T(8,128)(2,1)} %copy-done.6, ...), custom_call_target="tpu_custom_call" | custom-call | tf_op jit(solution)/shard_map/pallas_call | solution.py:123
  90.6 1.0 all-to-all-done.2
  91.6 0.1 reduce_sum.9
  91.6 0.7 all_to_all.34
  92.3 10.4 %all-to-all-start.3 = ((f32[8,1,8]{2,1,0:T(1,128)}), f32[8,1,8]{2,1,0:T(1,128)S(1)}, u32[]{:S(2)}, u32[]{:S(2)}) async-start(f32[8,1,8]{2,1,0:T(1,128)} %bitcast.6), calls=%async_computation.3 | async-start | bytes 8192 | tf_op jit(solution)/shard_map/all_to_all | solution.py:176
  102.8 3.3 %fusion.1 = (bf16[512,512]{1,0:T(8,128)(2,1)}, bf16[512,512]{1,0:T(8,128)(2,1)}, bf16[512,512]{1,0:T(8,128)(2,1)}, bf16[512,512]{1,0:T(8,128)(2,1)}) fusion(f32[512,512]{1,0:T(8,128)} %get-tuple-element.8, bf16[512,512]{1,0:T(8,128)(2,1)S(1)} %copy-done.8, bf16[512,512]{1,0:T(8,128)(2,1)S(1)} %copy-done.7, f32[512,512]{1,0:T(8,128)} %get-tuple-element.7, ...), kind=kLoop, calls=%fused_computation.7 | loop fusion | flops 3145728 | bytes 6291456 | tf_op jit(solution)/shard_map/convert_element_type | solution.py:174
  106.0 1.2 %all-to-all-done.3 = f32[8,1,8]{2,1,0:T(1,128)S(1)} async-done(((f32[8,1,8]{2,1,0:T(1,128)}), f32[8,1,8]{2,1,0:T(1,128)S(1)}, u32[]{:S(2)}, u32[]{:S(2)}) %all-to-all-start.3) | async-done | bytes 288 | tf_op jit(solution)/shard_map/all_to_all | solution.py:176
  107.3 0.7 copy.31
  (37 shorter events, 0.1 us)
Async XLA Ops:
  0.6 5.9 %copy-start.11 = (bf16[512,512]{1,0:T(8,128)(2,1)S(1)}, bf16[512,512]{1,0:T(8,128)(2,1)}, u32[]{:S(2)}) copy-start(bf16[512,512]{1,0:T(8,128)(2,1)} %param.10) | copy-start | bytes 1572868
  0.6 5.9 %copy-start.9 = (bf16[512,512]{1,0:T(8,128)(2,1)S(1)}, bf16[512,512]{1,0:T(8,128)(2,1)}, u32[]{:S(2)}) copy-start(bf16[512,512]{1,0:T(8,128)(2,1)} %param.7) | copy-start | bytes 1572868
  2.1 73.5 %copy-start = (bf16[512,512]{1,0:T(8,128)(2,1)}, bf16[512,512]{1,0:T(8,128)(2,1)S(1)}, u32[]{:S(2)}) copy-start(bf16[512,512]{1,0:T(8,128)(2,1)S(1)} %fusion.2.refs_4_) | copy-start | bytes 1572868
  2.1 15.0 %collective-permute-start = (bf16[512,512]{1,0:T(8,128)(2,1)S(1)}, bf16[512,512]{1,0:T(8,128)(2,1)S(1)}, u32[]{:S(2)}, u32[]{:S(2)}) collective-permute-start(bf16[512,512]{1,0:T(8,128)(2,1)S(1)} %fusion.2.refs_4_), channel_id=1, source_target_pairs={{0,8},{8,16},{16,24},{24,32},{32,40},{40,48},{48,56},{56,64},{64,7... | collective-permute-start | bytes 1572872 | tf_op jit(solution)/shard_map/ppermute | solution.py:20
  6.5 30.4 %copy-start.15 = (bf16[8,8]{1,0:T(8,128)(2,1)S(1)}, bf16[8,8]{1,0:T(8,128)(2,1)}, u32[]{:S(2)}) copy-start(bf16[8,8]{1,0:T(8,128)(2,1)} %param.13) | copy-start | bytes 388
  6.5 46.0 %copy-start.14 = (s32[16384]{0:T(1024)S(1)}, s32[16384]{0:T(1024)}, u32[]{:S(2)}) copy-start(s32[16384]{0:T(1024)} %param.11) | copy-start | bytes 196612
  6.7 71.5 %copy-start.1 = (bf16[512,512]{1,0:T(8,128)(2,1)}, bf16[512,512]{1,0:T(8,128)(2,1)S(1)}, u32[]{:S(2)}) copy-start(bf16[512,512]{1,0:T(8,128)(2,1)S(1)} %fusion.4.refs_5_) | copy-start | bytes 1572868
  6.7 14.7 %collective-permute-start.4 = (bf16[512,512]{1,0:T(8,128)(2,1)S(1)}, bf16[512,512]{1,0:T(8,128)(2,1)S(1)}, u32[]{:S(2)}, u32[]{:S(2)}) collective-permute-start(bf16[512,512]{1,0:T(8,128)(2,1)S(1)} %fusion.4.refs_5_), channel_id=1, source_target_pairs={{8,0},{16,8},{24,16},{32,24},{40,32},{48,40},{56,48},{64,56},{72,6... | collective-permute-start | bytes 1572872 | tf_op jit(solution)/shard_map/ppermute | solution.py:20
  17.0 61.1 %copy-start.3 = (bf16[512,512]{1,0:T(8,128)(2,1)}, bf16[512,512]{1,0:T(8,128)(2,1)S(1)}, u32[]{:S(2)}) copy-start(bf16[512,512]{1,0:T(8,128)(2,1)S(1)} %collective-permute-done.refs_3_) | copy-start | bytes 1572868
  17.0 13.8 %collective-permute-start.1 = (bf16[512,512]{1,0:T(8,128)(2,1)S(1)}, bf16[512,512]{1,0:T(8,128)(2,1)S(1)}, u32[]{:S(2)}, u32[]{:S(2)}) collective-permute-start(bf16[512,512]{1,0:T(8,128)(2,1)S(1)} %collective-permute-done.refs_3_), channel_id=1, source_target_pairs={{0,8},{8,16},{16,24},{24,32},{32,40},{40,48},{48,56},{56,64},{64,7... | collective-permute-start | bytes 1572872 | tf_op jit(solution)/shard_map/ppermute | solution.py:20
  21.4 9.5 %copy-start.13 = (bf16[512,512]{1,0:T(8,128)(2,1)}, bf16[512,512]{1,0:T(8,128)(2,1)S(1)}, u32[]{:S(2)}) copy-start(bf16[512,512]{1,0:T(8,128)(2,1)S(1)} %collective-permute-done.4.refs_6_) | copy-start | bytes 1572868
  21.4 14.2 %collective-permute-start.5 = (bf16[512,512]{1,0:T(8,128)(2,1)S(1)}, bf16[512,512]{1,0:T(8,128)(2,1)}, u32[]{:S(2)}, u32[]{:S(2)}) collective-permute-start(bf16[512,512]{1,0:T(8,128)(2,1)S(1)} %collective-permute-done.4.refs_6_), channel_id=1, source_target_pairs={{8,0},{16,8},{24,16},{32,24},{40,32},{48,40},{56,48},{64,56},{72,6... | collective-permute-start | bytes 1572872 | tf_op jit(solution)/shard_map/ppermute | solution.py:20
  30.9 47.3 %copy-start.4 = (bf16[512,512]{1,0:T(8,128)(2,1)}, bf16[512,512]{1,0:T(8,128)(2,1)S(1)}, u32[]{:S(2)}) copy-start(bf16[512,512]{1,0:T(8,128)(2,1)S(1)} %collective-permute-done.1.refs_2_) | copy-start | bytes 1572868
  30.9 13.5 %collective-permute-start.2 = (bf16[512,512]{1,0:T(8,128)(2,1)S(1)}, bf16[512,512]{1,0:T(8,128)(2,1)S(1)}, u32[]{:S(2)}, u32[]{:S(2)}) collective-permute-start(bf16[512,512]{1,0:T(8,128)(2,1)S(1)} %collective-permute-done.1.refs_2_), channel_id=1, source_target_pairs={{0,8},{8,16},{16,24},{24,32},{32,40},{40,48},{48,56},{56,64},{64,7... | collective-permute-start | bytes 1572872 | tf_op jit(solution)/shard_map/ppermute | solution.py:20
  35.7 15.5 %collective-permute-start.6 = (bf16[512,512]{1,0:T(8,128)(2,1)}, bf16[512,512]{1,0:T(8,128)(2,1)}, u32[]{:S(2)}, u32[]{:S(2)}) collective-permute-start(bf16[512,512]{1,0:T(8,128)(2,1)} %collective-permute-done.5.refs_7_), channel_id=1, source_target_pairs={{8,0},{16,8},{24,16},{32,24},{40,32},{48,40},{56,48},{64,56},{72,6... | collective-permute-start | bytes 1572872 | tf_op jit(solution)/shard_map/ppermute | solution.py:20
  37.6 14.9 %all-to-all-start = ((bf16[8,8,1]{0,2,1:T(2,128)(2,1)}), bf16[8,8,1]{0,2,1:T(2,128)(2,1)S(1)}, u32[]{:S(2)}, u32[]{:S(2)}) async-start(bf16[8,8,1]{0,2,1:T(2,128)(2,1)} %copy.25), calls=%async_computation | async-start | bytes 8192 | tf_op jit(solution)/shard_map/all_to_all | solution.py:146
  44.4 33.8 %copy-start.5 = (bf16[512,512]{1,0:T(8,128)(2,1)}, bf16[512,512]{1,0:T(8,128)(2,1)S(1)}, u32[]{:S(2)}) copy-start(bf16[512,512]{1,0:T(8,128)(2,1)S(1)} %collective-permute-done.2.refs_1_) | copy-start | bytes 1572868
  44.4 31.2 %collective-permute-start.3 = (bf16[512,512]{1,0:T(8,128)(2,1)S(1)}, bf16[512,512]{1,0:T(8,128)(2,1)S(1)}, u32[]{:S(2)}, u32[]{:S(2)}) collective-permute-start(bf16[512,512]{1,0:T(8,128)(2,1)S(1)} %collective-permute-done.2.refs_1_), channel_id=1, source_target_pairs={{0,8},{8,16},{16,24},{24,32},{32,40},{40,48},{48,56},{56,64},{64,7... | collective-permute-start | bytes 1572872 | tf_op jit(solution)/shard_map/ppermute | solution.py:20
  51.2 32.3 %collective-permute-start.7 = (bf16[512,512]{1,0:T(8,128)(2,1)}, bf16[512,512]{1,0:T(8,128)(2,1)}, u32[]{:S(2)}, u32[]{:S(2)}) collective-permute-start(bf16[512,512]{1,0:T(8,128)(2,1)} %collective-permute-done.6.refs_8_), channel_id=1, source_target_pairs={{8,0},{16,8},{24,16},{32,24},{40,32},{48,40},{56,48},{64,56},{72,6... | collective-permute-start | bytes 1572872 | tf_op jit(solution)/shard_map/ppermute | solution.py:20
  53.3 22.2 %all-to-all-start.1 = ((bf16[32,1,64]{2,1,0:T(2,128)(2,1)}), bf16[32,1,64]{2,1,0:T(2,128)(2,1)S(1)}, u32[]{:S(2)}, u32[]{:S(2)}) async-start(bf16[32,1,64]{2,1,0:T(2,128)(2,1)} %tile.9), calls=%async_computation.1 | async-start | bytes 32768 | tf_op jit(solution)/shard_map/all_to_all | solution.py:148
  68.6 9.7 %copy-start.2 = (s32[512,1]{1,0:T(8,128)}, s32[512,1]{1,0:T(8,128)S(1)}, u32[]{:S(2)}) copy-start(s32[512,1]{1,0:T(8,128)S(1)} %copy.26.ids_own) | copy-start | bytes 6148
  75.6 2.6 %copy-start.6 = (bf16[512,512]{1,0:T(8,128)(2,1)}, bf16[512,512]{1,0:T(8,128)(2,1)S(1)}, u32[]{:S(2)}) copy-start(bf16[512,512]{1,0:T(8,128)(2,1)S(1)} %collective-permute-done.3.refs_0_) | copy-start | bytes 1572868
  79.0 12.6 %all-to-all-start.2 = ((f32[32,1,64]{2,1,0:T(1,128)}), f32[32,1,64]{2,1,0:T(1,128)S(1)}, u32[]{:S(2)}, u32[]{:S(2)}) async-start(f32[32,1,64]{2,1,0:T(1,128)} %bitcast.5), calls=%async_computation.2 | async-start | bytes 32768 | tf_op jit(solution)/shard_map/all_to_all | solution.py:167
  83.5 19.2 %copy-start.7 = (bf16[512,512]{1,0:T(8,128)(2,1)S(1)}, bf16[512,512]{1,0:T(8,128)(2,1)}, u32[]{:S(2)}) copy-start(bf16[512,512]{1,0:T(8,128)(2,1)} %param.9) | copy-start | bytes 1572868
  83.5 19.2 %copy-start.8 = (bf16[512,512]{1,0:T(8,128)(2,1)S(1)}, bf16[512,512]{1,0:T(8,128)(2,1)}, u32[]{:S(2)}) copy-start(bf16[512,512]{1,0:T(8,128)(2,1)} %param.8) | copy-start | bytes 1572868
  83.5 19.2 %copy-start.10 = (bf16[512,512]{1,0:T(8,128)(2,1)S(1)}, bf16[512,512]{1,0:T(8,128)(2,1)}, u32[]{:S(2)}) copy-start(bf16[512,512]{1,0:T(8,128)(2,1)} %param.7) | copy-start | bytes 1572868
  83.5 19.2 %copy-start.12 = (bf16[512,512]{1,0:T(8,128)(2,1)S(1)}, bf16[512,512]{1,0:T(8,128)(2,1)}, u32[]{:S(2)}) copy-start(bf16[512,512]{1,0:T(8,128)(2,1)} %param.10) | copy-start | bytes 1572868
  92.3 15.0 %all-to-all-start.3 = ((f32[8,1,8]{2,1,0:T(1,128)}), f32[8,1,8]{2,1,0:T(1,128)S(1)}, u32[]{:S(2)}, u32[]{:S(2)}) async-start(f32[8,1,8]{2,1,0:T(1,128)} %bitcast.6), calls=%async_computation.3 | async-start | bytes 8192 | tf_op jit(solution)/shard_map/all_to_all | solution.py:176

commit v9 on v8

--- a/solution.py
+++ b/solution.py
@@ -152,9 +152,11 @@
 
     ahead = [mixed_in]
     behind = [conv_grad]
-    for _ in range(span):
+    for step in range(span):
         ahead.append(shifted(ahead[-1], "ctx", 1))
         behind.append(shifted(behind[-1], "ctx", -1))
+        if step == 0:
+            ahead[-1], behind[-1], taps = lax.optimization_barrier((ahead[-1], behind[-1], taps))
 
     ids_pad = jnp.concatenate(
         [jnp.full((hist,), -1, jnp.int32), doc_ids, jnp.full((hist,), -2, jnp.int32)]

time: 109 us -> 114 us (1.046)
  blocking collectives: 0 us -> 31.2 us
  starting transfers between devices: 58.1 us -> 40 us
  waiting for transfers between devices: 28.4 us -> 21.6 us
  local copies, waits for them, and re-layouts: 5.37 us -> 4.15 us
    all_to_all x0 -> x2, blocking collectives: none -> 31.2 us  [the longest x1 21.4 us: shards(): lax.all_to_all(jnp.tile(row, (count, 1)), 'ctx', 0, 0, tiled=True)]
    all_to_all x2 -> x0, starting transfers between devices: 20.3 us -> none  [the longest x1 13.6 us: shards(): lax.all_to_all(jnp.tile(row, (count, 1)), 'ctx', 0, 0, tiled=True)]
    all_to_all x2 -> x0, waiting for transfers between devices: 6.88 us -> none  [the longest x1 6.88 us: shards(): lax.all_to_all(jnp.tile(row, (count, 1)), 'ctx', 0, 0, tiled=True)]
    all_to_all x1, starting transfers between devices: 3.89 us -> 10.3 us  [shards(): lax.all_to_all(filter_part.reshape(count, FLEN // count), 'ctx', 0, 0, ti...]
    ppermute x8, starting transfers between devices: 23.4 us -> 20.3 us  [shifted(): lax.ppermute(value, axis, [(source, source + steps) for source in range(l...]
  transfers between devices with their start and end apart: 12 -> 10, of which waited for: 8 -> 5; matrix products, arithmetic and copies ran while one was open for 7% -> 5% of each run, Pallas kernels for 9% -> 8%
where the time goes in v9:
time: 114 us; the launch traced here: 113 us
  starting transfers between devices  40 us (35%)
  blocking collectives  31.2 us (27%)
  waiting for transfers between devices  21.6 us (19%)
  Pallas kernels  9.62 us (8%)
  other arithmetic  5.54 us (5%)
  local copies, waits for them, and re-layouts  4.15 us (4%)
    all_to_all x1, blocking collectives, shards(): lax.all_to_all(jnp.tile(row, (count, 1)), 'ctx', 0, 0, tiled=True)  21.4 us
    ppermute x8, starting transfers between devices, shifted(): lax.ppermute(value, axis, [(source, source + steps) for source in range(l...  20.3 us
    ppermute x8, waiting for transfers between devices, shifted(): lax.ppermute(value, axis, [(source, source + steps) for source in range(l...  19.4 us
    all_to_all x1, starting transfers between devices, shards(): lax.all_to_all(filter_part.reshape(count, FLEN // count), 'ctx', 0, 0, ti...  10.3 us
    all_to_all x1, blocking collectives, shards(): lax.all_to_all(filter_taps, 'tp', split_axis=1, concat_axis=0, tiled=True)  9.81 us
    all_to_all x1, starting transfers between devices, shards(): summed = lax.all_to_all(block_sum, 'tp', 0, 0, tiled=True).T  9.45 us
    pallas_call x1, Pallas kernels, local_conv(): pl.pallas_call(conv_kernel, out_shape=(jax.ShapeDtypeStruct((own, width),...  7.03 us
    convert_element_type x1, other arithmetic, shards(): value_grad = (mixed_grad * key_in.astype(jnp.float32)).astype(jnp.bfloat16)  3.26 us
  transfers between devices with their start and end apart: 10, of which 5 were waited for; matrix products, arithmetic and copies ran while one was open for 5% of the time, Pallas kernels for 8%

profile of v9, /device:TPU:1, one launch (start us, length us, event | category | flops | bytes accessed | tf_op | source)
XLA Modules:
  0.0 113.2 jit_solution(2435389944501162327)
XLA Ops:
  0.6 0.0 copy-start.11
  0.6 0.0 copy-start.9
  0.7 1.4 %fusion.2.refs_4_ = bf16[512,512]{1,0:T(8,128)(2,1)S(1)} fusion(bf16[512,512]{1,0:T(8,128)(2,1)} %param.9, bf16[512,512]{1,0:T(8,128)(2,1)} %param.8), kind=kLoop, calls=%fused_computation.8 | loop fusion | flops 1048576 | bytes 1572864 | tf_op jit(solution)/shard_map/convert_element_type | solution.py:150
  2.1 4.4 %collective-permute-start = (bf16[512,512]{1,0:T(8,128)(2,1)S(1)}, bf16[512,512]{1,0:T(8,128)(2,1)S(1)}, u32[]{:S(2)}, u32[]{:S(2)}) collective-permute-start(bf16[512,512]{1,0:T(8,128)(2,1)S(1)} %fusion.2.refs_4_), channel_id=1, source_target_pairs={{0,8},{8,16},{16,24},{24,32},{32,40},{40,48},{48,56},{56,64},{64,7... | collective-permute-start | bytes 1572872 | tf_op jit(solution)/shard_map/ppermute | solution.py:20
  6.5 0.0 copy-start.15
  6.5 0.1 fusion.4.refs_5_
  6.7 1.3 %collective-permute-start.1 = (bf16[512,512]{1,0:T(8,128)(2,1)S(1)}, bf16[512,512]{1,0:T(8,128)(2,1)S(1)}, u32[]{:S(2)}, u32[]{:S(2)}) collective-permute-start(bf16[512,512]{1,0:T(8,128)(2,1)S(1)} %fusion.4.refs_5_), channel_id=1, source_target_pairs={{8,0},{16,8},{24,16},{32,24},{40,32},{48,40},{56,48},{64,56},{72,6... | collective-permute-start | bytes 1572872 | tf_op jit(solution)/shard_map/ppermute | solution.py:20
  8.0 0.1 copy.25
  8.1 9.8 %all_to_all.40 = bf16[8,8,1]{0,2,1:T(2,128)(2,1)S(1)} all-to-all(bf16[8,8,1]{0,2,1:T(2,128)(2,1)S(1)} %copy.25), channel_id=1, replica_groups=mesh['ctx'=32,'tp'=8] {'tp'}, dimensions={1} | all-to-all | bytes 256 | tf_op jit(solution)/shard_map/all_to_all | solution.py:146
  17.9 0.0 copy-start.14
  17.9 0.1 tile.8
  18.0 21.4 %all_to_all.41 = bf16[32,1,64]{2,1,0:T(2,128)(2,1)S(1)} all-to-all(bf16[32,1,64]{2,1,0:T(2,128)(2,1)S(1)} %tile.9), channel_id=1, replica_groups=mesh['ctx'=32,'tp'=8] {'ctx'}, dimensions={0} | all-to-all | bytes 8192 | tf_op jit(solution)/shard_map/all_to_all | solution.py:148
  39.4 0.1 reduce.2
  39.5 0.1 reshape.61
  39.6 0.0 collective-permute-done.refs_3_
  39.6 0.0 collective-permute-done.1.refs_6_
  39.6 2.3 %collective-permute-start.2 = (bf16[512,512]{1,0:T(8,128)(2,1)S(1)}, bf16[512,512]{1,0:T(8,128)(2,1)S(1)}, u32[]{:S(2)}, u32[]{:S(2)}) collective-permute-start(bf16[512,512]{1,0:T(8,128)(2,1)S(1)} %collective-permute-done.refs_3_), channel_id=1, source_target_pairs={{0,8},{8,16},{16,24},{24,32},{32,40},{40,48},{48,56},{56,64},{64,7... | collective-permute-start | bytes 1572872 | tf_op jit(solution)/shard_map/ppermute | solution.py:20
  41.9 1.3 %collective-permute-start.5 = (bf16[512,512]{1,0:T(8,128)(2,1)S(1)}, bf16[512,512]{1,0:T(8,128)(2,1)}, u32[]{:S(2)}, u32[]{:S(2)}) collective-permute-start(bf16[512,512]{1,0:T(8,128)(2,1)S(1)} %collective-permute-done.1.refs_6_), channel_id=1, source_target_pairs={{8,0},{16,8},{24,16},{32,24},{40,32},{48,40},{56,48},{64,56},{72,6... | collective-permute-start | bytes 1572872 | tf_op jit(solution)/shard_map/ppermute | solution.py:20
  43.2 7.8 %collective-permute-done.2.refs_2_ = bf16[512,512]{1,0:T(8,128)(2,1)S(1)} collective-permute-done((bf16[512,512]{1,0:T(8,128)(2,1)S(1)}, bf16[512,512]{1,0:T(8,128)(2,1)S(1)}, u32[]{:S(2)}, u32[]{:S(2)}) %collective-permute-start.2) | collective-permute-done | bytes 524320 | tf_op jit(solution)/shard_map/ppermute | solution.py:20
  51.0 4.2 %collective-permute-start.3 = (bf16[512,512]{1,0:T(8,128)(2,1)S(1)}, bf16[512,512]{1,0:T(8,128)(2,1)S(1)}, u32[]{:S(2)}, u32[]{:S(2)}) collective-permute-start(bf16[512,512]{1,0:T(8,128)(2,1)S(1)} %collective-permute-done.2.refs_2_), channel_id=1, source_target_pairs={{0,8},{8,16},{16,24},{24,32},{32,40},{40,48},{48,56},{56,64},{64,7... | collective-permute-start | bytes 1572872 | tf_op jit(solution)/shard_map/ppermute | solution.py:20
  55.2 0.0 collective-permute-done.5.refs_7_
  55.2 1.3 %collective-permute-start.6 = (bf16[512,512]{1,0:T(8,128)(2,1)}, bf16[512,512]{1,0:T(8,128)(2,1)}, u32[]{:S(2)}, u32[]{:S(2)}) collective-permute-start(bf16[512,512]{1,0:T(8,128)(2,1)} %collective-permute-done.5.refs_7_), channel_id=1, source_target_pairs={{8,0},{16,8},{24,16},{32,24},{40,32},{48,40},{56,48},{64,56},{72,6... | collective-permute-start | bytes 1572872 | tf_op jit(solution)/shard_map/ppermute | solution.py:20
  56.5 7.0 %collective-permute-done.3.refs_1_ = bf16[512,512]{1,0:T(8,128)(2,1)S(1)} collective-permute-done((bf16[512,512]{1,0:T(8,128)(2,1)S(1)}, bf16[512,512]{1,0:T(8,128)(2,1)S(1)}, u32[]{:S(2)}, u32[]{:S(2)}) %collective-permute-start.3) | collective-permute-done | bytes 524320 | tf_op jit(solution)/shard_map/ppermute | solution.py:20
  63.6 4.2 %collective-permute-start.4 = (bf16[512,512]{1,0:T(8,128)(2,1)S(1)}, bf16[512,512]{1,0:T(8,128)(2,1)S(1)}, u32[]{:S(2)}, u32[]{:S(2)}) collective-permute-start(bf16[512,512]{1,0:T(8,128)(2,1)S(1)} %collective-permute-done.3.refs_1_), channel_id=1, source_target_pairs={{0,8},{8,16},{16,24},{24,32},{32,40},{40,48},{48,56},{56,64},{64,7... | collective-permute-start | bytes 1572872 | tf_op jit(solution)/shard_map/ppermute | solution.py:20
  67.8 0.0 collective-permute-done.6.refs_8_
  67.8 1.3 %collective-permute-start.7 = (bf16[512,512]{1,0:T(8,128)(2,1)}, bf16[512,512]{1,0:T(8,128)(2,1)}, u32[]{:S(2)}, u32[]{:S(2)}) collective-permute-start(bf16[512,512]{1,0:T(8,128)(2,1)} %collective-permute-done.6.refs_8_), channel_id=1, source_target_pairs={{8,0},{16,8},{24,16},{32,24},{40,32},{48,40},{56,48},{64,56},{72,6... | collective-permute-start | bytes 1572872 | tf_op jit(solution)/shard_map/ppermute | solution.py:20
  69.2 0.1 fusion.6
  69.3 0.6 reshape.65.ids_src
  69.9 0.1 dynamic_slice.9
  69.9 0.6 reshape.66.ids_rdr
  70.6 0.1 rev.3
  70.7 0.1 copy.26.ids_own
  70.9 4.5 %collective-permute-done.4.refs_0_ = bf16[512,512]{1,0:T(8,128)(2,1)S(1)} collective-permute-done((bf16[512,512]{1,0:T(8,128)(2,1)S(1)}, bf16[512,512]{1,0:T(8,128)(2,1)S(1)}, u32[]{:S(2)}, u32[]{:S(2)}) %collective-permute-start.4) | collective-permute-done | bytes 524320 | tf_op jit(solution)/shard_map/ppermute | solution.py:20
  75.4 2.6 %shard_map.111 = f32[1,2560]{1,0:T(1,128)S(1)} custom-call(s32[512,1]{1,0:T(8,128)S(1)} %copy.26.ids_own, s32[1,2560]{1,0:T(1,128)S(1)} %bitcast.16, bf16[512,512]{1,0:T(8,128)(2,1)S(1)} %collective-permute-done.4.refs_0_, bf16[512,512]{1,0:T(8,128)(2,1)S(1)} %collective-permute-done.3.refs_1_, bf16[512,512]{1,0:T(8,128)(2,1)S(1)} %collective-permute-done.2.refs_2_, ...), custom_call_target="tpu_custom_call" | custom-call | tf_op jit(solution)/shard_map/pallas_call | solution.py:110
  78.1 0.1 slice_reduce_fusion
  78.2 0.7 all_to_all.32
  78.8 10.3 %all-to-all-start.2 = ((f32[32,1,64]{2,1,0:T(1,128)}), f32[32,1,64]{2,1,0:T(1,128)S(1)}, u32[]{:S(2)}, u32[]{:S(2)}) async-start(f32[32,1,64]{2,1,0:T(1,128)} %bitcast.5), calls=%async_computation.2 | async-start | bytes 32768 | tf_op jit(solution)/shard_map/all_to_all | solution.py:169
  89.1 0.6 pad_convert_fusion
  89.7 0.0 collective-permute-done.7.refs_9_
  89.8 0.0 copy-start.12
  89.8 7.0 %shard_map.110 = (f32[512,512]{1,0:T(8,128)}, f32[512,512]{1,0:T(8,128)}) custom-call(f32[1,3072]{1,0:T(1,128)} %bitcast.18, s32[512,1]{1,0:T(8,128)} %copy-done.2, s32[1,2560]{1,0:T(1,128)} %reshape.65.ids_src, s32[1,2560]{1,0:T(1,128)} %reshape.66.ids_rdr, f32[1,512]{1,0:T(1,128)} %bitcast.21, bf16[512,512]{1,0:T(8,128)(2,1)} %copy-done.6, ...), custom_call_target="tpu_custom_call" | custom-call | tf_op jit(solution)/shard_map/pallas_call | solution.py:123
  96.8 1.0 all-to-all-done.2
  97.8 0.1 reduce_sum.9
  97.8 0.7 all_to_all.34
  98.5 9.4 %all-to-all-start.3 = ((f32[8,1,8]{2,1,0:T(1,128)}), f32[8,1,8]{2,1,0:T(1,128)S(1)}, u32[]{:S(2)}, u32[]{:S(2)}) async-start(f32[8,1,8]{2,1,0:T(1,128)} %bitcast.6), calls=%async_computation.3 | async-start | bytes 8192 | tf_op jit(solution)/shard_map/all_to_all | solution.py:178
  108.0 3.3 %fusion.1 = (bf16[512,512]{1,0:T(8,128)(2,1)}, bf16[512,512]{1,0:T(8,128)(2,1)}, bf16[512,512]{1,0:T(8,128)(2,1)}, bf16[512,512]{1,0:T(8,128)(2,1)}) fusion(f32[512,512]{1,0:T(8,128)} %get-tuple-element.14, bf16[512,512]{1,0:T(8,128)(2,1)S(1)} %copy-done.8, bf16[512,512]{1,0:T(8,128)(2,1)S(1)} %copy-done.7, f32[512,512]{1,0:T(8,128)} %get-tuple-element.13, ...), kind=kLoop, calls=%fused_computation.7 | loop fusion | flops 3145728 | bytes 6291456 | tf_op jit(solution)/shard_map/convert_element_type | solution.py:176
  111.3 1.2 %all-to-all-done.3 = f32[8,1,8]{2,1,0:T(1,128)S(1)} async-done(((f32[8,1,8]{2,1,0:T(1,128)}), f32[8,1,8]{2,1,0:T(1,128)S(1)}, u32[]{:S(2)}, u32[]{:S(2)}) %all-to-all-start.3) | async-done | bytes 288 | tf_op jit(solution)/shard_map/all_to_all | solution.py:178
  112.5 0.7 copy.31
  (35 shorter events, 0.1 us)
Async XLA Ops:
  0.6 5.9 %copy-start.11 = (bf16[512,512]{1,0:T(8,128)(2,1)S(1)}, bf16[512,512]{1,0:T(8,128)(2,1)}, u32[]{:S(2)}) copy-start(bf16[512,512]{1,0:T(8,128)(2,1)} %param.10) | copy-start | bytes 1572868
  0.6 5.9 %copy-start.9 = (bf16[512,512]{1,0:T(8,128)(2,1)S(1)}, bf16[512,512]{1,0:T(8,128)(2,1)}, u32[]{:S(2)}) copy-start(bf16[512,512]{1,0:T(8,128)(2,1)} %param.7) | copy-start | bytes 1572868
  2.1 73.3 %copy-start = (bf16[512,512]{1,0:T(8,128)(2,1)}, bf16[512,512]{1,0:T(8,128)(2,1)S(1)}, u32[]{:S(2)}) copy-start(bf16[512,512]{1,0:T(8,128)(2,1)S(1)} %fusion.2.refs_4_) | copy-start | bytes 1572868
  2.1 37.5 %collective-permute-start = (bf16[512,512]{1,0:T(8,128)(2,1)S(1)}, bf16[512,512]{1,0:T(8,128)(2,1)S(1)}, u32[]{:S(2)}, u32[]{:S(2)}) collective-permute-start(bf16[512,512]{1,0:T(8,128)(2,1)S(1)} %fusion.2.refs_4_), channel_id=1, source_target_pairs={{0,8},{8,16},{16,24},{24,32},{32,40},{40,48},{48,56},{56,64},{64,7... | collective-permute-start | bytes 1572872 | tf_op jit(solution)/shard_map/ppermute | solution.py:20
  6.5 1.5 %copy-start.15 = (bf16[8,8]{1,0:T(8,128)(2,1)S(1)}, bf16[8,8]{1,0:T(8,128)(2,1)}, u32[]{:S(2)}) copy-start(bf16[8,8]{1,0:T(8,128)(2,1)} %param.13) | copy-start | bytes 388
  6.7 71.3 %copy-start.1 = (bf16[512,512]{1,0:T(8,128)(2,1)}, bf16[512,512]{1,0:T(8,128)(2,1)S(1)}, u32[]{:S(2)}) copy-start(bf16[512,512]{1,0:T(8,128)(2,1)S(1)} %fusion.4.refs_5_) | copy-start | bytes 1572868
  6.7 32.9 %collective-permute-start.1 = (bf16[512,512]{1,0:T(8,128)(2,1)S(1)}, bf16[512,512]{1,0:T(8,128)(2,1)S(1)}, u32[]{:S(2)}, u32[]{:S(2)}) collective-permute-start(bf16[512,512]{1,0:T(8,128)(2,1)S(1)} %fusion.4.refs_5_), channel_id=1, source_target_pairs={{8,0},{16,8},{24,16},{32,24},{40,32},{48,40},{56,48},{64,56},{72,6... | collective-permute-start | bytes 1572872 | tf_op jit(solution)/shard_map/ppermute | solution.py:20
  17.9 51.3 %copy-start.14 = (s32[16384]{0:T(1024)S(1)}, s32[16384]{0:T(1024)}, u32[]{:S(2)}) copy-start(s32[16384]{0:T(1024)} %param.11) | copy-start | bytes 196612
  39.6 38.4 %copy-start.3 = (bf16[512,512]{1,0:T(8,128)(2,1)}, bf16[512,512]{1,0:T(8,128)(2,1)S(1)}, u32[]{:S(2)}) copy-start(bf16[512,512]{1,0:T(8,128)(2,1)S(1)} %collective-permute-done.refs_3_) | copy-start | bytes 1572868
  39.6 17.0 %copy-start.13 = (bf16[512,512]{1,0:T(8,128)(2,1)}, bf16[512,512]{1,0:T(8,128)(2,1)S(1)}, u32[]{:S(2)}) copy-start(bf16[512,512]{1,0:T(8,128)(2,1)S(1)} %collective-permute-done.1.refs_6_) | copy-start | bytes 1572868
  39.6 11.4 %collective-permute-start.2 = (bf16[512,512]{1,0:T(8,128)(2,1)S(1)}, bf16[512,512]{1,0:T(8,128)(2,1)S(1)}, u32[]{:S(2)}, u32[]{:S(2)}) collective-permute-start(bf16[512,512]{1,0:T(8,128)(2,1)S(1)} %collective-permute-done.refs_3_), channel_id=1, source_target_pairs={{0,8},{8,16},{16,24},{24,32},{32,40},{40,48},{48,56},{56,64},{64,7... | collective-permute-start | bytes 1572872 | tf_op jit(solution)/shard_map/ppermute | solution.py:20
  41.9 13.3 %collective-permute-start.5 = (bf16[512,512]{1,0:T(8,128)(2,1)S(1)}, bf16[512,512]{1,0:T(8,128)(2,1)}, u32[]{:S(2)}, u32[]{:S(2)}) collective-permute-start(bf16[512,512]{1,0:T(8,128)(2,1)S(1)} %collective-permute-done.1.refs_6_), channel_id=1, source_target_pairs={{8,0},{16,8},{24,16},{32,24},{40,32},{48,40},{56,48},{64,56},{72,6... | collective-permute-start | bytes 1572872 | tf_op jit(solution)/shard_map/ppermute | solution.py:20
  51.0 27.0 %copy-start.4 = (bf16[512,512]{1,0:T(8,128)(2,1)}, bf16[512,512]{1,0:T(8,128)(2,1)S(1)}, u32[]{:S(2)}) copy-start(bf16[512,512]{1,0:T(8,128)(2,1)S(1)} %collective-permute-done.2.refs_2_) | copy-start | bytes 1572868
  51.0 12.6 %collective-permute-start.3 = (bf16[512,512]{1,0:T(8,128)(2,1)S(1)}, bf16[512,512]{1,0:T(8,128)(2,1)S(1)}, u32[]{:S(2)}, u32[]{:S(2)}) collective-permute-start(bf16[512,512]{1,0:T(8,128)(2,1)S(1)} %collective-permute-done.2.refs_2_), channel_id=1, source_target_pairs={{0,8},{8,16},{16,24},{24,32},{32,40},{40,48},{48,56},{56,64},{64,7... | collective-permute-start | bytes 1572872 | tf_op jit(solution)/shard_map/ppermute | solution.py:20
  55.2 12.6 %collective-permute-start.6 = (bf16[512,512]{1,0:T(8,128)(2,1)}, bf16[512,512]{1,0:T(8,128)(2,1)}, u32[]{:S(2)}, u32[]{:S(2)}) collective-permute-start(bf16[512,512]{1,0:T(8,128)(2,1)} %collective-permute-done.5.refs_7_), channel_id=1, source_target_pairs={{8,0},{16,8},{24,16},{32,24},{40,32},{48,40},{56,48},{64,56},{72,6... | collective-permute-start | bytes 1572872 | tf_op jit(solution)/shard_map/ppermute | solution.py:20
  63.6 14.5 %copy-start.5 = (bf16[512,512]{1,0:T(8,128)(2,1)}, bf16[512,512]{1,0:T(8,128)(2,1)S(1)}, u32[]{:S(2)}) copy-start(bf16[512,512]{1,0:T(8,128)(2,1)S(1)} %collective-permute-done.3.refs_1_) | copy-start | bytes 1572868
  63.6 11.8 %collective-permute-start.4 = (bf16[512,512]{1,0:T(8,128)(2,1)S(1)}, bf16[512,512]{1,0:T(8,128)(2,1)S(1)}, u32[]{:S(2)}, u32[]{:S(2)}) collective-permute-start(bf16[512,512]{1,0:T(8,128)(2,1)S(1)} %collective-permute-done.3.refs_1_), channel_id=1, source_target_pairs={{0,8},{8,16},{16,24},{24,32},{32,40},{40,48},{48,56},{56,64},{64,7... | collective-permute-start | bytes 1572872 | tf_op jit(solution)/shard_map/ppermute | solution.py:20
  67.8 21.9 %collective-permute-start.7 = (bf16[512,512]{1,0:T(8,128)(2,1)}, bf16[512,512]{1,0:T(8,128)(2,1)}, u32[]{:S(2)}, u32[]{:S(2)}) collective-permute-start(bf16[512,512]{1,0:T(8,128)(2,1)} %collective-permute-done.6.refs_8_), channel_id=1, source_target_pairs={{8,0},{16,8},{24,16},{32,24},{40,32},{48,40},{56,48},{64,56},{72,6... | collective-permute-start | bytes 1572872 | tf_op jit(solution)/shard_map/ppermute | solution.py:20
  70.9 7.2 %copy-start.2 = (s32[512,1]{1,0:T(8,128)}, s32[512,1]{1,0:T(8,128)S(1)}, u32[]{:S(2)}) copy-start(s32[512,1]{1,0:T(8,128)S(1)} %copy.26.ids_own) | copy-start | bytes 6148
  75.4 2.6 %copy-start.6 = (bf16[512,512]{1,0:T(8,128)(2,1)}, bf16[512,512]{1,0:T(8,128)(2,1)S(1)}, u32[]{:S(2)}) copy-start(bf16[512,512]{1,0:T(8,128)(2,1)S(1)} %collective-permute-done.4.refs_0_) | copy-start | bytes 1572868
  78.8 19.0 %all-to-all-start.2 = ((f32[32,1,64]{2,1,0:T(1,128)}), f32[32,1,64]{2,1,0:T(1,128)S(1)}, u32[]{:S(2)}, u32[]{:S(2)}) async-start(f32[32,1,64]{2,1,0:T(1,128)} %bitcast.5), calls=%async_computation.2 | async-start | bytes 32768 | tf_op jit(solution)/shard_map/all_to_all | solution.py:169
  89.7 18.2 %copy-start.7 = (bf16[512,512]{1,0:T(8,128)(2,1)S(1)}, bf16[512,512]{1,0:T(8,128)(2,1)}, u32[]{:S(2)}) copy-start(bf16[512,512]{1,0:T(8,128)(2,1)} %param.9) | copy-start | bytes 1572868
  89.7 18.2 %copy-start.8 = (bf16[512,512]{1,0:T(8,128)(2,1)S(1)}, bf16[512,512]{1,0:T(8,128)(2,1)}, u32[]{:S(2)}) copy-start(bf16[512,512]{1,0:T(8,128)(2,1)} %param.8) | copy-start | bytes 1572868
  89.8 18.2 %copy-start.10 = (bf16[512,512]{1,0:T(8,128)(2,1)S(1)}, bf16[512,512]{1,0:T(8,128)(2,1)}, u32[]{:S(2)}) copy-start(bf16[512,512]{1,0:T(8,128)(2,1)} %param.7) | copy-start | bytes 1572868
  89.8 18.2 %copy-start.12 = (bf16[512,512]{1,0:T(8,128)(2,1)S(1)}, bf16[512,512]{1,0:T(8,128)(2,1)}, u32[]{:S(2)}) copy-start(bf16[512,512]{1,0:T(8,128)(2,1)} %param.10) | copy-start | bytes 1572868
  98.5 14.0 %all-to-all-start.3 = ((f32[8,1,8]{2,1,0:T(1,128)}), f32[8,1,8]{2,1,0:T(1,128)S(1)}, u32[]{:S(2)}, u32[]{:S(2)}) async-start(f32[8,1,8]{2,1,0:T(1,128)} %bitcast.6), calls=%async_computation.3 | async-start | bytes 8192 | tf_op jit(solution)/shard_map/all_to_all | solution.py:178

commit v10 on v7

--- a/solution.py
+++ b/solution.py
@@ -18,6 +18,24 @@
     count = lax.axis_size(axis)
     leading, last = (max(0, -steps), min(count, count - steps))
     return lax.ppermute(value, axis, [(source, source + steps) for source in range(leading, last)])
+
+
+def swapped(value, axis, bit):
+    count = lax.axis_size(axis)
+    return lax.ppermute(value, axis, [(source, source ^ bit) for source in range(count)])
+
+
+def gather_chunks(chunk, axis):
+    here = lax.axis_index(axis)
+    count = lax.axis_size(axis)
+    held = chunk
+    bit = 1
+    while bit < count:
+        other = swapped(held, axis, bit)
+        upper = (here & bit) != 0
+        held = jnp.concatenate([jnp.where(upper, other, held), jnp.where(upper, held, other)])
+        bit *= 2
+    return held
 
 
 def band_tiles(taps_row, fwd_tiles, bwd_tiles):
@@ -143,8 +161,9 @@
 
     count = lax.axis_size("ctx")
     groups = lax.axis_size("tp")
-    pieces = lax.all_to_all(filter_taps, "tp", split_axis=1, concat_axis=0, tiled=True)
-    taps = lax.all_to_all(jnp.tile(pieces, (count, 1)), "ctx", 0, 0, tiled=True).reshape(FLEN)
+    block = gather_chunks(filter_taps, "tp")
+    own_filter = lax.dynamic_slice_in_dim(block, lax.axis_index("tp"), 1, axis=1)[:, 0]
+    taps = gather_chunks(own_filter, "ctx")
 
     mixed_in = (key_in.astype(jnp.float32) * value_in.astype(jnp.float32)).astype(jnp.bfloat16)
     conv_grad = (out_grad.astype(jnp.float32) * query_in.astype(jnp.float32)).astype(jnp.bfloat16)

time: 109 us -> 104 us (0.954)
  waiting for transfers between devices: 28.4 us -> 14.7 us
  starting transfers between devices: 58.1 us -> 67.5 us
    ppermute x0 -> x8, starting transfers between devices: none -> 28.6 us  [swapped(): lax.ppermute(value, axis, [(source, source ^ bit) for source in range(cou...]
    all_to_all x2 -> x0, starting transfers between devices: 20.3 us -> none  [the longest x1 13.6 us: shards(): lax.all_to_all(jnp.tile(pieces, (count, 1)), 'ctx', 0, 0, tiled=True)]
    ppermute x8, waiting for transfers between devices: 19.3 us -> 5.68 us  [shifted(): lax.ppermute(value, axis, [(source, source + steps) for source in range(l...]
    all_to_all x1, starting transfers between devices: 3.89 us -> 11.7 us  [shards(): lax.all_to_all(filter_part.reshape(count, FLEN // count), 'ctx', 0, 0, ti...]
    all_to_all x2 -> x0, waiting for transfers between devices: 6.88 us -> none  [the longest x1 6.88 us: shards(): lax.all_to_all(jnp.tile(pieces, (count, 1)), 'ctx', 0, 0, tiled=True)]
    ppermute x0 -> x8, waiting for transfers between devices: none -> 6.76 us  [swapped(): lax.ppermute(value, axis, [(source, source ^ bit) for source in range(cou...]
    ppermute x8, starting transfers between devices: 23.4 us -> 18 us  [shifted(): lax.ppermute(value, axis, [(source, source + steps) for source in range(l...]
    all_to_all x1, starting transfers between devices: 10.4 us -> 9.33 us  [shards(): summed = lax.all_to_all(block_sum, 'tp', 0, 0, tiled=True).T]
  transfers between devices with their start and end apart: 12 -> 18, of which waited for: 8 -> 8; matrix products, arithmetic and copies ran while one was open for 7% -> 7% of each run, Pallas kernels for 9% -> 9%
where the time goes in v10:
time: 104 us
  starting transfers between devices  67.5 us (65%)
  waiting for transfers between devices  14.7 us (14%)
  Pallas kernels  9.6 us (9%)
  other arithmetic  6.02 us (6%)
  local copies, waits for them, and re-layouts  4.62 us (4%)
    ppermute x8, starting transfers between devices, swapped(): lax.ppermute(value, axis, [(source, source ^ bit) for source in range(cou...  28.6 us
    ppermute x8, starting transfers between devices, shifted(): lax.ppermute(value, axis, [(source, source + steps) for source in range(l...  18 us
    all_to_all x1, starting transfers between devices, shards(): lax.all_to_all(filter_part.reshape(count, FLEN // count), 'ctx', 0, 0, ti...  11.7 us
    all_to_all x1, starting transfers between devices, shards(): summed = lax.all_to_all(block_sum, 'tp', 0, 0, tiled=True).T  9.33 us
    pallas_call x1, Pallas kernels, local_conv(): pl.pallas_call(conv_kernel, out_shape=(jax.ShapeDtypeStruct((own, width),...  7.01 us
    ppermute x8, waiting for transfers between devices, swapped(): lax.ppermute(value, axis, [(source, source ^ bit) for source in range(cou...  6.76 us
    ppermute x8, waiting for transfers between devices, shifted(): lax.ppermute(value, axis, [(source, source + steps) for source in range(l...  5.68 us
    convert_element_type x1, other arithmetic, shards(): value_grad = (mixed_grad * key_in.astype(jnp.float32)).astype(jnp.bfloat16)  3.26 us
  transfers between devices with their start and end apart: 18, of which 8 were waited for; matrix products, arithmetic and copies ran while one was open for 7% of the time, Pallas kernels for 9%

profile of v10, /device:TPU:1, one launch (start us, length us, event | category | flops | bytes accessed | tf_op | source)
XLA Modules:
  0.0 103.5 jit_solution(12033594774821101743)
XLA Ops:
  0.6 0.8 copy.16
  1.4 3.2 %collective-permute-start = (bf16[8,8]{0,1:T(8,128)(2,1)S(1)}, bf16[8,8]{0,1:T(8,128)(2,1)S(1)}, u32[]{:S(2)}, u32[]{:S(2)}) collective-permute-start(bf16[8,8]{0,1:T(8,128)(2,1)S(1)} %copy.16), channel_id=1, source_target_pairs={{0,1},{1,0},{2,3},{3,2},{4,5},{5,4},{6,7},{7,6},{8,9},{9,8},{10,11... | collective-permute-start | bytes 392 | tf_op jit(solution)/shard_map/ppermute | solution.py:25
  4.6 1.3 %fusion.2.refs_4_ = bf16[512,512]{1,0:T(8,128)(2,1)S(1)} fusion(bf16[512,512]{1,0:T(8,128)(2,1)} %param.9, bf16[512,512]{1,0:T(8,128)(2,1)} %param.8), kind=kLoop, calls=%fused_computation.8 | loop fusion | flops 1048576 | bytes 1572864 | tf_op jit(solution)/shard_map/convert_element_type | solution.py:168
  6.0 1.9 %collective-permute-start.8 = (bf16[512,512]{1,0:T(8,128)(2,1)S(1)}, bf16[512,512]{1,0:T(8,128)(2,1)S(1)}, u32[]{:S(2)}, u32[]{:S(2)}) collective-permute-start(bf16[512,512]{1,0:T(8,128)(2,1)S(1)} %fusion.2.refs_4_), channel_id=1, source_target_pairs={{0,8},{8,16},{16,24},{24,32},{32,40},{40,48},{48,56},{56,64},{64,7... | collective-permute-start | bytes 1572872 | tf_op jit(solution)/shard_map/ppermute | solution.py:20
  7.8 0.1 fusion.4.refs_5_
  8.0 1.3 %collective-permute-start.12 = (bf16[512,512]{1,0:T(8,128)(2,1)S(1)}, bf16[512,512]{1,0:T(8,128)(2,1)S(1)}, u32[]{:S(2)}, u32[]{:S(2)}) collective-permute-start(bf16[512,512]{1,0:T(8,128)(2,1)S(1)} %fusion.4.refs_5_), channel_id=1, source_target_pairs={{8,0},{16,8},{24,16},{32,24},{40,32},{48,40},{56,48},{64,56},{72,6... | collective-permute-start | bytes 1572872 | tf_op jit(solution)/shard_map/ppermute | solution.py:20
  9.3 0.1 pad_maximum_fusion
  9.4 1.3 %collective-permute-start.1 = (bf16[16,8]{0,1:T(8,128)(2,1)S(1)}, bf16[16,8]{0,1:T(8,128)(2,1)S(1)}, u32[]{:S(2)}, u32[]{:S(2)}) collective-permute-start(bf16[16,8]{0,1:T(8,128)(2,1)S(1)} %pad_maximum_fusion), channel_id=1, source_target_pairs={{0,2},{1,3},{2,0},{3,1},{4,6},{5,7},{6,4},{7,5},{8,10},{9,11},{10,... | collective-permute-start | bytes 776 | tf_op jit(solution)/shard_map/ppermute | solution.py:25
  10.7 1.1 %collective-permute-done.1 = bf16[16,8]{0,1:T(8,128)(2,1)S(1)} collective-permute-done((bf16[16,8]{0,1:T(8,128)(2,1)S(1)}, bf16[16,8]{0,1:T(8,128)(2,1)S(1)}, u32[]{:S(2)}, u32[]{:S(2)}) %collective-permute-start.1) | collective-permute-done | bytes 288 | tf_op jit(solution)/shard_map/ppermute | solution.py:25
  11.9 0.1 broadcast_select_fusion.3
  12.0 0.1 pad_maximum_fusion.1
  12.0 2.9 %collective-permute-start.2 = (bf16[32,8]{0,1:T(8,128)(2,1)S(1)}, bf16[32,8]{0,1:T(8,128)(2,1)S(1)}, u32[]{:S(2)}, u32[]{:S(2)}) collective-permute-start(bf16[32,8]{0,1:T(8,128)(2,1)S(1)} %pad_maximum_fusion.1), channel_id=1, source_target_pairs={{0,4},{1,5},{2,6},{3,7},{4,0},{5,1},{6,2},{7,3},{8,12},{9,13},{10,... | collective-permute-start | bytes 1544 | tf_op jit(solution)/shard_map/ppermute | solution.py:25
  15.0 1.0 collective-permute-done.2
  16.1 0.1 pad_maximum_fusion.2
  16.2 2.6 %collective-permute-start.3 = (bf16[64]{0:T(256)(128)(2,1)S(1)}, bf16[64]{0:T(256)(128)(2,1)S(1)}, u32[]{:S(2)}, u32[]{:S(2)}) collective-permute-start(bf16[64]{0:T(256)(128)(2,1)S(1)} %dynamic-slice_bitcast_fusion), channel_id=1, source_target_pairs={{0,8},{8,0},{16,24},{24,16},{32,40},{40,32},{48,56},{56,48},{64,72... | collective-permute-start | bytes 392 | tf_op jit(solution)/shard_map/ppermute | solution.py:25
  18.7 0.2 collective-permute-done.8.refs_3_
  19.0 4.1 %collective-permute-start.9 = (bf16[512,512]{1,0:T(8,128)(2,1)S(1)}, bf16[512,512]{1,0:T(8,128)(2,1)S(1)}, u32[]{:S(2)}, u32[]{:S(2)}) collective-permute-start(bf16[512,512]{1,0:T(8,128)(2,1)S(1)} %collective-permute-done.8.refs_3_), channel_id=1, source_target_pairs={{0,8},{8,16},{16,24},{24,32},{32,40},{40,48},{48,56},{56,64},{64,7... | collective-permute-start | bytes 1572872 | tf_op jit(solution)/shard_map/ppermute | solution.py:20
  23.1 0.2 collective-permute-done.3
  23.3 0.1 pad_maximum_fusion.5
  23.4 4.3 %collective-permute-start.4 = (bf16[128]{0:T(256)(128)(2,1)S(1)}, bf16[128]{0:T(256)(128)(2,1)S(1)}, u32[]{:S(2)}, u32[]{:S(2)}) collective-permute-start(bf16[128]{0:T(256)(128)(2,1)S(1)} %pad_maximum_fusion.5), channel_id=1, source_target_pairs={{0,16},{8,24},{16,0},{24,8},{32,48},{40,56},{48,32},{56,40},{64,80... | collective-permute-start | bytes 776 | tf_op jit(solution)/shard_map/ppermute | solution.py:25
  27.8 1.3 %collective-permute-start.13 = (bf16[512,512]{1,0:T(8,128)(2,1)S(1)}, bf16[512,512]{1,0:T(8,128)(2,1)}, u32[]{:S(2)}, u32[]{:S(2)}) collective-permute-start(bf16[512,512]{1,0:T(8,128)(2,1)S(1)} %collective-permute-done.12.refs_6_), channel_id=1, source_target_pairs={{8,0},{16,8},{24,16},{32,24},{40,32},{48,40},{56,48},{64,56},{72,6... | collective-permute-start | bytes 1572872 | tf_op jit(solution)/shard_map/ppermute | solution.py:20
  29.0 4.4 %collective-permute-done.4 = bf16[128]{0:T(256)(128)(2,1)S(1)} collective-permute-done((bf16[128]{0:T(256)(128)(2,1)S(1)}, bf16[128]{0:T(256)(128)(2,1)S(1)}, u32[]{:S(2)}, u32[]{:S(2)}) %collective-permute-start.4) | collective-permute-done | bytes 288 | tf_op jit(solution)/shard_map/ppermute | solution.py:25
  33.4 0.1 broadcast_select_fusion.11
  33.5 5.7 %collective-permute-start.5 = (bf16[256]{0:T(256)(128)(2,1)S(1)}, bf16[256]{0:T(256)(128)(2,1)S(1)}, u32[]{:S(2)}, u32[]{:S(2)}) collective-permute-start(bf16[256]{0:T(256)(128)(2,1)S(1)} %pad_maximum_fusion.6), channel_id=1, source_target_pairs={{0,32},{8,40},{16,48},{24,56},{32,0},{40,8},{48,16},{56,24},{64,96... | collective-permute-start | bytes 1544 | tf_op jit(solution)/shard_map/ppermute | solution.py:25
  39.2 2.7 %collective-permute-start.10 = (bf16[512,512]{1,0:T(8,128)(2,1)S(1)}, bf16[512,512]{1,0:T(8,128)(2,1)S(1)}, u32[]{:S(2)}, u32[]{:S(2)}) collective-permute-start(bf16[512,512]{1,0:T(8,128)(2,1)S(1)} %collective-permute-done.9.refs_2_), channel_id=1, source_target_pairs={{0,8},{8,16},{16,24},{24,32},{32,40},{40,48},{48,56},{56,64},{64,7... | collective-permute-start | bytes 1572872 | tf_op jit(solution)/shard_map/ppermute | solution.py:20
  42.0 2.0 %collective-permute-start.6 = (bf16[512]{0:T(512)(128)(2,1)S(1)}, bf16[512]{0:T(512)(128)(2,1)S(1)}, u32[]{:S(2)}, u32[]{:S(2)}) collective-permute-start(bf16[512]{0:T(512)(128)(2,1)S(1)} %pad_maximum_fusion.4), channel_id=1, source_target_pairs={{0,64},{8,72},{16,80},{24,88},{32,96},{40,104},{48,112},{56,120},{... | collective-permute-start | bytes 3080 | tf_op jit(solution)/shard_map/ppermute | solution.py:25
  44.0 1.3 %collective-permute-start.14 = (bf16[512,512]{1,0:T(8,128)(2,1)}, bf16[512,512]{1,0:T(8,128)(2,1)}, u32[]{:S(2)}, u32[]{:S(2)}) collective-permute-start(bf16[512,512]{1,0:T(8,128)(2,1)} %collective-permute-done.13.refs_7_), channel_id=1, source_target_pairs={{8,0},{16,8},{24,16},{32,24},{40,32},{48,40},{56,48},{64,56},{72,6... | collective-permute-start | bytes 1572872 | tf_op jit(solution)/shard_map/ppermute | solution.py:20
  45.3 5.4 %collective-permute-done.10.refs_1_ = bf16[512,512]{1,0:T(8,128)(2,1)S(1)} collective-permute-done((bf16[512,512]{1,0:T(8,128)(2,1)S(1)}, bf16[512,512]{1,0:T(8,128)(2,1)S(1)}, u32[]{:S(2)}, u32[]{:S(2)}) %collective-permute-start.10) | collective-permute-done | bytes 524320 | tf_op jit(solution)/shard_map/ppermute | solution.py:20
  50.8 4.1 %collective-permute-start.11 = (bf16[512,512]{1,0:T(8,128)(2,1)S(1)}, bf16[512,512]{1,0:T(8,128)(2,1)S(1)}, u32[]{:S(2)}, u32[]{:S(2)}) collective-permute-start(bf16[512,512]{1,0:T(8,128)(2,1)S(1)} %collective-permute-done.10.refs_1_), channel_id=1, source_target_pairs={{0,8},{8,16},{16,24},{24,32},{32,40},{40,48},{48,56},{56,64},{64,7... | collective-permute-start | bytes 1572872 | tf_op jit(solution)/shard_map/ppermute | solution.py:20
  54.9 6.5 %collective-permute-start.7 = (bf16[1024]{0:T(1024)(128)(2,1)S(1)}, bf16[1024]{0:T(1024)(128)(2,1)S(1)}, u32[]{:S(2)}, u32[]{:S(2)}) collective-permute-start(bf16[1024]{0:T(1024)(128)(2,1)S(1)} %pad_maximum_fusion.3), channel_id=1, source_target_pairs={{0,128},{8,136},{16,144},{24,152},{32,160},{40,168},{48,176},{56,1... | collective-permute-start | bytes 6152 | tf_op jit(solution)/shard_map/ppermute | solution.py:25
  61.4 1.3 %collective-permute-start.15 = (bf16[512,512]{1,0:T(8,128)(2,1)}, bf16[512,512]{1,0:T(8,128)(2,1)}, u32[]{:S(2)}, u32[]{:S(2)}) collective-permute-start(bf16[512,512]{1,0:T(8,128)(2,1)} %collective-permute-done.14.refs_8_), channel_id=1, source_target_pairs={{8,0},{16,8},{24,16},{32,24},{40,32},{48,40},{56,48},{64,56},{72,6... | collective-permute-start | bytes 1572872 | tf_op jit(solution)/shard_map/ppermute | solution.py:20
  62.7 0.1 fusion.11
  62.8 0.6 reshape.46.ids_src
  63.5 0.6 reshape.47.ids_rdr
  64.1 0.1 rev.3
  64.3 0.1 copy.19.ids_own
  64.5 2.6 %shard_map.111 = f32[1,2560]{1,0:T(1,128)S(1)} custom-call(s32[512,1]{1,0:T(8,128)S(1)} %copy.19.ids_own, s32[1,2560]{1,0:T(1,128)S(1)} %bitcast.17, bf16[512,512]{1,0:T(8,128)(2,1)S(1)} %collective-permute-done.11.refs_0_, bf16[512,512]{1,0:T(8,128)(2,1)S(1)} %collective-permute-done.10.refs_1_, bf16[512,512]{1,0:T(8,128)(2,1)S(1)} %collective-permute-done.9.refs_2_, ...), custom_call_target="tpu_custom_call" | custom-call | tf_op jit(solution)/shard_map/pallas_call | solution.py:128
  67.1 0.1 slice_reduce_fusion
  67.2 0.7 all_to_all.12
  67.9 11.7 %all-to-all-start = ((f32[32,1,64]{2,1,0:T(1,128)}), f32[32,1,64]{2,1,0:T(1,128)S(1)}, u32[]{:S(2)}, u32[]{:S(2)}) async-start(f32[32,1,64]{2,1,0:T(1,128)} %bitcast.4), calls=%async_computation | async-start | bytes 32768 | tf_op jit(solution)/shard_map/all_to_all | solution.py:185
  79.6 0.6 fusion.10
  80.2 7.0 %shard_map.110 = (f32[512,512]{1,0:T(8,128)}, f32[512,512]{1,0:T(8,128)}) custom-call(f32[1,3072]{1,0:T(1,128)} %bitcast.19, s32[512,1]{1,0:T(8,128)} %copy-done.2, s32[1,2560]{1,0:T(1,128)} %reshape.46.ids_src, s32[1,2560]{1,0:T(1,128)} %reshape.47.ids_rdr, f32[1,512]{1,0:T(1,128)} %bitcast.22, bf16[512,512]{1,0:T(8,128)(2,1)} %copy-done.6, ...), custom_call_target="tpu_custom_call" | custom-call | tf_op jit(solution)/shard_map/pallas_call | solution.py:141
  87.2 1.0 all-to-all-done
  88.3 0.7 all_to_all.14
  89.0 9.3 %all-to-all-start.1 = ((f32[8,1,8]{2,1,0:T(1,128)}), f32[8,1,8]{2,1,0:T(1,128)S(1)}, u32[]{:S(2)}, u32[]{:S(2)}) async-start(f32[8,1,8]{2,1,0:T(1,128)} %bitcast.5), calls=%async_computation.1 | async-start | bytes 8192 | tf_op jit(solution)/shard_map/all_to_all | solution.py:194
  98.3 3.3 %fusion.1 = (bf16[512,512]{1,0:T(8,128)(2,1)}, bf16[512,512]{1,0:T(8,128)(2,1)}, bf16[512,512]{1,0:T(8,128)(2,1)}, bf16[512,512]{1,0:T(8,128)(2,1)}) fusion(f32[512,512]{1,0:T(8,128)} %get-tuple-element.8, bf16[512,512]{1,0:T(8,128)(2,1)S(1)} %copy-done.8, bf16[512,512]{1,0:T(8,128)(2,1)S(1)} %copy-done.7, f32[512,512]{1,0:T(8,128)} %get-tuple-element.7, ...), kind=kLoop, calls=%fused_computation.7 | loop fusion | flops 3145728 | bytes 6291456 | tf_op jit(solution)/shard_map/convert_element_type | solution.py:192
  101.6 1.2 %all-to-all-done.1 = f32[8,1,8]{2,1,0:T(1,128)S(1)} async-done(((f32[8,1,8]{2,1,0:T(1,128)}), f32[8,1,8]{2,1,0:T(1,128)S(1)}, u32[]{:S(2)}, u32[]{:S(2)}) %all-to-all-start.1) | async-done | bytes 288 | tf_op jit(solution)/shard_map/all_to_all | solution.py:194
  102.8 0.7 copy.24
  (58 shorter events, 0.4 us)
Async XLA Ops:
  1.4 6.4 %copy-start.9 = (bf16[512,512]{1,0:T(8,128)(2,1)S(1)}, bf16[512,512]{1,0:T(8,128)(2,1)}, u32[]{:S(2)}) copy-start(bf16[512,512]{1,0:T(8,128)(2,1)} %param.7) | copy-start | bytes 1572868
  1.4 6.4 %copy-start.11 = (bf16[512,512]{1,0:T(8,128)(2,1)S(1)}, bf16[512,512]{1,0:T(8,128)(2,1)}, u32[]{:S(2)}) copy-start(bf16[512,512]{1,0:T(8,128)(2,1)} %param.10) | copy-start | bytes 1572868
  1.4 7.9 %collective-permute-start = (bf16[8,8]{0,1:T(8,128)(2,1)S(1)}, bf16[8,8]{0,1:T(8,128)(2,1)S(1)}, u32[]{:S(2)}, u32[]{:S(2)}) collective-permute-start(bf16[8,8]{0,1:T(8,128)(2,1)S(1)} %copy.16), channel_id=1, source_target_pairs={{0,1},{1,0},{2,3},{3,2},{4,5},{5,4},{6,7},{7,6},{8,9},{9,8},{10,11... | collective-permute-start | bytes 392 | tf_op jit(solution)/shard_map/ppermute | solution.py:25
  5.9 58.5 %copy-start = (bf16[512,512]{1,0:T(8,128)(2,1)}, bf16[512,512]{1,0:T(8,128)(2,1)S(1)}, u32[]{:S(2)}) copy-start(bf16[512,512]{1,0:T(8,128)(2,1)S(1)} %fusion.2.refs_4_) | copy-start | bytes 1572868
  6.0 13.0 %collective-permute-start.8 = (bf16[512,512]{1,0:T(8,128)(2,1)S(1)}, bf16[512,512]{1,0:T(8,128)(2,1)S(1)}, u32[]{:S(2)}, u32[]{:S(2)}) collective-permute-start(bf16[512,512]{1,0:T(8,128)(2,1)S(1)} %fusion.2.refs_4_), channel_id=1, source_target_pairs={{0,8},{8,16},{16,24},{24,32},{32,40},{40,48},{48,56},{56,64},{64,7... | collective-permute-start | bytes 1572872 | tf_op jit(solution)/shard_map/ppermute | solution.py:20
  8.0 59.1 %copy-start.1 = (bf16[512,512]{1,0:T(8,128)(2,1)}, bf16[512,512]{1,0:T(8,128)(2,1)S(1)}, u32[]{:S(2)}) copy-start(bf16[512,512]{1,0:T(8,128)(2,1)S(1)} %fusion.4.refs_5_) | copy-start | bytes 1572868
  8.0 19.8 %collective-permute-start.12 = (bf16[512,512]{1,0:T(8,128)(2,1)S(1)}, bf16[512,512]{1,0:T(8,128)(2,1)S(1)}, u32[]{:S(2)}, u32[]{:S(2)}) collective-permute-start(bf16[512,512]{1,0:T(8,128)(2,1)S(1)} %fusion.4.refs_5_), channel_id=1, source_target_pairs={{8,0},{16,8},{24,16},{32,24},{40,32},{48,40},{56,48},{64,56},{72,6... | collective-permute-start | bytes 1572872 | tf_op jit(solution)/shard_map/ppermute | solution.py:20
  9.3 36.0 %copy-start.14 = (s32[16384]{0:T(1024)S(1)}, s32[16384]{0:T(1024)}, u32[]{:S(2)}) copy-start(s32[16384]{0:T(1024)} %param.11) | copy-start | bytes 196612
  9.4 2.5 %collective-permute-start.1 = (bf16[16,8]{0,1:T(8,128)(2,1)S(1)}, bf16[16,8]{0,1:T(8,128)(2,1)S(1)}, u32[]{:S(2)}, u32[]{:S(2)}) collective-permute-start(bf16[16,8]{0,1:T(8,128)(2,1)S(1)} %pad_maximum_fusion), channel_id=1, source_target_pairs={{0,2},{1,3},{2,0},{3,1},{4,6},{5,7},{6,4},{7,5},{8,10},{9,11},{10,... | collective-permute-start | bytes 776 | tf_op jit(solution)/shard_map/ppermute | solution.py:25
  12.0 4.0 %collective-permute-start.2 = (bf16[32,8]{0,1:T(8,128)(2,1)S(1)}, bf16[32,8]{0,1:T(8,128)(2,1)S(1)}, u32[]{:S(2)}, u32[]{:S(2)}) collective-permute-start(bf16[32,8]{0,1:T(8,128)(2,1)S(1)} %pad_maximum_fusion.1), channel_id=1, source_target_pairs={{0,4},{1,5},{2,6},{3,7},{4,0},{5,1},{6,2},{7,3},{8,12},{9,13},{10,... | collective-permute-start | bytes 1544 | tf_op jit(solution)/shard_map/ppermute | solution.py:25
  16.2 7.2 %collective-permute-start.3 = (bf16[64]{0:T(256)(128)(2,1)S(1)}, bf16[64]{0:T(256)(128)(2,1)S(1)}, u32[]{:S(2)}, u32[]{:S(2)}) collective-permute-start(bf16[64]{0:T(256)(128)(2,1)S(1)} %dynamic-slice_bitcast_fusion), channel_id=1, source_target_pairs={{0,8},{8,0},{16,24},{24,16},{32,40},{40,32},{48,56},{56,48},{64,72... | collective-permute-start | bytes 392 | tf_op jit(solution)/shard_map/ppermute | solution.py:25
  19.0 48.1 %copy-start.3 = (bf16[512,512]{1,0:T(8,128)(2,1)}, bf16[512,512]{1,0:T(8,128)(2,1)S(1)}, u32[]{:S(2)}) copy-start(bf16[512,512]{1,0:T(8,128)(2,1)S(1)} %collective-permute-done.8.refs_3_) | copy-start | bytes 1572868
  19.0 20.3 %collective-permute-start.9 = (bf16[512,512]{1,0:T(8,128)(2,1)S(1)}, bf16[512,512]{1,0:T(8,128)(2,1)S(1)}, u32[]{:S(2)}, u32[]{:S(2)}) collective-permute-start(bf16[512,512]{1,0:T(8,128)(2,1)S(1)} %collective-permute-done.8.refs_3_), channel_id=1, source_target_pairs={{0,8},{8,16},{16,24},{24,32},{32,40},{40,48},{48,56},{56,64},{64,7... | collective-permute-start | bytes 1572872 | tf_op jit(solution)/shard_map/ppermute | solution.py:20
  23.4 10.0 %collective-permute-start.4 = (bf16[128]{0:T(256)(128)(2,1)S(1)}, bf16[128]{0:T(256)(128)(2,1)S(1)}, u32[]{:S(2)}, u32[]{:S(2)}) collective-permute-start(bf16[128]{0:T(256)(128)(2,1)S(1)} %pad_maximum_fusion.5), channel_id=1, source_target_pairs={{0,16},{8,24},{16,0},{24,8},{32,48},{40,56},{48,32},{56,40},{64,80... | collective-permute-start | bytes 776 | tf_op jit(solution)/shard_map/ppermute | solution.py:25
  27.8 17.6 %copy-start.13 = (bf16[512,512]{1,0:T(8,128)(2,1)}, bf16[512,512]{1,0:T(8,128)(2,1)S(1)}, u32[]{:S(2)}) copy-start(bf16[512,512]{1,0:T(8,128)(2,1)S(1)} %collective-permute-done.12.refs_6_) | copy-start | bytes 1572868
  27.8 16.2 %collective-permute-start.13 = (bf16[512,512]{1,0:T(8,128)(2,1)S(1)}, bf16[512,512]{1,0:T(8,128)(2,1)}, u32[]{:S(2)}, u32[]{:S(2)}) collective-permute-start(bf16[512,512]{1,0:T(8,128)(2,1)S(1)} %collective-permute-done.12.refs_6_), channel_id=1, source_target_pairs={{8,0},{16,8},{24,16},{32,24},{40,32},{48,40},{56,48},{64,56},{72,6... | collective-permute-start | bytes 1572872 | tf_op jit(solution)/shard_map/ppermute | solution.py:20
  33.5 8.5 %collective-permute-start.5 = (bf16[256]{0:T(256)(128)(2,1)S(1)}, bf16[256]{0:T(256)(128)(2,1)S(1)}, u32[]{:S(2)}, u32[]{:S(2)}) collective-permute-start(bf16[256]{0:T(256)(128)(2,1)S(1)} %pad_maximum_fusion.6), channel_id=1, source_target_pairs={{0,32},{8,40},{16,48},{24,56},{32,0},{40,8},{48,16},{56,24},{64,96... | collective-permute-start | bytes 1544 | tf_op jit(solution)/shard_map/ppermute | solution.py:25
  39.2 27.9 %copy-start.4 = (bf16[512,512]{1,0:T(8,128)(2,1)}, bf16[512,512]{1,0:T(8,128)(2,1)S(1)}, u32[]{:S(2)}) copy-start(bf16[512,512]{1,0:T(8,128)(2,1)S(1)} %collective-permute-done.9.refs_2_) | copy-start | bytes 1572868
  39.2 11.5 %collective-permute-start.10 = (bf16[512,512]{1,0:T(8,128)(2,1)S(1)}, bf16[512,512]{1,0:T(8,128)(2,1)S(1)}, u32[]{:S(2)}, u32[]{:S(2)}) collective-permute-start(bf16[512,512]{1,0:T(8,128)(2,1)S(1)} %collective-permute-done.9.refs_2_), channel_id=1, source_target_pairs={{0,8},{8,16},{16,24},{24,32},{32,40},{40,48},{48,56},{56,64},{64,7... | collective-permute-start | bytes 1572872 | tf_op jit(solution)/shard_map/ppermute | solution.py:20
  42.0 12.9 %collective-permute-start.6 = (bf16[512]{0:T(512)(128)(2,1)S(1)}, bf16[512]{0:T(512)(128)(2,1)S(1)}, u32[]{:S(2)}, u32[]{:S(2)}) collective-permute-start(bf16[512]{0:T(512)(128)(2,1)S(1)} %pad_maximum_fusion.4), channel_id=1, source_target_pairs={{0,64},{8,72},{16,80},{24,88},{32,96},{40,104},{48,112},{56,120},{... | collective-permute-start | bytes 3080 | tf_op jit(solution)/shard_map/ppermute | solution.py:25
  44.0 17.5 %collective-permute-start.14 = (bf16[512,512]{1,0:T(8,128)(2,1)}, bf16[512,512]{1,0:T(8,128)(2,1)}, u32[]{:S(2)}, u32[]{:S(2)}) collective-permute-start(bf16[512,512]{1,0:T(8,128)(2,1)} %collective-permute-done.13.refs_7_), channel_id=1, source_target_pairs={{8,0},{16,8},{24,16},{32,24},{40,32},{48,40},{56,48},{64,56},{72,6... | collective-permute-start | bytes 1572872 | tf_op jit(solution)/shard_map/ppermute | solution.py:20
  50.8 16.4 %copy-start.5 = (bf16[512,512]{1,0:T(8,128)(2,1)}, bf16[512,512]{1,0:T(8,128)(2,1)S(1)}, u32[]{:S(2)}) copy-start(bf16[512,512]{1,0:T(8,128)(2,1)S(1)} %collective-permute-done.10.refs_1_) | copy-start | bytes 1572868
  50.8 13.7 %collective-permute-start.11 = (bf16[512,512]{1,0:T(8,128)(2,1)S(1)}, bf16[512,512]{1,0:T(8,128)(2,1)S(1)}, u32[]{:S(2)}, u32[]{:S(2)}) collective-permute-start(bf16[512,512]{1,0:T(8,128)(2,1)S(1)} %collective-permute-done.10.refs_1_), channel_id=1, source_target_pairs={{0,8},{8,16},{16,24},{24,32},{32,40},{40,48},{48,56},{56,64},{64,7... | collective-permute-start | bytes 1572872 | tf_op jit(solution)/shard_map/ppermute | solution.py:20
  54.9 9.5 %collective-permute-start.7 = (bf16[1024]{0:T(1024)(128)(2,1)S(1)}, bf16[1024]{0:T(1024)(128)(2,1)S(1)}, u32[]{:S(2)}, u32[]{:S(2)}) collective-permute-start(bf16[1024]{0:T(1024)(128)(2,1)S(1)} %pad_maximum_fusion.3), channel_id=1, source_target_pairs={{0,128},{8,136},{16,144},{24,152},{32,160},{40,168},{48,176},{56,1... | collective-permute-start | bytes 6152 | tf_op jit(solution)/shard_map/ppermute | solution.py:25
  61.4 18.8 %collective-permute-start.15 = (bf16[512,512]{1,0:T(8,128)(2,1)}, bf16[512,512]{1,0:T(8,128)(2,1)}, u32[]{:S(2)}, u32[]{:S(2)}) collective-permute-start(bf16[512,512]{1,0:T(8,128)(2,1)} %collective-permute-done.14.refs_8_), channel_id=1, source_target_pairs={{8,0},{16,8},{24,16},{32,24},{40,32},{48,40},{56,48},{64,56},{72,6... | collective-permute-start | bytes 1572872 | tf_op jit(solution)/shard_map/ppermute | solution.py:20
  64.4 2.7 %copy-start.2 = (s32[512,1]{1,0:T(8,128)}, s32[512,1]{1,0:T(8,128)S(1)}, u32[]{:S(2)}) copy-start(s32[512,1]{1,0:T(8,128)S(1)} %copy.19.ids_own) | copy-start | bytes 6148
  64.5 2.7 %copy-start.6 = (bf16[512,512]{1,0:T(8,128)(2,1)}, bf16[512,512]{1,0:T(8,128)(2,1)S(1)}, u32[]{:S(2)}) copy-start(bf16[512,512]{1,0:T(8,128)(2,1)S(1)} %collective-permute-done.11.refs_0_) | copy-start | bytes 1572868
  67.9 20.3 %all-to-all-start = ((f32[32,1,64]{2,1,0:T(1,128)}), f32[32,1,64]{2,1,0:T(1,128)S(1)}, u32[]{:S(2)}, u32[]{:S(2)}) async-start(f32[32,1,64]{2,1,0:T(1,128)} %bitcast.4), calls=%async_computation | async-start | bytes 32768 | tf_op jit(solution)/shard_map/all_to_all | solution.py:185
  80.2 18.1 %copy-start.7 = (bf16[512,512]{1,0:T(8,128)(2,1)S(1)}, bf16[512,512]{1,0:T(8,128)(2,1)}, u32[]{:S(2)}) copy-start(bf16[512,512]{1,0:T(8,128)(2,1)} %param.9) | copy-start | bytes 1572868
  80.2 18.1 %copy-start.8 = (bf16[512,512]{1,0:T(8,128)(2,1)S(1)}, bf16[512,512]{1,0:T(8,128)(2,1)}, u32[]{:S(2)}) copy-start(bf16[512,512]{1,0:T(8,128)(2,1)} %param.8) | copy-start | bytes 1572868
  80.2 18.1 %copy-start.10 = (bf16[512,512]{1,0:T(8,128)(2,1)S(1)}, bf16[512,512]{1,0:T(8,128)(2,1)}, u32[]{:S(2)}) copy-start(bf16[512,512]{1,0:T(8,128)(2,1)} %param.7) | copy-start | bytes 1572868
  80.2 18.1 %copy-start.12 = (bf16[512,512]{1,0:T(8,128)(2,1)S(1)}, bf16[512,512]{1,0:T(8,128)(2,1)}, u32[]{:S(2)}) copy-start(bf16[512,512]{1,0:T(8,128)(2,1)} %param.10) | copy-start | bytes 1572868
  89.0 13.9 %all-to-all-start.1 = ((f32[8,1,8]{2,1,0:T(1,128)}), f32[8,1,8]{2,1,0:T(1,128)S(1)}, u32[]{:S(2)}, u32[]{:S(2)}) async-start(f32[8,1,8]{2,1,0:T(1,128)} %bitcast.5), calls=%async_computation.1 | async-start | bytes 8192 | tf_op jit(solution)/shard_map/all_to_all | solution.py:194

commit v11 on v10

--- a/solution.py
+++ b/solution.py
@@ -182,8 +182,9 @@
     ids_rdr = lax.dynamic_slice_in_dim(ids_pad, here * rows + hist, hist + rows)
 
     filter_part = filter_sums(ids_own, ids_src, ahead[::-1], conv_grad)
-    spread = lax.all_to_all(filter_part.reshape(count, FLEN // count), "ctx", 0, 0, tiled=True)
-    block_sum = jnp.sum(spread, axis=0).reshape(groups, FLEN // (count * groups))
+    every = ("ctx", "tp")
+    devices = lax.axis_size(every)
+    spread = lax.all_to_all(filter_part.reshape(devices, FLEN // devices), every, 0, 0, tiled=True)
     conv, mixed_grad = local_conv(taps, ids_own, ids_src, ids_rdr, skip_gain, ahead[::-1], behind)
 
     mixed_out = (query_in.astype(jnp.float32) * conv).astype(jnp.bfloat16)
@@ -191,7 +192,7 @@
     key_grad = (mixed_grad * value_in.astype(jnp.float32)).astype(jnp.bfloat16)
     value_grad = (mixed_grad * key_in.astype(jnp.float32)).astype(jnp.bfloat16)
 
-    summed = lax.all_to_all(block_sum, "tp", 0, 0, tiled=True).T
+    summed = jnp.sum(spread.reshape(devices // groups, groups, FLEN // devices), axis=0).T
     tokens = lax.axis_size("ctx") * rows
     filter_grad = summed * (1.0 / math.sqrt(FGROUP * tokens))
     return (mixed_out, query_grad, key_grad, value_grad, filter_grad)

time: 104 us -> 105 us (level)
  waiting for transfers between devices: 14.7 us -> 20 us
  starting transfers between devices: 67.5 us -> 63.6 us
    ppermute x8, waiting for transfers between devices: 6.76 us -> 11.6 us  [swapped(): lax.ppermute(value, axis, [(source, source ^ bit) for source in range(cou...]
    ppermute x8, starting transfers between devices: 28.6 us -> 26.4 us  [swapped(): lax.ppermute(value, axis, [(source, source ^ bit) for source in range(cou...]
    all_to_all x2 -> x1, starting transfers between devices: 21 us -> 19.9 us  [shards(): lax.all_to_all(filter_part.reshape(devices, FLEN // devices), every, 0, 0...]
    all_to_all x2 -> x1, waiting for transfers between devices: 2.25 us -> 2.47 us  [shards(): lax.all_to_all(filter_part.reshape(devices, FLEN // devices), every, 0, 0...]
  transfers between devices with their start and end apart: 18 -> 17, of which waited for: 8 -> 6; matrix products, arithmetic and copies ran while one was open for 7% -> 7% of each run, Pallas kernels for 9% -> 9%
where the time goes in v11:
time: 105 us; the launch traced here: 104 us
  starting transfers between devices  63.6 us (61%)
  waiting for transfers between devices  20 us (19%)
  Pallas kernels  9.62 us (9%)
  other arithmetic  6.08 us (6%)
  local copies, waits for them, and re-layouts  4.04 us (4%)
    ppermute x8, starting transfers between devices, swapped(): lax.ppermute(value, axis, [(source, source ^ bit) for source in range(cou...  26.4 us
    all_to_all x1, starting transfers between devices, shards(): lax.all_to_all(filter_part.reshape(devices, FLEN // devices), every, 0, 0...  19.9 us
    ppermute x8, starting transfers between devices, shifted(): lax.ppermute(value, axis, [(source, source + steps) for source in range(l...  17.3 us
    ppermute x8, waiting for transfers between devices, swapped(): lax.ppermute(value, axis, [(source, source ^ bit) for source in range(cou...  11.6 us
    pallas_call x1, Pallas kernels, local_conv(): pl.pallas_call(conv_kernel, out_shape=(jax.ShapeDtypeStruct((own, width),...  7.02 us
    ppermute x8, waiting for transfers between devices, shifted(): lax.ppermute(value, axis, [(source, source + steps) for source in range(l...  5.87 us
    convert_element_type x1, other arithmetic, shards(): value_grad = (mixed_grad * key_in.astype(jnp.float32)).astype(jnp.bfloat16)  3.26 us
    pallas_call x1, Pallas kernels, filter_sums(): pl.pallas_call(filter_kernel, out_shape=jax.ShapeDtypeStruct((1, (MAXCH +...  2.6 us
  transfers between devices with their start and end apart: 17, of which 6 were waited for; matrix products, arithmetic and copies ran while one was open for 7% of the time, Pallas kernels for 9%

profile of v11, /device:TPU:1, one launch (start us, length us, event | category | flops | bytes accessed | tf_op | source)
XLA Modules:
  0.0 104.3 jit_solution(4461340237985695151)
XLA Ops:
  0.6 0.8 copy.14
  1.4 3.2 %collective-permute-start = (bf16[8,8]{0,1:T(8,128)(2,1)S(1)}, bf16[8,8]{0,1:T(8,128)(2,1)S(1)}, u32[]{:S(2)}, u32[]{:S(2)}) collective-permute-start(bf16[8,8]{0,1:T(8,128)(2,1)S(1)} %copy.14), channel_id=1, source_target_pairs={{0,1},{1,0},{2,3},{3,2},{4,5},{5,4},{6,7},{7,6},{8,9},{9,8},{10,11... | collective-permute-start | bytes 392 | tf_op jit(solution)/shard_map/ppermute | solution.py:25
  4.6 1.3 %fusion.2.refs_4_ = bf16[512,512]{1,0:T(8,128)(2,1)S(1)} fusion(bf16[512,512]{1,0:T(8,128)(2,1)} %param.9, bf16[512,512]{1,0:T(8,128)(2,1)} %param.8), kind=kLoop, calls=%fused_computation.8 | loop fusion | flops 1048576 | bytes 1572864 | tf_op jit(solution)/shard_map/convert_element_type | solution.py:168
  6.0 1.9 %collective-permute-start.8 = (bf16[512,512]{1,0:T(8,128)(2,1)S(1)}, bf16[512,512]{1,0:T(8,128)(2,1)S(1)}, u32[]{:S(2)}, u32[]{:S(2)}) collective-permute-start(bf16[512,512]{1,0:T(8,128)(2,1)S(1)} %fusion.2.refs_4_), channel_id=1, source_target_pairs={{0,8},{8,16},{16,24},{24,32},{32,40},{40,48},{48,56},{56,64},{64,7... | collective-permute-start | bytes 1572872 | tf_op jit(solution)/shard_map/ppermute | solution.py:20
  7.8 0.1 fusion.4.refs_5_
  8.0 1.3 %collective-permute-start.12 = (bf16[512,512]{1,0:T(8,128)(2,1)S(1)}, bf16[512,512]{1,0:T(8,128)(2,1)S(1)}, u32[]{:S(2)}, u32[]{:S(2)}) collective-permute-start(bf16[512,512]{1,0:T(8,128)(2,1)S(1)} %fusion.4.refs_5_), channel_id=1, source_target_pairs={{8,0},{16,8},{24,16},{32,24},{40,32},{48,40},{56,48},{64,56},{72,6... | collective-permute-start | bytes 1572872 | tf_op jit(solution)/shard_map/ppermute | solution.py:20
  9.3 0.0 copy-start.14
  9.3 0.1 pad_maximum_fusion
  9.4 1.3 %collective-permute-start.1 = (bf16[16,8]{0,1:T(8,128)(2,1)S(1)}, bf16[16,8]{0,1:T(8,128)(2,1)S(1)}, u32[]{:S(2)}, u32[]{:S(2)}) collective-permute-start(bf16[16,8]{0,1:T(8,128)(2,1)S(1)} %pad_maximum_fusion), channel_id=1, source_target_pairs={{0,2},{1,3},{2,0},{3,1},{4,6},{5,7},{6,4},{7,5},{8,10},{9,11},{10,... | collective-permute-start | bytes 776 | tf_op jit(solution)/shard_map/ppermute | solution.py:25
  10.7 1.1 %collective-permute-done.1 = bf16[16,8]{0,1:T(8,128)(2,1)S(1)} collective-permute-done((bf16[16,8]{0,1:T(8,128)(2,1)S(1)}, bf16[16,8]{0,1:T(8,128)(2,1)S(1)}, u32[]{:S(2)}, u32[]{:S(2)}) %collective-permute-start.1) | collective-permute-done | bytes 288 | tf_op jit(solution)/shard_map/ppermute | solution.py:25
  11.9 0.1 broadcast_select_fusion.3
  12.0 0.1 pad_maximum_fusion.1
  12.0 2.9 %collective-permute-start.2 = (bf16[32,8]{0,1:T(8,128)(2,1)S(1)}, bf16[32,8]{0,1:T(8,128)(2,1)S(1)}, u32[]{:S(2)}, u32[]{:S(2)}) collective-permute-start(bf16[32,8]{0,1:T(8,128)(2,1)S(1)} %pad_maximum_fusion.1), channel_id=1, source_target_pairs={{0,4},{1,5},{2,6},{3,7},{4,0},{5,1},{6,2},{7,3},{8,12},{9,13},{10,... | collective-permute-start | bytes 1544 | tf_op jit(solution)/shard_map/ppermute | solution.py:25
  15.0 1.0 collective-permute-done.2
  16.0 0.1 broadcast_select_fusion.5
  16.1 0.1 pad_maximum_fusion.2
  16.2 2.6 %collective-permute-start.3 = (bf16[64]{0:T(256)(128)(2,1)S(1)}, bf16[64]{0:T(256)(128)(2,1)S(1)}, u32[]{:S(2)}, u32[]{:S(2)}) collective-permute-start(bf16[64]{0:T(256)(128)(2,1)S(1)} %dynamic-slice_bitcast_fusion), channel_id=1, source_target_pairs={{0,8},{8,0},{16,24},{24,16},{32,40},{40,32},{48,56},{56,48},{64,72... | collective-permute-start | bytes 392 | tf_op jit(solution)/shard_map/ppermute | solution.py:25
  18.7 4.6 %collective-permute-done.3 = bf16[64]{0:T(256)(128)(2,1)S(1)} collective-permute-done((bf16[64]{0:T(256)(128)(2,1)S(1)}, bf16[64]{0:T(256)(128)(2,1)S(1)}, u32[]{:S(2)}, u32[]{:S(2)}) %collective-permute-start.3) | collective-permute-done | bytes 160 | tf_op jit(solution)/shard_map/ppermute | solution.py:25
  23.3 0.1 pad_maximum_fusion.5
  23.4 4.3 %collective-permute-start.4 = (bf16[128]{0:T(256)(128)(2,1)S(1)}, bf16[128]{0:T(256)(128)(2,1)S(1)}, u32[]{:S(2)}, u32[]{:S(2)}) collective-permute-start(bf16[128]{0:T(256)(128)(2,1)S(1)} %pad_maximum_fusion.5), channel_id=1, source_target_pairs={{0,16},{8,24},{16,0},{24,8},{32,48},{40,56},{48,32},{56,40},{64,80... | collective-permute-start | bytes 776 | tf_op jit(solution)/shard_map/ppermute | solution.py:25
  27.8 1.3 %collective-permute-start.9 = (bf16[512,512]{1,0:T(8,128)(2,1)S(1)}, bf16[512,512]{1,0:T(8,128)(2,1)S(1)}, u32[]{:S(2)}, u32[]{:S(2)}) collective-permute-start(bf16[512,512]{1,0:T(8,128)(2,1)S(1)} %collective-permute-done.8.refs_3_), channel_id=1, source_target_pairs={{0,8},{8,16},{16,24},{24,32},{32,40},{40,48},{48,56},{56,64},{64,7... | collective-permute-start | bytes 1572872 | tf_op jit(solution)/shard_map/ppermute | solution.py:20
  29.1 1.3 %collective-permute-start.13 = (bf16[512,512]{1,0:T(8,128)(2,1)S(1)}, bf16[512,512]{1,0:T(8,128)(2,1)}, u32[]{:S(2)}, u32[]{:S(2)}) collective-permute-start(bf16[512,512]{1,0:T(8,128)(2,1)S(1)} %collective-permute-done.12.refs_6_), channel_id=1, source_target_pairs={{8,0},{16,8},{24,16},{32,24},{40,32},{48,40},{56,48},{64,56},{72,6... | collective-permute-start | bytes 1572872 | tf_op jit(solution)/shard_map/ppermute | solution.py:20
  30.4 0.1 broadcast_select_fusion.11
  30.5 6.5 %collective-permute-start.5 = (bf16[256]{0:T(256)(128)(2,1)S(1)}, bf16[256]{0:T(256)(128)(2,1)S(1)}, u32[]{:S(2)}, u32[]{:S(2)}) collective-permute-start(bf16[256]{0:T(256)(128)(2,1)S(1)} %pad_maximum_fusion.6), channel_id=1, source_target_pairs={{0,32},{8,40},{16,48},{24,56},{32,0},{40,8},{48,16},{56,24},{64,96... | collective-permute-start | bytes 1544 | tf_op jit(solution)/shard_map/ppermute | solution.py:25
  37.0 4.9 %collective-permute-done.5 = bf16[256]{0:T(256)(128)(2,1)S(1)} collective-permute-done((bf16[256]{0:T(256)(128)(2,1)S(1)}, bf16[256]{0:T(256)(128)(2,1)S(1)}, u32[]{:S(2)}, u32[]{:S(2)}) %collective-permute-start.5) | collective-permute-done | bytes 544 | tf_op jit(solution)/shard_map/ppermute | solution.py:25
  41.9 1.3 %collective-permute-start.6 = (bf16[512]{0:T(512)(128)(2,1)S(1)}, bf16[512]{0:T(512)(128)(2,1)S(1)}, u32[]{:S(2)}, u32[]{:S(2)}) collective-permute-start(bf16[512]{0:T(512)(128)(2,1)S(1)} %pad_maximum_fusion.4), channel_id=1, source_target_pairs={{0,64},{8,72},{16,80},{24,88},{32,96},{40,104},{48,112},{56,120},{... | collective-permute-start | bytes 3080 | tf_op jit(solution)/shard_map/ppermute | solution.py:25
  43.2 4.8 %collective-permute-start.10 = (bf16[512,512]{1,0:T(8,128)(2,1)S(1)}, bf16[512,512]{1,0:T(8,128)(2,1)S(1)}, u32[]{:S(2)}, u32[]{:S(2)}) collective-permute-start(bf16[512,512]{1,0:T(8,128)(2,1)S(1)} %collective-permute-done.9.refs_2_), channel_id=1, source_target_pairs={{0,8},{8,16},{16,24},{24,32},{32,40},{40,48},{48,56},{56,64},{64,7... | collective-permute-start | bytes 1572872 | tf_op jit(solution)/shard_map/ppermute | solution.py:20
  48.0 1.3 %collective-permute-start.14 = (bf16[512,512]{1,0:T(8,128)(2,1)}, bf16[512,512]{1,0:T(8,128)(2,1)}, u32[]{:S(2)}, u32[]{:S(2)}) collective-permute-start(bf16[512,512]{1,0:T(8,128)(2,1)} %collective-permute-done.13.refs_7_), channel_id=1, source_target_pairs={{8,0},{16,8},{24,16},{32,24},{40,32},{48,40},{56,48},{64,56},{72,6... | collective-permute-start | bytes 1572872 | tf_op jit(solution)/shard_map/ppermute | solution.py:20
  49.4 5.8 %collective-permute-done.10.refs_1_ = bf16[512,512]{1,0:T(8,128)(2,1)S(1)} collective-permute-done((bf16[512,512]{1,0:T(8,128)(2,1)S(1)}, bf16[512,512]{1,0:T(8,128)(2,1)S(1)}, u32[]{:S(2)}, u32[]{:S(2)}) %collective-permute-start.10) | collective-permute-done | bytes 524320 | tf_op jit(solution)/shard_map/ppermute | solution.py:20
  55.3 4.1 %collective-permute-start.11 = (bf16[512,512]{1,0:T(8,128)(2,1)S(1)}, bf16[512,512]{1,0:T(8,128)(2,1)S(1)}, u32[]{:S(2)}, u32[]{:S(2)}) collective-permute-start(bf16[512,512]{1,0:T(8,128)(2,1)S(1)} %collective-permute-done.10.refs_1_), channel_id=1, source_target_pairs={{0,8},{8,16},{16,24},{24,32},{32,40},{40,48},{48,56},{56,64},{64,7... | collective-permute-start | bytes 1572872 | tf_op jit(solution)/shard_map/ppermute | solution.py:20
  59.4 4.2 %collective-permute-start.7 = (bf16[1024]{0:T(1024)(128)(2,1)S(1)}, bf16[1024]{0:T(1024)(128)(2,1)S(1)}, u32[]{:S(2)}, u32[]{:S(2)}) collective-permute-start(bf16[1024]{0:T(1024)(128)(2,1)S(1)} %pad_maximum_fusion.3), channel_id=1, source_target_pairs={{0,128},{8,136},{16,144},{24,152},{32,160},{40,168},{48,176},{56,1... | collective-permute-start | bytes 6152 | tf_op jit(solution)/shard_map/ppermute | solution.py:25
  63.6 1.3 %collective-permute-start.15 = (bf16[512,512]{1,0:T(8,128)(2,1)}, bf16[512,512]{1,0:T(8,128)(2,1)}, u32[]{:S(2)}, u32[]{:S(2)}) collective-permute-start(bf16[512,512]{1,0:T(8,128)(2,1)} %collective-permute-done.14.refs_8_), channel_id=1, source_target_pairs={{8,0},{16,8},{24,16},{32,24},{40,32},{48,40},{56,48},{64,56},{72,6... | collective-permute-start | bytes 1572872 | tf_op jit(solution)/shard_map/ppermute | solution.py:20
  64.9 0.1 fusion.11
  65.0 0.6 reshape.44.ids_src
  65.6 0.1 dynamic_slice.13
  65.7 0.6 reshape.45.ids_rdr
  66.3 0.1 rev.3
  66.5 0.1 copy.17.ids_own
  66.7 0.7 fusion.10
  67.4 2.6 %shard_map.111 = f32[1,2560]{1,0:T(1,128)S(1)} custom-call(s32[512,1]{1,0:T(8,128)S(1)} %copy.17.ids_own, s32[1,2560]{1,0:T(1,128)S(1)} %bitcast.16, bf16[512,512]{1,0:T(8,128)(2,1)S(1)} %collective-permute-done.11.refs_0_, bf16[512,512]{1,0:T(8,128)(2,1)S(1)} %collective-permute-done.10.refs_1_, bf16[512,512]{1,0:T(8,128)(2,1)S(1)} %collective-permute-done.9.refs_2_, ...), custom_call_target="tpu_custom_call" | custom-call | tf_op jit(solution)/shard_map/pallas_call | solution.py:128
  70.0 0.1 slice_reduce_fusion
  70.1 0.8 all_to_all.6
  70.9 19.9 %all-to-all-start = ((f32[256,1,8]{2,1,0:T(1,128)}), f32[256,1,8]{2,1,0:T(1,128)S(1)}, u32[]{:S(2)}, u32[]{:S(2)}) async-start(f32[256,1,8]{2,1,0:T(1,128)} %bitcast.4), calls=%async_computation | async-start | bytes 262144 | tf_op jit(solution)/shard_map/all_to_all | solution.py:187
  90.8 0.0 copy-start.10
  90.8 7.0 %shard_map.110 = (f32[512,512]{1,0:T(8,128)}, f32[512,512]{1,0:T(8,128)}) custom-call(f32[1,3072]{1,0:T(1,128)} %bitcast.19, s32[512,1]{1,0:T(8,128)} %copy-done.2, s32[1,2560]{1,0:T(1,128)} %reshape.44.ids_src, s32[1,2560]{1,0:T(1,128)} %reshape.45.ids_rdr, f32[1,512]{1,0:T(1,128)} %bitcast.21, bf16[512,512]{1,0:T(8,128)(2,1)} %copy-done.6, ...), custom_call_target="tpu_custom_call" | custom-call | tf_op jit(solution)/shard_map/pallas_call | solution.py:141
  97.9 3.3 %fusion.1 = (bf16[512,512]{1,0:T(8,128)(2,1)}, bf16[512,512]{1,0:T(8,128)(2,1)}, bf16[512,512]{1,0:T(8,128)(2,1)}, bf16[512,512]{1,0:T(8,128)(2,1)}) fusion(f32[512,512]{1,0:T(8,128)} %get-tuple-element.8, bf16[512,512]{1,0:T(8,128)(2,1)S(1)} %copy-done.8, bf16[512,512]{1,0:T(8,128)(2,1)S(1)} %copy-done.7, f32[512,512]{1,0:T(8,128)} %get-tuple-element.7, ...), kind=kLoop, calls=%fused_computation.7 | loop fusion | flops 3145728 | bytes 6291456 | tf_op jit(solution)/shard_map/convert_element_type | solution.py:193
  101.2 2.5 %all-to-all-done = f32[256,1,8]{2,1,0:T(1,128)S(1)} async-done(((f32[256,1,8]{2,1,0:T(1,128)}), f32[256,1,8]{2,1,0:T(1,128)S(1)}, u32[]{:S(2)}, u32[]{:S(2)}) %all-to-all-start) | async-done | bytes 8224 | tf_op jit(solution)/shard_map/all_to_all | solution.py:187
  103.7 0.7 copy.20
  (55 shorter events, 0.3 us)
Async XLA Ops:
  1.4 6.4 %copy-start.9 = (bf16[512,512]{1,0:T(8,128)(2,1)S(1)}, bf16[512,512]{1,0:T(8,128)(2,1)}, u32[]{:S(2)}) copy-start(bf16[512,512]{1,0:T(8,128)(2,1)} %param.7) | copy-start | bytes 1572868
  1.4 6.4 %copy-start.11 = (bf16[512,512]{1,0:T(8,128)(2,1)S(1)}, bf16[512,512]{1,0:T(8,128)(2,1)}, u32[]{:S(2)}) copy-start(bf16[512,512]{1,0:T(8,128)(2,1)} %param.10) | copy-start | bytes 1572868
  1.4 7.9 %collective-permute-start = (bf16[8,8]{0,1:T(8,128)(2,1)S(1)}, bf16[8,8]{0,1:T(8,128)(2,1)S(1)}, u32[]{:S(2)}, u32[]{:S(2)}) collective-permute-start(bf16[8,8]{0,1:T(8,128)(2,1)S(1)} %copy.14), channel_id=1, source_target_pairs={{0,1},{1,0},{2,3},{3,2},{4,5},{5,4},{6,7},{7,6},{8,9},{9,8},{10,11... | collective-permute-start | bytes 392 | tf_op jit(solution)/shard_map/ppermute | solution.py:25
  5.9 61.4 %copy-start = (bf16[512,512]{1,0:T(8,128)(2,1)}, bf16[512,512]{1,0:T(8,128)(2,1)S(1)}, u32[]{:S(2)}) copy-start(bf16[512,512]{1,0:T(8,128)(2,1)S(1)} %fusion.2.refs_4_) | copy-start | bytes 1572868
  6.0 21.8 %collective-permute-start.8 = (bf16[512,512]{1,0:T(8,128)(2,1)S(1)}, bf16[512,512]{1,0:T(8,128)(2,1)S(1)}, u32[]{:S(2)}, u32[]{:S(2)}) collective-permute-start(bf16[512,512]{1,0:T(8,128)(2,1)S(1)} %fusion.2.refs_4_), channel_id=1, source_target_pairs={{0,8},{8,16},{16,24},{24,32},{32,40},{40,48},{48,56},{56,64},{64,7... | collective-permute-start | bytes 1572872 | tf_op jit(solution)/shard_map/ppermute | solution.py:20
  8.0 62.0 %copy-start.1 = (bf16[512,512]{1,0:T(8,128)(2,1)}, bf16[512,512]{1,0:T(8,128)(2,1)S(1)}, u32[]{:S(2)}) copy-start(bf16[512,512]{1,0:T(8,128)(2,1)S(1)} %fusion.4.refs_5_) | copy-start | bytes 1572868
  8.0 21.1 %collective-permute-start.12 = (bf16[512,512]{1,0:T(8,128)(2,1)S(1)}, bf16[512,512]{1,0:T(8,128)(2,1)S(1)}, u32[]{:S(2)}, u32[]{:S(2)}) collective-permute-start(bf16[512,512]{1,0:T(8,128)(2,1)S(1)} %fusion.4.refs_5_), channel_id=1, source_target_pairs={{8,0},{16,8},{24,16},{32,24},{40,32},{48,40},{56,48},{64,56},{72,6... | collective-permute-start | bytes 1572872 | tf_op jit(solution)/shard_map/ppermute | solution.py:20
  9.3 40.0 %copy-start.14 = (s32[16384]{0:T(1024)S(1)}, s32[16384]{0:T(1024)}, u32[]{:S(2)}) copy-start(s32[16384]{0:T(1024)} %param.11) | copy-start | bytes 196612
  9.4 2.5 %collective-permute-start.1 = (bf16[16,8]{0,1:T(8,128)(2,1)S(1)}, bf16[16,8]{0,1:T(8,128)(2,1)S(1)}, u32[]{:S(2)}, u32[]{:S(2)}) collective-permute-start(bf16[16,8]{0,1:T(8,128)(2,1)S(1)} %pad_maximum_fusion), channel_id=1, source_target_pairs={{0,2},{1,3},{2,0},{3,1},{4,6},{5,7},{6,4},{7,5},{8,10},{9,11},{10,... | collective-permute-start | bytes 776 | tf_op jit(solution)/shard_map/ppermute | solution.py:25
  12.0 4.0 %collective-permute-start.2 = (bf16[32,8]{0,1:T(8,128)(2,1)S(1)}, bf16[32,8]{0,1:T(8,128)(2,1)S(1)}, u32[]{:S(2)}, u32[]{:S(2)}) collective-permute-start(bf16[32,8]{0,1:T(8,128)(2,1)S(1)} %pad_maximum_fusion.1), channel_id=1, source_target_pairs={{0,4},{1,5},{2,6},{3,7},{4,0},{5,1},{6,2},{7,3},{8,12},{9,13},{10,... | collective-permute-start | bytes 1544 | tf_op jit(solution)/shard_map/ppermute | solution.py:25
  16.2 7.2 %collective-permute-start.3 = (bf16[64]{0:T(256)(128)(2,1)S(1)}, bf16[64]{0:T(256)(128)(2,1)S(1)}, u32[]{:S(2)}, u32[]{:S(2)}) collective-permute-start(bf16[64]{0:T(256)(128)(2,1)S(1)} %dynamic-slice_bitcast_fusion), channel_id=1, source_target_pairs={{0,8},{8,0},{16,24},{24,16},{32,40},{40,32},{48,56},{56,48},{64,72... | collective-permute-start | bytes 392 | tf_op jit(solution)/shard_map/ppermute | solution.py:25
  23.4 7.0 %collective-permute-start.4 = (bf16[128]{0:T(256)(128)(2,1)S(1)}, bf16[128]{0:T(256)(128)(2,1)S(1)}, u32[]{:S(2)}, u32[]{:S(2)}) collective-permute-start(bf16[128]{0:T(256)(128)(2,1)S(1)} %pad_maximum_fusion.5), channel_id=1, source_target_pairs={{0,16},{8,24},{16,0},{24,8},{32,48},{40,56},{48,32},{56,40},{64,80... | collective-permute-start | bytes 776 | tf_op jit(solution)/shard_map/ppermute | solution.py:25
  27.8 42.2 %copy-start.3 = (bf16[512,512]{1,0:T(8,128)(2,1)}, bf16[512,512]{1,0:T(8,128)(2,1)S(1)}, u32[]{:S(2)}) copy-start(bf16[512,512]{1,0:T(8,128)(2,1)S(1)} %collective-permute-done.8.refs_3_) | copy-start | bytes 1572868
  27.8 15.4 %collective-permute-start.9 = (bf16[512,512]{1,0:T(8,128)(2,1)S(1)}, bf16[512,512]{1,0:T(8,128)(2,1)S(1)}, u32[]{:S(2)}, u32[]{:S(2)}) collective-permute-start(bf16[512,512]{1,0:T(8,128)(2,1)S(1)} %collective-permute-done.8.refs_3_), channel_id=1, source_target_pairs={{0,8},{8,16},{16,24},{24,32},{32,40},{40,48},{48,56},{56,64},{64,7... | collective-permute-start | bytes 1572872 | tf_op jit(solution)/shard_map/ppermute | solution.py:20
  29.1 20.3 %copy-start.13 = (bf16[512,512]{1,0:T(8,128)(2,1)}, bf16[512,512]{1,0:T(8,128)(2,1)S(1)}, u32[]{:S(2)}) copy-start(bf16[512,512]{1,0:T(8,128)(2,1)S(1)} %collective-permute-done.12.refs_6_) | copy-start | bytes 1572868
  29.1 18.9 %collective-permute-start.13 = (bf16[512,512]{1,0:T(8,128)(2,1)S(1)}, bf16[512,512]{1,0:T(8,128)(2,1)}, u32[]{:S(2)}, u32[]{:S(2)}) collective-permute-start(bf16[512,512]{1,0:T(8,128)(2,1)S(1)} %collective-permute-done.12.refs_6_), channel_id=1, source_target_pairs={{8,0},{16,8},{24,16},{32,24},{40,32},{48,40},{56,48},{64,56},{72,6... | collective-permute-start | bytes 1572872 | tf_op jit(solution)/shard_map/ppermute | solution.py:20
  30.5 11.4 %collective-permute-start.5 = (bf16[256]{0:T(256)(128)(2,1)S(1)}, bf16[256]{0:T(256)(128)(2,1)S(1)}, u32[]{:S(2)}, u32[]{:S(2)}) collective-permute-start(bf16[256]{0:T(256)(128)(2,1)S(1)} %pad_maximum_fusion.6), channel_id=1, source_target_pairs={{0,32},{8,40},{16,48},{24,56},{32,0},{40,8},{48,16},{56,24},{64,96... | collective-permute-start | bytes 1544 | tf_op jit(solution)/shard_map/ppermute | solution.py:25
  41.9 7.5 %collective-permute-start.6 = (bf16[512]{0:T(512)(128)(2,1)S(1)}, bf16[512]{0:T(512)(128)(2,1)S(1)}, u32[]{:S(2)}, u32[]{:S(2)}) collective-permute-start(bf16[512]{0:T(512)(128)(2,1)S(1)} %pad_maximum_fusion.4), channel_id=1, source_target_pairs={{0,64},{8,72},{16,80},{24,88},{32,96},{40,104},{48,112},{56,120},{... | collective-permute-start | bytes 3080 | tf_op jit(solution)/shard_map/ppermute | solution.py:25
  43.2 26.8 %copy-start.4 = (bf16[512,512]{1,0:T(8,128)(2,1)}, bf16[512,512]{1,0:T(8,128)(2,1)S(1)}, u32[]{:S(2)}) copy-start(bf16[512,512]{1,0:T(8,128)(2,1)S(1)} %collective-permute-done.9.refs_2_) | copy-start | bytes 1572868
  43.2 12.1 %collective-permute-start.10 = (bf16[512,512]{1,0:T(8,128)(2,1)S(1)}, bf16[512,512]{1,0:T(8,128)(2,1)S(1)}, u32[]{:S(2)}, u32[]{:S(2)}) collective-permute-start(bf16[512,512]{1,0:T(8,128)(2,1)S(1)} %collective-permute-done.9.refs_2_), channel_id=1, source_target_pairs={{0,8},{8,16},{16,24},{24,32},{32,40},{40,48},{48,56},{56,64},{64,7... | collective-permute-start | bytes 1572872 | tf_op jit(solution)/shard_map/ppermute | solution.py:20
  48.0 15.6 %collective-permute-start.14 = (bf16[512,512]{1,0:T(8,128)(2,1)}, bf16[512,512]{1,0:T(8,128)(2,1)}, u32[]{:S(2)}, u32[]{:S(2)}) collective-permute-start(bf16[512,512]{1,0:T(8,128)(2,1)} %collective-permute-done.13.refs_7_), channel_id=1, source_target_pairs={{8,0},{16,8},{24,16},{32,24},{40,32},{48,40},{56,48},{64,56},{72,6... | collective-permute-start | bytes 1572872 | tf_op jit(solution)/shard_map/ppermute | solution.py:20
  55.3 14.7 %copy-start.5 = (bf16[512,512]{1,0:T(8,128)(2,1)}, bf16[512,512]{1,0:T(8,128)(2,1)S(1)}, u32[]{:S(2)}) copy-start(bf16[512,512]{1,0:T(8,128)(2,1)S(1)} %collective-permute-done.10.refs_1_) | copy-start | bytes 1572868
  55.3 12.1 %collective-permute-start.11 = (bf16[512,512]{1,0:T(8,128)(2,1)S(1)}, bf16[512,512]{1,0:T(8,128)(2,1)S(1)}, u32[]{:S(2)}, u32[]{:S(2)}) collective-permute-start(bf16[512,512]{1,0:T(8,128)(2,1)S(1)} %collective-permute-done.10.refs_1_), channel_id=1, source_target_pairs={{0,8},{8,16},{16,24},{24,32},{32,40},{40,48},{48,56},{56,64},{64,7... | collective-permute-start | bytes 1572872 | tf_op jit(solution)/shard_map/ppermute | solution.py:20
  59.4 7.2 %collective-permute-start.7 = (bf16[1024]{0:T(1024)(128)(2,1)S(1)}, bf16[1024]{0:T(1024)(128)(2,1)S(1)}, u32[]{:S(2)}, u32[]{:S(2)}) collective-permute-start(bf16[1024]{0:T(1024)(128)(2,1)S(1)} %pad_maximum_fusion.3), channel_id=1, source_target_pairs={{0,128},{8,136},{16,144},{24,152},{32,160},{40,168},{48,176},{56,1... | collective-permute-start | bytes 6152 | tf_op jit(solution)/shard_map/ppermute | solution.py:25
  63.6 27.1 %collective-permute-start.15 = (bf16[512,512]{1,0:T(8,128)(2,1)}, bf16[512,512]{1,0:T(8,128)(2,1)}, u32[]{:S(2)}, u32[]{:S(2)}) collective-permute-start(bf16[512,512]{1,0:T(8,128)(2,1)} %collective-permute-done.14.refs_8_), channel_id=1, source_target_pairs={{8,0},{16,8},{24,16},{32,24},{40,32},{48,40},{56,48},{64,56},{72,6... | collective-permute-start | bytes 1572872 | tf_op jit(solution)/shard_map/ppermute | solution.py:20
  66.6 3.4 %copy-start.2 = (s32[512,1]{1,0:T(8,128)}, s32[512,1]{1,0:T(8,128)S(1)}, u32[]{:S(2)}) copy-start(s32[512,1]{1,0:T(8,128)S(1)} %copy.17.ids_own) | copy-start | bytes 6148
  67.3 2.7 %copy-start.6 = (bf16[512,512]{1,0:T(8,128)(2,1)}, bf16[512,512]{1,0:T(8,128)(2,1)S(1)}, u32[]{:S(2)}) copy-start(bf16[512,512]{1,0:T(8,128)(2,1)S(1)} %collective-permute-done.11.refs_0_) | copy-start | bytes 1572868
  70.9 32.8 %all-to-all-start = ((f32[256,1,8]{2,1,0:T(1,128)}), f32[256,1,8]{2,1,0:T(1,128)S(1)}, u32[]{:S(2)}, u32[]{:S(2)}) async-start(f32[256,1,8]{2,1,0:T(1,128)} %bitcast.4), calls=%async_computation | async-start | bytes 262144 | tf_op jit(solution)/shard_map/all_to_all | solution.py:187
  90.8 7.1 %copy-start.7 = (bf16[512,512]{1,0:T(8,128)(2,1)S(1)}, bf16[512,512]{1,0:T(8,128)(2,1)}, u32[]{:S(2)}) copy-start(bf16[512,512]{1,0:T(8,128)(2,1)} %param.9) | copy-start | bytes 1572868
  90.8 7.1 %copy-start.8 = (bf16[512,512]{1,0:T(8,128)(2,1)S(1)}, bf16[512,512]{1,0:T(8,128)(2,1)}, u32[]{:S(2)}) copy-start(bf16[512,512]{1,0:T(8,128)(2,1)} %param.8) | copy-start | bytes 1572868
  90.8 7.1 %copy-start.10 = (bf16[512,512]{1,0:T(8,128)(2,1)S(1)}, bf16[512,512]{1,0:T(8,128)(2,1)}, u32[]{:S(2)}) copy-start(bf16[512,512]{1,0:T(8,128)(2,1)} %param.7) | copy-start | bytes 1572868
  90.8 7.1 %copy-start.12 = (bf16[512,512]{1,0:T(8,128)(2,1)S(1)}, bf16[512,512]{1,0:T(8,128)(2,1)}, u32[]{:S(2)}) copy-start(bf16[512,512]{1,0:T(8,128)(2,1)} %param.10) | copy-start | bytes 1572868

commit v12 on v10

--- a/solution.py
+++ b/solution.py
@@ -182,9 +182,10 @@
     ids_rdr = lax.dynamic_slice_in_dim(ids_pad, here * rows + hist, hist + rows)
 
     filter_part = filter_sums(ids_own, ids_src, ahead[::-1], conv_grad)
+    conv, mixed_grad = local_conv(taps, ids_own, ids_src, ids_rdr, skip_gain, ahead[::-1], behind)
+    filter_part, conv, mixed_grad = lax.optimization_barrier((filter_part, conv, mixed_grad))
     spread = lax.all_to_all(filter_part.reshape(count, FLEN // count), "ctx", 0, 0, tiled=True)
     block_sum = jnp.sum(spread, axis=0).reshape(groups, FLEN // (count * groups))
-    conv, mixed_grad = local_conv(taps, ids_own, ids_src, ids_rdr, skip_gain, ahead[::-1], behind)
 
     mixed_out = (query_in.astype(jnp.float32) * conv).astype(jnp.bfloat16)
     query_grad = (out_grad.astype(jnp.float32) * conv).astype(jnp.bfloat16)

time: 104 us -> 115 us (1.11)
  blocking collectives: 0 us -> 16.7 us
  starting transfers between devices: 67.5 us -> 58.2 us
  waiting for transfers between devices: 14.7 us -> 19.3 us
    all_to_all x0 -> x1, blocking collectives: none -> 16.7 us  [shards(): lax.all_to_all(filter_part.reshape(count, FLEN // count), 'ctx', 0, 0, ti...]
    all_to_all x1 -> x0, starting transfers between devices: 11.7 us -> none  [shards(): lax.all_to_all(filter_part.reshape(count, FLEN // count), 'ctx', 0, 0, ti...]
    ppermute x8, waiting for transfers between devices: 6.76 us -> 11.6 us  [swapped(): lax.ppermute(value, axis, [(source, source ^ bit) for source in range(cou...]
    ppermute x8, starting transfers between devices: 28.6 us -> 30.6 us  [swapped(): lax.ppermute(value, axis, [(source, source ^ bit) for source in range(cou...]
  transfers between devices with their start and end apart: 18 -> 17, of which waited for: 8 -> 8; matrix products, arithmetic and copies ran while one was open for 7% -> 7% of each run, Pallas kernels for 9% -> 2%
where the time goes in v12:
time: 115 us
  starting transfers between devices  58.2 us (51%)
  waiting for transfers between devices  19.3 us (17%)
  blocking collectives  16.7 us (15%)
  Pallas kernels  9.61 us (8%)
  other arithmetic  6.07 us (5%)
  local copies, waits for them, and re-layouts  4 us (3%)
    ppermute x8, starting transfers between devices, swapped(): lax.ppermute(value, axis, [(source, source ^ bit) for source in range(cou...  30.6 us
    ppermute x8, starting transfers between devices, shifted(): lax.ppermute(value, axis, [(source, source + steps) for source in range(l...  17.3 us
    all_to_all x1, blocking collectives, shards(): lax.all_to_all(filter_part.reshape(count, FLEN // count), 'ctx', 0, 0, ti...  16.7 us
    ppermute x8, waiting for transfers between devices, swapped(): lax.ppermute(value, axis, [(source, source ^ bit) for source in range(cou...  11.6 us
    all_to_all x1, starting transfers between devices, shards(): summed = lax.all_to_all(block_sum, 'tp', 0, 0, tiled=True).T  10.3 us
    pallas_call x1, Pallas kernels, local_conv(): pl.pallas_call(conv_kernel, out_shape=(jax.ShapeDtypeStruct((own, width),...  7.01 us
    ppermute x8, waiting for transfers between devices, shifted(): lax.ppermute(value, axis, [(source, source + steps) for source in range(l...  6.39 us
    convert_element_type x1, other arithmetic, shards(): value_grad = (mixed_grad * key_in.astype(jnp.float32)).astype(jnp.bfloat16)  3.26 us
  transfers between devices with their start and end apart: 17, of which 8 were waited for; matrix products, arithmetic and copies ran while one was open for 7% of the time, Pallas kernels for 2%

profile of v12, /device:TPU:1, one launch (start us, length us, event | category | flops | bytes accessed | tf_op | source)
XLA Modules:
  0.0 114.8 jit_solution(3343392225686981336)
XLA Ops:
  0.6 0.8 copy.33
  1.4 3.2 %collective-permute-start.4 = (bf16[8,8]{0,1:T(8,128)(2,1)S(1)}, bf16[8,8]{0,1:T(8,128)(2,1)S(1)}, u32[]{:S(2)}, u32[]{:S(2)}) collective-permute-start(bf16[8,8]{0,1:T(8,128)(2,1)S(1)} %copy.33), channel_id=1, source_target_pairs={{0,1},{1,0},{2,3},{3,2},{4,5},{5,4},{6,7},{7,6},{8,9},{9,8},{10,11... | collective-permute-start | bytes 392 | tf_op jit(solution)/shard_map/ppermute | solution.py:25
  4.6 1.3 %fusion.2.refs_4_ = bf16[512,512]{1,0:T(8,128)(2,1)S(1)} fusion(bf16[512,512]{1,0:T(8,128)(2,1)} %param.9, bf16[512,512]{1,0:T(8,128)(2,1)} %param.8), kind=kLoop, calls=%fused_computation.8 | loop fusion | flops 1048576 | bytes 1572864 | tf_op jit(solution)/shard_map/convert_element_type | solution.py:168
  6.0 1.9 %collective-permute-start = (bf16[512,512]{1,0:T(8,128)(2,1)S(1)}, bf16[512,512]{1,0:T(8,128)(2,1)S(1)}, u32[]{:S(2)}, u32[]{:S(2)}) collective-permute-start(bf16[512,512]{1,0:T(8,128)(2,1)S(1)} %fusion.2.refs_4_), channel_id=1, source_target_pairs={{0,8},{8,16},{16,24},{24,32},{32,40},{40,48},{48,56},{56,64},{64,7... | collective-permute-start | bytes 1572872 | tf_op jit(solution)/shard_map/ppermute | solution.py:20
  7.8 0.1 fusion.4.refs_5_
  8.0 1.3 %collective-permute-start.12 = (bf16[512,512]{1,0:T(8,128)(2,1)S(1)}, bf16[512,512]{1,0:T(8,128)(2,1)S(1)}, u32[]{:S(2)}, u32[]{:S(2)}) collective-permute-start(bf16[512,512]{1,0:T(8,128)(2,1)S(1)} %fusion.4.refs_5_), channel_id=1, source_target_pairs={{8,0},{16,8},{24,16},{32,24},{40,32},{48,40},{56,48},{64,56},{72,6... | collective-permute-start | bytes 1572872 | tf_op jit(solution)/shard_map/ppermute | solution.py:20
  9.3 0.1 pad_maximum_fusion
  9.4 1.3 %collective-permute-start.5 = (bf16[16,8]{0,1:T(8,128)(2,1)S(1)}, bf16[16,8]{0,1:T(8,128)(2,1)S(1)}, u32[]{:S(2)}, u32[]{:S(2)}) collective-permute-start(bf16[16,8]{0,1:T(8,128)(2,1)S(1)} %pad_maximum_fusion), channel_id=1, source_target_pairs={{0,2},{1,3},{2,0},{3,1},{4,6},{5,7},{6,4},{7,5},{8,10},{9,11},{10,... | collective-permute-start | bytes 776 | tf_op jit(solution)/shard_map/ppermute | solution.py:25
  10.7 1.1 collective-permute-done.5
  11.9 0.1 broadcast_select_fusion.3
  12.0 0.1 pad_maximum_fusion.1
  12.0 2.9 %collective-permute-start.6 = (bf16[32,8]{0,1:T(8,128)(2,1)S(1)}, bf16[32,8]{0,1:T(8,128)(2,1)S(1)}, u32[]{:S(2)}, u32[]{:S(2)}) collective-permute-start(bf16[32,8]{0,1:T(8,128)(2,1)S(1)} %pad_maximum_fusion.1), channel_id=1, source_target_pairs={{0,4},{1,5},{2,6},{3,7},{4,0},{5,1},{6,2},{7,3},{8,12},{9,13},{10,... | collective-permute-start | bytes 1544 | tf_op jit(solution)/shard_map/ppermute | solution.py:25
  15.0 1.0 collective-permute-done.6
  16.0 0.1 broadcast_select_fusion.5
  16.1 0.1 pad_maximum_fusion.2
  16.2 2.6 %collective-permute-start.7 = (bf16[64]{0:T(256)(128)(2,1)S(1)}, bf16[64]{0:T(256)(128)(2,1)S(1)}, u32[]{:S(2)}, u32[]{:S(2)}) collective-permute-start(bf16[64]{0:T(256)(128)(2,1)S(1)} %dynamic-slice_bitcast_fusion), channel_id=1, source_target_pairs={{0,8},{8,0},{16,24},{24,16},{32,40},{40,32},{48,56},{56,48},{64,72... | collective-permute-start | bytes 392 | tf_op jit(solution)/shard_map/ppermute | solution.py:25
  18.7 4.6 %collective-permute-done.7 = bf16[64]{0:T(256)(128)(2,1)S(1)} collective-permute-done((bf16[64]{0:T(256)(128)(2,1)S(1)}, bf16[64]{0:T(256)(128)(2,1)S(1)}, u32[]{:S(2)}, u32[]{:S(2)}) %collective-permute-start.7) | collective-permute-done | bytes 160 | tf_op jit(solution)/shard_map/ppermute | solution.py:25
  23.3 0.1 pad_maximum_fusion.5
  23.4 4.3 %collective-permute-start.8 = (bf16[128]{0:T(256)(128)(2,1)S(1)}, bf16[128]{0:T(256)(128)(2,1)S(1)}, u32[]{:S(2)}, u32[]{:S(2)}) collective-permute-start(bf16[128]{0:T(256)(128)(2,1)S(1)} %pad_maximum_fusion.5), channel_id=1, source_target_pairs={{0,16},{8,24},{16,0},{24,8},{32,48},{40,56},{48,32},{56,40},{64,80... | collective-permute-start | bytes 776 | tf_op jit(solution)/shard_map/ppermute | solution.py:25
  27.8 1.3 %collective-permute-start.1 = (bf16[512,512]{1,0:T(8,128)(2,1)S(1)}, bf16[512,512]{1,0:T(8,128)(2,1)S(1)}, u32[]{:S(2)}, u32[]{:S(2)}) collective-permute-start(bf16[512,512]{1,0:T(8,128)(2,1)S(1)} %collective-permute-done.refs_3_), channel_id=1, source_target_pairs={{0,8},{8,16},{16,24},{24,32},{32,40},{40,48},{48,56},{56,64},{64,7... | collective-permute-start | bytes 1572872 | tf_op jit(solution)/shard_map/ppermute | solution.py:20
  29.1 1.3 %collective-permute-start.13 = (bf16[512,512]{1,0:T(8,128)(2,1)S(1)}, bf16[512,512]{1,0:T(8,128)(2,1)}, u32[]{:S(2)}, u32[]{:S(2)}) collective-permute-start(bf16[512,512]{1,0:T(8,128)(2,1)S(1)} %collective-permute-done.12.refs_6_), channel_id=1, source_target_pairs={{8,0},{16,8},{24,16},{32,24},{40,32},{48,40},{56,48},{64,56},{72,6... | collective-permute-start | bytes 1572872 | tf_op jit(solution)/shard_map/ppermute | solution.py:20
  30.4 0.1 broadcast_select_fusion.11
  30.5 6.5 %collective-permute-start.9 = (bf16[256]{0:T(256)(128)(2,1)S(1)}, bf16[256]{0:T(256)(128)(2,1)S(1)}, u32[]{:S(2)}, u32[]{:S(2)}) collective-permute-start(bf16[256]{0:T(256)(128)(2,1)S(1)} %pad_maximum_fusion.6), channel_id=1, source_target_pairs={{0,32},{8,40},{16,48},{24,56},{32,0},{40,8},{48,16},{56,24},{64,96... | collective-permute-start | bytes 1544 | tf_op jit(solution)/shard_map/ppermute | solution.py:25
  37.0 4.9 %collective-permute-done.9 = bf16[256]{0:T(256)(128)(2,1)S(1)} collective-permute-done((bf16[256]{0:T(256)(128)(2,1)S(1)}, bf16[256]{0:T(256)(128)(2,1)S(1)}, u32[]{:S(2)}, u32[]{:S(2)}) %collective-permute-start.9) | collective-permute-done | bytes 544 | tf_op jit(solution)/shard_map/ppermute | solution.py:25
  41.9 1.3 %collective-permute-start.10 = (bf16[512]{0:T(512)(128)(2,1)S(1)}, bf16[512]{0:T(512)(128)(2,1)S(1)}, u32[]{:S(2)}, u32[]{:S(2)}) collective-permute-start(bf16[512]{0:T(512)(128)(2,1)S(1)} %pad_maximum_fusion.4), channel_id=1, source_target_pairs={{0,64},{8,72},{16,80},{24,88},{32,96},{40,104},{48,112},{56,120},{... | collective-permute-start | bytes 3080 | tf_op jit(solution)/shard_map/ppermute | solution.py:25
  43.2 4.8 %collective-permute-start.2 = (bf16[512,512]{1,0:T(8,128)(2,1)S(1)}, bf16[512,512]{1,0:T(8,128)(2,1)S(1)}, u32[]{:S(2)}, u32[]{:S(2)}) collective-permute-start(bf16[512,512]{1,0:T(8,128)(2,1)S(1)} %collective-permute-done.1.refs_2_), channel_id=1, source_target_pairs={{0,8},{8,16},{16,24},{24,32},{32,40},{40,48},{48,56},{56,64},{64,7... | collective-permute-start | bytes 1572872 | tf_op jit(solution)/shard_map/ppermute | solution.py:20
  48.0 1.3 %collective-permute-start.14 = (bf16[512,512]{1,0:T(8,128)(2,1)}, bf16[512,512]{1,0:T(8,128)(2,1)}, u32[]{:S(2)}, u32[]{:S(2)}) collective-permute-start(bf16[512,512]{1,0:T(8,128)(2,1)} %collective-permute-done.13.refs_7_), channel_id=1, source_target_pairs={{8,0},{16,8},{24,16},{32,24},{40,32},{48,40},{56,48},{64,56},{72,6... | collective-permute-start | bytes 1572872 | tf_op jit(solution)/shard_map/ppermute | solution.py:20
  49.4 5.8 %collective-permute-done.2.refs_1_ = bf16[512,512]{1,0:T(8,128)(2,1)S(1)} collective-permute-done((bf16[512,512]{1,0:T(8,128)(2,1)S(1)}, bf16[512,512]{1,0:T(8,128)(2,1)S(1)}, u32[]{:S(2)}, u32[]{:S(2)}) %collective-permute-start.2) | collective-permute-done | bytes 524320 | tf_op jit(solution)/shard_map/ppermute | solution.py:20
  55.3 4.1 %collective-permute-start.3 = (bf16[512,512]{1,0:T(8,128)(2,1)S(1)}, bf16[512,512]{1,0:T(8,128)(2,1)S(1)}, u32[]{:S(2)}, u32[]{:S(2)}) collective-permute-start(bf16[512,512]{1,0:T(8,128)(2,1)S(1)} %collective-permute-done.2.refs_1_), channel_id=1, source_target_pairs={{0,8},{8,16},{16,24},{24,32},{32,40},{40,48},{48,56},{56,64},{64,7... | collective-permute-start | bytes 1572872 | tf_op jit(solution)/shard_map/ppermute | solution.py:20
  59.5 1.3 %collective-permute-start.15 = (bf16[512,512]{1,0:T(8,128)(2,1)}, bf16[512,512]{1,0:T(8,128)(2,1)}, u32[]{:S(2)}, u32[]{:S(2)}) collective-permute-start(bf16[512,512]{1,0:T(8,128)(2,1)} %collective-permute-done.14.refs_8_), channel_id=1, source_target_pairs={{8,0},{16,8},{24,16},{32,24},{40,32},{48,40},{56,48},{64,56},{72,6... | collective-permute-start | bytes 1572872 | tf_op jit(solution)/shard_map/ppermute | solution.py:20
  60.8 8.4 %collective-permute-start.11 = (bf16[1024]{0:T(1024)(128)(2,1)S(1)}, bf16[1024]{0:T(1024)(128)(2,1)S(1)}, u32[]{:S(2)}, u32[]{:S(2)}) collective-permute-start(bf16[1024]{0:T(1024)(128)(2,1)S(1)} %pad_maximum_fusion.3), channel_id=1, source_target_pairs={{0,128},{8,136},{16,144},{24,152},{32,160},{40,168},{48,176},{56,1... | collective-permute-start | bytes 6152 | tf_op jit(solution)/shard_map/ppermute | solution.py:25
  69.2 0.1 fusion.11
  69.2 0.6 reshape.49.ids_src
  69.9 0.6 reshape.50.ids_rdr
  70.5 0.1 rev.3
  70.7 0.1 copy.32.ids_own
  70.9 0.7 fusion.10
  71.6 2.6 %shard_map.110 = f32[1,2560]{1,0:T(1,128)S(1)} custom-call(s32[512,1]{1,0:T(8,128)S(1)} %copy.32.ids_own, s32[1,2560]{1,0:T(1,128)S(1)} %bitcast.18, bf16[512,512]{1,0:T(8,128)(2,1)S(1)} %collective-permute-done.3.refs_0_, bf16[512,512]{1,0:T(8,128)(2,1)S(1)} %collective-permute-done.2.refs_1_, bf16[512,512]{1,0:T(8,128)(2,1)S(1)} %collective-permute-done.1.refs_2_, ...), custom_call_target="tpu_custom_call" | custom-call | tf_op jit(solution)/shard_map/pallas_call | solution.py:128
  74.2 0.1 slice.4
  74.3 0.5 collective-permute-done.15.refs_9_
  74.8 7.0 %shard_map.111 = (f32[512,512]{1,0:T(8,128)}, f32[512,512]{1,0:T(8,128)}) custom-call(f32[1,3072]{1,0:T(1,128)} %bitcast.21, s32[512,1]{1,0:T(8,128)} %copy-done.2, s32[1,2560]{1,0:T(1,128)} %reshape.49.ids_src, s32[1,2560]{1,0:T(1,128)} %reshape.50.ids_rdr, f32[1,512]{1,0:T(1,128)} %bitcast.25, bf16[512,512]{1,0:T(8,128)(2,1)} %copy-done.6, ...), custom_call_target="tpu_custom_call" | custom-call | tf_op jit(solution)/shard_map/pallas_call | solution.py:141
  81.8 0.1 all_to_all.12
  81.9 16.7 %all_to_all.18 = f32[32,1,64]{2,1,0:T(1,128)S(1)} all-to-all(f32[32,1,64]{2,1,0:T(1,128)S(1)} %all_to_all.12), channel_id=1, replica_groups=mesh['ctx'=32,'tp'=8] {'ctx'}, dimensions={0} | all-to-all | bytes 16384 | tf_op jit(solution)/shard_map/all_to_all | solution.py:187
  98.6 0.7 all_to_all.14
  99.3 10.3 %all-to-all-start.1 = ((f32[8,1,8]{2,1,0:T(1,128)}), f32[8,1,8]{2,1,0:T(1,128)S(1)}, u32[]{:S(2)}, u32[]{:S(2)}) async-start(f32[8,1,8]{2,1,0:T(1,128)} %bitcast.6), calls=%async_computation.1 | async-start | bytes 8192 | tf_op jit(solution)/shard_map/all_to_all | solution.py:195
  109.6 3.3 %fusion.1 = (bf16[512,512]{1,0:T(8,128)(2,1)}, bf16[512,512]{1,0:T(8,128)(2,1)}, bf16[512,512]{1,0:T(8,128)(2,1)}, bf16[512,512]{1,0:T(8,128)(2,1)}) fusion(f32[512,512]{1,0:T(8,128)} %get-tuple-element.13, bf16[512,512]{1,0:T(8,128)(2,1)S(1)} %copy-done.8, bf16[512,512]{1,0:T(8,128)(2,1)S(1)} %copy-done.7, f32[512,512]{1,0:T(8,128)} %get-tuple-element.12, ...), kind=kLoop, calls=%fused_computation.7 | loop fusion | flops 3145728 | bytes 6291456 | tf_op jit(solution)/shard_map/convert_element_type | solution.py:193
  112.9 1.2 %all-to-all-done.1 = f32[8,1,8]{2,1,0:T(1,128)S(1)} async-done(((f32[8,1,8]{2,1,0:T(1,128)}), f32[8,1,8]{2,1,0:T(1,128)S(1)}, u32[]{:S(2)}, u32[]{:S(2)}) %all-to-all-start.1) | async-done | bytes 288 | tf_op jit(solution)/shard_map/all_to_all | solution.py:195
  114.1 0.7 copy.40
  (57 shorter events, 0.4 us)
Async XLA Ops:
  1.4 6.4 %copy-start.9 = (bf16[512,512]{1,0:T(8,128)(2,1)S(1)}, bf16[512,512]{1,0:T(8,128)(2,1)}, u32[]{:S(2)}) copy-start(bf16[512,512]{1,0:T(8,128)(2,1)} %param.7) | copy-start | bytes 1572868
  1.4 6.4 %copy-start.11 = (bf16[512,512]{1,0:T(8,128)(2,1)S(1)}, bf16[512,512]{1,0:T(8,128)(2,1)}, u32[]{:S(2)}) copy-start(bf16[512,512]{1,0:T(8,128)(2,1)} %param.10) | copy-start | bytes 1572868
  1.4 7.9 %collective-permute-start.4 = (bf16[8,8]{0,1:T(8,128)(2,1)S(1)}, bf16[8,8]{0,1:T(8,128)(2,1)S(1)}, u32[]{:S(2)}, u32[]{:S(2)}) collective-permute-start(bf16[8,8]{0,1:T(8,128)(2,1)S(1)} %copy.33), channel_id=1, source_target_pairs={{0,1},{1,0},{2,3},{3,2},{4,5},{5,4},{6,7},{7,6},{8,9},{9,8},{10,11... | collective-permute-start | bytes 392 | tf_op jit(solution)/shard_map/ppermute | solution.py:25
  5.9 65.6 %copy-start = (bf16[512,512]{1,0:T(8,128)(2,1)}, bf16[512,512]{1,0:T(8,128)(2,1)S(1)}, u32[]{:S(2)}) copy-start(bf16[512,512]{1,0:T(8,128)(2,1)S(1)} %fusion.2.refs_4_) | copy-start | bytes 1572868
  6.0 21.8 %collective-permute-start = (bf16[512,512]{1,0:T(8,128)(2,1)S(1)}, bf16[512,512]{1,0:T(8,128)(2,1)S(1)}, u32[]{:S(2)}, u32[]{:S(2)}) collective-permute-start(bf16[512,512]{1,0:T(8,128)(2,1)S(1)} %fusion.2.refs_4_), channel_id=1, source_target_pairs={{0,8},{8,16},{16,24},{24,32},{32,40},{40,48},{48,56},{56,64},{64,7... | collective-permute-start | bytes 1572872 | tf_op jit(solution)/shard_map/ppermute | solution.py:20
  8.0 66.2 %copy-start.1 = (bf16[512,512]{1,0:T(8,128)(2,1)}, bf16[512,512]{1,0:T(8,128)(2,1)S(1)}, u32[]{:S(2)}) copy-start(bf16[512,512]{1,0:T(8,128)(2,1)S(1)} %fusion.4.refs_5_) | copy-start | bytes 1572868
  8.0 21.1 %collective-permute-start.12 = (bf16[512,512]{1,0:T(8,128)(2,1)S(1)}, bf16[512,512]{1,0:T(8,128)(2,1)S(1)}, u32[]{:S(2)}, u32[]{:S(2)}) collective-permute-start(bf16[512,512]{1,0:T(8,128)(2,1)S(1)} %fusion.4.refs_5_), channel_id=1, source_target_pairs={{8,0},{16,8},{24,16},{32,24},{40,32},{48,40},{56,48},{64,56},{72,6... | collective-permute-start | bytes 1572872 | tf_op jit(solution)/shard_map/ppermute | solution.py:20
  9.3 40.0 %copy-start.14 = (s32[16384]{0:T(1024)S(1)}, s32[16384]{0:T(1024)}, u32[]{:S(2)}) copy-start(s32[16384]{0:T(1024)} %param.11) | copy-start | bytes 196612
  9.4 2.5 %collective-permute-start.5 = (bf16[16,8]{0,1:T(8,128)(2,1)S(1)}, bf16[16,8]{0,1:T(8,128)(2,1)S(1)}, u32[]{:S(2)}, u32[]{:S(2)}) collective-permute-start(bf16[16,8]{0,1:T(8,128)(2,1)S(1)} %pad_maximum_fusion), channel_id=1, source_target_pairs={{0,2},{1,3},{2,0},{3,1},{4,6},{5,7},{6,4},{7,5},{8,10},{9,11},{10,... | collective-permute-start | bytes 776 | tf_op jit(solution)/shard_map/ppermute | solution.py:25
  12.0 4.0 %collective-permute-start.6 = (bf16[32,8]{0,1:T(8,128)(2,1)S(1)}, bf16[32,8]{0,1:T(8,128)(2,1)S(1)}, u32[]{:S(2)}, u32[]{:S(2)}) collective-permute-start(bf16[32,8]{0,1:T(8,128)(2,1)S(1)} %pad_maximum_fusion.1), channel_id=1, source_target_pairs={{0,4},{1,5},{2,6},{3,7},{4,0},{5,1},{6,2},{7,3},{8,12},{9,13},{10,... | collective-permute-start | bytes 1544 | tf_op jit(solution)/shard_map/ppermute | solution.py:25
  16.2 7.2 %collective-permute-start.7 = (bf16[64]{0:T(256)(128)(2,1)S(1)}, bf16[64]{0:T(256)(128)(2,1)S(1)}, u32[]{:S(2)}, u32[]{:S(2)}) collective-permute-start(bf16[64]{0:T(256)(128)(2,1)S(1)} %dynamic-slice_bitcast_fusion), channel_id=1, source_target_pairs={{0,8},{8,0},{16,24},{24,16},{32,40},{40,32},{48,56},{56,48},{64,72... | collective-permute-start | bytes 392 | tf_op jit(solution)/shard_map/ppermute | solution.py:25
  23.4 7.0 %collective-permute-start.8 = (bf16[128]{0:T(256)(128)(2,1)S(1)}, bf16[128]{0:T(256)(128)(2,1)S(1)}, u32[]{:S(2)}, u32[]{:S(2)}) collective-permute-start(bf16[128]{0:T(256)(128)(2,1)S(1)} %pad_maximum_fusion.5), channel_id=1, source_target_pairs={{0,16},{8,24},{16,0},{24,8},{32,48},{40,56},{48,32},{56,40},{64,80... | collective-permute-start | bytes 776 | tf_op jit(solution)/shard_map/ppermute | solution.py:25
  27.8 46.4 %copy-start.3 = (bf16[512,512]{1,0:T(8,128)(2,1)}, bf16[512,512]{1,0:T(8,128)(2,1)S(1)}, u32[]{:S(2)}) copy-start(bf16[512,512]{1,0:T(8,128)(2,1)S(1)} %collective-permute-done.refs_3_) | copy-start | bytes 1572868
  27.8 15.4 %collective-permute-start.1 = (bf16[512,512]{1,0:T(8,128)(2,1)S(1)}, bf16[512,512]{1,0:T(8,128)(2,1)S(1)}, u32[]{:S(2)}, u32[]{:S(2)}) collective-permute-start(bf16[512,512]{1,0:T(8,128)(2,1)S(1)} %collective-permute-done.refs_3_), channel_id=1, source_target_pairs={{0,8},{8,16},{16,24},{24,32},{32,40},{40,48},{48,56},{56,64},{64,7... | collective-permute-start | bytes 1572872 | tf_op jit(solution)/shard_map/ppermute | solution.py:20
  29.1 20.3 %copy-start.13 = (bf16[512,512]{1,0:T(8,128)(2,1)}, bf16[512,512]{1,0:T(8,128)(2,1)S(1)}, u32[]{:S(2)}) copy-start(bf16[512,512]{1,0:T(8,128)(2,1)S(1)} %collective-permute-done.12.refs_6_) | copy-start | bytes 1572868
  29.1 18.9 %collective-permute-start.13 = (bf16[512,512]{1,0:T(8,128)(2,1)S(1)}, bf16[512,512]{1,0:T(8,128)(2,1)}, u32[]{:S(2)}, u32[]{:S(2)}) collective-permute-start(bf16[512,512]{1,0:T(8,128)(2,1)S(1)} %collective-permute-done.12.refs_6_), channel_id=1, source_target_pairs={{8,0},{16,8},{24,16},{32,24},{40,32},{48,40},{56,48},{64,56},{72,6... | collective-permute-start | bytes 1572872 | tf_op jit(solution)/shard_map/ppermute | solution.py:20
  30.5 11.4 %collective-permute-start.9 = (bf16[256]{0:T(256)(128)(2,1)S(1)}, bf16[256]{0:T(256)(128)(2,1)S(1)}, u32[]{:S(2)}, u32[]{:S(2)}) collective-permute-start(bf16[256]{0:T(256)(128)(2,1)S(1)} %pad_maximum_fusion.6), channel_id=1, source_target_pairs={{0,32},{8,40},{16,48},{24,56},{32,0},{40,8},{48,16},{56,24},{64,96... | collective-permute-start | bytes 1544 | tf_op jit(solution)/shard_map/ppermute | solution.py:25
  41.9 7.5 %collective-permute-start.10 = (bf16[512]{0:T(512)(128)(2,1)S(1)}, bf16[512]{0:T(512)(128)(2,1)S(1)}, u32[]{:S(2)}, u32[]{:S(2)}) collective-permute-start(bf16[512]{0:T(512)(128)(2,1)S(1)} %pad_maximum_fusion.4), channel_id=1, source_target_pairs={{0,64},{8,72},{16,80},{24,88},{32,96},{40,104},{48,112},{56,120},{... | collective-permute-start | bytes 3080 | tf_op jit(solution)/shard_map/ppermute | solution.py:25
  43.2 31.0 %copy-start.4 = (bf16[512,512]{1,0:T(8,128)(2,1)}, bf16[512,512]{1,0:T(8,128)(2,1)S(1)}, u32[]{:S(2)}) copy-start(bf16[512,512]{1,0:T(8,128)(2,1)S(1)} %collective-permute-done.1.refs_2_) | copy-start | bytes 1572868
  43.2 12.1 %collective-permute-start.2 = (bf16[512,512]{1,0:T(8,128)(2,1)S(1)}, bf16[512,512]{1,0:T(8,128)(2,1)S(1)}, u32[]{:S(2)}, u32[]{:S(2)}) collective-permute-start(bf16[512,512]{1,0:T(8,128)(2,1)S(1)} %collective-permute-done.1.refs_2_), channel_id=1, source_target_pairs={{0,8},{8,16},{16,24},{24,32},{32,40},{40,48},{48,56},{56,64},{64,7... | collective-permute-start | bytes 1572872 | tf_op jit(solution)/shard_map/ppermute | solution.py:20
  48.0 11.4 %collective-permute-start.14 = (bf16[512,512]{1,0:T(8,128)(2,1)}, bf16[512,512]{1,0:T(8,128)(2,1)}, u32[]{:S(2)}, u32[]{:S(2)}) collective-permute-start(bf16[512,512]{1,0:T(8,128)(2,1)} %collective-permute-done.13.refs_7_), channel_id=1, source_target_pairs={{8,0},{16,8},{24,16},{32,24},{40,32},{48,40},{56,48},{64,56},{72,6... | collective-permute-start | bytes 1572872 | tf_op jit(solution)/shard_map/ppermute | solution.py:20
  55.3 18.9 %copy-start.5 = (bf16[512,512]{1,0:T(8,128)(2,1)}, bf16[512,512]{1,0:T(8,128)(2,1)S(1)}, u32[]{:S(2)}) copy-start(bf16[512,512]{1,0:T(8,128)(2,1)S(1)} %collective-permute-done.2.refs_1_) | copy-start | bytes 1572868
  55.3 16.3 %collective-permute-start.3 = (bf16[512,512]{1,0:T(8,128)(2,1)S(1)}, bf16[512,512]{1,0:T(8,128)(2,1)S(1)}, u32[]{:S(2)}, u32[]{:S(2)}) collective-permute-start(bf16[512,512]{1,0:T(8,128)(2,1)S(1)} %collective-permute-done.2.refs_1_), channel_id=1, source_target_pairs={{0,8},{8,16},{16,24},{24,32},{32,40},{40,48},{48,56},{56,64},{64,7... | collective-permute-start | bytes 1572872 | tf_op jit(solution)/shard_map/ppermute | solution.py:20
  59.5 15.3 %collective-permute-start.15 = (bf16[512,512]{1,0:T(8,128)(2,1)}, bf16[512,512]{1,0:T(8,128)(2,1)}, u32[]{:S(2)}, u32[]{:S(2)}) collective-permute-start(bf16[512,512]{1,0:T(8,128)(2,1)} %collective-permute-done.14.refs_8_), channel_id=1, source_target_pairs={{8,0},{16,8},{24,16},{32,24},{40,32},{48,40},{56,48},{64,56},{72,6... | collective-permute-start | bytes 1572872 | tf_op jit(solution)/shard_map/ppermute | solution.py:20
  60.8 10.1 %collective-permute-start.11 = (bf16[1024]{0:T(1024)(128)(2,1)S(1)}, bf16[1024]{0:T(1024)(128)(2,1)S(1)}, u32[]{:S(2)}, u32[]{:S(2)}) collective-permute-start(bf16[1024]{0:T(1024)(128)(2,1)S(1)} %pad_maximum_fusion.3), channel_id=1, source_target_pairs={{0,128},{8,136},{16,144},{24,152},{32,160},{40,168},{48,176},{56,1... | collective-permute-start | bytes 6152 | tf_op jit(solution)/shard_map/ppermute | solution.py:25
  70.8 3.4 %copy-start.2 = (s32[512,1]{1,0:T(8,128)}, s32[512,1]{1,0:T(8,128)S(1)}, u32[]{:S(2)}) copy-start(s32[512,1]{1,0:T(8,128)S(1)} %copy.32.ids_own) | copy-start | bytes 6148
  71.6 2.6 %copy-start.6 = (bf16[512,512]{1,0:T(8,128)(2,1)}, bf16[512,512]{1,0:T(8,128)(2,1)S(1)}, u32[]{:S(2)}) copy-start(bf16[512,512]{1,0:T(8,128)(2,1)S(1)} %collective-permute-done.3.refs_0_) | copy-start | bytes 1572868
  74.8 34.8 %copy-start.7 = (bf16[512,512]{1,0:T(8,128)(2,1)S(1)}, bf16[512,512]{1,0:T(8,128)(2,1)}, u32[]{:S(2)}) copy-start(bf16[512,512]{1,0:T(8,128)(2,1)} %param.9) | copy-start | bytes 1572868
  74.8 34.8 %copy-start.8 = (bf16[512,512]{1,0:T(8,128)(2,1)S(1)}, bf16[512,512]{1,0:T(8,128)(2,1)}, u32[]{:S(2)}) copy-start(bf16[512,512]{1,0:T(8,128)(2,1)} %param.8) | copy-start | bytes 1572868
  74.8 34.8 %copy-start.10 = (bf16[512,512]{1,0:T(8,128)(2,1)S(1)}, bf16[512,512]{1,0:T(8,128)(2,1)}, u32[]{:S(2)}) copy-start(bf16[512,512]{1,0:T(8,128)(2,1)} %param.7) | copy-start | bytes 1572868
  74.8 34.8 %copy-start.12 = (bf16[512,512]{1,0:T(8,128)(2,1)S(1)}, bf16[512,512]{1,0:T(8,128)(2,1)}, u32[]{:S(2)}) copy-start(bf16[512,512]{1,0:T(8,128)(2,1)} %param.10) | copy-start | bytes 1572868
  99.3 14.9 %all-to-all-start.1 = ((f32[8,1,8]{2,1,0:T(1,128)}), f32[8,1,8]{2,1,0:T(1,128)S(1)}, u32[]{:S(2)}, u32[]{:S(2)}) async-start(f32[8,1,8]{2,1,0:T(1,128)} %bitcast.6), calls=%async_computation.1 | async-start | bytes 8192 | tf_op jit(solution)/shard_map/all_to_all | solution.py:195
